TPU v7x, 512 devices: a whole 4x8x8 slice. The times are simulated.
512 devices in a mesh: tensor: 16 (over z_lo, x, core), dp: 32 (over y, z_hi).
Axes of the slice: x: 4, y: 8, z: 8 (z_hi: 4, z_lo: 2; z = z_hi * 2 + z_lo), core: 2. Of those that a mesh axis runs over, the one named last changes fastest.
Arguments:
- activations: bfloat16 [4096, 4096], P('dp', 'tensor'), may hold values from -6 to 6
- out_grad: bfloat16 [4096, 4096], P('dp', 'tensor'), may hold values from -6 to 6
- up_blocks: bfloat16 [1024, 128, 128], P(('tensor', 'dp')), may hold values from -0.1875 to 0.1875
- up_rows: int32 [1024], P('tensor'), may hold values from 0 to 31, as said below
- down_blocks: bfloat16 [1024, 128, 128], P(('tensor', 'dp')), may hold values from -0.09375 to 0.09375
- down_rows: int32 [1024], P('tensor'), may hold values from 0 to 31, as said below
Outputs:
- output: bfloat16 [4096, 4096], P('dp')
- input_grad: bfloat16 [4096, 4096], P('dp')
- up_grad: bfloat16 [1024, 128, 128], P(('tensor', 'dp'))
- down_grad: bfloat16 [1024, 128, 128], P(('tensor', 'dp'))
Inputs may be any that keep to these rules, and one draw needn't show every extreme that they name: `up_rows`: entry b is the input row block of up block b, whose hidden block is b // 8; the 8 entries of one hidden block are distinct; every row block is named by 32 entries. `down_rows`: entry b is the output block of down block b, whose hidden block is b // 8; the 8 entries of one hidden block are distinct; every output block is named by 32 entries.
All inputs are finite; a program needn't handle non-finite values.
Results may differ from a plain program's by a relative error of at most 0.022.
Values may be sent and summed in bfloat16 or wider, within the bound.
No kernel may reach another device: no remote copies, remote signals or barrier semaphores. Data moves between devices by JAX's collectives and lax.ppermute only.
A program may use at most 64 MiB of HBM per device.

v0:
```python
import math

import jax
import jax.numpy as jnp
from jax import lax
from jax.sharding import PartitionSpec as P

K = 8


def normal_cdf(value):
    return 0.5 * (1.0 + jax.scipy.special.erf(value * 0.7071067811865476))


def gelu_slope(value):
    return normal_cdf(value) + value * jnp.exp(-0.5 * value * value) * 0.3989422804014327


def per_device(activations, out_grad, up_blocks, up_rows, down_blocks, down_rows):
    block_size = up_blocks.shape[1]
    groups = up_rows.shape[0] // K
    full_input = lax.all_gather(activations, "tensor", axis=1, tiled=True)
    up_all, down_all = (
        lax.all_gather(up_blocks, "dp", axis=0, tiled=True),
        lax.all_gather(down_blocks, "dp", axis=0, tiled=True),
    )
    tokens = full_input.shape[0]
    width = full_input.shape[1]
    row_blocks = width // block_size
    scale = 1.0 / math.sqrt(tokens * lax.axis_size("dp"))
    up_tiles = up_all.reshape(groups, K, block_size, block_size)
    down_tiles = down_all.reshape(groups, K, block_size, block_size)
    up_index = up_rows.reshape(groups, K)
    down_index = down_rows.reshape(groups, K)
    picked_in = full_input.reshape(tokens, row_blocks, block_size)[:, up_index]
    preact = jnp.einsum("tgki,gkio->tgo", picked_in, up_tiles, preferred_element_type=jnp.float32)
    hidden = (preact * normal_cdf(preact)).astype(jnp.bfloat16)
    product = jnp.einsum("tgh,gkho->tgko", hidden, down_tiles, preferred_element_type=jnp.float32)
    out_start = jnp.zeros((tokens, row_blocks, block_size), jnp.float32)
    out_part = (
        out_start.at[:, down_rows]
        .add(product.reshape(tokens, groups * K, block_size))
        .reshape(tokens, width)
    )
    output = lax.psum(out_part.astype(jnp.bfloat16), "tensor")
    full_grad = lax.all_gather(out_grad, "tensor", axis=1, tiled=True)
    picked_grad = full_grad.reshape(tokens, row_blocks, block_size)[:, down_index]
    down_term = (
        jnp.einsum("tgh,tgko->gkho", hidden, picked_grad, preferred_element_type=jnp.float32)
        * scale
    )
    down_term = down_term.reshape(groups * K, block_size, block_size)
    hidden_grad = jnp.einsum(
        "tgko,gkho->tgh", picked_grad, down_tiles, preferred_element_type=jnp.float32
    )
    preact_grad = (hidden_grad * gelu_slope(preact)).astype(jnp.bfloat16)
    back = jnp.einsum("tgo,gkio->tgki", preact_grad, up_tiles, preferred_element_type=jnp.float32)
    in_start = jnp.zeros((tokens, row_blocks, block_size), jnp.float32)
    in_part = (
        in_start.at[:, up_rows]
        .add(back.reshape(tokens, groups * K, block_size))
        .reshape(tokens, width)
    )
    input_grad = lax.psum(in_part.astype(jnp.bfloat16), "tensor")
    up_term = (
        jnp.einsum("tgki,tgo->gkio", picked_in, preact_grad, preferred_element_type=jnp.float32)
        * scale
    )
    up_term = up_term.reshape(groups * K, block_size, block_size)
    up_sum, down_sum = (
        lax.psum_scatter(
            up_term.astype(jnp.bfloat16), "dp", scatter_dimension=0, tiled=True
        ).astype(jnp.float32),
        lax.psum_scatter(
            down_term.astype(jnp.bfloat16), "dp", scatter_dimension=0, tiled=True
        ).astype(jnp.float32),
    )
    return (output, input_grad, up_sum.astype(jnp.bfloat16), down_sum.astype(jnp.bfloat16))


def solution(mesh):
    placed = (
        P("dp", "tensor"),
        P("dp", "tensor"),
        P(("tensor", "dp"), None, None),
        P("tensor"),
        P(("tensor", "dp"), None, None),
        P("tensor"),
    )
    return jax.shard_map(
        per_device,
        mesh=mesh,
        in_specs=placed,
        out_specs=(
            P("dp", None),
            P("dp", None),
            P(("tensor", "dp"), None, None),
            P(("tensor", "dp"), None, None),
        ),
        check_vma=False,
    )
```

profile of v0, /device:TPU:6, one launch (start us, length us, event | category | flops | bytes accessed | tf_op | source)
XLA Modules:
  0.0 908.6 jit_solution(15931236211702621775)
XLA Ops:
  7.2 0.0 all-gather.5.cloned.1.call-start
  7.2 1.6 copy.37
  8.8 0.0 all-gather.11.cloned.1.call-start
  8.9 1.6 copy.42
  10.5 0.0 all-gather.7.cloned.1.call-start
  10.5 0.7 all-gather.7.cloned.1.call-update
  11.2 0.0 all-gather.9.cloned.1.call-start
  11.2 0.5 all-gather.9.cloned.1.call-update
  11.8 0.0 all-reduce.3.cloned.1.call-start
  11.8 0.7 reshape.97
  12.6 0.1 reshape.106
  12.6 0.7 reshape.102
  13.4 0.1 reshape.114
  13.5 0.7 compare_select_fusion.3
  14.2 0.7 compare_select_fusion.2
  14.8 37.5 %all-gather.5.cloned.1.call-done = bf16[128,4096]{0,1:T(8,128)(2,1)} async-done(((bf16[128,256]{0,1:T(8,128)(2,1)}), bf16[128,4096]{0,1:T(8,128)(2,1)}) %all-gather.5.cloned.1.call-update) | async-done | bytes 1048592 | tf_op jit(solution)/shard_map/all_gather | solution.py:22
  52.3 1.6 copy.38
  53.9 39.0 %all-gather.11.cloned.1.call-done = bf16[128,4096]{0,1:T(8,128)(2,1)} async-done(((bf16[128,256]{0,1:T(8,128)(2,1)}), bf16[128,4096]{0,1:T(8,128)(2,1)}) %all-gather.11.cloned.1.call-update) | async-done | bytes 1048592 | tf_op jit(solution)/shard_map/all_gather | solution.py:46
  92.9 2.3 copy.43
  95.2 0.9 gather_fusion
  96.1 4.1 gather_fusion.1
  100.3 84.3 %all-gather.7.cloned.1.call-done = bf16[64,128,128]{2,1,0:T(8,128)(2,1)} async-done(((bf16[2,128,128]{2,1,0:T(8,128)(2,1)}), bf16[64,128,128]{2,1,0:T(8,128)(2,1)}) %all-gather.7.cloned.1.call-update) | async-done | bytes 2097168 | tf_op jit(solution)/shard_map/all_gather | solution.py:24
  184.5 2.3 convolution_bitcast_fusion.1
  186.8 83.7 %all-gather.9.cloned.1.call-done = bf16[64,128,128]{2,1,0:T(8,128)(2,1)} async-done(((bf16[2,128,128]{2,1,0:T(8,128)(2,1)}), bf16[64,128,128]{2,1,0:T(8,128)(2,1)}) %all-gather.9.cloned.1.call-update) | async-done | bytes 2097168 | tf_op jit(solution)/shard_map/all_gather | solution.py:25
  270.6 4.2 fusion.11
  274.8 0.2 broadcast.57.clone
  275.0 8.8 scatter_fusion
  283.8 1.1 convert_element_type.38
  285.0 2.4 copy.41
  287.4 2.5 fusion.4
  289.9 2.7 fusion.13
  292.5 0.2 broadcast.57.clone.1
  292.8 8.8 scatter_fusion.1
  301.6 1.1 convert_element_type.41
  302.7 2.4 copy.46
  305.2 0.0 reduce-scatter.3.cloned.1.call-start
  305.2 2.6 copy.39
  307.8 3.6 multiply_convert_fusion.1
  311.5 0.0 reduce-scatter.5.cloned.1.call-start
  311.5 1.5 copy-done.4
  313.1 2.6 copy.44
  315.7 2.3 multiply_convert_fusion
  318.0 2.9 copy.47
  320.9 110.6 %all-reduce.3.cloned.1.call-done = (bf16[128,4096]{0,1:T(8,128)(2,1)}, bf16[128,4096]{0,1:T(8,128)(2,1)}) async-done(((bf16[128,4096]{0,1:T(8,128)(2,1)}, bf16[128,4096]{0,1:T(8,128)(2,1)}), (bf16[128,4096]{0,1:T(8,128)(2,1)}, bf16[128,4096]{0,1:T(8,128)(2,1)})) %all-reduce.3.cloned.1.call-update) | async-done | bytes 2097168 | tf_op jit(solution)/shard_map/psum | solution.py:45
  431.5 2.4 copy.48
  433.9 1.3 copy.49
  435.2 234.6 %reduce-scatter.3.cloned.1.call-done = bf16[2,128,128]{2,1,0:T(8,128)(2,1)} async-done(((bf16[64,128,128]{2,1,0:T(8,128)(2,1)}), bf16[2,128,128]{2,1,0:T(8,128)(2,1)}) %reduce-scatter.3.cloned.1.call-update) | async-done | bytes 65552 | tf_op jit(solution)/shard_map/reduce_scatter | solution.py:71
  669.8 232.0 %reduce-scatter.5.cloned.1.call-done = bf16[2,128,128]{2,1,0:T(8,128)(2,1)} async-done(((bf16[64,128,128]{2,1,0:T(8,128)(2,1)}), bf16[2,128,128]{2,1,0:T(8,128)(2,1)}) %reduce-scatter.5.cloned.1.call-update) | async-done | bytes 65552 | tf_op jit(solution)/shard_map/reduce_scatter | solution.py:74
  (20 shorter events, 0.1 us)
Async XLA Ops:
  7.2 45.1 %all-gather.5.cloned.1.call-start = ((), (), s32[]{:S(2)}) async-start(), calls=%async_computation.2 | async-start | bytes 1114112 | tf_op jit(solution)/shard_map/all_gather | solution.py:22
  8.8 84.1 %all-gather.11.cloned.1.call-start = ((), (), s32[]{:S(2)}) async-start(), calls=%async_computation.5 | async-start | bytes 1114112 | tf_op jit(solution)/shard_map/all_gather | solution.py:46
  10.5 174.1 %all-gather.7.cloned.1.call-start = ((), (), s32[]{:S(2)}) async-start(), calls=%async_computation.3 | async-start | bytes 2162688 | tf_op jit(solution)/shard_map/all_gather | solution.py:24
  11.2 259.4 %all-gather.9.cloned.1.call-start = ((), (), s32[]{:S(2)}) async-start(), calls=%async_computation.4 | async-start | bytes 2162688 | tf_op jit(solution)/shard_map/all_gather | solution.py:25
  11.8 419.8 %all-reduce.3.cloned.1.call-start = ((), (), s32[]{:S(2)}) async-start(), calls=%async_computation.8 | async-start | bytes 4194304 | tf_op jit(solution)/shard_map/psum | solution.py:45
  96.1 88.4 %copy-start = (bf16[64,128,128]{2,1,0:T(8,128)(2,1)}, bf16[64,128,128]{2,1,0:T(8,128)(2,1)S(1)}, u32[]{:S(2)}) copy-start(bf16[64,128,128]{2,1,0:T(8,128)(2,1)S(1)} %gather_fusion) | copy-start | bytes 6291460
  285.0 2.4 copy-start.3
  287.4 2.5 copy-start.2
  302.7 2.5 copy-start.1
  305.2 364.6 %reduce-scatter.3.cloned.1.call-start = ((), (), s32[]{:S(2)}) async-start(), calls=%async_computation.6 | async-start | bytes 2162688 | tf_op jit(solution)/shard_map/reduce_scatter | solution.py:71
  311.5 1.6 copy-start.4
  311.5 590.3 %reduce-scatter.5.cloned.1.call-start = ((), (), s32[]{:S(2)}) async-start(), calls=%async_computation.7 | async-start | bytes 2162688 | tf_op jit(solution)/shard_map/reduce_scatter | solution.py:74
  431.5 2.4 copy-start.5
Sparse Core Ops, SparseCore 0:
  10.7 41.5 all-gather.4
  55.0 37.8 all-gather.10
  96.1 88.4 all-gather.6
  187.6 82.9 all-gather.8
  305.3 126.1 all-reduce.2
  436.4 233.3 reduce-scatter.2
  675.5 226.2 reduce-scatter.4
where the time goes:
time: 909 us
  waiting for transfers between devices  823 us (91%)
  local copies, waits for them, and re-layouts  32.3 us (4%)
  other arithmetic  21.2 us (2%)
  matrix products  17.6 us (2%)
  between operations  14.2 us (2%)
    reduce_scatter x1, waiting for transfers between devices, per_device(): lax.psum_scatter(up_term.astype(jnp.bfloat16), 'dp', scatter_dimension=0,...  235 us
    reduce_scatter x1, waiting for transfers between devices, per_device(): lax.psum_scatter(down_term.astype(jnp.bfloat16), 'dp', scatter_dimension=...  232 us
    psum x1, waiting for transfers between devices, per_device(): output = lax.psum(out_part.astype(jnp.bfloat16), 'tensor')  111 us
    all_gather x1, waiting for transfers between devices, per_device(): lax.all_gather(up_blocks, 'dp', axis=0, tiled=True)  84.3 us
    all_gather x1, waiting for transfers between devices, per_device(): lax.all_gather(down_blocks, 'dp', axis=0, tiled=True)  83.7 us
    all_gather x1, waiting for transfers between devices, per_device(): full_grad = lax.all_gather(out_grad, 'tensor', axis=1, tiled=True)  39 us
    all_gather x1, waiting for transfers between devices, per_device(): full_input = lax.all_gather(activations, 'tensor', axis=1, tiled=True)  37.5 us
  transfers between devices with their start and end apart: 7, of which 7 were waited for; matrix products, arithmetic and copies ran while one was open for 4% of the time, Pallas kernels for 0%

commit v1 on v0

v1 whole, which is shorter than its diff:
```python
import math

import jax
import jax.numpy as jnp
from jax import lax
from jax.sharding import PartitionSpec as P

K = 8


def normal_cdf(value):
    return 0.5 * (1.0 + jax.scipy.special.erf(value * 0.7071067811865476))


def gelu_slope(value):
    return normal_cdf(value) + value * jnp.exp(-0.5 * value * value) * 0.3989422804014327


def gather_all(x, axis_name):
    n = lax.axis_size(axis_name)
    spread = jnp.broadcast_to(x[None], (n,) + x.shape)
    return lax.all_to_all(spread, axis_name, 0, 0, tiled=True)


def scatter_sum(x, axis_name):
    got = lax.all_to_all(x, axis_name, 0, 0, tiled=True)
    return got.astype(jnp.float32).sum(axis=0).astype(jnp.bfloat16)


def per_device(activations, out_grad, up_blocks, up_rows, down_blocks, down_rows):
    block_size = up_blocks.shape[1]
    groups = up_rows.shape[0] // K
    n_tensor = lax.axis_size("tensor")
    n_dp = lax.axis_size("dp")
    tokens = activations.shape[0]
    shard_width = activations.shape[1]
    width = shard_width * n_tensor
    row_blocks = width // block_size

    feats = gather_all(jnp.stack([activations, out_grad]), "tensor")
    feats = jnp.moveaxis(feats, 0, 2).reshape(2, tokens, width)
    full_input, full_grad = feats[0], feats[1]
    weights = gather_all(jnp.stack([up_blocks, down_blocks]), "dp")
    weights = jnp.moveaxis(weights, 1, 0).reshape(2, -1, block_size, block_size)
    up_all, down_all = weights[0], weights[1]

    scale = 1.0 / math.sqrt(tokens * n_dp)
    up_tiles = up_all.reshape(groups, K, block_size, block_size)
    down_tiles = down_all.reshape(groups, K, block_size, block_size)
    up_index = up_rows.reshape(groups, K)
    down_index = down_rows.reshape(groups, K)
    picked_in = full_input.reshape(tokens, row_blocks, block_size)[:, up_index]
    preact = jnp.einsum("tgki,gkio->tgo", picked_in, up_tiles, preferred_element_type=jnp.float32)
    hidden = (preact * normal_cdf(preact)).astype(jnp.bfloat16)
    product = jnp.einsum("tgh,gkho->tgko", hidden, down_tiles, preferred_element_type=jnp.float32)
    out_start = jnp.zeros((tokens, row_blocks, block_size), jnp.float32)
    out_part = out_start.at[:, down_rows].add(product.reshape(tokens, groups * K, block_size))
    picked_grad = full_grad.reshape(tokens, row_blocks, block_size)[:, down_index]
    down_term = (
        jnp.einsum("tgh,tgko->gkho", hidden, picked_grad, preferred_element_type=jnp.float32)
        * scale
    )
    hidden_grad = jnp.einsum(
        "tgko,gkho->tgh", picked_grad, down_tiles, preferred_element_type=jnp.float32
    )
    preact_grad = (hidden_grad * gelu_slope(preact)).astype(jnp.bfloat16)
    back = jnp.einsum("tgo,gkio->tgki", preact_grad, up_tiles, preferred_element_type=jnp.float32)
    in_start = jnp.zeros((tokens, row_blocks, block_size), jnp.float32)
    in_part = in_start.at[:, up_rows].add(back.reshape(tokens, groups * K, block_size))
    up_term = (
        jnp.einsum("tgki,tgo->gkio", picked_in, preact_grad, preferred_element_type=jnp.float32)
        * scale
    )

    parts = jnp.stack([out_part, in_part]).astype(jnp.bfloat16)
    parts = parts.reshape(2, tokens, n_tensor, shard_width)
    mine = scatter_sum(jnp.moveaxis(parts, 2, 0), "tensor")
    both = gather_all(mine, "tensor")
    both = jnp.moveaxis(both, 0, 2).reshape(2, tokens, width)

    terms = jnp.stack([up_term, down_term]).astype(jnp.bfloat16)
    terms = terms.reshape(2, n_dp, -1, block_size, block_size)
    grads = scatter_sum(jnp.moveaxis(terms, 1, 0), "dp")
    return (both[0], both[1], grads[0], grads[1])


def solution(mesh):
    placed = (
        P("dp", "tensor"),
        P("dp", "tensor"),
        P(("tensor", "dp"), None, None),
        P("tensor"),
        P(("tensor", "dp"), None, None),
        P("tensor"),
    )
    return jax.shard_map(
        per_device,
        mesh=mesh,
        in_specs=placed,
        out_specs=(
            P("dp", None),
            P("dp", None),
            P(("tensor", "dp"), None, None),
            P(("tensor", "dp"), None, None),
        ),
        check_vma=False,
    )
```

time: 909 us -> 457 us (0.50)
  the two profiles are of different devices: /device:TPU:6 before, /device:TPU:350 now
where the time goes in v1:
time: 457 us; the launch traced here: 456 us
  waiting for transfers between devices  280 us (61%)
  local copies, waits for them, and re-layouts  52.2 us (11%)
  starting transfers between devices  45.2 us (10%)
  blocking collectives  41.6 us (9%)
  other arithmetic  26.6 us (6%)
  matrix products  9.83 us (2%)
    all_to_all x3, waiting for transfers between devices, gather_all(): return lax.all_to_all(spread, axis_name, 0, 0, tiled=True)  151 us
    all_to_all x1, waiting for transfers between devices, scatter_sum(): got = lax.all_to_all(x, axis_name, 0, 0, tiled=True)  128 us
    all_to_all x1, blocking collectives, scatter_sum(): got = lax.all_to_all(x, axis_name, 0, 0, tiled=True)  41.6 us
    all_to_all x3, starting transfers between devices, gather_all(): return lax.all_to_all(spread, axis_name, 0, 0, tiled=True)  25.8 us
    all_to_all x1, starting transfers between devices, scatter_sum(): got = lax.all_to_all(x, axis_name, 0, 0, tiled=True)  19.4 us
  transfers between devices with their start and end apart: 4, of which 4 were waited for; matrix products, arithmetic and copies ran while one was open for 7% of the time, Pallas kernels for 0%

profile of v1, /device:TPU:350, one launch (start us, length us, event | category | flops | bytes accessed | tf_op | source)
XLA Modules:
  0.0 455.9 jit_solution(17401433427666723816)
XLA Ops:
  0.6 0.9 pad_maximum_fusion.1
  1.6 1.8 broadcast_in_dim.12
  3.5 5.8 %all-to-all-start.1 = ((bf16[16,2,128,256]{2,3,1,0:T(8,128)(2,1)}), bf16[16,2,128,256]{2,3,1,0:T(8,128)(2,1)S(1)}, u32[]{:S(2)}, u32[]{:S(2)}) async-start(bf16[16,2,128,256]{2,3,1,0:T(8,128)(2,1)} %broadcast_in_dim.12), calls=%async_computation.1 | async-start | bytes 4194304 | tf_op jit(solution)/shard_map/all_to_all | solution.py:22
  9.5 28.7 %all-to-all-done.1 = bf16[16,2,128,256]{2,3,1,0:T(8,128)(2,1)S(1)} async-done(((bf16[16,2,128,256]{2,3,1,0:T(8,128)(2,1)}), bf16[16,2,128,256]{2,3,1,0:T(8,128)(2,1)S(1)}, u32[]{:S(2)}, u32[]{:S(2)}) %all-to-all-start.1) | async-done | bytes 2097184 | tf_op jit(solution)/shard_map/all_to_all | solution.py:22
  38.1 3.0 broadcast_in_dim.11
  41.2 12.5 %all-to-all-start = ((bf16[32,2,2,128,128]{3,4,2,1,0:T(8,128)(2,1)}), bf16[32,2,2,128,128]{3,4,2,1,0:T(8,128)(2,1)}, u32[]{:S(2)}, u32[]{:S(2)}) async-start(bf16[32,2,2,128,128]{3,4,2,1,0:T(8,128)(2,1)} %broadcast_in_dim.11), calls=%async_computation | async-start | bytes 8388608 | tf_op jit(solution)/shard_map/all_to_all | solution.py:22
  54.4 0.7 copy.68
  55.0 1.3 copy.74
  56.4 0.9 gather_fusion
  57.3 4.1 gather_fusion.1
  61.4 109.7 %all-to-all-done = bf16[32,2,2,128,128]{3,4,2,1,0:T(8,128)(2,1)} async-done(((bf16[32,2,2,128,128]{3,4,2,1,0:T(8,128)(2,1)}), bf16[32,2,2,128,128]{3,4,2,1,0:T(8,128)(2,1)}, u32[]{:S(2)}, u32[]{:S(2)}) %all-to-all-start) | async-done | bytes 4194336 | tf_op jit(solution)/shard_map/all_to_all | solution.py:22
  171.2 2.7 fusion.13
  173.9 0.7 convolution_bitcast_fusion.1
  174.7 2.7 fusion.11
  177.3 0.9 fusion.4
  178.2 2.8 fusion.16
  181.0 5.6 %copy.80 = f32[128,64,128]{2,0,1:T(8,128)} copy(f32[128,64,128]{0,2,1:T(8,128)} %bitcast.101) | data formatting | bytes 8388608 | tf_op jit(solution)/shard_map/reshape | solution.py:69
  186.6 0.2 broadcast.60.clone
  186.8 8.8 %scatter_fusion.1 = f32[128,32,128]{2,0,1:T(8,128)S(1)} fusion(f32[128,32,128]{2,0,1:T(8,128)S(1)} %broadcast.60.clone, s32[64]{0:T(128)S(1)} %compare_select_fusion.2, f32[64,128,128]{2,1,0:T(8,128)} %bitcast.100), kind=kCustom, calls=%fused_computation.3 | custom fusion | flops 1048576 | bytes 12583168 | tf_op jit(solution)/shard_map/scatter-add | solution.py:69
  195.7 1.1 convert.20
  196.8 2.3 copy.81
  199.1 5.6 %copy.72 = f32[128,64,128]{2,0,1:T(8,128)} copy(f32[128,64,128]{0,2,1:T(8,128)} %bitcast.102) | data formatting | bytes 8388608 | tf_op jit(solution)/shard_map/reshape | solution.py:57
  204.7 0.2 broadcast.60.clone.1
  204.9 8.8 %scatter_fusion = f32[128,32,128]{2,0,1:T(8,128)S(1)} fusion(f32[128,32,128]{2,0,1:T(8,128)S(1)} %broadcast.60.clone.1, s32[64]{0:T(128)S(1)} %compare_select_fusion.3, f32[64,128,128]{2,1,0:T(8,128)} %bitcast.99), kind=kCustom, calls=%fused_computation.2 | custom fusion | flops 1048576 | bytes 12583168 | tf_op jit(solution)/shard_map/scatter-add | solution.py:57
  213.7 1.1 convert.19
  214.9 1.7 copy.73
  216.6 0.2 maximum_bitcast_fusion.1
  216.8 0.2 copy.82
  217.0 41.6 %all_to_all.25 = bf16[16,2,128,256]{2,3,1,0:T(8,128)(2,1)S(1)} all-to-all(bf16[16,2,128,256]{2,3,1,0:T(8,128)(2,1)S(1)} %copy.82), channel_id=1, replica_groups=mesh['tensor'=16,'dp'=32] {'tensor'}, dimensions={0} | all-to-all | bytes 4194304 | tf_op jit(solution)/shard_map/all_to_all | solution.py:26
  258.7 0.3 reduce_sum.24
  259.1 1.6 broadcast_in_dim.14
  260.7 7.4 %all-to-all-start.3 = ((bf16[16,2,128,256]{3,2,1,0:T(8,128)(2,1)}), bf16[16,2,128,256]{3,2,1,0:T(8,128)(2,1)}, u32[]{:S(2)}, u32[]{:S(2)}) async-start(bf16[16,2,128,256]{3,2,1,0:T(8,128)(2,1)} %broadcast_in_dim.14), calls=%async_computation.3 | async-start | bytes 4194304 | tf_op jit(solution)/shard_map/all_to_all | solution.py:22
  268.1 2.6 copy.69
  270.7 3.0 copy.75
  273.7 2.1 multiply_convert_fusion
  275.8 4.2 copy.89
  280.0 0.7 multiply_convert_fusion.1
  280.7 0.9 copy-done.4
  281.6 2.3 maximum_bitcast_fusion
  283.9 12.8 %all-to-all-done.3 = bf16[16,2,128,256]{3,2,1,0:T(8,128)(2,1)} async-done(((bf16[16,2,128,256]{3,2,1,0:T(8,128)(2,1)}), bf16[16,2,128,256]{3,2,1,0:T(8,128)(2,1)}, u32[]{:S(2)}, u32[]{:S(2)}) %all-to-all-start.3) | async-done | bytes 2097184 | tf_op jit(solution)/shard_map/all_to_all | solution.py:22
  296.7 19.4 %all-to-all-start.4 = ((bf16[32,2,2,128,128]{4,3,2,1,0:T(8,128)(2,1)}), bf16[32,2,2,128,128]{4,3,2,1,0:T(8,128)(2,1)}, u32[]{:S(2)}, u32[]{:S(2)}) async-start(bf16[32,2,2,128,128]{4,3,2,1,0:T(8,128)(2,1)} %maximum_bitcast_fusion), calls=%async_computation.4 | async-start | bytes 8388608 | tf_op jit(solution)/shard_map/all_to_all | solution.py:26
  316.1 3.0 copy.85
  319.1 1.2 fusion.14
  320.3 2.3 copy.90
  322.6 1.3 copy.91
  323.9 128.4 %all-to-all-done.4 = bf16[32,2,2,128,128]{4,3,2,1,0:T(8,128)(2,1)} async-done(((bf16[32,2,2,128,128]{4,3,2,1,0:T(8,128)(2,1)}), bf16[32,2,2,128,128]{4,3,2,1,0:T(8,128)(2,1)}, u32[]{:S(2)}, u32[]{:S(2)}) %all-to-all-start.4) | async-done | bytes 4194336 | tf_op jit(solution)/shard_map/all_to_all | solution.py:26
  452.2 3.0 reduce_sum.25
  455.2 0.7 slice_bitcast_fusion
  (35 shorter events, 1.1 us)
Async XLA Ops:
  3.5 5.8 %copy-start.6 = (bf16[2,128,128]{2,1,0:T(8,128)(2,1)S(1)}, bf16[2,128,128]{2,1,0:T(8,128)(2,1)}, u32[]{:S(2)}) copy-start(bf16[2,128,128]{2,1,0:T(8,128)(2,1)} %param.10) | copy-start | bytes 196612
  3.5 5.8 %copy-start.7 = (bf16[2,128,128]{2,1,0:T(8,128)(2,1)S(1)}, bf16[2,128,128]{2,1,0:T(8,128)(2,1)}, u32[]{:S(2)}) copy-start(bf16[2,128,128]{2,1,0:T(8,128)(2,1)} %param.8) | copy-start | bytes 196612
  3.5 34.7 %all-to-all-start.1 = ((bf16[16,2,128,256]{2,3,1,0:T(8,128)(2,1)}), bf16[16,2,128,256]{2,3,1,0:T(8,128)(2,1)S(1)}, u32[]{:S(2)}, u32[]{:S(2)}) async-start(bf16[16,2,128,256]{2,3,1,0:T(8,128)(2,1)} %broadcast_in_dim.12), calls=%async_computation.1 | async-start | bytes 4194304 | tf_op jit(solution)/shard_map/all_to_all | solution.py:22
  41.2 12.5 %copy-start.8 = (s32[64]{0:T(128)S(1)}, s32[64]{0:T(128)}, u32[]{:S(2)}) copy-start(s32[64]{0:T(128)} %param.9) | copy-start | bytes 772
  41.2 12.7 %copy-start.9 = (s32[64]{0:T(128)S(1)}, s32[64]{0:T(128)}, u32[]{:S(2)}) copy-start(s32[64]{0:T(128)} %param.11) | copy-start | bytes 772
  41.2 130.0 %all-to-all-start = ((bf16[32,2,2,128,128]{3,4,2,1,0:T(8,128)(2,1)}), bf16[32,2,2,128,128]{3,4,2,1,0:T(8,128)(2,1)}, u32[]{:S(2)}, u32[]{:S(2)}) async-start(bf16[32,2,2,128,128]{3,4,2,1,0:T(8,128)(2,1)} %broadcast_in_dim.11), calls=%async_computation | async-start | bytes 8388608 | tf_op jit(solution)/shard_map/all_to_all | solution.py:22
  57.3 116.6 %copy-start = (bf16[64,128,128]{2,1,0:T(8,128)(2,1)}, bf16[64,128,128]{2,1,0:T(8,128)(2,1)S(1)}, u32[]{:S(2)}) copy-start(bf16[64,128,128]{2,1,0:T(8,128)(2,1)S(1)} %gather_fusion) | copy-start | bytes 6291460
  174.6 2.7 copy-start.2
  214.9 1.7 copy-start.5
  260.7 7.4 %copy-start.1 = (bf16[64,128,128]{2,1,0:T(8,128)(2,1)S(1)}, bf16[64,128,128]{2,1,0:T(8,128)(2,1)}, u32[]{:S(2)}) copy-start(bf16[64,128,128]{2,1,0:T(8,128)(2,1)} %copy-done) | copy-start | bytes 6291460
  260.7 36.0 %all-to-all-start.3 = ((bf16[16,2,128,256]{3,2,1,0:T(8,128)(2,1)}), bf16[16,2,128,256]{3,2,1,0:T(8,128)(2,1)}, u32[]{:S(2)}, u32[]{:S(2)}) async-start(bf16[16,2,128,256]{3,2,1,0:T(8,128)(2,1)} %broadcast_in_dim.14), calls=%async_computation.3 | async-start | bytes 4194304 | tf_op jit(solution)/shard_map/all_to_all | solution.py:22
  275.8 4.2 copy-start.3
  280.0 1.6 copy-start.4
  296.7 155.6 %all-to-all-start.4 = ((bf16[32,2,2,128,128]{4,3,2,1,0:T(8,128)(2,1)}), bf16[32,2,2,128,128]{4,3,2,1,0:T(8,128)(2,1)}, u32[]{:S(2)}, u32[]{:S(2)}) async-start(bf16[32,2,2,128,128]{4,3,2,1,0:T(8,128)(2,1)} %maximum_bitcast_fusion), calls=%async_computation.4 | async-start | bytes 8388608 | tf_op jit(solution)/shard_map/all_to_all | solution.py:26

commit v2 on v1

--- a/solution.py
+++ b/solution.py
@@ -27,6 +27,58 @@
     return got.astype(jnp.float32).sum(axis=0).astype(jnp.bfloat16)
 
 
+Z_HI = 4
+
+
+def dp_shift(n_y, n_z, dy, dz):
+    return [
+        (y * n_z + z, ((y + dy) % n_y) * n_z + (z + dz) % n_z)
+        for y in range(n_y)
+        for z in range(n_z)
+    ]
+
+
+def dp_gather_rel(x, n_y, n_z):
+    by_z = [x] + [lax.ppermute(x, "dp", dp_shift(n_y, n_z, 0, b)) for b in range(1, n_z)]
+    held = jnp.stack(by_z)
+    n_f, n_b = n_y // 2, (n_y - 1) // 2
+    fwd, bwd = [held], []
+    cur_f = cur_b = held
+    for k in range(1, n_f + 1):
+        cur_f = lax.ppermute(cur_f, "dp", dp_shift(n_y, n_z, 1, 0))
+        fwd.append(cur_f)
+        if k <= n_b:
+            cur_b = lax.ppermute(cur_b, "dp", dp_shift(n_y, n_z, -1, 0))
+            bwd.append(cur_b)
+    rel = fwd + [bwd[n_y - a - 1] for a in range(len(fwd), n_y)]
+    return jnp.stack(rel)
+
+
+def dp_scatter_rel(terms, n_y, n_z):
+    n_f, n_b = n_y // 2, (n_y - 1) // 2
+    got_f = got_b = None
+    for k in range(1, n_f + 1):
+        part = terms[(n_y - n_f - 1 + k) % n_y].astype(jnp.float32)
+        if got_f is not None:
+            part = part + got_f.astype(jnp.float32)
+        got_f = lax.ppermute(part.astype(jnp.bfloat16), "dp", dp_shift(n_y, n_z, 1, 0))
+    for k in range(1, n_b + 1):
+        part = terms[n_b + 1 - k].astype(jnp.float32)
+        if got_b is not None:
+            part = part + got_b.astype(jnp.float32)
+        got_b = lax.ppermute(part.astype(jnp.bfloat16), "dp", dp_shift(n_y, n_z, -1, 0))
+    acc = terms[0].astype(jnp.float32)
+    if got_f is not None:
+        acc = acc + got_f.astype(jnp.float32)
+    if got_b is not None:
+        acc = acc + got_b.astype(jnp.float32)
+    total = acc[0]
+    for b in range(1, n_z):
+        sent = lax.ppermute(acc[b].astype(jnp.bfloat16), "dp", dp_shift(n_y, n_z, 0, -b))
+        total = total + sent.astype(jnp.float32)
+    return total.astype(jnp.bfloat16)
+
+
 def per_device(activations, out_grad, up_blocks, up_rows, down_blocks, down_rows):
     block_size = up_blocks.shape[1]
     groups = up_rows.shape[0] // K
@@ -40,9 +92,22 @@
     feats = gather_all(jnp.stack([activations, out_grad]), "tensor")
     feats = jnp.moveaxis(feats, 0, 2).reshape(2, tokens, width)
     full_input, full_grad = feats[0], feats[1]
-    weights = gather_all(jnp.stack([up_blocks, down_blocks]), "dp")
-    weights = jnp.moveaxis(weights, 1, 0).reshape(2, -1, block_size, block_size)
+    per_dev = up_blocks.shape[0]
+    n_z = Z_HI
+    n_y = n_dp // n_z
+    if n_z * per_dev != K:
+        raise ValueError("layout")
+    weights = dp_gather_rel(jnp.stack([up_blocks, down_blocks]), n_y, n_z)
+    weights = jnp.moveaxis(weights, 2, 0).reshape(2, -1, block_size, block_size)
     up_all, down_all = weights[0], weights[1]
+    me = lax.axis_index("dp")
+    my_y, my_z = me // n_z, me % n_z
+    a = jnp.arange(n_y, dtype=jnp.int32)[:, None, None]
+    b = jnp.arange(n_z, dtype=jnp.int32)[None, :, None]
+    r = jnp.arange(per_dev, dtype=jnp.int32)[None, None, :]
+    order = ((((my_y - a) % n_y) * n_z + (my_z - b) % n_z) * per_dev + r).reshape(-1)
+    up_rows = up_rows[order]
+    down_rows = down_rows[order]
 
     scale = 1.0 / math.sqrt(tokens * n_dp)
     up_tiles = up_all.reshape(groups, K, block_size, block_size)
@@ -79,8 +144,8 @@
     both = jnp.moveaxis(both, 0, 2).reshape(2, tokens, width)
 
     terms = jnp.stack([up_term, down_term]).astype(jnp.bfloat16)
-    terms = terms.reshape(2, n_dp, -1, block_size, block_size)
-    grads = scatter_sum(jnp.moveaxis(terms, 1, 0), "dp")
+    terms = terms.reshape(2, n_y, n_z, per_dev, block_size, block_size)
+    grads = dp_scatter_rel(jnp.moveaxis(terms, 0, 2), n_y, n_z)
     return (both[0], both[1], grads[0], grads[1])
 
 

time: 457 us -> 294 us (0.64)
  the two profiles are of different devices: /device:TPU:350 before, /device:TPU:6 now
where the time goes in v2:
time: 294 us; the launch traced here: 290 us
  starting transfers between devices  94.4 us (32%)
  waiting for transfers between devices  85.4 us (29%)
  local copies, waits for them, and re-layouts  58.7 us (20%)
  other arithmetic  34.5 us (12%)
  matrix products  15.4 us (5%)
    ppermute x3, waiting for transfers between devices, dp_scatter_rel(): lax.ppermute(part.astype(jnp.bfloat16), 'dp', dp_shift(n_y, n_z, -1, 0))  27.4 us
    ppermute x4, waiting for transfers between devices, dp_gather_rel(): cur_f = lax.ppermute(cur_f, 'dp', dp_shift(n_y, n_z, 1, 0))  25.3 us
    ppermute x4, waiting for transfers between devices, dp_scatter_rel(): lax.ppermute(part.astype(jnp.bfloat16), 'dp', dp_shift(n_y, n_z, 1, 0))  21.4 us
    ppermute x3, starting transfers between devices, dp_gather_rel(): lax.ppermute(x, 'dp', dp_shift(n_y, n_z, 0, b))  18.9 us
    ppermute x3, starting transfers between devices, dp_gather_rel(): cur_b = lax.ppermute(cur_b, 'dp', dp_shift(n_y, n_z, -1, 0))  16.3 us
    all_to_all x2, starting transfers between devices, gather_all(): return lax.all_to_all(spread, axis_name, 0, 0, tiled=True)  11.6 us
    ppermute x3, starting transfers between devices, dp_scatter_rel(): lax.ppermute(acc[b].astype(jnp.bfloat16), 'dp', dp_shift(n_y, n_z, 0, -b))  11.3 us
    ppermute x3, starting transfers between devices, dp_scatter_rel(): lax.ppermute(part.astype(jnp.bfloat16), 'dp', dp_shift(n_y, n_z, -1, 0))  10.5 us
  transfers between devices with their start and end apart: 23, of which 16 were waited for; matrix products, arithmetic and copies ran while one was open for 15% of the time, Pallas kernels for 0%

profile of v2, /device:TPU:6, one launch (start us, length us, event | category | flops | bytes accessed | tf_op | source)
XLA Modules:
  0.0 289.6 jit_solution(7542644848384703284)
XLA Ops:
  1.5 6.1 %collective-permute-start = (bf16[2,2,128,128]{3,2,1,0:T(8,128)(2,1)S(1)}, bf16[2,2,128,128]{3,2,1,0:T(8,128)(2,1)S(1)}, u32[]{:S(2)}, u32[]{:S(2)}) collective-permute-start(bf16[2,2,128,128]{3,2,1,0:T(8,128)(2,1)S(1)} %get-tuple-element.26), channel_id=1, source_target_pairs={{0,1},{1,2},{2,3},{3,0},{4,5},{5,6},{6,7},{7,4},{8,9},{9,10},{10,1... | collective-permute-start | bytes 393224 | tf_op jit(solution)/shard_map/ppermute | solution.py:42
  7.6 9.1 %collective-permute-start.1 = (bf16[2,2,128,128]{3,2,1,0:T(8,128)(2,1)S(1)}, bf16[2,2,128,128]{3,2,1,0:T(8,128)(2,1)S(1)}, u32[]{:S(2)}, u32[]{:S(2)}) collective-permute-start(bf16[2,2,128,128]{3,2,1,0:T(8,128)(2,1)S(1)} %get-tuple-element.26), channel_id=1, source_target_pairs={{0,2},{1,3},{2,0},{3,1},{4,6},{5,7},{6,4},{7,5},{8,10},{9,11},{10,... | collective-permute-start | bytes 393224 | tf_op jit(solution)/shard_map/ppermute | solution.py:42
  16.8 3.7 %collective-permute-start.2 = (bf16[2,2,128,128]{3,2,1,0:T(8,128)(2,1)S(1)}, bf16[2,2,128,128]{3,2,1,0:T(8,128)(2,1)S(1)}, u32[]{:S(2)}, u32[]{:S(2)}) collective-permute-start(bf16[2,2,128,128]{3,2,1,0:T(8,128)(2,1)S(1)} %get-tuple-element.26), channel_id=1, source_target_pairs={{0,3},{1,0},{2,1},{3,2},{4,7},{5,4},{6,5},{7,6},{8,11},{9,8},{10,9... | collective-permute-start | bytes 393224 | tf_op jit(solution)/shard_map/ppermute | solution.py:42
  23.3 5.8 %all-to-all-start = ((bf16[16,2,128,256]{2,3,1,0:T(8,128)(2,1)}), bf16[16,2,128,256]{2,3,1,0:T(8,128)(2,1)S(1)}, u32[]{:S(2)}, u32[]{:S(2)}) async-start(bf16[16,2,128,256]{2,3,1,0:T(8,128)(2,1)} %broadcast_in_dim.4), calls=%async_computation | async-start | bytes 4194304 | tf_op jit(solution)/shard_map/all_to_all | solution.py:22
  30.1 3.5 %collective-permute-start.3 = (bf16[4,2,2,128,128]{4,3,2,1,0:T(8,128)(2,1)S(1)}, bf16[4,2,2,128,128]{4,3,2,1,0:T(8,128)(2,1)S(1)}, u32[]{:S(2)}, u32[]{:S(2)}) collective-permute-start(bf16[4,2,2,128,128]{4,3,2,1,0:T(8,128)(2,1)S(1)} %pad_maximum_fusion), channel_id=1, source_target_pairs={{0,4},{1,5},{2,6},{3,7},{4,8},{5,9},{6,10},{7,11},{8,12},{9,13},{1... | collective-permute-start | bytes 1572872 | tf_op jit(solution)/shard_map/ppermute | solution.py:48
  35.2 12.4 %collective-permute-done.3 = bf16[4,2,2,128,128]{4,3,2,1,0:T(8,128)(2,1)S(1)} collective-permute-done((bf16[4,2,2,128,128]{4,3,2,1,0:T(8,128)(2,1)S(1)}, bf16[4,2,2,128,128]{4,3,2,1,0:T(8,128)(2,1)S(1)}, u32[]{:S(2)}, u32[]{:S(2)}) %collective-permute-start.3) | collective-permute-done | bytes 524320 | tf_op jit(solution)/shard_map/ppermute | solution.py:48
  47.6 1.9 collective-permute-start.4
  51.5 5.1 %collective-permute-start.7 = (bf16[4,2,2,128,128]{4,3,2,1,0:T(8,128)(2,1)}, bf16[4,2,2,128,128]{4,3,2,1,0:T(8,128)(2,1)S(1)}, u32[]{:S(2)}, u32[]{:S(2)}) collective-permute-start(bf16[4,2,2,128,128]{4,3,2,1,0:T(8,128)(2,1)} %copy-done.13), channel_id=1, source_target_pairs={{0,28},{1,29},{2,30},{3,31},{4,0},{5,1},{6,2},{7,3},{8,4},{9,5},{1... | collective-permute-start | bytes 1572872 | tf_op jit(solution)/shard_map/ppermute | solution.py:51
  58.7 5.4 %collective-permute-done.4 = bf16[4,2,2,128,128]{4,3,2,1,0:T(8,128)(2,1)} collective-permute-done((bf16[4,2,2,128,128]{4,3,2,1,0:T(8,128)(2,1)S(1)}, bf16[4,2,2,128,128]{4,3,2,1,0:T(8,128)(2,1)}, u32[]{:S(2)}, u32[]{:S(2)}) %collective-permute-start.4) | collective-permute-done | bytes 524320 | tf_op jit(solution)/shard_map/ppermute | solution.py:48
  67.5 5.5 %collective-permute-start.8 = (bf16[4,2,2,128,128]{4,3,2,1,0:T(8,128)(2,1)S(1)}, bf16[4,2,2,128,128]{4,3,2,1,0:T(8,128)(2,1)}, u32[]{:S(2)}, u32[]{:S(2)}) collective-permute-start(bf16[4,2,2,128,128]{4,3,2,1,0:T(8,128)(2,1)S(1)} %collective-permute-done.7), channel_id=1, source_target_pairs={{0,28},{1,29},{2,30},{3,31},{4,0},{5,1},{6,2},{7,3},{8,4},{9,5},{1... | collective-permute-start | bytes 1572872 | tf_op jit(solution)/shard_map/ppermute | solution.py:51
  76.5 3.4 %collective-permute-done.5 = bf16[4,2,2,128,128]{4,3,2,1,0:T(8,128)(2,1)} collective-permute-done((bf16[4,2,2,128,128]{4,3,2,1,0:T(8,128)(2,1)}, bf16[4,2,2,128,128]{4,3,2,1,0:T(8,128)(2,1)}, u32[]{:S(2)}, u32[]{:S(2)}) %collective-permute-start.5) | collective-permute-done | bytes 524320 | tf_op jit(solution)/shard_map/ppermute | solution.py:48
  82.6 5.7 %collective-permute-start.9 = (bf16[4,2,2,128,128]{4,3,2,1,0:T(8,128)(2,1)}, bf16[4,2,2,128,128]{4,3,2,1,0:T(8,128)(2,1)S(1)}, u32[]{:S(2)}, u32[]{:S(2)}) collective-permute-start(bf16[4,2,2,128,128]{4,3,2,1,0:T(8,128)(2,1)} %collective-permute-done.8), channel_id=1, source_target_pairs={{0,28},{1,29},{2,30},{3,31},{4,0},{5,1},{6,2},{7,3},{8,4},{9,5},{1... | collective-permute-start | bytes 1572872 | tf_op jit(solution)/shard_map/ppermute | solution.py:51
  90.6 4.1 %collective-permute-done.6 = bf16[4,2,2,128,128]{4,3,2,1,0:T(8,128)(2,1)S(1)} collective-permute-done((bf16[4,2,2,128,128]{4,3,2,1,0:T(8,128)(2,1)}, bf16[4,2,2,128,128]{4,3,2,1,0:T(8,128)(2,1)S(1)}, u32[]{:S(2)}, u32[]{:S(2)}) %collective-permute-start.6) | collective-permute-done | bytes 524320 | tf_op jit(solution)/shard_map/ppermute | solution.py:48
  94.7 2.6 collective-permute-done.9
  98.6 2.5 fusion.32
  103.4 2.2 gather_fusion.2
  105.6 3.9 %convolution_bitcast_fusion.1 = f32[128,8,128]{0,2,1:T(8,128)} fusion(bf16[8,8,128,128]{3,2,1,0:T(8,128)(2,1)} %bitcast.179, bf16[128,8,8,128]{3,0,2,1:T(8,128)(2,1)S(1)} %bitcast.177), kind=kOutput, calls=%fused_computation.14 | convolution fusion | flops 268435456 | bytes 4718592 | tf_op jit(solution)/shard_map/tgki,gkio->tgo/dot_general | solution.py:118
  110.5 5.2 %fusion.28 = f32[8,8,128,128]{3,2,1,0:T(8,128)} fusion(bf16[8,8,128,128]{3,2,1,0:T(8,128)(2,1)} %bitcast.190, f32[128,8,128]{0,2,1:T(8,128)} %convolution_bitcast_fusion.1), kind=kOutput, calls=%fused_computation.90 | convolution fusion | flops 269090816 | bytes 6815744 | tf_op jit(solution)/shard_map/tgh,gkho->tgko/dot_general | solution.py:120
  116.5 5.7 %copy.78 = f32[128,64,128]{2,0,1:T(8,128)} copy(f32[128,64,128]{0,2,1:T(8,128)} %bitcast.184) | data formatting | bytes 8388608 | tf_op jit(solution)/shard_map/reshape | solution.py:122
  122.9 8.8 %scatter_fusion = f32[128,32,128]{2,0,1:T(8,128)S(1)} fusion(f32[128,32,128]{2,0,1:T(8,128)S(1)} %broadcast.211.clone.1, s32[64]{0:T(128)S(1)} %copy-done.16, f32[64,128,128]{2,1,0:T(8,128)} %bitcast.182), kind=kCustom, calls=%fused_computation.4 | custom fusion | flops 1048576 | bytes 12583168 | tf_op jit(solution)/shard_map/scatter-add | solution.py:122
  132.8 2.4 copy.79
  135.2 2.7 fusion.35
  137.9 5.7 %copy.86 = f32[128,64,128]{2,0,1:T(8,128)} copy(f32[128,64,128]{0,2,1:T(8,128)} %bitcast.183) | data formatting | bytes 8388608 | tf_op jit(solution)/shard_map/reshape | solution.py:134
  144.2 8.8 %scatter_fusion.1 = f32[128,32,128]{2,0,1:T(8,128)S(1)} fusion(f32[128,32,128]{2,0,1:T(8,128)S(1)} %broadcast.211.clone, s32[64]{0:T(128)S(1)} %copy-done.15, f32[64,128,128]{2,1,0:T(8,128)} %bitcast.181), kind=kCustom, calls=%fused_computation.5 | custom fusion | flops 1048576 | bytes 12583168 | tf_op jit(solution)/shard_map/scatter-add | solution.py:134
  157.7 6.3 %all-to-all-start.1 = ((bf16[16,2,128,256]{2,3,1,0:T(8,128)(2,1)}), bf16[16,2,128,256]{2,3,1,0:T(8,128)(2,1)}, u32[]{:S(2)}, u32[]{:S(2)}) async-start(bf16[16,2,128,256]{2,3,1,0:T(8,128)(2,1)} %copy.88), calls=%async_computation.1 | async-start | bytes 4194304 | tf_op jit(solution)/shard_map/all_to_all | solution.py:26
  163.9 2.6 copy.75
  166.6 3.0 %copy.81 = bf16[8,8,128,128]{2,3,1,0:T(8,128)(2,1)S(1)} copy(bf16[8,8,128,128]{3,2,1,0:T(8,128)(2,1)} %bitcast.186) | data formatting | bytes 4194304 | tf_op jit(solution)/shard_map/gather | solution.py:123
  169.6 2.1 multiply_convert_fusion
  171.7 4.1 %copy.95 = bf16[1,8,4,2,128,128]{5,4,3,0,2,1:T(8,128)(2,1)} copy(bf16[1,8,4,2,128,128]{4,5,3,2,1,0:T(8,128)(2,1)} %bitcast.189) | data formatting | bytes 4194304 | tf_op jit(solution)/shard_map/stack | solution.py:146
  178.7 2.6 collective-permute-start.10
  181.4 15.0 %collective-permute-done.10 = bf16[4,2,2,128,128]{4,3,2,1,0:T(8,128)(2,1)S(1)} collective-permute-done((bf16[4,2,2,128,128]{4,3,2,1,0:T(8,128)(2,1)S(1)}, bf16[4,2,2,128,128]{4,3,2,1,0:T(8,128)(2,1)S(1)}, u32[]{:S(2)}, u32[]{:S(2)}) %collective-permute-start.10) | collective-permute-done | bytes 524320 | tf_op jit(solution)/shard_map/ppermute | solution.py:64
  196.5 1.9 collective-permute-start.11
  202.1 5.7 %all-to-all-start.2 = ((bf16[16,2,128,256]{3,2,1,0:T(8,128)(2,1)}), bf16[16,2,128,256]{3,2,1,0:T(8,128)(2,1)S(1)}, u32[]{:S(2)}, u32[]{:S(2)}) async-start(bf16[16,2,128,256]{3,2,1,0:T(8,128)(2,1)} %broadcast_in_dim.5), calls=%async_computation.2 | async-start | bytes 4194304 | tf_op jit(solution)/shard_map/all_to_all | solution.py:22
  207.8 5.1 %collective-permute-start.14 = (bf16[4,2,2,128,128]{4,3,2,1,0:T(8,128)(2,1)}, bf16[4,2,2,128,128]{4,3,2,1,0:T(8,128)(2,1)S(1)}, u32[]{:S(2)}, u32[]{:S(2)}) collective-permute-start(bf16[4,2,2,128,128]{4,3,2,1,0:T(8,128)(2,1)} %get-tuple-element.13), channel_id=1, source_target_pairs={{0,28},{1,29},{2,30},{3,31},{4,0},{5,1},{6,2},{7,3},{8,4},{9,5},{1... | collective-permute-start | bytes 1572872 | tf_op jit(solution)/shard_map/ppermute | solution.py:69
  214.3 1.9 collective-permute-start.12
  216.3 8.5 %collective-permute-done.14 = bf16[4,2,2,128,128]{4,3,2,1,0:T(8,128)(2,1)S(1)} collective-permute-done((bf16[4,2,2,128,128]{4,3,2,1,0:T(8,128)(2,1)}, bf16[4,2,2,128,128]{4,3,2,1,0:T(8,128)(2,1)S(1)}, u32[]{:S(2)}, u32[]{:S(2)}) %collective-permute-start.14) | collective-permute-done | bytes 524320 | tf_op jit(solution)/shard_map/ppermute | solution.py:69
  224.8 6.3 %collective-permute-done.12 = bf16[4,2,2,128,128]{4,3,2,1,0:T(8,128)(2,1)S(1)} collective-permute-done((bf16[4,2,2,128,128]{4,3,2,1,0:T(8,128)(2,1)S(1)}, bf16[4,2,2,128,128]{4,3,2,1,0:T(8,128)(2,1)S(1)}, u32[]{:S(2)}, u32[]{:S(2)}) %collective-permute-start.12) | collective-permute-done | bytes 524320 | tf_op jit(solution)/shard_map/ppermute | solution.py:64
  232.6 1.9 collective-permute-start.15
  234.5 3.9 %collective-permute-start.13 = (bf16[4,2,2,128,128]{4,3,2,1,0:T(8,128)(2,1)S(1)}, bf16[4,2,2,128,128]{4,3,2,1,0:T(8,128)(2,1)S(1)}, u32[]{:S(2)}, u32[]{:S(2)}) collective-permute-start(bf16[4,2,2,128,128]{4,3,2,1,0:T(8,128)(2,1)S(1)} %get-tuple-element.10), channel_id=1, source_target_pairs={{0,4},{1,5},{2,6},{3,7},{4,8},{5,9},{6,10},{7,11},{8,12},{9,13},{1... | collective-permute-start | bytes 1572872 | tf_op jit(solution)/shard_map/ppermute | solution.py:64
  238.4 8.7 %collective-permute-done.15 = bf16[4,2,2,128,128]{4,3,2,1,0:T(8,128)(2,1)S(1)} collective-permute-done((bf16[4,2,2,128,128]{4,3,2,1,0:T(8,128)(2,1)S(1)}, bf16[4,2,2,128,128]{4,3,2,1,0:T(8,128)(2,1)S(1)}, u32[]{:S(2)}, u32[]{:S(2)}) %collective-permute-start.15) | collective-permute-done | bytes 524320 | tf_op jit(solution)/shard_map/ppermute | solution.py:69
  248.4 3.4 %collective-permute-start.16 = (bf16[4,2,2,128,128]{4,3,2,1,0:T(8,128)(2,1)S(1)}, bf16[4,2,2,128,128]{4,3,2,1,0:T(8,128)(2,1)S(1)}, u32[]{:S(2)}, u32[]{:S(2)}) collective-permute-start(bf16[4,2,2,128,128]{4,3,2,1,0:T(8,128)(2,1)S(1)} %fusion.6), channel_id=1, source_target_pairs={{0,28},{1,29},{2,30},{3,31},{4,0},{5,1},{6,2},{7,3},{8,4},{9,5},{1... | collective-permute-start | bytes 1572872 | tf_op jit(solution)/shard_map/ppermute | solution.py:69
  251.8 10.2 %collective-permute-done.16 = bf16[4,2,2,128,128]{4,3,2,1,0:T(8,128)(2,1)S(1)} collective-permute-done((bf16[4,2,2,128,128]{4,3,2,1,0:T(8,128)(2,1)S(1)}, bf16[4,2,2,128,128]{4,3,2,1,0:T(8,128)(2,1)S(1)}, u32[]{:S(2)}, u32[]{:S(2)}) %collective-permute-start.16) | collective-permute-done | bytes 524320 | tf_op jit(solution)/shard_map/ppermute | solution.py:69
  263.4 4.4 %collective-permute-start.17 = (bf16[2,2,128,128]{3,2,1,0:T(8,128)(2,1)S(1)}, bf16[2,2,128,128]{3,2,1,0:T(8,128)(2,1)S(1)}, u32[]{:S(2)}, u32[]{:S(2)}) collective-permute-start(bf16[2,2,128,128]{3,2,1,0:T(8,128)(2,1)S(1)} %get-tuple-element.20), channel_id=1, source_target_pairs={{0,3},{1,0},{2,1},{3,2},{4,7},{5,4},{6,5},{7,6},{8,11},{9,8},{10,9... | collective-permute-start | bytes 393224 | tf_op jit(solution)/shard_map/ppermute | solution.py:77
  267.8 4.2 %collective-permute-start.18 = (bf16[2,2,128,128]{3,2,1,0:T(8,128)(2,1)S(1)}, bf16[2,2,128,128]{3,2,1,0:T(8,128)(2,1)S(1)}, u32[]{:S(2)}, u32[]{:S(2)}) collective-permute-start(bf16[2,2,128,128]{3,2,1,0:T(8,128)(2,1)S(1)} %get-tuple-element.22), channel_id=1, source_target_pairs={{0,2},{1,3},{2,0},{3,1},{4,6},{5,7},{6,4},{7,5},{8,10},{9,11},{10,... | collective-permute-start | bytes 393224 | tf_op jit(solution)/shard_map/ppermute | solution.py:77
  271.9 2.7 collective-permute-start.19
  274.7 5.1 %collective-permute-done.18 = bf16[2,2,128,128]{3,2,1,0:T(8,128)(2,1)S(1)} collective-permute-done((bf16[2,2,128,128]{3,2,1,0:T(8,128)(2,1)S(1)}, bf16[2,2,128,128]{3,2,1,0:T(8,128)(2,1)S(1)}, u32[]{:S(2)}, u32[]{:S(2)}) %collective-permute-start.18) | collective-permute-done | bytes 131104 | tf_op jit(solution)/shard_map/ppermute | solution.py:77
  279.7 2.4 collective-permute-done.19
  282.9 2.4 copy.91
  (108 shorter events, 51.6 us)
Async XLA Ops:
  0.6 48.9 %copy-start = (s32[64]{0:T(128)S(1)}, s32[64]{0:T(128)}, u32[]{:S(2)}) copy-start(s32[64]{0:T(128)} %param.9) | copy-start | bytes 772
  1.5 27.6 %collective-permute-start = (bf16[2,2,128,128]{3,2,1,0:T(8,128)(2,1)S(1)}, bf16[2,2,128,128]{3,2,1,0:T(8,128)(2,1)S(1)}, u32[]{:S(2)}, u32[]{:S(2)}) collective-permute-start(bf16[2,2,128,128]{3,2,1,0:T(8,128)(2,1)S(1)} %get-tuple-element.26), channel_id=1, source_target_pairs={{0,1},{1,2},{2,3},{3,0},{4,5},{5,6},{6,7},{7,4},{8,9},{9,10},{10,1... | collective-permute-start | bytes 393224 | tf_op jit(solution)/shard_map/ppermute | solution.py:42
  7.6 21.5 %collective-permute-start.1 = (bf16[2,2,128,128]{3,2,1,0:T(8,128)(2,1)S(1)}, bf16[2,2,128,128]{3,2,1,0:T(8,128)(2,1)S(1)}, u32[]{:S(2)}, u32[]{:S(2)}) collective-permute-start(bf16[2,2,128,128]{3,2,1,0:T(8,128)(2,1)S(1)} %get-tuple-element.26), channel_id=1, source_target_pairs={{0,2},{1,3},{2,0},{3,1},{4,6},{5,7},{6,4},{7,5},{8,10},{9,11},{10,... | collective-permute-start | bytes 393224 | tf_op jit(solution)/shard_map/ppermute | solution.py:42
  16.8 12.6 %collective-permute-start.2 = (bf16[2,2,128,128]{3,2,1,0:T(8,128)(2,1)S(1)}, bf16[2,2,128,128]{3,2,1,0:T(8,128)(2,1)S(1)}, u32[]{:S(2)}, u32[]{:S(2)}) collective-permute-start(bf16[2,2,128,128]{3,2,1,0:T(8,128)(2,1)S(1)} %get-tuple-element.26), channel_id=1, source_target_pairs={{0,3},{1,0},{2,1},{3,2},{4,7},{5,4},{6,5},{7,6},{8,11},{9,8},{10,9... | collective-permute-start | bytes 393224 | tf_op jit(solution)/shard_map/ppermute | solution.py:42
  23.3 33.4 %copy-start.2 = (s32[64]{0:T(128)S(1)}, s32[64]{0:T(128)}, u32[]{:S(2)}) copy-start(s32[64]{0:T(128)} %param.11) | copy-start | bytes 772
  23.3 77.8 %all-to-all-start = ((bf16[16,2,128,256]{2,3,1,0:T(8,128)(2,1)}), bf16[16,2,128,256]{2,3,1,0:T(8,128)(2,1)S(1)}, u32[]{:S(2)}, u32[]{:S(2)}) async-start(bf16[16,2,128,256]{2,3,1,0:T(8,128)(2,1)} %broadcast_in_dim.4), calls=%async_computation | async-start | bytes 4194304 | tf_op jit(solution)/shard_map/all_to_all | solution.py:22
  29.4 0.7 copy-start.14
  30.1 20.7 %copy-start.13 = (bf16[4,2,2,128,128]{4,3,2,1,0:T(8,128)(2,1)}, bf16[4,2,2,128,128]{4,3,2,1,0:T(8,128)(2,1)S(1)}, u32[]{:S(2)}) copy-start(bf16[4,2,2,128,128]{4,3,2,1,0:T(8,128)(2,1)S(1)} %pad_maximum_fusion) | copy-start | bytes 1572868
  30.1 17.5 %collective-permute-start.3 = (bf16[4,2,2,128,128]{4,3,2,1,0:T(8,128)(2,1)S(1)}, bf16[4,2,2,128,128]{4,3,2,1,0:T(8,128)(2,1)S(1)}, u32[]{:S(2)}, u32[]{:S(2)}) collective-permute-start(bf16[4,2,2,128,128]{4,3,2,1,0:T(8,128)(2,1)S(1)} %pad_maximum_fusion), channel_id=1, source_target_pairs={{0,4},{1,5},{2,6},{3,7},{4,8},{5,9},{6,10},{7,11},{8,12},{9,13},{1... | collective-permute-start | bytes 1572872 | tf_op jit(solution)/shard_map/ppermute | solution.py:48
  47.6 16.5 %collective-permute-start.4 = (bf16[4,2,2,128,128]{4,3,2,1,0:T(8,128)(2,1)S(1)}, bf16[4,2,2,128,128]{4,3,2,1,0:T(8,128)(2,1)}, u32[]{:S(2)}, u32[]{:S(2)}) collective-permute-start(bf16[4,2,2,128,128]{4,3,2,1,0:T(8,128)(2,1)S(1)} %collective-permute-done.3), channel_id=1, source_target_pairs={{0,4},{1,5},{2,6},{3,7},{4,8},{5,9},{6,10},{7,11},{8,12},{9,13},{1... | collective-permute-start | bytes 1572872 | tf_op jit(solution)/shard_map/ppermute | solution.py:48
  51.5 16.0 %collective-permute-start.7 = (bf16[4,2,2,128,128]{4,3,2,1,0:T(8,128)(2,1)}, bf16[4,2,2,128,128]{4,3,2,1,0:T(8,128)(2,1)S(1)}, u32[]{:S(2)}, u32[]{:S(2)}) collective-permute-start(bf16[4,2,2,128,128]{4,3,2,1,0:T(8,128)(2,1)} %copy-done.13), channel_id=1, source_target_pairs={{0,28},{1,29},{2,30},{3,31},{4,0},{5,1},{6,2},{7,3},{8,4},{9,5},{1... | collective-permute-start | bytes 1572872 | tf_op jit(solution)/shard_map/ppermute | solution.py:51
  64.1 15.8 %collective-permute-start.5 = (bf16[4,2,2,128,128]{4,3,2,1,0:T(8,128)(2,1)}, bf16[4,2,2,128,128]{4,3,2,1,0:T(8,128)(2,1)}, u32[]{:S(2)}, u32[]{:S(2)}) collective-permute-start(bf16[4,2,2,128,128]{4,3,2,1,0:T(8,128)(2,1)} %collective-permute-done.4), channel_id=1, source_target_pairs={{0,4},{1,5},{2,6},{3,7},{4,8},{5,9},{6,10},{7,11},{8,12},{9,13},{1... | collective-permute-start | bytes 1572872 | tf_op jit(solution)/shard_map/ppermute | solution.py:48
  67.5 15.1 %collective-permute-start.8 = (bf16[4,2,2,128,128]{4,3,2,1,0:T(8,128)(2,1)S(1)}, bf16[4,2,2,128,128]{4,3,2,1,0:T(8,128)(2,1)}, u32[]{:S(2)}, u32[]{:S(2)}) collective-permute-start(bf16[4,2,2,128,128]{4,3,2,1,0:T(8,128)(2,1)S(1)} %collective-permute-done.7), channel_id=1, source_target_pairs={{0,28},{1,29},{2,30},{3,31},{4,0},{5,1},{6,2},{7,3},{8,4},{9,5},{1... | collective-permute-start | bytes 1572872 | tf_op jit(solution)/shard_map/ppermute | solution.py:51
  79.9 14.8 %collective-permute-start.6 = (bf16[4,2,2,128,128]{4,3,2,1,0:T(8,128)(2,1)}, bf16[4,2,2,128,128]{4,3,2,1,0:T(8,128)(2,1)S(1)}, u32[]{:S(2)}, u32[]{:S(2)}) collective-permute-start(bf16[4,2,2,128,128]{4,3,2,1,0:T(8,128)(2,1)} %collective-permute-done.5), channel_id=1, source_target_pairs={{0,4},{1,5},{2,6},{3,7},{4,8},{5,9},{6,10},{7,11},{8,12},{9,13},{1... | collective-permute-start | bytes 1572872 | tf_op jit(solution)/shard_map/ppermute | solution.py:48
  82.6 14.7 %collective-permute-start.9 = (bf16[4,2,2,128,128]{4,3,2,1,0:T(8,128)(2,1)}, bf16[4,2,2,128,128]{4,3,2,1,0:T(8,128)(2,1)S(1)}, u32[]{:S(2)}, u32[]{:S(2)}) collective-permute-start(bf16[4,2,2,128,128]{4,3,2,1,0:T(8,128)(2,1)} %collective-permute-done.8), channel_id=1, source_target_pairs={{0,28},{1,29},{2,30},{3,31},{4,0},{5,1},{6,2},{7,3},{8,4},{9,5},{1... | collective-permute-start | bytes 1572872 | tf_op jit(solution)/shard_map/ppermute | solution.py:51
  105.5 4.0 %copy-start.3 = (bf16[64,128,128]{2,1,0:T(8,128)(2,1)}, bf16[64,128,128]{2,1,0:T(8,128)(2,1)S(1)}, u32[]{:S(2)}) copy-start(bf16[64,128,128]{2,1,0:T(8,128)(2,1)S(1)} %gather_fusion.2) | copy-start | bytes 6291460
  110.5 5.3 %copy-start.7 = (bf16[64,128,128]{2,1,0:T(8,128)(2,1)}, bf16[64,128,128]{2,1,0:T(8,128)(2,1)S(1)}, u32[]{:S(2)}) copy-start(bf16[64,128,128]{2,1,0:T(8,128)(2,1)S(1)} %gather_fusion.3) | copy-start | bytes 6291460
  110.5 5.3 %copy-start.9 = (bf16[1,8,4,2,128,128]{5,4,3,0,2,1:T(8,128)(2,1)S(1)}, bf16[1,8,4,2,128,128]{5,4,3,0,2,1:T(8,128)(2,1)}, u32[]{:S(2)}) copy-start(bf16[1,8,4,2,128,128]{5,4,3,0,2,1:T(8,128)(2,1)} %get-tuple-element.14) | copy-start | bytes 6291460
  110.5 5.3 %copy-start.11 = (f32[128,8,128]{0,2,1:T(8,128)S(1)}, f32[128,8,128]{0,2,1:T(8,128)}, u32[]{:S(2)}) copy-start(f32[128,8,128]{0,2,1:T(8,128)} %convolution_bitcast_fusion.1) | copy-start | bytes 1572868
  122.2 0.7 copy-start.16
  132.8 2.4 copy-start.5
  143.6 0.7 copy-start.15
  154.2 1.7 copy-start.12
  157.7 6.3 %copy-start.4 = (bf16[64,128,128]{2,1,0:T(8,128)(2,1)S(1)}, bf16[64,128,128]{2,1,0:T(8,128)(2,1)}, u32[]{:S(2)}) copy-start(bf16[64,128,128]{2,1,0:T(8,128)(2,1)} %copy-done.3) | copy-start | bytes 6291460
  157.7 40.8 %all-to-all-start.1 = ((bf16[16,2,128,256]{2,3,1,0:T(8,128)(2,1)}), bf16[16,2,128,256]{2,3,1,0:T(8,128)(2,1)}, u32[]{:S(2)}, u32[]{:S(2)}) async-start(bf16[16,2,128,256]{2,3,1,0:T(8,128)(2,1)} %copy.88), calls=%async_computation.1 | async-start | bytes 4194304 | tf_op jit(solution)/shard_map/all_to_all | solution.py:26
  171.7 4.1 %copy-start.8 = (bf16[8,8,128,128]{2,3,1,0:T(8,128)(2,1)S(1)}, bf16[8,8,128,128]{2,3,1,0:T(8,128)(2,1)}, u32[]{:S(2)}) copy-start(bf16[8,8,128,128]{2,3,1,0:T(8,128)(2,1)} %copy.75) | copy-start | bytes 6291460
  175.8 1.6 copy-start.10
  177.7 18.6 %copy-start.6 = (bf16[8,4,2,2,128,128]{5,4,3,2,1,0:T(8,128)(2,1)}, bf16[8,4,2,2,128,128]{5,4,3,2,1,0:T(8,128)(2,1)S(1)}, u32[]{:S(2)}) copy-start(bf16[8,4,2,2,128,128]{5,4,3,2,1,0:T(8,128)(2,1)S(1)} %maximum_bitcast_fusion) | copy-start | bytes 12582916
  178.7 17.7 %collective-permute-start.10 = (bf16[4,2,2,128,128]{4,3,2,1,0:T(8,128)(2,1)S(1)}, bf16[4,2,2,128,128]{4,3,2,1,0:T(8,128)(2,1)S(1)}, u32[]{:S(2)}, u32[]{:S(2)}) collective-permute-start(bf16[4,2,2,128,128]{4,3,2,1,0:T(8,128)(2,1)S(1)} %get-tuple-element.12), channel_id=1, source_target_pairs={{0,4},{1,5},{2,6},{3,7},{4,8},{5,9},{6,10},{7,11},{8,12},{9,13},{1... | collective-permute-start | bytes 1572872 | tf_op jit(solution)/shard_map/ppermute | solution.py:64
  196.5 16.6 %collective-permute-start.11 = (bf16[4,2,2,128,128]{4,3,2,1,0:T(8,128)(2,1)S(1)}, bf16[4,2,2,128,128]{4,3,2,1,0:T(8,128)(2,1)S(1)}, u32[]{:S(2)}, u32[]{:S(2)}) collective-permute-start(bf16[4,2,2,128,128]{4,3,2,1,0:T(8,128)(2,1)S(1)} %fusion.7), channel_id=1, source_target_pairs={{0,4},{1,5},{2,6},{3,7},{4,8},{5,9},{6,10},{7,11},{8,12},{9,13},{1... | collective-permute-start | bytes 1572872 | tf_op jit(solution)/shard_map/ppermute | solution.py:64
  202.1 80.8 %all-to-all-start.2 = ((bf16[16,2,128,256]{3,2,1,0:T(8,128)(2,1)}), bf16[16,2,128,256]{3,2,1,0:T(8,128)(2,1)S(1)}, u32[]{:S(2)}, u32[]{:S(2)}) async-start(bf16[16,2,128,256]{3,2,1,0:T(8,128)(2,1)} %broadcast_in_dim.5), calls=%async_computation.2 | async-start | bytes 4194304 | tf_op jit(solution)/shard_map/all_to_all | solution.py:22
  207.8 16.9 %collective-permute-start.14 = (bf16[4,2,2,128,128]{4,3,2,1,0:T(8,128)(2,1)}, bf16[4,2,2,128,128]{4,3,2,1,0:T(8,128)(2,1)S(1)}, u32[]{:S(2)}, u32[]{:S(2)}) collective-permute-start(bf16[4,2,2,128,128]{4,3,2,1,0:T(8,128)(2,1)} %get-tuple-element.13), channel_id=1, source_target_pairs={{0,28},{1,29},{2,30},{3,31},{4,0},{5,1},{6,2},{7,3},{8,4},{9,5},{1... | collective-permute-start | bytes 1572872 | tf_op jit(solution)/shard_map/ppermute | solution.py:69
  214.3 16.7 %collective-permute-start.12 = (bf16[4,2,2,128,128]{4,3,2,1,0:T(8,128)(2,1)S(1)}, bf16[4,2,2,128,128]{4,3,2,1,0:T(8,128)(2,1)S(1)}, u32[]{:S(2)}, u32[]{:S(2)}) collective-permute-start(bf16[4,2,2,128,128]{4,3,2,1,0:T(8,128)(2,1)S(1)} %fusion.8), channel_id=1, source_target_pairs={{0,4},{1,5},{2,6},{3,7},{4,8},{5,9},{6,10},{7,11},{8,12},{9,13},{1... | collective-permute-start | bytes 1572872 | tf_op jit(solution)/shard_map/ppermute | solution.py:64
  232.6 14.6 %collective-permute-start.15 = (bf16[4,2,2,128,128]{4,3,2,1,0:T(8,128)(2,1)S(1)}, bf16[4,2,2,128,128]{4,3,2,1,0:T(8,128)(2,1)S(1)}, u32[]{:S(2)}, u32[]{:S(2)}) collective-permute-start(bf16[4,2,2,128,128]{4,3,2,1,0:T(8,128)(2,1)S(1)} %get-tuple-element.11), channel_id=1, source_target_pairs={{0,28},{1,29},{2,30},{3,31},{4,0},{5,1},{6,2},{7,3},{8,4},{9,5},{1... | collective-permute-start | bytes 1572872 | tf_op jit(solution)/shard_map/ppermute | solution.py:69
  234.5 17.3 %collective-permute-start.13 = (bf16[4,2,2,128,128]{4,3,2,1,0:T(8,128)(2,1)S(1)}, bf16[4,2,2,128,128]{4,3,2,1,0:T(8,128)(2,1)S(1)}, u32[]{:S(2)}, u32[]{:S(2)}) collective-permute-start(bf16[4,2,2,128,128]{4,3,2,1,0:T(8,128)(2,1)S(1)} %get-tuple-element.10), channel_id=1, source_target_pairs={{0,4},{1,5},{2,6},{3,7},{4,8},{5,9},{6,10},{7,11},{8,12},{9,13},{1... | collective-permute-start | bytes 1572872 | tf_op jit(solution)/shard_map/ppermute | solution.py:64
  248.4 13.7 %collective-permute-start.16 = (bf16[4,2,2,128,128]{4,3,2,1,0:T(8,128)(2,1)S(1)}, bf16[4,2,2,128,128]{4,3,2,1,0:T(8,128)(2,1)S(1)}, u32[]{:S(2)}, u32[]{:S(2)}) collective-permute-start(bf16[4,2,2,128,128]{4,3,2,1,0:T(8,128)(2,1)S(1)} %fusion.6), channel_id=1, source_target_pairs={{0,28},{1,29},{2,30},{3,31},{4,0},{5,1},{6,2},{7,3},{8,4},{9,5},{1... | collective-permute-start | bytes 1572872 | tf_op jit(solution)/shard_map/ppermute | solution.py:69
  263.4 11.3 %collective-permute-start.17 = (bf16[2,2,128,128]{3,2,1,0:T(8,128)(2,1)S(1)}, bf16[2,2,128,128]{3,2,1,0:T(8,128)(2,1)S(1)}, u32[]{:S(2)}, u32[]{:S(2)}) collective-permute-start(bf16[2,2,128,128]{3,2,1,0:T(8,128)(2,1)S(1)} %get-tuple-element.20), channel_id=1, source_target_pairs={{0,3},{1,0},{2,1},{3,2},{4,7},{5,4},{6,5},{7,6},{8,11},{9,8},{10,9... | collective-permute-start | bytes 393224 | tf_op jit(solution)/shard_map/ppermute | solution.py:77
  267.8 12.0 %collective-permute-start.18 = (bf16[2,2,128,128]{3,2,1,0:T(8,128)(2,1)S(1)}, bf16[2,2,128,128]{3,2,1,0:T(8,128)(2,1)S(1)}, u32[]{:S(2)}, u32[]{:S(2)}) collective-permute-start(bf16[2,2,128,128]{3,2,1,0:T(8,128)(2,1)S(1)} %get-tuple-element.22), channel_id=1, source_target_pairs={{0,2},{1,3},{2,0},{3,1},{4,6},{5,7},{6,4},{7,5},{8,10},{9,11},{10,... | collective-permute-start | bytes 393224 | tf_op jit(solution)/shard_map/ppermute | solution.py:77
  271.9 10.2 %collective-permute-start.19 = (bf16[2,2,128,128]{3,2,1,0:T(8,128)(2,1)S(1)}, bf16[2,2,128,128]{3,2,1,0:T(8,128)(2,1)S(1)}, u32[]{:S(2)}, u32[]{:S(2)}) collective-permute-start(bf16[2,2,128,128]{3,2,1,0:T(8,128)(2,1)S(1)} %get-tuple-element.21), channel_id=1, source_target_pairs={{0,1},{1,2},{2,3},{3,0},{4,5},{5,6},{6,7},{7,4},{8,9},{9,10},{10,1... | collective-permute-start | bytes 393224 | tf_op jit(solution)/shard_map/ppermute | solution.py:77
  286.9 2.6 copy-start.1

commit v3 on v2

--- a/solution.py
+++ b/solution.py
@@ -97,9 +97,8 @@
     n_y = n_dp // n_z
     if n_z * per_dev != K:
         raise ValueError("layout")
-    weights = dp_gather_rel(jnp.stack([up_blocks, down_blocks]), n_y, n_z)
-    weights = jnp.moveaxis(weights, 2, 0).reshape(2, -1, block_size, block_size)
-    up_all, down_all = weights[0], weights[1]
+    up_all = dp_gather_rel(up_blocks, n_y, n_z).reshape(-1, block_size, block_size)
+    down_all = dp_gather_rel(down_blocks, n_y, n_z).reshape(-1, block_size, block_size)
     me = lax.axis_index("dp")
     my_y, my_z = me // n_z, me % n_z
     a = jnp.arange(n_y, dtype=jnp.int32)[:, None, None]
@@ -143,10 +142,13 @@
     both = gather_all(mine, "tensor")
     both = jnp.moveaxis(both, 0, 2).reshape(2, tokens, width)
 
-    terms = jnp.stack([up_term, down_term]).astype(jnp.bfloat16)
-    terms = terms.reshape(2, n_y, n_z, per_dev, block_size, block_size)
-    grads = dp_scatter_rel(jnp.moveaxis(terms, 0, 2), n_y, n_z)
-    return (both[0], both[1], grads[0], grads[1])
+    down_sum = dp_scatter_rel(
+        down_term.astype(jnp.bfloat16).reshape(n_y, n_z, per_dev, block_size, block_size), n_y, n_z
+    )
+    up_sum = dp_scatter_rel(
+        up_term.astype(jnp.bfloat16).reshape(n_y, n_z, per_dev, block_size, block_size), n_y, n_z
+    )
+    return (both[0], both[1], up_sum, down_sum)
 
 
 def solution(mesh):

time: 294 us -> 327 us (1.11)
  starting transfers between devices: 94.4 us -> 185 us
  waiting for transfers between devices: 85.4 us -> 10.9 us
  local copies, waits for them, and re-layouts: 58.7 us -> 77.9 us
  other arithmetic: 34.5 us -> 29.6 us
  matrix products: 15.4 us -> 18.9 us
    ppermute x3 -> x6, waiting for transfers between devices: 27.4 us -> 0.02 us  [dp_scatter_rel(): lax.ppermute(part.astype(jnp.bfloat16), 'dp', dp_shift(n_y, n_z, -1, 0))]
    ppermute x4 -> x8, waiting for transfers between devices: 25.3 us -> 0.77 us  [dp_gather_rel(): cur_f = lax.ppermute(cur_f, 'dp', dp_shift(n_y, n_z, 1, 0))]
    all_to_all x1, starting transfers between devices: 6.28 us -> 28.4 us  [scatter_sum(): got = lax.all_to_all(x, axis_name, 0, 0, tiled=True)]
    ppermute x0 -> x14, local copies, waits for them, and re-layouts: none -> 16.2 us  [the longest x8 11.7 us: dp_gather_rel(): cur_f = lax.ppermute(cur_f, 'dp', dp_shift(n_y, n_z, 1, 0))]
    ppermute x3 -> x6, starting transfers between devices: 10.5 us -> 26.5 us  [dp_scatter_rel(): lax.ppermute(part.astype(jnp.bfloat16), 'dp', dp_shift(n_y, n_z, -1, 0))]
    ppermute x4 -> x8, waiting for transfers between devices: 21.4 us -> 5.64 us  [dp_scatter_rel(): lax.ppermute(part.astype(jnp.bfloat16), 'dp', dp_shift(n_y, n_z, 1, 0))]
    ppermute x4 -> x8, starting transfers between devices: 9.21 us -> 21.3 us  [dp_gather_rel(): cur_f = lax.ppermute(cur_f, 'dp', dp_shift(n_y, n_z, 1, 0))]
    ppermute x3 -> x6, starting transfers between devices: 11.3 us -> 23.2 us  [dp_scatter_rel(): lax.ppermute(acc[b].astype(jnp.bfloat16), 'dp', dp_shift(n_y, n_z, 0, -b))]
  transfers between devices with their start and end apart: 23 -> 43, of which waited for: 16 -> 6; matrix products, arithmetic and copies ran while one was open for 15% -> 19% of each run, Pallas kernels for 0% -> 0%
where the time goes in v3:
time: 327 us; the launch traced here: 324 us
  starting transfers between devices  185 us (57%)
  local copies, waits for them, and re-layouts  77.9 us (24%)
  other arithmetic  29.6 us (9%)
  matrix products  18.9 us (6%)
  waiting for transfers between devices  10.9 us (3%)
    ppermute x6, starting transfers between devices, dp_gather_rel(): lax.ppermute(x, 'dp', dp_shift(n_y, n_z, 0, b))  30.6 us
    all_to_all x1, starting transfers between devices, scatter_sum(): got = lax.all_to_all(x, axis_name, 0, 0, tiled=True)  28.4 us
    ppermute x6, starting transfers between devices, dp_scatter_rel(): lax.ppermute(part.astype(jnp.bfloat16), 'dp', dp_shift(n_y, n_z, -1, 0))  26.5 us
    ppermute x6, starting transfers between devices, dp_scatter_rel(): lax.ppermute(acc[b].astype(jnp.bfloat16), 'dp', dp_shift(n_y, n_z, 0, -b))  23.2 us
    ppermute x6, starting transfers between devices, dp_gather_rel(): cur_b = lax.ppermute(cur_b, 'dp', dp_shift(n_y, n_z, -1, 0))  23 us
    ppermute x8, starting transfers between devices, dp_gather_rel(): cur_f = lax.ppermute(cur_f, 'dp', dp_shift(n_y, n_z, 1, 0))  21.3 us
    ppermute x8, starting transfers between devices, dp_scatter_rel(): lax.ppermute(part.astype(jnp.bfloat16), 'dp', dp_shift(n_y, n_z, 1, 0))  20.4 us
    unnamed x64, local copies, waits for them, and re-layouts  12 us
  transfers between devices with their start and end apart: 43, of which 6 were waited for; matrix products, arithmetic and copies ran while one was open for 19% of the time, Pallas kernels for 0%

profile of v3, /device:TPU:6, one launch (start us, length us, event | category | flops | bytes accessed | tf_op | source)
XLA Modules:
  0.0 324.0 jit_solution(1797398578812945876)
XLA Ops:
  0.6 6.1 %collective-permute-start.10 = (bf16[2,128,128]{2,1,0:T(8,128)(2,1)}, bf16[2,128,128]{2,1,0:T(8,128)(2,1)S(1)}, u32[]{:S(2)}, u32[]{:S(2)}) collective-permute-start(bf16[2,128,128]{2,1,0:T(8,128)(2,1)} %param.8), channel_id=1, source_target_pairs={{0,1},{1,2},{2,3},{3,0},{4,5},{5,6},{6,7},{7,4},{8,9},{9,10},{10,1... | collective-permute-start | bytes 196616 | tf_op jit(solution)/shard_map/ppermute | solution.py:42
  6.7 9.1 %collective-permute-start.11 = (bf16[2,128,128]{2,1,0:T(8,128)(2,1)}, bf16[2,128,128]{2,1,0:T(8,128)(2,1)S(1)}, u32[]{:S(2)}, u32[]{:S(2)}) collective-permute-start(bf16[2,128,128]{2,1,0:T(8,128)(2,1)} %param.8), channel_id=1, source_target_pairs={{0,2},{1,3},{2,0},{3,1},{4,6},{5,7},{6,4},{7,5},{8,10},{9,11},{10,... | collective-permute-start | bytes 196616 | tf_op jit(solution)/shard_map/ppermute | solution.py:42
  15.9 3.7 %collective-permute-start.12 = (bf16[2,128,128]{2,1,0:T(8,128)(2,1)}, bf16[2,128,128]{2,1,0:T(8,128)(2,1)S(1)}, u32[]{:S(2)}, u32[]{:S(2)}) collective-permute-start(bf16[2,128,128]{2,1,0:T(8,128)(2,1)} %param.8), channel_id=1, source_target_pairs={{0,3},{1,0},{2,1},{3,2},{4,7},{5,4},{6,5},{7,6},{8,11},{9,8},{10,9... | collective-permute-start | bytes 196616 | tf_op jit(solution)/shard_map/ppermute | solution.py:42
  19.5 3.1 collective-permute-start
  22.6 3.1 collective-permute-start.1
  28.6 5.8 %all-to-all-start = ((bf16[16,2,128,256]{2,3,1,0:T(8,128)(2,1)}), bf16[16,2,128,256]{2,3,1,0:T(8,128)(2,1)}, u32[]{:S(2)}, u32[]{:S(2)}) async-start(bf16[16,2,128,256]{2,3,1,0:T(8,128)(2,1)} %broadcast_in_dim.4), calls=%async_computation | async-start | bytes 4194304 | tf_op jit(solution)/shard_map/all_to_all | solution.py:22
  36.5 5.5 %collective-permute-start.2 = (bf16[2,128,128]{2,1,0:T(8,128)(2,1)S(1)}, bf16[2,128,128]{2,1,0:T(8,128)(2,1)S(1)}, u32[]{:S(2)}, u32[]{:S(2)}) collective-permute-start(bf16[2,128,128]{2,1,0:T(8,128)(2,1)S(1)} %copy-done.23), channel_id=1, source_target_pairs={{0,3},{1,0},{2,1},{3,2},{4,7},{5,4},{6,5},{7,6},{8,11},{9,8},{10,9... | collective-permute-start | bytes 196616 | tf_op jit(solution)/shard_map/ppermute | solution.py:42
  42.1 3.5 %collective-permute-start.13 = (bf16[4,2,128,128]{3,2,1,0:T(8,128)(2,1)S(1)}, bf16[4,2,128,128]{3,2,1,0:T(8,128)(2,1)}, u32[]{:S(2)}, u32[]{:S(2)}) collective-permute-start(bf16[4,2,128,128]{3,2,1,0:T(8,128)(2,1)S(1)} %pad_maximum_fusion.1), channel_id=1, source_target_pairs={{0,4},{1,5},{2,6},{3,7},{4,8},{5,9},{6,10},{7,11},{8,12},{9,13},{1... | collective-permute-start | bytes 786440 | tf_op jit(solution)/shard_map/ppermute | solution.py:48
  45.7 3.5 %collective-permute-start.3 = (bf16[4,2,128,128]{3,2,1,0:T(8,128)(2,1)S(1)}, bf16[4,2,128,128]{3,2,1,0:T(8,128)(2,1)}, u32[]{:S(2)}, u32[]{:S(2)}) collective-permute-start(bf16[4,2,128,128]{3,2,1,0:T(8,128)(2,1)S(1)} %pad_maximum_fusion), channel_id=1, source_target_pairs={{0,4},{1,5},{2,6},{3,7},{4,8},{5,9},{6,10},{7,11},{8,12},{9,13},{1... | collective-permute-start | bytes 786440 | tf_op jit(solution)/shard_map/ppermute | solution.py:48
  49.3 3.6 %collective-permute-start.17 = (bf16[4,2,128,128]{3,2,1,0:T(8,128)(2,1)S(1)}, bf16[4,2,128,128]{3,2,1,0:T(8,128)(2,1)S(1)}, u32[]{:S(2)}, u32[]{:S(2)}) collective-permute-start(bf16[4,2,128,128]{3,2,1,0:T(8,128)(2,1)S(1)} %pad_maximum_fusion.1), channel_id=1, source_target_pairs={{0,28},{1,29},{2,30},{3,31},{4,0},{5,1},{6,2},{7,3},{8,4},{9,5},{1... | collective-permute-start | bytes 786440 | tf_op jit(solution)/shard_map/ppermute | solution.py:51
  52.9 3.6 %collective-permute-start.7 = (bf16[4,2,128,128]{3,2,1,0:T(8,128)(2,1)S(1)}, bf16[4,2,128,128]{3,2,1,0:T(8,128)(2,1)S(1)}, u32[]{:S(2)}, u32[]{:S(2)}) collective-permute-start(bf16[4,2,128,128]{3,2,1,0:T(8,128)(2,1)S(1)} %pad_maximum_fusion), channel_id=1, source_target_pairs={{0,28},{1,29},{2,30},{3,31},{4,0},{5,1},{6,2},{7,3},{8,4},{9,5},{1... | collective-permute-start | bytes 786440 | tf_op jit(solution)/shard_map/ppermute | solution.py:51
  61.7 5.1 %collective-permute-start.18 = (bf16[4,2,128,128]{3,2,1,0:T(8,128)(2,1)S(1)}, bf16[4,2,128,128]{3,2,1,0:T(8,128)(2,1)S(1)}, u32[]{:S(2)}, u32[]{:S(2)}) collective-permute-start(bf16[4,2,128,128]{3,2,1,0:T(8,128)(2,1)S(1)} %collective-permute-done.17), channel_id=1, source_target_pairs={{0,28},{1,29},{2,30},{3,31},{4,0},{5,1},{6,2},{7,3},{8,4},{9,5},{1... | collective-permute-start | bytes 786440 | tf_op jit(solution)/shard_map/ppermute | solution.py:51
  66.8 2.9 collective-permute-start.8
  71.8 3.0 collective-permute-start.15
  78.0 5.0 %collective-permute-start.19 = (bf16[4,2,128,128]{3,2,1,0:T(8,128)(2,1)S(1)}, bf16[4,2,128,128]{3,2,1,0:T(8,128)(2,1)}, u32[]{:S(2)}, u32[]{:S(2)}) collective-permute-start(bf16[4,2,128,128]{3,2,1,0:T(8,128)(2,1)S(1)} %collective-permute-done.18), channel_id=1, source_target_pairs={{0,28},{1,29},{2,30},{3,31},{4,0},{5,1},{6,2},{7,3},{8,4},{9,5},{1... | collective-permute-start | bytes 786440 | tf_op jit(solution)/shard_map/ppermute | solution.py:51
  83.0 2.9 collective-permute-start.9
  89.3 3.0 collective-permute-start.16
  120.5 3.9 %convolution_bitcast_fusion.1 = f32[128,8,128]{0,2,1:T(8,128)} fusion(bf16[8,8,128,128]{2,3,1,0:T(8,128)(2,1)} %copy-done.7, bf16[128,8,8,128]{3,0,2,1:T(8,128)(2,1)S(1)} %bitcast.204), kind=kOutput, calls=%fused_computation.14 | convolution fusion | flops 268435456 | bytes 4718592 | tf_op jit(solution)/shard_map/tgki,gkio->tgo/dot_general | solution.py:117
  125.4 5.2 %fusion.34 = f32[8,8,128,128]{3,2,1,0:T(8,128)} fusion(bf16[8,8,128,128]{2,3,1,0:T(8,128)(2,1)} %bitcast_dynamic-update-slice_fusion.8, f32[128,8,128]{0,2,1:T(8,128)} %convolution_bitcast_fusion.1), kind=kOutput, calls=%fused_computation.101 | convolution fusion | flops 269090816 | bytes 6815744 | tf_op jit(solution)/shard_map/tgh,gkho->tgko/dot_general | solution.py:119
  130.6 2.5 fusion.7
  133.0 5.7 %copy.152 = f32[128,64,128]{2,0,1:T(8,128)} copy(f32[128,64,128]{0,2,1:T(8,128)} %bitcast.211) | data formatting | bytes 8388608 | tf_op jit(solution)/shard_map/reshape | solution.py:121
  139.0 8.8 %scatter_fusion = f32[128,32,128]{2,0,1:T(8,128)S(1)} fusion(f32[128,32,128]{2,0,1:T(8,128)S(1)} %broadcast.211.clone.1, s32[64]{0:T(128)S(1)} %fusion.31, f32[64,128,128]{2,1,0:T(8,128)} %bitcast.209), kind=kCustom, calls=%fused_computation.4 | custom fusion | flops 1048576 | bytes 12583168 | tf_op jit(solution)/shard_map/scatter-add | solution.py:121
  148.9 2.4 copy.153
  151.3 2.8 fusion.43
  154.1 5.7 %copy.160 = f32[128,64,128]{2,0,1:T(8,128)} copy(f32[128,64,128]{0,2,1:T(8,128)} %bitcast.210) | data formatting | bytes 8388608 | tf_op jit(solution)/shard_map/reshape | solution.py:133
  160.1 8.8 %scatter_fusion.1 = f32[128,32,128]{2,0,1:T(8,128)S(1)} fusion(f32[128,32,128]{2,0,1:T(8,128)S(1)} %broadcast.211.clone, s32[64]{0:T(128)S(1)} %fusion.32, f32[64,128,128]{2,1,0:T(8,128)} %bitcast.208), kind=kCustom, calls=%fused_computation.5 | custom fusion | flops 1048576 | bytes 12583168 | tf_op jit(solution)/shard_map/scatter-add | solution.py:133
  173.4 28.4 %all-to-all-start.1 = ((bf16[16,2,128,256]{2,3,1,0:T(8,128)(2,1)}), bf16[16,2,128,256]{2,3,1,0:T(8,128)(2,1)}, u32[]{:S(2)}, u32[]{:S(2)}) async-start(bf16[16,2,128,256]{2,3,1,0:T(8,128)(2,1)} %copy.162), calls=%async_computation.1 | async-start | bytes 4194304 | tf_op jit(solution)/shard_map/all_to_all | solution.py:26
  201.8 2.7 copy.155
  204.4 2.3 fusion.2
  209.6 3.9 %collective-permute-start.30 = (bf16[4,2,128,128]{3,2,1,0:T(8,128)(2,1)}, bf16[4,2,128,128]{3,2,1,0:T(8,128)(2,1)}, u32[]{:S(2)}, u32[]{:S(2)}) collective-permute-start(bf16[4,2,128,128]{3,2,1,0:T(8,128)(2,1)} %copy.168), channel_id=1, source_target_pairs={{0,4},{1,5},{2,6},{3,7},{4,8},{5,9},{6,10},{7,11},{8,12},{9,13},{1... | collective-permute-start | bytes 786440 | tf_op jit(solution)/shard_map/ppermute | solution.py:64
  214.3 3.3 %collective-permute-start.34 = (bf16[4,2,128,128]{3,2,1,0:T(8,128)(2,1)}, bf16[4,2,128,128]{3,2,1,0:T(8,128)(2,1)}, u32[]{:S(2)}, u32[]{:S(2)}) collective-permute-start(bf16[4,2,128,128]{3,2,1,0:T(8,128)(2,1)} %copy.173), channel_id=1, source_target_pairs={{0,28},{1,29},{2,30},{3,31},{4,0},{5,1},{6,2},{7,3},{8,4},{9,5},{1... | collective-permute-start | bytes 786440 | tf_op jit(solution)/shard_map/ppermute | solution.py:69
  217.7 2.7 copy.149
  220.4 2.3 multiply_convert_fusion.1
  228.1 3.9 %collective-permute-start.20 = (bf16[4,2,128,128]{3,2,1,0:T(8,128)(2,1)}, bf16[4,2,128,128]{3,2,1,0:T(8,128)(2,1)}, u32[]{:S(2)}, u32[]{:S(2)}) collective-permute-start(bf16[4,2,128,128]{3,2,1,0:T(8,128)(2,1)} %bitcast.66), channel_id=1, source_target_pairs={{0,4},{1,5},{2,6},{3,7},{4,8},{5,9},{6,10},{7,11},{8,12},{9,13},{1... | collective-permute-start | bytes 786440 | tf_op jit(solution)/shard_map/ppermute | solution.py:64
  232.0 3.1 collective-permute-start.24
  238.8 5.7 %all-to-all-start.2 = ((bf16[16,2,128,256]{3,2,1,0:T(8,128)(2,1)}), bf16[16,2,128,256]{3,2,1,0:T(8,128)(2,1)S(1)}, u32[]{:S(2)}, u32[]{:S(2)}) async-start(bf16[16,2,128,256]{3,2,1,0:T(8,128)(2,1)} %broadcast_in_dim.5), calls=%async_computation.2 | async-start | bytes 4194304 | tf_op jit(solution)/shard_map/all_to_all | solution.py:22
  245.8 2.8 collective-permute-start.31
  249.8 4.5 %collective-permute-start.35 = (bf16[4,2,128,128]{3,2,1,0:T(8,128)(2,1)S(1)}, bf16[4,2,128,128]{3,2,1,0:T(8,128)(2,1)S(1)}, u32[]{:S(2)}, u32[]{:S(2)}) collective-permute-start(bf16[4,2,128,128]{3,2,1,0:T(8,128)(2,1)S(1)} %add_convert_fusion.1), channel_id=1, source_target_pairs={{0,28},{1,29},{2,30},{3,31},{4,0},{5,1},{6,2},{7,3},{8,4},{9,5},{1... | collective-permute-start | bytes 786440 | tf_op jit(solution)/shard_map/ppermute | solution.py:69
  258.4 5.3 %collective-permute-start.25 = (bf16[4,2,128,128]{3,2,1,0:T(8,128)(2,1)S(1)}, bf16[4,2,128,128]{3,2,1,0:T(8,128)(2,1)S(1)}, u32[]{:S(2)}, u32[]{:S(2)}) collective-permute-start(bf16[4,2,128,128]{3,2,1,0:T(8,128)(2,1)S(1)} %fusion.12), channel_id=1, source_target_pairs={{0,28},{1,29},{2,30},{3,31},{4,0},{5,1},{6,2},{7,3},{8,4},{9,5},{1... | collective-permute-start | bytes 786440 | tf_op jit(solution)/shard_map/ppermute | solution.py:69
  265.7 5.1 %collective-permute-start.36 = (bf16[4,2,128,128]{3,2,1,0:T(8,128)(2,1)S(1)}, bf16[4,2,128,128]{3,2,1,0:T(8,128)(2,1)S(1)}, u32[]{:S(2)}, u32[]{:S(2)}) collective-permute-start(bf16[4,2,128,128]{3,2,1,0:T(8,128)(2,1)S(1)} %add_convert_fusion), channel_id=1, source_target_pairs={{0,28},{1,29},{2,30},{3,31},{4,0},{5,1},{6,2},{7,3},{8,4},{9,5},{1... | collective-permute-start | bytes 786440 | tf_op jit(solution)/shard_map/ppermute | solution.py:69
  276.3 5.1 %collective-permute-start.26 = (bf16[4,2,128,128]{3,2,1,0:T(8,128)(2,1)S(1)}, bf16[4,2,128,128]{3,2,1,0:T(8,128)(2,1)S(1)}, u32[]{:S(2)}, u32[]{:S(2)}) collective-permute-start(bf16[4,2,128,128]{3,2,1,0:T(8,128)(2,1)S(1)} %fusion.13), channel_id=1, source_target_pairs={{0,28},{1,29},{2,30},{3,31},{4,0},{5,1},{6,2},{7,3},{8,4},{9,5},{1... | collective-permute-start | bytes 786440 | tf_op jit(solution)/shard_map/ppermute | solution.py:69
  285.4 2.6 collective-permute-done.33
  290.0 6.9 %collective-permute-start.38 = (bf16[2,128,128]{2,1,0:T(8,128)(2,1)S(1)}, bf16[2,128,128]{2,1,0:T(8,128)(2,1)S(1)}, u32[]{:S(2)}, u32[]{:S(2)}) collective-permute-start(bf16[2,128,128]{2,1,0:T(8,128)(2,1)S(1)} %get-tuple-element.34), channel_id=1, source_target_pairs={{0,2},{1,3},{2,0},{3,1},{4,6},{5,7},{6,4},{7,5},{8,10},{9,11},{10,... | collective-permute-start | bytes 196616 | tf_op jit(solution)/shard_map/ppermute | solution.py:77
  299.0 6.0 %collective-permute-start.27 = (bf16[2,128,128]{2,1,0:T(8,128)(2,1)S(1)}, bf16[2,128,128]{2,1,0:T(8,128)(2,1)S(1)}, u32[]{:S(2)}, u32[]{:S(2)}) collective-permute-start(bf16[2,128,128]{2,1,0:T(8,128)(2,1)S(1)} %get-tuple-element.35), channel_id=1, source_target_pairs={{0,3},{1,0},{2,1},{3,2},{4,7},{5,4},{6,5},{7,6},{8,11},{9,8},{10,9... | collective-permute-start | bytes 196616 | tf_op jit(solution)/shard_map/ppermute | solution.py:77
  305.0 2.9 collective-permute-start.28
  307.9 3.6 %collective-permute-start.29 = (bf16[2,128,128]{2,1,0:T(8,128)(2,1)S(1)}, bf16[2,128,128]{2,1,0:T(8,128)(2,1)S(1)}, u32[]{:S(2)}, u32[]{:S(2)}) collective-permute-start(bf16[2,128,128]{2,1,0:T(8,128)(2,1)S(1)} %get-tuple-element.36), channel_id=1, source_target_pairs={{0,1},{1,2},{2,3},{3,0},{4,5},{5,6},{6,7},{7,4},{8,9},{9,10},{10,1... | collective-permute-start | bytes 196616 | tf_op jit(solution)/shard_map/ppermute | solution.py:77
  312.2 4.3 %collective-permute-done.28 = bf16[2,128,128]{2,1,0:T(8,128)(2,1)S(1)} collective-permute-done((bf16[2,128,128]{2,1,0:T(8,128)(2,1)S(1)}, bf16[2,128,128]{2,1,0:T(8,128)(2,1)S(1)}, u32[]{:S(2)}, u32[]{:S(2)}) %collective-permute-start.28) | collective-permute-done | bytes 65568 | tf_op jit(solution)/shard_map/ppermute | solution.py:77
  317.3 2.4 copy.165
  (200 shorter events, 94.3 us)
Async XLA Ops:
  0.6 34.1 %copy-start = (s32[64]{0:T(128)S(1)}, s32[64]{0:T(128)}, u32[]{:S(2)}) copy-start(s32[64]{0:T(128)} %param.9) | copy-start | bytes 772
  0.6 35.9 %collective-permute-start.10 = (bf16[2,128,128]{2,1,0:T(8,128)(2,1)}, bf16[2,128,128]{2,1,0:T(8,128)(2,1)S(1)}, u32[]{:S(2)}, u32[]{:S(2)}) collective-permute-start(bf16[2,128,128]{2,1,0:T(8,128)(2,1)} %param.8), channel_id=1, source_target_pairs={{0,1},{1,2},{2,3},{3,0},{4,5},{5,6},{6,7},{7,4},{8,9},{9,10},{10,1... | collective-permute-start | bytes 196616 | tf_op jit(solution)/shard_map/ppermute | solution.py:42
  6.7 35.3 %collective-permute-start.11 = (bf16[2,128,128]{2,1,0:T(8,128)(2,1)}, bf16[2,128,128]{2,1,0:T(8,128)(2,1)S(1)}, u32[]{:S(2)}, u32[]{:S(2)}) collective-permute-start(bf16[2,128,128]{2,1,0:T(8,128)(2,1)} %param.8), channel_id=1, source_target_pairs={{0,2},{1,3},{2,0},{3,1},{4,6},{5,7},{6,4},{7,5},{8,10},{9,11},{10,... | collective-permute-start | bytes 196616 | tf_op jit(solution)/shard_map/ppermute | solution.py:42
  15.9 26.2 %collective-permute-start.12 = (bf16[2,128,128]{2,1,0:T(8,128)(2,1)}, bf16[2,128,128]{2,1,0:T(8,128)(2,1)S(1)}, u32[]{:S(2)}, u32[]{:S(2)}) collective-permute-start(bf16[2,128,128]{2,1,0:T(8,128)(2,1)} %param.8), channel_id=1, source_target_pairs={{0,3},{1,0},{2,1},{3,2},{4,7},{5,4},{6,5},{7,6},{8,11},{9,8},{10,9... | collective-permute-start | bytes 196616 | tf_op jit(solution)/shard_map/ppermute | solution.py:42
  19.5 26.1 %collective-permute-start = (bf16[2,128,128]{2,1,0:T(8,128)(2,1)}, bf16[2,128,128]{2,1,0:T(8,128)(2,1)S(1)}, u32[]{:S(2)}, u32[]{:S(2)}) collective-permute-start(bf16[2,128,128]{2,1,0:T(8,128)(2,1)} %param.10), channel_id=1, source_target_pairs={{0,1},{1,2},{2,3},{3,0},{4,5},{5,6},{6,7},{7,4},{8,9},{9,10},{10,1... | collective-permute-start | bytes 196616 | tf_op jit(solution)/shard_map/ppermute | solution.py:42
  22.6 23.0 %collective-permute-start.1 = (bf16[2,128,128]{2,1,0:T(8,128)(2,1)}, bf16[2,128,128]{2,1,0:T(8,128)(2,1)S(1)}, u32[]{:S(2)}, u32[]{:S(2)}) collective-permute-start(bf16[2,128,128]{2,1,0:T(8,128)(2,1)} %param.10), channel_id=1, source_target_pairs={{0,2},{1,3},{2,0},{3,1},{4,6},{5,7},{6,4},{7,5},{8,10},{9,11},{10,... | collective-permute-start | bytes 196616 | tf_op jit(solution)/shard_map/ppermute | solution.py:42
  28.6 85.9 %all-to-all-start = ((bf16[16,2,128,256]{2,3,1,0:T(8,128)(2,1)}), bf16[16,2,128,256]{2,3,1,0:T(8,128)(2,1)}, u32[]{:S(2)}, u32[]{:S(2)}) async-start(bf16[16,2,128,256]{2,3,1,0:T(8,128)(2,1)} %broadcast_in_dim.4), calls=%async_computation | async-start | bytes 4194304 | tf_op jit(solution)/shard_map/all_to_all | solution.py:22
  36.5 9.1 %collective-permute-start.2 = (bf16[2,128,128]{2,1,0:T(8,128)(2,1)S(1)}, bf16[2,128,128]{2,1,0:T(8,128)(2,1)S(1)}, u32[]{:S(2)}, u32[]{:S(2)}) collective-permute-start(bf16[2,128,128]{2,1,0:T(8,128)(2,1)S(1)} %copy-done.23), channel_id=1, source_target_pairs={{0,3},{1,0},{2,1},{3,2},{4,7},{5,4},{6,5},{7,6},{8,11},{9,8},{10,9... | collective-permute-start | bytes 196616 | tf_op jit(solution)/shard_map/ppermute | solution.py:42
  42.1 14.4 %collective-permute-start.13 = (bf16[4,2,128,128]{3,2,1,0:T(8,128)(2,1)S(1)}, bf16[4,2,128,128]{3,2,1,0:T(8,128)(2,1)}, u32[]{:S(2)}, u32[]{:S(2)}) collective-permute-start(bf16[4,2,128,128]{3,2,1,0:T(8,128)(2,1)S(1)} %pad_maximum_fusion.1), channel_id=1, source_target_pairs={{0,4},{1,5},{2,6},{3,7},{4,8},{5,9},{6,10},{7,11},{8,12},{9,13},{1... | collective-permute-start | bytes 786440 | tf_op jit(solution)/shard_map/ppermute | solution.py:48
  45.7 13.9 %collective-permute-start.3 = (bf16[4,2,128,128]{3,2,1,0:T(8,128)(2,1)S(1)}, bf16[4,2,128,128]{3,2,1,0:T(8,128)(2,1)}, u32[]{:S(2)}, u32[]{:S(2)}) collective-permute-start(bf16[4,2,128,128]{3,2,1,0:T(8,128)(2,1)S(1)} %pad_maximum_fusion), channel_id=1, source_target_pairs={{0,4},{1,5},{2,6},{3,7},{4,8},{5,9},{6,10},{7,11},{8,12},{9,13},{1... | collective-permute-start | bytes 786440 | tf_op jit(solution)/shard_map/ppermute | solution.py:48
  49.3 12.3 %collective-permute-start.17 = (bf16[4,2,128,128]{3,2,1,0:T(8,128)(2,1)S(1)}, bf16[4,2,128,128]{3,2,1,0:T(8,128)(2,1)S(1)}, u32[]{:S(2)}, u32[]{:S(2)}) collective-permute-start(bf16[4,2,128,128]{3,2,1,0:T(8,128)(2,1)S(1)} %pad_maximum_fusion.1), channel_id=1, source_target_pairs={{0,28},{1,29},{2,30},{3,31},{4,0},{5,1},{6,2},{7,3},{8,4},{9,5},{1... | collective-permute-start | bytes 786440 | tf_op jit(solution)/shard_map/ppermute | solution.py:51
  52.9 13.9 %collective-permute-start.7 = (bf16[4,2,128,128]{3,2,1,0:T(8,128)(2,1)S(1)}, bf16[4,2,128,128]{3,2,1,0:T(8,128)(2,1)S(1)}, u32[]{:S(2)}, u32[]{:S(2)}) collective-permute-start(bf16[4,2,128,128]{3,2,1,0:T(8,128)(2,1)S(1)} %pad_maximum_fusion), channel_id=1, source_target_pairs={{0,28},{1,29},{2,30},{3,31},{4,0},{5,1},{6,2},{7,3},{8,4},{9,5},{1... | collective-permute-start | bytes 786440 | tf_op jit(solution)/shard_map/ppermute | solution.py:51
  56.5 15.2 %collective-permute-start.14 = (bf16[4,2,128,128]{3,2,1,0:T(8,128)(2,1)}, bf16[4,2,128,128]{3,2,1,0:T(8,128)(2,1)}, u32[]{:S(2)}, u32[]{:S(2)}) collective-permute-start(bf16[4,2,128,128]{3,2,1,0:T(8,128)(2,1)} %collective-permute-done.13), channel_id=1, source_target_pairs={{0,4},{1,5},{2,6},{3,7},{4,8},{5,9},{6,10},{7,11},{8,12},{9,13},{1... | collective-permute-start | bytes 786440 | tf_op jit(solution)/shard_map/ppermute | solution.py:48
  59.5 15.2 %collective-permute-start.4 = (bf16[4,2,128,128]{3,2,1,0:T(8,128)(2,1)}, bf16[4,2,128,128]{3,2,1,0:T(8,128)(2,1)}, u32[]{:S(2)}, u32[]{:S(2)}) collective-permute-start(bf16[4,2,128,128]{3,2,1,0:T(8,128)(2,1)} %collective-permute-done.3), channel_id=1, source_target_pairs={{0,4},{1,5},{2,6},{3,7},{4,8},{5,9},{6,10},{7,11},{8,12},{9,13},{1... | collective-permute-start | bytes 786440 | tf_op jit(solution)/shard_map/ppermute | solution.py:48
  61.7 16.4 %collective-permute-start.18 = (bf16[4,2,128,128]{3,2,1,0:T(8,128)(2,1)S(1)}, bf16[4,2,128,128]{3,2,1,0:T(8,128)(2,1)S(1)}, u32[]{:S(2)}, u32[]{:S(2)}) collective-permute-start(bf16[4,2,128,128]{3,2,1,0:T(8,128)(2,1)S(1)} %collective-permute-done.17), channel_id=1, source_target_pairs={{0,28},{1,29},{2,30},{3,31},{4,0},{5,1},{6,2},{7,3},{8,4},{9,5},{1... | collective-permute-start | bytes 786440 | tf_op jit(solution)/shard_map/ppermute | solution.py:51
  66.8 16.2 %collective-permute-start.8 = (bf16[4,2,128,128]{3,2,1,0:T(8,128)(2,1)S(1)}, bf16[4,2,128,128]{3,2,1,0:T(8,128)(2,1)}, u32[]{:S(2)}, u32[]{:S(2)}) collective-permute-start(bf16[4,2,128,128]{3,2,1,0:T(8,128)(2,1)S(1)} %collective-permute-done.7), channel_id=1, source_target_pairs={{0,28},{1,29},{2,30},{3,31},{4,0},{5,1},{6,2},{7,3},{8,4},{9,5},{1... | collective-permute-start | bytes 786440 | tf_op jit(solution)/shard_map/ppermute | solution.py:51
  71.8 17.5 %collective-permute-start.15 = (bf16[4,2,128,128]{3,2,1,0:T(8,128)(2,1)}, bf16[4,2,128,128]{3,2,1,0:T(8,128)(2,1)}, u32[]{:S(2)}, u32[]{:S(2)}) collective-permute-start(bf16[4,2,128,128]{3,2,1,0:T(8,128)(2,1)} %collective-permute-done.14), channel_id=1, source_target_pairs={{0,4},{1,5},{2,6},{3,7},{4,8},{5,9},{6,10},{7,11},{8,12},{9,13},{1... | collective-permute-start | bytes 786440 | tf_op jit(solution)/shard_map/ppermute | solution.py:48
  74.8 17.5 %collective-permute-start.5 = (bf16[4,2,128,128]{3,2,1,0:T(8,128)(2,1)}, bf16[4,2,128,128]{3,2,1,0:T(8,128)(2,1)}, u32[]{:S(2)}, u32[]{:S(2)}) collective-permute-start(bf16[4,2,128,128]{3,2,1,0:T(8,128)(2,1)} %collective-permute-done.4), channel_id=1, source_target_pairs={{0,4},{1,5},{2,6},{3,7},{4,8},{5,9},{6,10},{7,11},{8,12},{9,13},{1... | collective-permute-start | bytes 786440 | tf_op jit(solution)/shard_map/ppermute | solution.py:48
  78.0 22.1 %collective-permute-start.19 = (bf16[4,2,128,128]{3,2,1,0:T(8,128)(2,1)S(1)}, bf16[4,2,128,128]{3,2,1,0:T(8,128)(2,1)}, u32[]{:S(2)}, u32[]{:S(2)}) collective-permute-start(bf16[4,2,128,128]{3,2,1,0:T(8,128)(2,1)S(1)} %collective-permute-done.18), channel_id=1, source_target_pairs={{0,28},{1,29},{2,30},{3,31},{4,0},{5,1},{6,2},{7,3},{8,4},{9,5},{1... | collective-permute-start | bytes 786440 | tf_op jit(solution)/shard_map/ppermute | solution.py:51
  83.0 18.9 %collective-permute-start.9 = (bf16[4,2,128,128]{3,2,1,0:T(8,128)(2,1)}, bf16[4,2,128,128]{3,2,1,0:T(8,128)(2,1)}, u32[]{:S(2)}, u32[]{:S(2)}) collective-permute-start(bf16[4,2,128,128]{3,2,1,0:T(8,128)(2,1)} %collective-permute-done.8), channel_id=1, source_target_pairs={{0,28},{1,29},{2,30},{3,31},{4,0},{5,1},{6,2},{7,3},{8,4},{9,5},{1... | collective-permute-start | bytes 786440 | tf_op jit(solution)/shard_map/ppermute | solution.py:51
  89.3 16.3 %collective-permute-start.16 = (bf16[4,2,128,128]{3,2,1,0:T(8,128)(2,1)}, bf16[4,2,128,128]{3,2,1,0:T(8,128)(2,1)}, u32[]{:S(2)}, u32[]{:S(2)}) collective-permute-start(bf16[4,2,128,128]{3,2,1,0:T(8,128)(2,1)} %collective-permute-done.15), channel_id=1, source_target_pairs={{0,4},{1,5},{2,6},{3,7},{4,8},{5,9},{6,10},{7,11},{8,12},{9,13},{1... | collective-permute-start | bytes 786440 | tf_op jit(solution)/shard_map/ppermute | solution.py:48
  92.3 15.1 %collective-permute-start.6 = (bf16[4,2,128,128]{3,2,1,0:T(8,128)(2,1)}, bf16[4,2,128,128]{3,2,1,0:T(8,128)(2,1)}, u32[]{:S(2)}, u32[]{:S(2)}) collective-permute-start(bf16[4,2,128,128]{3,2,1,0:T(8,128)(2,1)} %collective-permute-done.5), channel_id=1, source_target_pairs={{0,4},{1,5},{2,6},{3,7},{4,8},{5,9},{6,10},{7,11},{8,12},{9,13},{1... | collective-permute-start | bytes 786440 | tf_op jit(solution)/shard_map/ppermute | solution.py:48
  173.4 28.4 %copy-start.6 = (bf16[64,128,128]{2,1,0:T(8,128)(2,1)S(1)}, bf16[64,128,128]{2,1,0:T(8,128)(2,1)}, u32[]{:S(2)}) copy-start(bf16[64,128,128]{2,1,0:T(8,128)(2,1)} %copy-done.5) | copy-start | bytes 6291460
  173.4 61.8 %all-to-all-start.1 = ((bf16[16,2,128,256]{2,3,1,0:T(8,128)(2,1)}), bf16[16,2,128,256]{2,3,1,0:T(8,128)(2,1)}, u32[]{:S(2)}, u32[]{:S(2)}) async-start(bf16[16,2,128,256]{2,3,1,0:T(8,128)(2,1)} %copy.162), calls=%async_computation.1 | async-start | bytes 4194304 | tf_op jit(solution)/shard_map/all_to_all | solution.py:26
  209.6 35.0 %collective-permute-start.30 = (bf16[4,2,128,128]{3,2,1,0:T(8,128)(2,1)}, bf16[4,2,128,128]{3,2,1,0:T(8,128)(2,1)}, u32[]{:S(2)}, u32[]{:S(2)}) collective-permute-start(bf16[4,2,128,128]{3,2,1,0:T(8,128)(2,1)} %copy.168), channel_id=1, source_target_pairs={{0,4},{1,5},{2,6},{3,7},{4,8},{5,9},{6,10},{7,11},{8,12},{9,13},{1... | collective-permute-start | bytes 786440 | tf_op jit(solution)/shard_map/ppermute | solution.py:64
  214.3 34.3 %collective-permute-start.34 = (bf16[4,2,128,128]{3,2,1,0:T(8,128)(2,1)}, bf16[4,2,128,128]{3,2,1,0:T(8,128)(2,1)}, u32[]{:S(2)}, u32[]{:S(2)}) collective-permute-start(bf16[4,2,128,128]{3,2,1,0:T(8,128)(2,1)} %copy.173), channel_id=1, source_target_pairs={{0,28},{1,29},{2,30},{3,31},{4,0},{5,1},{6,2},{7,3},{8,4},{9,5},{1... | collective-permute-start | bytes 786440 | tf_op jit(solution)/shard_map/ppermute | solution.py:69
  228.1 26.2 %collective-permute-start.20 = (bf16[4,2,128,128]{3,2,1,0:T(8,128)(2,1)}, bf16[4,2,128,128]{3,2,1,0:T(8,128)(2,1)}, u32[]{:S(2)}, u32[]{:S(2)}) collective-permute-start(bf16[4,2,128,128]{3,2,1,0:T(8,128)(2,1)} %bitcast.66), channel_id=1, source_target_pairs={{0,4},{1,5},{2,6},{3,7},{4,8},{5,9},{6,10},{7,11},{8,12},{9,13},{1... | collective-permute-start | bytes 786440 | tf_op jit(solution)/shard_map/ppermute | solution.py:64
  232.0 25.3 %collective-permute-start.24 = (bf16[4,2,128,128]{3,2,1,0:T(8,128)(2,1)}, bf16[4,2,128,128]{3,2,1,0:T(8,128)(2,1)}, u32[]{:S(2)}, u32[]{:S(2)}) collective-permute-start(bf16[4,2,128,128]{3,2,1,0:T(8,128)(2,1)} %bitcast.69), channel_id=1, source_target_pairs={{0,28},{1,29},{2,30},{3,31},{4,0},{5,1},{6,2},{7,3},{8,4},{9,5},{1... | collective-permute-start | bytes 786440 | tf_op jit(solution)/shard_map/ppermute | solution.py:69
  238.8 78.5 %all-to-all-start.2 = ((bf16[16,2,128,256]{3,2,1,0:T(8,128)(2,1)}), bf16[16,2,128,256]{3,2,1,0:T(8,128)(2,1)S(1)}, u32[]{:S(2)}, u32[]{:S(2)}) async-start(bf16[16,2,128,256]{3,2,1,0:T(8,128)(2,1)} %broadcast_in_dim.5), calls=%async_computation.2 | async-start | bytes 4194304 | tf_op jit(solution)/shard_map/all_to_all | solution.py:22
  245.8 19.9 %copy-start.11 = (f32[4,2,128,128]{3,2,1,0:T(8,128)S(1)}, f32[4,2,128,128]{3,2,1,0:T(8,128)}, u32[]{:S(2)}) copy-start(f32[4,2,128,128]{3,2,1,0:T(8,128)} %copy.175) | copy-start | bytes 1572868
  245.8 17.8 %collective-permute-start.31 = (bf16[4,2,128,128]{3,2,1,0:T(8,128)(2,1)S(1)}, bf16[4,2,128,128]{3,2,1,0:T(8,128)(2,1)S(1)}, u32[]{:S(2)}, u32[]{:S(2)}) collective-permute-start(bf16[4,2,128,128]{3,2,1,0:T(8,128)(2,1)S(1)} %add_convert_fusion.4), channel_id=1, source_target_pairs={{0,4},{1,5},{2,6},{3,7},{4,8},{5,9},{6,10},{7,11},{8,12},{9,13},{1... | collective-permute-start | bytes 786440 | tf_op jit(solution)/shard_map/ppermute | solution.py:64
  249.8 21.1 %copy-start.14 = (bf16[1,8,128,128]{3,2,1,0:T(8,128)(2,1)S(1)}, bf16[1,8,128,128]{3,2,1,0:T(8,128)(2,1)}, u32[]{:S(2)}) copy-start(bf16[1,8,128,128]{3,2,1,0:T(8,128)(2,1)} %get-tuple-element.26) | copy-start | bytes 786436
  249.8 15.8 %collective-permute-start.35 = (bf16[4,2,128,128]{3,2,1,0:T(8,128)(2,1)S(1)}, bf16[4,2,128,128]{3,2,1,0:T(8,128)(2,1)S(1)}, u32[]{:S(2)}, u32[]{:S(2)}) collective-permute-start(bf16[4,2,128,128]{3,2,1,0:T(8,128)(2,1)S(1)} %add_convert_fusion.1), channel_id=1, source_target_pairs={{0,28},{1,29},{2,30},{3,31},{4,0},{5,1},{6,2},{7,3},{8,4},{9,5},{1... | collective-permute-start | bytes 786440 | tf_op jit(solution)/shard_map/ppermute | solution.py:69
  255.4 15.5 %collective-permute-start.21 = (bf16[4,2,128,128]{3,2,1,0:T(8,128)(2,1)S(1)}, bf16[4,2,128,128]{3,2,1,0:T(8,128)(2,1)S(1)}, u32[]{:S(2)}, u32[]{:S(2)}) collective-permute-start(bf16[4,2,128,128]{3,2,1,0:T(8,128)(2,1)S(1)} %fusion.14), channel_id=1, source_target_pairs={{0,4},{1,5},{2,6},{3,7},{4,8},{5,9},{6,10},{7,11},{8,12},{9,13},{1... | collective-permute-start | bytes 786440 | tf_op jit(solution)/shard_map/ppermute | solution.py:64
  258.4 17.8 %collective-permute-start.25 = (bf16[4,2,128,128]{3,2,1,0:T(8,128)(2,1)S(1)}, bf16[4,2,128,128]{3,2,1,0:T(8,128)(2,1)S(1)}, u32[]{:S(2)}, u32[]{:S(2)}) collective-permute-start(bf16[4,2,128,128]{3,2,1,0:T(8,128)(2,1)S(1)} %fusion.12), channel_id=1, source_target_pairs={{0,28},{1,29},{2,30},{3,31},{4,0},{5,1},{6,2},{7,3},{8,4},{9,5},{1... | collective-permute-start | bytes 786440 | tf_op jit(solution)/shard_map/ppermute | solution.py:69
  263.7 10.3 %collective-permute-start.32 = (bf16[4,2,128,128]{3,2,1,0:T(8,128)(2,1)S(1)}, bf16[4,2,128,128]{3,2,1,0:T(8,128)(2,1)S(1)}, u32[]{:S(2)}, u32[]{:S(2)}) collective-permute-start(bf16[4,2,128,128]{3,2,1,0:T(8,128)(2,1)S(1)} %add_convert_fusion.3), channel_id=1, source_target_pairs={{0,4},{1,5},{2,6},{3,7},{4,8},{5,9},{6,10},{7,11},{8,12},{9,13},{1... | collective-permute-start | bytes 786440 | tf_op jit(solution)/shard_map/ppermute | solution.py:64
  265.7 19.6 %collective-permute-start.36 = (bf16[4,2,128,128]{3,2,1,0:T(8,128)(2,1)S(1)}, bf16[4,2,128,128]{3,2,1,0:T(8,128)(2,1)S(1)}, u32[]{:S(2)}, u32[]{:S(2)}) collective-permute-start(bf16[4,2,128,128]{3,2,1,0:T(8,128)(2,1)S(1)} %add_convert_fusion), channel_id=1, source_target_pairs={{0,28},{1,29},{2,30},{3,31},{4,0},{5,1},{6,2},{7,3},{8,4},{9,5},{1... | collective-permute-start | bytes 786440 | tf_op jit(solution)/shard_map/ppermute | solution.py:69
  271.0 12.3 %collective-permute-start.22 = (bf16[4,2,128,128]{3,2,1,0:T(8,128)(2,1)S(1)}, bf16[4,2,128,128]{3,2,1,0:T(8,128)(2,1)S(1)}, u32[]{:S(2)}, u32[]{:S(2)}) collective-permute-start(bf16[4,2,128,128]{3,2,1,0:T(8,128)(2,1)S(1)} %fusion.15), channel_id=1, source_target_pairs={{0,4},{1,5},{2,6},{3,7},{4,8},{5,9},{6,10},{7,11},{8,12},{9,13},{1... | collective-permute-start | bytes 786440 | tf_op jit(solution)/shard_map/ppermute | solution.py:64
  274.1 24.7 %copy-start.20 = (bf16[1,8,128,128]{3,2,1,0:T(8,128)(2,1)S(1)}, bf16[1,8,128,128]{3,2,1,0:T(8,128)(2,1)}, u32[]{:S(2)}) copy-start(bf16[1,8,128,128]{3,2,1,0:T(8,128)(2,1)} %get-tuple-element.20) | copy-start | bytes 786436
  274.1 13.8 %collective-permute-start.33 = (bf16[4,2,128,128]{3,2,1,0:T(8,128)(2,1)S(1)}, bf16[4,2,128,128]{3,2,1,0:T(8,128)(2,1)S(1)}, u32[]{:S(2)}, u32[]{:S(2)}) collective-permute-start(bf16[4,2,128,128]{3,2,1,0:T(8,128)(2,1)S(1)} %add_convert_fusion.2), channel_id=1, source_target_pairs={{0,4},{1,5},{2,6},{3,7},{4,8},{5,9},{6,10},{7,11},{8,12},{9,13},{1... | collective-permute-start | bytes 786440 | tf_op jit(solution)/shard_map/ppermute | solution.py:64
  276.3 22.5 %collective-permute-start.26 = (bf16[4,2,128,128]{3,2,1,0:T(8,128)(2,1)S(1)}, bf16[4,2,128,128]{3,2,1,0:T(8,128)(2,1)S(1)}, u32[]{:S(2)}, u32[]{:S(2)}) collective-permute-start(bf16[4,2,128,128]{3,2,1,0:T(8,128)(2,1)S(1)} %fusion.13), channel_id=1, source_target_pairs={{0,28},{1,29},{2,30},{3,31},{4,0},{5,1},{6,2},{7,3},{8,4},{9,5},{1... | collective-permute-start | bytes 786440 | tf_op jit(solution)/shard_map/ppermute | solution.py:69
  283.4 15.4 %collective-permute-start.23 = (bf16[4,2,128,128]{3,2,1,0:T(8,128)(2,1)S(1)}, bf16[4,2,128,128]{3,2,1,0:T(8,128)(2,1)S(1)}, u32[]{:S(2)}, u32[]{:S(2)}) collective-permute-start(bf16[4,2,128,128]{3,2,1,0:T(8,128)(2,1)S(1)} %fusion.16), channel_id=1, source_target_pairs={{0,4},{1,5},{2,6},{3,7},{4,8},{5,9},{6,10},{7,11},{8,12},{9,13},{1... | collective-permute-start | bytes 786440 | tf_op jit(solution)/shard_map/ppermute | solution.py:64
  288.1 19.8 %collective-permute-start.37 = (bf16[2,128,128]{2,1,0:T(8,128)(2,1)S(1)}, bf16[2,128,128]{2,1,0:T(8,128)(2,1)S(1)}, u32[]{:S(2)}, u32[]{:S(2)}) collective-permute-start(bf16[2,128,128]{2,1,0:T(8,128)(2,1)S(1)} %get-tuple-element.32), channel_id=1, source_target_pairs={{0,3},{1,0},{2,1},{3,2},{4,7},{5,4},{6,5},{7,6},{8,11},{9,8},{10,9... | collective-permute-start | bytes 196616 | tf_op jit(solution)/shard_map/ppermute | solution.py:77
  290.0 21.5 %collective-permute-start.38 = (bf16[2,128,128]{2,1,0:T(8,128)(2,1)S(1)}, bf16[2,128,128]{2,1,0:T(8,128)(2,1)S(1)}, u32[]{:S(2)}, u32[]{:S(2)}) collective-permute-start(bf16[2,128,128]{2,1,0:T(8,128)(2,1)S(1)} %get-tuple-element.34), channel_id=1, source_target_pairs={{0,2},{1,3},{2,0},{3,1},{4,6},{5,7},{6,4},{7,5},{8,10},{9,11},{10,... | collective-permute-start | bytes 196616 | tf_op jit(solution)/shard_map/ppermute | solution.py:77
  296.9 14.7 %collective-permute-start.39 = (bf16[2,128,128]{2,1,0:T(8,128)(2,1)S(1)}, bf16[2,128,128]{2,1,0:T(8,128)(2,1)S(1)}, u32[]{:S(2)}, u32[]{:S(2)}) collective-permute-start(bf16[2,128,128]{2,1,0:T(8,128)(2,1)S(1)} %get-tuple-element.33), channel_id=1, source_target_pairs={{0,1},{1,2},{2,3},{3,0},{4,5},{5,6},{6,7},{7,4},{8,9},{9,10},{10,1... | collective-permute-start | bytes 196616 | tf_op jit(solution)/shard_map/ppermute | solution.py:77
  299.0 13.2 %collective-permute-start.27 = (bf16[2,128,128]{2,1,0:T(8,128)(2,1)S(1)}, bf16[2,128,128]{2,1,0:T(8,128)(2,1)S(1)}, u32[]{:S(2)}, u32[]{:S(2)}) collective-permute-start(bf16[2,128,128]{2,1,0:T(8,128)(2,1)S(1)} %get-tuple-element.35), channel_id=1, source_target_pairs={{0,3},{1,0},{2,1},{3,2},{4,7},{5,4},{6,5},{7,6},{8,11},{9,8},{10,9... | collective-permute-start | bytes 196616 | tf_op jit(solution)/shard_map/ppermute | solution.py:77
  305.0 11.5 %collective-permute-start.28 = (bf16[2,128,128]{2,1,0:T(8,128)(2,1)S(1)}, bf16[2,128,128]{2,1,0:T(8,128)(2,1)S(1)}, u32[]{:S(2)}, u32[]{:S(2)}) collective-permute-start(bf16[2,128,128]{2,1,0:T(8,128)(2,1)S(1)} %get-tuple-element.37), channel_id=1, source_target_pairs={{0,2},{1,3},{2,0},{3,1},{4,6},{5,7},{6,4},{7,5},{8,10},{9,11},{10,... | collective-permute-start | bytes 196616 | tf_op jit(solution)/shard_map/ppermute | solution.py:77
  307.9 8.7 %collective-permute-start.29 = (bf16[2,128,128]{2,1,0:T(8,128)(2,1)S(1)}, bf16[2,128,128]{2,1,0:T(8,128)(2,1)S(1)}, u32[]{:S(2)}, u32[]{:S(2)}) collective-permute-start(bf16[2,128,128]{2,1,0:T(8,128)(2,1)S(1)} %get-tuple-element.36), channel_id=1, source_target_pairs={{0,1},{1,2},{2,3},{3,0},{4,5},{5,6},{6,7},{7,4},{8,9},{9,10},{10,1... | collective-permute-start | bytes 196616 | tf_op jit(solution)/shard_map/ppermute | solution.py:77
  (19 other events, 135.5 us)

commit v4 on v2

--- a/solution.py
+++ b/solution.py
@@ -30,60 +30,53 @@
 Z_HI = 4
 
 
-def dp_shift(n_y, n_z, dy, dz):
-    return [
-        (y * n_z + z, ((y + dy) % n_y) * n_z + (z + dz) % n_z)
-        for y in range(n_y)
-        for z in range(n_z)
-    ]
+def y_shift(n_y, dy):
+    return [(y, (y + dy) % n_y) for y in range(n_y)]
 
 
-def dp_gather_rel(x, n_y, n_z):
-    by_z = [x] + [lax.ppermute(x, "dp", dp_shift(n_y, n_z, 0, b)) for b in range(1, n_z)]
-    held = jnp.stack(by_z)
+def dp_gather_rel(x, n_y):
+    held = gather_all(x, "zh")
     n_f, n_b = n_y // 2, (n_y - 1) // 2
     fwd, bwd = [held], []
     cur_f = cur_b = held
     for k in range(1, n_f + 1):
-        cur_f = lax.ppermute(cur_f, "dp", dp_shift(n_y, n_z, 1, 0))
+        cur_f = lax.ppermute(cur_f, "y", y_shift(n_y, 1))
         fwd.append(cur_f)
         if k <= n_b:
-            cur_b = lax.ppermute(cur_b, "dp", dp_shift(n_y, n_z, -1, 0))
+            cur_b = lax.ppermute(cur_b, "y", y_shift(n_y, -1))
             bwd.append(cur_b)
     rel = fwd + [bwd[n_y - a - 1] for a in range(len(fwd), n_y)]
     return jnp.stack(rel)
 
 
-def dp_scatter_rel(terms, n_y, n_z):
+def dp_scatter_rel(terms, n_y):
     n_f, n_b = n_y // 2, (n_y - 1) // 2
     got_f = got_b = None
     for k in range(1, n_f + 1):
         part = terms[(n_y - n_f - 1 + k) % n_y].astype(jnp.float32)
         if got_f is not None:
             part = part + got_f.astype(jnp.float32)
-        got_f = lax.ppermute(part.astype(jnp.bfloat16), "dp", dp_shift(n_y, n_z, 1, 0))
+        got_f = lax.ppermute(part.astype(jnp.bfloat16), "y", y_shift(n_y, 1))
     for k in range(1, n_b + 1):
         part = terms[n_b + 1 - k].astype(jnp.float32)
         if got_b is not None:
             part = part + got_b.astype(jnp.float32)
-        got_b = lax.ppermute(part.astype(jnp.bfloat16), "dp", dp_shift(n_y, n_z, -1, 0))
+        got_b = lax.ppermute(part.astype(jnp.bfloat16), "y", y_shift(n_y, -1))
     acc = terms[0].astype(jnp.float32)
     if got_f is not None:
         acc = acc + got_f.astype(jnp.float32)
     if got_b is not None:
         acc = acc + got_b.astype(jnp.float32)
-    total = acc[0]
-    for b in range(1, n_z):
-        sent = lax.ppermute(acc[b].astype(jnp.bfloat16), "dp", dp_shift(n_y, n_z, 0, -b))
-        total = total + sent.astype(jnp.float32)
-    return total.astype(jnp.bfloat16)
+    return scatter_sum(acc.astype(jnp.bfloat16), "zh")
 
 
 def per_device(activations, out_grad, up_blocks, up_rows, down_blocks, down_rows):
     block_size = up_blocks.shape[1]
     groups = up_rows.shape[0] // K
     n_tensor = lax.axis_size("tensor")
-    n_dp = lax.axis_size("dp")
+    n_y = lax.axis_size("y")
+    n_z = lax.axis_size("zh")
+    n_dp = n_y * n_z
     tokens = activations.shape[0]
     shard_width = activations.shape[1]
     width = shard_width * n_tensor
@@ -93,19 +86,16 @@
     feats = jnp.moveaxis(feats, 0, 2).reshape(2, tokens, width)
     full_input, full_grad = feats[0], feats[1]
     per_dev = up_blocks.shape[0]
-    n_z = Z_HI
-    n_y = n_dp // n_z
     if n_z * per_dev != K:
         raise ValueError("layout")
-    weights = dp_gather_rel(jnp.stack([up_blocks, down_blocks]), n_y, n_z)
+    weights = dp_gather_rel(jnp.stack([up_blocks, down_blocks]), n_y)
     weights = jnp.moveaxis(weights, 2, 0).reshape(2, -1, block_size, block_size)
     up_all, down_all = weights[0], weights[1]
-    me = lax.axis_index("dp")
-    my_y, my_z = me // n_z, me % n_z
+    my_y = lax.axis_index("y")
     a = jnp.arange(n_y, dtype=jnp.int32)[:, None, None]
     b = jnp.arange(n_z, dtype=jnp.int32)[None, :, None]
     r = jnp.arange(per_dev, dtype=jnp.int32)[None, None, :]
-    order = ((((my_y - a) % n_y) * n_z + (my_z - b) % n_z) * per_dev + r).reshape(-1)
+    order = ((((my_y - a) % n_y) * n_z + b) * per_dev + r).reshape(-1)
     up_rows = up_rows[order]
     down_rows = down_rows[order]
 
@@ -145,28 +135,34 @@
 
     terms = jnp.stack([up_term, down_term]).astype(jnp.bfloat16)
     terms = terms.reshape(2, n_y, n_z, per_dev, block_size, block_size)
-    grads = dp_scatter_rel(jnp.moveaxis(terms, 0, 2), n_y, n_z)
+    grads = dp_scatter_rel(jnp.moveaxis(terms, 0, 2), n_y)
     return (both[0], both[1], grads[0], grads[1])
 
 
 def solution(mesh):
+    n_dp = mesh.shape["dp"]
+    n_z = Z_HI if n_dp % Z_HI == 0 else 1
+    split = jax.sharding.Mesh(
+        mesh.devices.reshape(mesh.shape["tensor"], n_dp // n_z, n_z), ("tensor", "y", "zh")
+    )
+    dp = ("y", "zh")
     placed = (
-        P("dp", "tensor"),
-        P("dp", "tensor"),
-        P(("tensor", "dp"), None, None),
+        P(dp, "tensor"),
+        P(dp, "tensor"),
+        P(("tensor",) + dp, None, None),
         P("tensor"),
-        P(("tensor", "dp"), None, None),
+        P(("tensor",) + dp, None, None),
         P("tensor"),
     )
     return jax.shard_map(
         per_device,
-        mesh=mesh,
+        mesh=split,
         in_specs=placed,
         out_specs=(
-            P("dp", None),
-            P("dp", None),
-            P(("tensor", "dp"), None, None),
-            P(("tensor", "dp"), None, None),
+            P(dp, None),
+            P(dp, None),
+            P(("tensor",) + dp, None, None),
+            P(("tensor",) + dp, None, None),
         ),
         check_vma=False,
     )

time: 294 us -> 321 us (1.092)
  waiting for transfers between devices: 85.4 us -> 135 us
  starting transfers between devices: 94.4 us -> 80.7 us
  local copies, waits for them, and re-layouts: 58.7 us -> 52.7 us
  other arithmetic: 34.5 us -> 29.6 us
    all_to_all x2 -> x3, waiting for transfers between devices: 0.01 us -> 43 us  [gather_all(): return lax.all_to_all(spread, axis_name, 0, 0, tiled=True)]
    ppermute x20 -> x14, starting transfers between devices: 76.5 us -> 48.1 us  [the longest x3 15.7 us: dp_gather_rel(): cur_b = lax.ppermute(cur_b, 'y', y_shift(n_y, -1))]
    all_to_all x1 -> x2, waiting for transfers between devices: 0.01 us -> 13 us  [scatter_sum(): got = lax.all_to_all(x, axis_name, 0, 0, tiled=True)]
    all_to_all x2 -> x3, starting transfers between devices: 11.6 us -> 23.2 us  [gather_all(): return lax.all_to_all(spread, axis_name, 0, 0, tiled=True)]
    ppermute x20 -> x14, waiting for transfers between devices: 85.4 us -> 79.1 us  [the longest x4 35.7 us: dp_gather_rel(): cur_f = lax.ppermute(cur_f, 'y', y_shift(n_y, 1))]
    another operation x5 -> x3, other arithmetic: 4.51 us -> 1.23 us  [the longest x1 0.92 us: per_device(): weights = dp_gather_rel(jnp.stack([up_blocks, down_blocks]), n_y)]
    convert_element_type x5, other arithmetic: 4.2 us -> 7.43 us  [the longest x3 4.1 us: dp_scatter_rel(): got_f = lax.ppermute(part.astype(jnp.bfloat16), 'y', y_shift(n_y, 1))]
    all_to_all x1 -> x2, starting transfers between devices: 6.28 us -> 9.33 us  [scatter_sum(): got = lax.all_to_all(x, axis_name, 0, 0, tiled=True)]
  transfers between devices with their start and end apart: 23 -> 19, of which waited for: 16 -> 12; matrix products, arithmetic and copies ran while one was open for 15% -> 16% of each run, Pallas kernels for 0% -> 0%
where the time goes in v4:
time: 321 us; the launch traced here: 317 us
  waiting for transfers between devices  135 us (42%)
  starting transfers between devices  80.7 us (25%)
  local copies, waits for them, and re-layouts  52.7 us (16%)
  other arithmetic  29.6 us (9%)
  matrix products  18.2 us (6%)
    all_to_all x3, waiting for transfers between devices, gather_all(): return lax.all_to_all(spread, axis_name, 0, 0, tiled=True)  43 us
    ppermute x4, waiting for transfers between devices, dp_gather_rel(): cur_f = lax.ppermute(cur_f, 'y', y_shift(n_y, 1))  35.7 us
    all_to_all x3, starting transfers between devices, gather_all(): return lax.all_to_all(spread, axis_name, 0, 0, tiled=True)  23.2 us
    ppermute x4, waiting for transfers between devices, dp_scatter_rel(): got_f = lax.ppermute(part.astype(jnp.bfloat16), 'y', y_shift(n_y, 1))  22.9 us
    ppermute x3, waiting for transfers between devices, dp_scatter_rel(): got_b = lax.ppermute(part.astype(jnp.bfloat16), 'y', y_shift(n_y, -1))  18.2 us
    ppermute x3, starting transfers between devices, dp_gather_rel(): cur_b = lax.ppermute(cur_b, 'y', y_shift(n_y, -1))  15.7 us
    ppermute x4, starting transfers between devices, dp_scatter_rel(): got_f = lax.ppermute(part.astype(jnp.bfloat16), 'y', y_shift(n_y, 1))  14.5 us
    all_to_all x2, waiting for transfers between devices, scatter_sum(): got = lax.all_to_all(x, axis_name, 0, 0, tiled=True)  13 us
  transfers between devices with their start and end apart: 19, of which 12 were waited for; matrix products, arithmetic and copies ran while one was open for 16% of the time, Pallas kernels for 0%

profile of v4, /device:TPU:6, one launch (start us, length us, event | category | flops | bytes accessed | tf_op | source)
XLA Modules:
  0.0 317.5 jit_solution(10806629680553576721)
XLA Ops:
  2.6 10.3 %all-to-all-start = ((bf16[4,2,2,128,128]{3,4,2,1,0:T(8,128)(2,1)}), bf16[4,2,2,128,128]{3,4,2,1,0:T(8,128)(2,1)S(1)}, u32[]{:S(2)}, u32[]{:S(2)}) async-start(bf16[4,2,2,128,128]{3,4,2,1,0:T(8,128)(2,1)} %broadcast_in_dim.6), calls=%async_computation | async-start | bytes 1048576 | tf_op jit(solution)/shard_map/all_to_all | solution.py:22
  13.2 14.4 %all-to-all-done = bf16[4,2,2,128,128]{3,4,2,1,0:T(8,128)(2,1)S(1)} async-done(((bf16[4,2,2,128,128]{3,4,2,1,0:T(8,128)(2,1)}), bf16[4,2,2,128,128]{3,4,2,1,0:T(8,128)(2,1)S(1)}, u32[]{:S(2)}, u32[]{:S(2)}) %all-to-all-start) | async-done | bytes 524320 | tf_op jit(solution)/shard_map/all_to_all | solution.py:22
  29.4 7.8 %all-to-all-start.1 = ((bf16[16,2,128,256]{2,3,1,0:T(8,128)(2,1)}), bf16[16,2,128,256]{2,3,1,0:T(8,128)(2,1)S(1)}, u32[]{:S(2)}, u32[]{:S(2)}) async-start(bf16[16,2,128,256]{2,3,1,0:T(8,128)(2,1)} %broadcast_in_dim.7), calls=%async_computation.1 | async-start | bytes 4194304 | tf_op jit(solution)/shard_map/all_to_all | solution.py:22
  37.1 3.5 %collective-permute-start = (bf16[4,2,2,128,128]{3,4,2,1,0:T(8,128)(2,1)S(1)}, bf16[4,2,2,128,128]{3,4,2,1,0:T(8,128)(2,1)}, u32[]{:S(2)}, u32[]{:S(2)}) collective-permute-start(bf16[4,2,2,128,128]{3,4,2,1,0:T(8,128)(2,1)S(1)} %all-to-all-done), channel_id=1, source_target_pairs={{0,4},{4,8},{8,12},{12,16},{16,20},{20,24},{24,28},{28,0},{1,5},{5... | collective-permute-start | bytes 1572872 | tf_op jit(solution)/shard_map/ppermute | solution.py:43
  41.7 13.1 %collective-permute-done = bf16[4,2,2,128,128]{3,4,2,1,0:T(8,128)(2,1)} collective-permute-done((bf16[4,2,2,128,128]{3,4,2,1,0:T(8,128)(2,1)S(1)}, bf16[4,2,2,128,128]{3,4,2,1,0:T(8,128)(2,1)}, u32[]{:S(2)}, u32[]{:S(2)}) %collective-permute-start) | collective-permute-done | bytes 524320 | tf_op jit(solution)/shard_map/ppermute | solution.py:43
  54.8 1.9 collective-permute-start.1
  57.6 5.1 %collective-permute-start.4 = (bf16[4,2,2,128,128]{3,4,2,1,0:T(8,128)(2,1)S(1)}, bf16[4,2,2,128,128]{3,4,2,1,0:T(8,128)(2,1)S(1)}, u32[]{:S(2)}, u32[]{:S(2)}) collective-permute-start(bf16[4,2,2,128,128]{3,4,2,1,0:T(8,128)(2,1)S(1)} %all-to-all-done), channel_id=1, source_target_pairs={{0,28},{4,0},{8,4},{12,8},{16,12},{20,16},{24,20},{28,24},{1,29},{... | collective-permute-start | bytes 1572872 | tf_op jit(solution)/shard_map/ppermute | solution.py:46
  62.9 8.8 %collective-permute-done.1 = bf16[4,2,2,128,128]{3,4,2,1,0:T(8,128)(2,1)} collective-permute-done((bf16[4,2,2,128,128]{3,4,2,1,0:T(8,128)(2,1)}, bf16[4,2,2,128,128]{3,4,2,1,0:T(8,128)(2,1)}, u32[]{:S(2)}, u32[]{:S(2)}) %collective-permute-start.1) | collective-permute-done | bytes 524320 | tf_op jit(solution)/shard_map/ppermute | solution.py:43
  73.6 5.4 %collective-permute-start.5 = (bf16[4,2,2,128,128]{3,4,2,1,0:T(8,128)(2,1)S(1)}, bf16[4,2,2,128,128]{3,4,2,1,0:T(8,128)(2,1)S(1)}, u32[]{:S(2)}, u32[]{:S(2)}) collective-permute-start(bf16[4,2,2,128,128]{3,4,2,1,0:T(8,128)(2,1)S(1)} %collective-permute-done.4), channel_id=1, source_target_pairs={{0,28},{4,0},{8,4},{12,8},{16,12},{20,16},{24,20},{28,24},{1,29},{... | collective-permute-start | bytes 1572872 | tf_op jit(solution)/shard_map/ppermute | solution.py:46
  79.1 8.5 %collective-permute-done.2 = bf16[4,2,2,128,128]{3,4,2,1,0:T(8,128)(2,1)S(1)} collective-permute-done((bf16[4,2,2,128,128]{3,4,2,1,0:T(8,128)(2,1)}, bf16[4,2,2,128,128]{3,4,2,1,0:T(8,128)(2,1)S(1)}, u32[]{:S(2)}, u32[]{:S(2)}) %collective-permute-start.2) | collective-permute-done | bytes 524320 | tf_op jit(solution)/shard_map/ppermute | solution.py:43
  87.6 1.9 collective-permute-start.3
  90.6 5.1 %collective-permute-start.6 = (bf16[4,2,2,128,128]{3,4,2,1,0:T(8,128)(2,1)S(1)}, bf16[4,2,2,128,128]{3,4,2,1,0:T(8,128)(2,1)S(1)}, u32[]{:S(2)}, u32[]{:S(2)}) collective-permute-start(bf16[4,2,2,128,128]{3,4,2,1,0:T(8,128)(2,1)S(1)} %collective-permute-done.5), channel_id=1, source_target_pairs={{0,28},{4,0},{8,4},{12,8},{16,12},{20,16},{24,20},{28,24},{1,29},{... | collective-permute-start | bytes 1572872 | tf_op jit(solution)/shard_map/ppermute | solution.py:46
  97.0 5.3 %collective-permute-done.3 = bf16[4,2,2,128,128]{3,4,2,1,0:T(8,128)(2,1)S(1)} collective-permute-done((bf16[4,2,2,128,128]{3,4,2,1,0:T(8,128)(2,1)S(1)}, bf16[4,2,2,128,128]{3,4,2,1,0:T(8,128)(2,1)S(1)}, u32[]{:S(2)}, u32[]{:S(2)}) %collective-permute-start.3) | collective-permute-done | bytes 524320 | tf_op jit(solution)/shard_map/ppermute | solution.py:43
  102.4 2.2 collective-permute-done.6
  104.9 2.6 fusion.25
  109.7 2.2 gather_fusion.2
  111.9 3.9 %convolution_bitcast_fusion.1 = f32[128,8,128]{0,2,1:T(8,128)} fusion(bf16[8,8,128,128]{2,3,1,0:T(8,128)(2,1)} %bitcast.155, bf16[128,8,8,128]{3,0,2,1:T(8,128)(2,1)S(1)} %bitcast.153), kind=kOutput, calls=%fused_computation.14 | convolution fusion | flops 268435456 | bytes 4718592 | tf_op jit(solution)/shard_map/tgki,gkio->tgo/dot_general | solution.py:108
  116.8 4.5 %fusion.23 = f32[8,8,128,128]{3,2,1,0:T(8,128)} fusion(bf16[8,8,128,128]{2,3,1,0:T(8,128)(2,1)} %bitcast.157, f32[128,8,128]{0,2,1:T(8,128)} %convolution_bitcast_fusion.1), kind=kOutput, calls=%fused_computation.77 | convolution fusion | flops 269090816 | bytes 6815744 | tf_op jit(solution)/shard_map/tgh,gkho->tgko/dot_general | solution.py:110
  122.2 3.9 %copy.97 = bf16[8,8,128,128]{2,3,1,0:T(8,128)(2,1)} copy(bf16[8,8,128,128]{3,2,1,0:T(8,128)(2,1)} %bitcast.154) | data formatting | bytes 4194304 | tf_op jit(solution)/shard_map/gather | solution.py:107
  126.1 4.6 %fusion.28 = f32[8,8,128,128]{3,2,1,0:T(8,128)} fusion(bf16[8,8,128,128]{2,3,1,0:T(8,128)(2,1)} %bitcast.156, bf16[128,8,128,1]{0,2,3,1:T(8,128)(2,1)S(1)} %fusion.4), kind=kOutput, calls=%fused_computation.81 | convolution fusion | flops 268435456 | bytes 6553600 | tf_op jit(solution)/shard_map/tgo,gkio->tgki/dot_general | solution.py:122
  130.7 2.1 multiply_convert_fusion.1
  132.8 2.6 copy.103
  135.4 2.3 multiply_convert_fusion
  137.8 2.7 copy.117
  140.4 2.6 maximum_bitcast_fusion
  143.0 2.0 copy-done.5
  146.1 2.1 collective-permute-start.7
  148.2 5.6 %copy.108 = f32[128,64,128]{2,0,1:T(8,128)} copy(f32[128,64,128]{0,2,1:T(8,128)} %bitcast.159) | data formatting | bytes 8388608 | tf_op jit(solution)/shard_map/reshape | solution.py:124
  154.0 8.8 %scatter_fusion.1 = f32[128,32,128]{2,0,1:T(8,128)S(1)} fusion(f32[128,32,128]{2,0,1:T(8,128)S(1)} %broadcast.171.clone, s32[64]{0:T(128)S(1)} %fusion.21, f32[64,128,128]{2,1,0:T(8,128)} %bitcast.161), kind=kCustom, calls=%fused_computation.5 | custom fusion | flops 1048576 | bytes 12583168 | tf_op jit(solution)/shard_map/scatter-add | solution.py:124
  164.3 5.7 %copy.100 = f32[128,64,128]{2,0,1:T(8,128)} copy(f32[128,64,128]{0,2,1:T(8,128)} %bitcast.162) | data formatting | bytes 8388608 | tf_op jit(solution)/shard_map/reshape | solution.py:112
  170.2 8.8 %scatter_fusion = f32[128,32,128]{2,0,1:T(8,128)S(1)} fusion(f32[128,32,128]{2,0,1:T(8,128)S(1)} %broadcast.171.clone.1, s32[64]{0:T(128)S(1)} %fusion.20, f32[64,128,128]{2,1,0:T(8,128)} %bitcast.160), kind=kCustom, calls=%fused_computation.4 | custom fusion | flops 1048576 | bytes 12583168 | tf_op jit(solution)/shard_map/scatter-add | solution.py:112
  182.1 5.9 %all-to-all-start.2 = ((bf16[16,2,128,256]{2,3,1,0:T(8,128)(2,1)}), bf16[16,2,128,256]{2,3,1,0:T(8,128)(2,1)S(1)}, u32[]{:S(2)}, u32[]{:S(2)}) async-start(bf16[16,2,128,256]{2,3,1,0:T(8,128)(2,1)} %copy.110), calls=%async_computation.2 | async-start | bytes 4194304 | tf_op jit(solution)/shard_map/all_to_all | solution.py:26
  189.3 5.4 %collective-permute-start.8 = (bf16[4,2,2,128,128]{4,3,2,1,0:T(8,128)(2,1)S(1)}, bf16[4,2,2,128,128]{4,3,2,1,0:T(8,128)(2,1)S(1)}, u32[]{:S(2)}, u32[]{:S(2)}) collective-permute-start(bf16[4,2,2,128,128]{4,3,2,1,0:T(8,128)(2,1)S(1)} %fusion.7), channel_id=1, source_target_pairs={{0,4},{4,8},{8,12},{12,16},{16,20},{20,24},{24,28},{28,0},{1,5},{5... | collective-permute-start | bytes 1572872 | tf_op jit(solution)/shard_map/ppermute | solution.py:59
  194.7 2.1 collective-permute-start.11
  196.9 10.3 %collective-permute-done.8 = bf16[4,2,2,128,128]{4,3,2,1,0:T(8,128)(2,1)S(1)} collective-permute-done((bf16[4,2,2,128,128]{4,3,2,1,0:T(8,128)(2,1)S(1)}, bf16[4,2,2,128,128]{4,3,2,1,0:T(8,128)(2,1)S(1)}, u32[]{:S(2)}, u32[]{:S(2)}) %collective-permute-start.8) | collective-permute-done | bytes 524320 | tf_op jit(solution)/shard_map/ppermute | solution.py:59
  208.4 3.9 %collective-permute-start.9 = (bf16[4,2,2,128,128]{4,3,2,1,0:T(8,128)(2,1)S(1)}, bf16[4,2,2,128,128]{4,3,2,1,0:T(8,128)(2,1)S(1)}, u32[]{:S(2)}, u32[]{:S(2)}) collective-permute-start(bf16[4,2,2,128,128]{4,3,2,1,0:T(8,128)(2,1)S(1)} %fusion.8), channel_id=1, source_target_pairs={{0,4},{4,8},{8,12},{12,16},{16,20},{20,24},{24,28},{28,0},{1,5},{5... | collective-permute-start | bytes 1572872 | tf_op jit(solution)/shard_map/ppermute | solution.py:59
  212.3 12.7 %collective-permute-done.9 = bf16[4,2,2,128,128]{4,3,2,1,0:T(8,128)(2,1)S(1)} collective-permute-done((bf16[4,2,2,128,128]{4,3,2,1,0:T(8,128)(2,1)S(1)}, bf16[4,2,2,128,128]{4,3,2,1,0:T(8,128)(2,1)S(1)}, u32[]{:S(2)}, u32[]{:S(2)}) %collective-permute-start.9) | collective-permute-done | bytes 524320 | tf_op jit(solution)/shard_map/ppermute | solution.py:59
  226.5 2.7 collective-permute-start.12
  229.2 3.1 collective-permute-start.10
  232.4 8.6 %collective-permute-done.12 = bf16[4,2,2,128,128]{4,3,2,1,0:T(8,128)(2,1)S(1)} collective-permute-done((bf16[4,2,2,128,128]{4,3,2,1,0:T(8,128)(2,1)S(1)}, bf16[4,2,2,128,128]{4,3,2,1,0:T(8,128)(2,1)S(1)}, u32[]{:S(2)}, u32[]{:S(2)}) %collective-permute-start.12) | collective-permute-done | bytes 524320 | tf_op jit(solution)/shard_map/ppermute | solution.py:64
  242.2 3.9 %collective-permute-start.13 = (bf16[4,2,2,128,128]{4,3,2,1,0:T(8,128)(2,1)S(1)}, bf16[4,2,2,128,128]{4,3,2,1,0:T(8,128)(2,1)S(1)}, u32[]{:S(2)}, u32[]{:S(2)}) collective-permute-start(bf16[4,2,2,128,128]{4,3,2,1,0:T(8,128)(2,1)S(1)} %fusion.6), channel_id=1, source_target_pairs={{0,28},{4,0},{8,4},{12,8},{16,12},{20,16},{24,20},{28,24},{1,29},{... | collective-permute-start | bytes 1572872 | tf_op jit(solution)/shard_map/ppermute | solution.py:64
  246.1 9.6 %collective-permute-done.13 = bf16[4,2,2,128,128]{4,3,2,1,0:T(8,128)(2,1)S(1)} collective-permute-done((bf16[4,2,2,128,128]{4,3,2,1,0:T(8,128)(2,1)S(1)}, bf16[4,2,2,128,128]{4,3,2,1,0:T(8,128)(2,1)S(1)}, u32[]{:S(2)}, u32[]{:S(2)}) %collective-permute-start.13) | collective-permute-done | bytes 524320 | tf_op jit(solution)/shard_map/ppermute | solution.py:64
  255.7 2.1 fusion.11
  257.8 3.5 %all-to-all-start.4 = ((bf16[4,2,2,128,128]{4,3,2,1,0:T(8,128)(2,1)}), bf16[4,2,2,128,128]{4,3,2,1,0:T(8,128)(2,1)S(1)}, u32[]{:S(2)}, u32[]{:S(2)}) async-start(bf16[4,2,2,128,128]{4,3,2,1,0:T(8,128)(2,1)} %fusion.11), calls=%async_computation.4 | async-start | bytes 1048576 | tf_op jit(solution)/shard_map/all_to_all | solution.py:26
  261.7 13.0 %all-to-all-done.4 = bf16[4,2,2,128,128]{4,3,2,1,0:T(8,128)(2,1)S(1)} async-done(((bf16[4,2,2,128,128]{4,3,2,1,0:T(8,128)(2,1)}), bf16[4,2,2,128,128]{4,3,2,1,0:T(8,128)(2,1)S(1)}, u32[]{:S(2)}, u32[]{:S(2)}) %all-to-all-start.4) | async-done | bytes 524320 | tf_op jit(solution)/shard_map/all_to_all | solution.py:26
  276.3 5.1 %all-to-all-start.3 = ((bf16[16,2,128,256]{3,2,1,0:T(8,128)(2,1)}), bf16[16,2,128,256]{3,2,1,0:T(8,128)(2,1)S(1)}, u32[]{:S(2)}, u32[]{:S(2)}) async-start(bf16[16,2,128,256]{3,2,1,0:T(8,128)(2,1)} %broadcast_in_dim.8), calls=%async_computation.3 | async-start | bytes 4194304 | tf_op jit(solution)/shard_map/all_to_all | solution.py:22
  282.2 28.6 %all-to-all-done.3 = bf16[16,2,128,256]{3,2,1,0:T(8,128)(2,1)S(1)} async-done(((bf16[16,2,128,256]{3,2,1,0:T(8,128)(2,1)}), bf16[16,2,128,256]{3,2,1,0:T(8,128)(2,1)S(1)}, u32[]{:S(2)}, u32[]{:S(2)}) %all-to-all-start.3) | async-done | bytes 2097184 | tf_op jit(solution)/shard_map/all_to_all | solution.py:22
  310.8 2.4 copy.113
  (89 shorter events, 33.1 us)
Async XLA Ops:
  0.6 40.2 %copy-start = (s32[64]{0:T(128)S(1)}, s32[64]{0:T(128)}, u32[]{:S(2)}) copy-start(s32[64]{0:T(128)} %param.9) | copy-start | bytes 772
  0.6 12.3 %copy-start.11 = (bf16[128,256]{1,0:T(8,128)(2,1)S(1)}, bf16[128,256]{1,0:T(8,128)(2,1)}, u32[]{:S(2)}) copy-start(bf16[128,256]{1,0:T(8,128)(2,1)} %param.6) | copy-start | bytes 196612
  0.7 12.3 %copy-start.10 = (bf16[128,256]{1,0:T(8,128)(2,1)S(1)}, bf16[128,256]{1,0:T(8,128)(2,1)}, u32[]{:S(2)}) copy-start(bf16[128,256]{1,0:T(8,128)(2,1)} %param.7) | copy-start | bytes 196612
  2.6 24.9 %all-to-all-start = ((bf16[4,2,2,128,128]{3,4,2,1,0:T(8,128)(2,1)}), bf16[4,2,2,128,128]{3,4,2,1,0:T(8,128)(2,1)S(1)}, u32[]{:S(2)}, u32[]{:S(2)}) async-start(bf16[4,2,2,128,128]{3,4,2,1,0:T(8,128)(2,1)} %broadcast_in_dim.6), calls=%async_computation | async-start | bytes 1048576 | tf_op jit(solution)/shard_map/all_to_all | solution.py:22
  29.3 27.4 %copy-start.2 = (s32[64]{0:T(128)S(1)}, s32[64]{0:T(128)}, u32[]{:S(2)}) copy-start(s32[64]{0:T(128)} %param.11) | copy-start | bytes 772
  29.4 78.1 %all-to-all-start.1 = ((bf16[16,2,128,256]{2,3,1,0:T(8,128)(2,1)}), bf16[16,2,128,256]{2,3,1,0:T(8,128)(2,1)S(1)}, u32[]{:S(2)}, u32[]{:S(2)}) async-start(bf16[16,2,128,256]{2,3,1,0:T(8,128)(2,1)} %broadcast_in_dim.7), calls=%async_computation.1 | async-start | bytes 4194304 | tf_op jit(solution)/shard_map/all_to_all | solution.py:22
  37.1 17.7 %collective-permute-start = (bf16[4,2,2,128,128]{3,4,2,1,0:T(8,128)(2,1)S(1)}, bf16[4,2,2,128,128]{3,4,2,1,0:T(8,128)(2,1)}, u32[]{:S(2)}, u32[]{:S(2)}) collective-permute-start(bf16[4,2,2,128,128]{3,4,2,1,0:T(8,128)(2,1)S(1)} %all-to-all-done), channel_id=1, source_target_pairs={{0,4},{4,8},{8,12},{12,16},{16,20},{20,24},{24,28},{28,0},{1,5},{5... | collective-permute-start | bytes 1572872 | tf_op jit(solution)/shard_map/ppermute | solution.py:43
  54.8 16.9 %collective-permute-start.1 = (bf16[4,2,2,128,128]{3,4,2,1,0:T(8,128)(2,1)}, bf16[4,2,2,128,128]{3,4,2,1,0:T(8,128)(2,1)}, u32[]{:S(2)}, u32[]{:S(2)}) collective-permute-start(bf16[4,2,2,128,128]{3,4,2,1,0:T(8,128)(2,1)} %collective-permute-done), channel_id=1, source_target_pairs={{0,4},{4,8},{8,12},{12,16},{16,20},{20,24},{24,28},{28,0},{1,5},{5... | collective-permute-start | bytes 1572872 | tf_op jit(solution)/shard_map/ppermute | solution.py:43
  57.6 16.0 %collective-permute-start.4 = (bf16[4,2,2,128,128]{3,4,2,1,0:T(8,128)(2,1)S(1)}, bf16[4,2,2,128,128]{3,4,2,1,0:T(8,128)(2,1)S(1)}, u32[]{:S(2)}, u32[]{:S(2)}) collective-permute-start(bf16[4,2,2,128,128]{3,4,2,1,0:T(8,128)(2,1)S(1)} %all-to-all-done), channel_id=1, source_target_pairs={{0,28},{4,0},{8,4},{12,8},{16,12},{20,16},{24,20},{28,24},{1,29},{... | collective-permute-start | bytes 1572872 | tf_op jit(solution)/shard_map/ppermute | solution.py:46
  71.7 15.9 %collective-permute-start.2 = (bf16[4,2,2,128,128]{3,4,2,1,0:T(8,128)(2,1)}, bf16[4,2,2,128,128]{3,4,2,1,0:T(8,128)(2,1)S(1)}, u32[]{:S(2)}, u32[]{:S(2)}) collective-permute-start(bf16[4,2,2,128,128]{3,4,2,1,0:T(8,128)(2,1)} %collective-permute-done.1), channel_id=1, source_target_pairs={{0,4},{4,8},{8,12},{12,16},{16,20},{20,24},{24,28},{28,0},{1,5},{5... | collective-permute-start | bytes 1572872 | tf_op jit(solution)/shard_map/ppermute | solution.py:43
  73.6 17.0 %collective-permute-start.5 = (bf16[4,2,2,128,128]{3,4,2,1,0:T(8,128)(2,1)S(1)}, bf16[4,2,2,128,128]{3,4,2,1,0:T(8,128)(2,1)S(1)}, u32[]{:S(2)}, u32[]{:S(2)}) collective-permute-start(bf16[4,2,2,128,128]{3,4,2,1,0:T(8,128)(2,1)S(1)} %collective-permute-done.4), channel_id=1, source_target_pairs={{0,28},{4,0},{8,4},{12,8},{16,12},{20,16},{24,20},{28,24},{1,29},{... | collective-permute-start | bytes 1572872 | tf_op jit(solution)/shard_map/ppermute | solution.py:46
  87.6 14.7 %collective-permute-start.3 = (bf16[4,2,2,128,128]{3,4,2,1,0:T(8,128)(2,1)S(1)}, bf16[4,2,2,128,128]{3,4,2,1,0:T(8,128)(2,1)S(1)}, u32[]{:S(2)}, u32[]{:S(2)}) collective-permute-start(bf16[4,2,2,128,128]{3,4,2,1,0:T(8,128)(2,1)S(1)} %collective-permute-done.2), channel_id=1, source_target_pairs={{0,4},{4,8},{8,12},{12,16},{16,20},{20,24},{24,28},{28,0},{1,5},{5... | collective-permute-start | bytes 1572872 | tf_op jit(solution)/shard_map/ppermute | solution.py:43
  90.6 14.0 %collective-permute-start.6 = (bf16[4,2,2,128,128]{3,4,2,1,0:T(8,128)(2,1)S(1)}, bf16[4,2,2,128,128]{3,4,2,1,0:T(8,128)(2,1)S(1)}, u32[]{:S(2)}, u32[]{:S(2)}) collective-permute-start(bf16[4,2,2,128,128]{3,4,2,1,0:T(8,128)(2,1)S(1)} %collective-permute-done.5), channel_id=1, source_target_pairs={{0,28},{4,0},{8,4},{12,8},{16,12},{20,16},{24,20},{28,24},{1,29},{... | collective-permute-start | bytes 1572872 | tf_op jit(solution)/shard_map/ppermute | solution.py:46
  111.9 3.9 %copy-start.3 = (bf16[64,128,128]{2,1,0:T(8,128)(2,1)}, bf16[64,128,128]{2,1,0:T(8,128)(2,1)S(1)}, u32[]{:S(2)}) copy-start(bf16[64,128,128]{2,1,0:T(8,128)(2,1)S(1)} %gather_fusion.2) | copy-start | bytes 6291460
  116.8 4.5 %copy-start.4 = (bf16[1,8,4,2,128,128]{4,5,3,0,2,1:T(8,128)(2,1)S(1)}, bf16[1,8,4,2,128,128]{4,5,3,0,2,1:T(8,128)(2,1)}, u32[]{:S(2)}) copy-start(bf16[1,8,4,2,128,128]{4,5,3,0,2,1:T(8,128)(2,1)} %get-tuple-element.12) | copy-start | bytes 6291460
  116.8 4.5 %copy-start.7 = (f32[128,8,128]{0,2,1:T(8,128)S(1)}, f32[128,8,128]{0,2,1:T(8,128)}, u32[]{:S(2)}) copy-start(f32[128,8,128]{0,2,1:T(8,128)} %convolution_bitcast_fusion.1) | copy-start | bytes 1572868
  126.1 4.6 %copy-start.6 = (bf16[8,8,128,128]{2,3,1,0:T(8,128)(2,1)S(1)}, bf16[8,8,128,128]{2,3,1,0:T(8,128)(2,1)}, u32[]{:S(2)}) copy-start(bf16[8,8,128,128]{2,3,1,0:T(8,128)(2,1)} %copy.97) | copy-start | bytes 6291460
  143.0 2.0 copy-start.5
  146.1 41.9 %collective-permute-start.7 = (bf16[4,2,2,128,128]{4,3,2,1,0:T(8,128)(2,1)}, bf16[4,2,2,128,128]{4,3,2,1,0:T(8,128)(2,1)}, u32[]{:S(2)}, u32[]{:S(2)}) collective-permute-start(bf16[4,2,2,128,128]{4,3,2,1,0:T(8,128)(2,1)} %get-tuple-element.10), channel_id=1, source_target_pairs={{0,4},{4,8},{8,12},{12,16},{16,20},{20,24},{24,28},{28,0},{1,5},{5... | collective-permute-start | bytes 1572872 | tf_op jit(solution)/shard_map/ppermute | solution.py:59
  179.2 1.2 copy-start.8
  182.1 12.6 %copy-start.9 = (bf16[4,2,2,128,128]{4,3,2,1,0:T(8,128)(2,1)S(1)}, bf16[4,2,2,128,128]{4,3,2,1,0:T(8,128)(2,1)}, u32[]{:S(2)}) copy-start(bf16[4,2,2,128,128]{4,3,2,1,0:T(8,128)(2,1)} %get-tuple-element.11) | copy-start | bytes 1572868
  182.1 75.7 %all-to-all-start.2 = ((bf16[16,2,128,256]{2,3,1,0:T(8,128)(2,1)}), bf16[16,2,128,256]{2,3,1,0:T(8,128)(2,1)S(1)}, u32[]{:S(2)}, u32[]{:S(2)}) async-start(bf16[16,2,128,256]{2,3,1,0:T(8,128)(2,1)} %copy.110), calls=%async_computation.2 | async-start | bytes 4194304 | tf_op jit(solution)/shard_map/all_to_all | solution.py:26
  189.3 17.8 %collective-permute-start.8 = (bf16[4,2,2,128,128]{4,3,2,1,0:T(8,128)(2,1)S(1)}, bf16[4,2,2,128,128]{4,3,2,1,0:T(8,128)(2,1)S(1)}, u32[]{:S(2)}, u32[]{:S(2)}) collective-permute-start(bf16[4,2,2,128,128]{4,3,2,1,0:T(8,128)(2,1)S(1)} %fusion.7), channel_id=1, source_target_pairs={{0,4},{4,8},{8,12},{12,16},{16,20},{20,24},{24,28},{28,0},{1,5},{5... | collective-permute-start | bytes 1572872 | tf_op jit(solution)/shard_map/ppermute | solution.py:59
  194.7 17.6 %collective-permute-start.11 = (bf16[4,2,2,128,128]{4,3,2,1,0:T(8,128)(2,1)S(1)}, bf16[4,2,2,128,128]{4,3,2,1,0:T(8,128)(2,1)S(1)}, u32[]{:S(2)}, u32[]{:S(2)}) collective-permute-start(bf16[4,2,2,128,128]{4,3,2,1,0:T(8,128)(2,1)S(1)} %copy-done.9), channel_id=1, source_target_pairs={{0,28},{4,0},{8,4},{12,8},{16,12},{20,16},{24,20},{28,24},{1,29},{... | collective-permute-start | bytes 1572872 | tf_op jit(solution)/shard_map/ppermute | solution.py:64
  208.4 16.6 %collective-permute-start.9 = (bf16[4,2,2,128,128]{4,3,2,1,0:T(8,128)(2,1)S(1)}, bf16[4,2,2,128,128]{4,3,2,1,0:T(8,128)(2,1)S(1)}, u32[]{:S(2)}, u32[]{:S(2)}) collective-permute-start(bf16[4,2,2,128,128]{4,3,2,1,0:T(8,128)(2,1)S(1)} %fusion.8), channel_id=1, source_target_pairs={{0,4},{4,8},{8,12},{12,16},{16,20},{20,24},{24,28},{28,0},{1,5},{5... | collective-permute-start | bytes 1572872 | tf_op jit(solution)/shard_map/ppermute | solution.py:59
  226.5 14.5 %collective-permute-start.12 = (bf16[4,2,2,128,128]{4,3,2,1,0:T(8,128)(2,1)S(1)}, bf16[4,2,2,128,128]{4,3,2,1,0:T(8,128)(2,1)S(1)}, u32[]{:S(2)}, u32[]{:S(2)}) collective-permute-start(bf16[4,2,2,128,128]{4,3,2,1,0:T(8,128)(2,1)S(1)} %get-tuple-element.9), channel_id=1, source_target_pairs={{0,28},{4,0},{8,4},{12,8},{16,12},{20,16},{24,20},{28,24},{1,29},{... | collective-permute-start | bytes 1572872 | tf_op jit(solution)/shard_map/ppermute | solution.py:64
  229.2 16.9 %collective-permute-start.10 = (bf16[4,2,2,128,128]{4,3,2,1,0:T(8,128)(2,1)S(1)}, bf16[4,2,2,128,128]{4,3,2,1,0:T(8,128)(2,1)S(1)}, u32[]{:S(2)}, u32[]{:S(2)}) collective-permute-start(bf16[4,2,2,128,128]{4,3,2,1,0:T(8,128)(2,1)S(1)} %get-tuple-element.8), channel_id=1, source_target_pairs={{0,4},{4,8},{8,12},{12,16},{16,20},{20,24},{24,28},{28,0},{1,5},{5... | collective-permute-start | bytes 1572872 | tf_op jit(solution)/shard_map/ppermute | solution.py:59
  242.2 13.5 %collective-permute-start.13 = (bf16[4,2,2,128,128]{4,3,2,1,0:T(8,128)(2,1)S(1)}, bf16[4,2,2,128,128]{4,3,2,1,0:T(8,128)(2,1)S(1)}, u32[]{:S(2)}, u32[]{:S(2)}) collective-permute-start(bf16[4,2,2,128,128]{4,3,2,1,0:T(8,128)(2,1)S(1)} %fusion.6), channel_id=1, source_target_pairs={{0,28},{4,0},{8,4},{12,8},{16,12},{20,16},{24,20},{28,24},{1,29},{... | collective-permute-start | bytes 1572872 | tf_op jit(solution)/shard_map/ppermute | solution.py:64
  257.8 16.9 %all-to-all-start.4 = ((bf16[4,2,2,128,128]{4,3,2,1,0:T(8,128)(2,1)}), bf16[4,2,2,128,128]{4,3,2,1,0:T(8,128)(2,1)S(1)}, u32[]{:S(2)}, u32[]{:S(2)}) async-start(bf16[4,2,2,128,128]{4,3,2,1,0:T(8,128)(2,1)} %fusion.11), calls=%async_computation.4 | async-start | bytes 1048576 | tf_op jit(solution)/shard_map/all_to_all | solution.py:26
  276.3 34.5 %all-to-all-start.3 = ((bf16[16,2,128,256]{3,2,1,0:T(8,128)(2,1)}), bf16[16,2,128,256]{3,2,1,0:T(8,128)(2,1)S(1)}, u32[]{:S(2)}, u32[]{:S(2)}) async-start(bf16[16,2,128,256]{3,2,1,0:T(8,128)(2,1)} %broadcast_in_dim.8), calls=%async_computation.3 | async-start | bytes 4194304 | tf_op jit(solution)/shard_map/all_to_all | solution.py:22
  314.9 2.6 copy-start.1

commit v5 on v2

--- a/solution.py
+++ b/solution.py
@@ -118,8 +118,13 @@
     preact = jnp.einsum("tgki,gkio->tgo", picked_in, up_tiles, preferred_element_type=jnp.float32)
     hidden = (preact * normal_cdf(preact)).astype(jnp.bfloat16)
     product = jnp.einsum("tgh,gkho->tgko", hidden, down_tiles, preferred_element_type=jnp.float32)
-    out_start = jnp.zeros((tokens, row_blocks, block_size), jnp.float32)
-    out_part = out_start.at[:, down_rows].add(product.reshape(tokens, groups * K, block_size))
+    span = jnp.arange(row_blocks, dtype=jnp.int32)
+    highest = lax.Precision.HIGHEST
+    down_hot = (down_rows[:, None] == span).astype(jnp.float32)
+    out_part = jnp.einsum(
+        "tbo,br->tro", product.reshape(tokens, groups * K, block_size), down_hot,
+        precision=highest, preferred_element_type=jnp.float32,
+    )
     picked_grad = full_grad.reshape(tokens, row_blocks, block_size)[:, down_index]
     down_term = (
         jnp.einsum("tgh,tgko->gkho", hidden, picked_grad, preferred_element_type=jnp.float32)
@@ -130,8 +135,11 @@
     )
     preact_grad = (hidden_grad * gelu_slope(preact)).astype(jnp.bfloat16)
     back = jnp.einsum("tgo,gkio->tgki", preact_grad, up_tiles, preferred_element_type=jnp.float32)
-    in_start = jnp.zeros((tokens, row_blocks, block_size), jnp.float32)
-    in_part = in_start.at[:, up_rows].add(back.reshape(tokens, groups * K, block_size))
+    up_hot = (up_rows[:, None] == span).astype(jnp.float32)
+    in_part = jnp.einsum(
+        "tbi,br->tri", back.reshape(tokens, groups * K, block_size), up_hot,
+        precision=highest, preferred_element_type=jnp.float32,
+    )
     up_term = (
         jnp.einsum("tgki,tgo->gkio", picked_in, preact_grad, preferred_element_type=jnp.float32)
         * scale

time: 294 us -> 285 us (0.969)
  other arithmetic: 34.5 us -> 13 us
  matrix products: 15.4 us -> 23.5 us
  waiting for transfers between devices: 85.4 us -> 89.2 us
    scatter-add x2 -> x0, other arithmetic: 17.6 us -> none  [the longest x1 8.8 us: per_device(): in_start.at[:, up_rows].add(back.reshape(tokens, groups * K, block_size))]
    dot_general x0 -> x2, matrix products: none -> 9.54 us  [the longest x1 4.77 us: per_device(): jnp.einsum('tbo,br->tro', product.reshape(tokens, groups * K, block_size)...]
    ppermute x4, waiting for transfers between devices: 25.3 us -> 30.4 us  [dp_gather_rel(): cur_f = lax.ppermute(cur_f, 'dp', dp_shift(n_y, n_z, 1, 0))]
    another operation x4, local copies, waits for them, and re-layouts: 4.56 us -> 8.71 us  [per_device(): parts = jnp.stack([out_part, in_part]).astype(jnp.bfloat16)]
    unnamed x42 -> x38, local copies, waits for them, and re-layouts: 8.64 us -> 7.16 us
  transfers between devices with their start and end apart: 23 -> 23, of which waited for: 16 -> 15; matrix products, arithmetic and copies ran while one was open for 15% -> 14% of each run, Pallas kernels for 0% -> 0%
where the time goes in v5:
time: 285 us; the launch traced here: 280 us
  starting transfers between devices  93.7 us (33%)
  waiting for transfers between devices  89.2 us (31%)
  local copies, waits for them, and re-layouts  59.8 us (21%)
  matrix products  23.5 us (8%)
  other arithmetic  13 us (5%)
    ppermute x4, waiting for transfers between devices, dp_gather_rel(): cur_f = lax.ppermute(cur_f, 'dp', dp_shift(n_y, n_z, 1, 0))  30.4 us
    ppermute x3, waiting for transfers between devices, dp_scatter_rel(): lax.ppermute(part.astype(jnp.bfloat16), 'dp', dp_shift(n_y, n_z, -1, 0))  27 us
    ppermute x4, waiting for transfers between devices, dp_scatter_rel(): lax.ppermute(part.astype(jnp.bfloat16), 'dp', dp_shift(n_y, n_z, 1, 0))  21.6 us
    ppermute x3, starting transfers between devices, dp_gather_rel(): lax.ppermute(x, 'dp', dp_shift(n_y, n_z, 0, b))  18.9 us
    ppermute x3, starting transfers between devices, dp_gather_rel(): cur_b = lax.ppermute(cur_b, 'dp', dp_shift(n_y, n_z, -1, 0))  15.9 us
    all_to_all x2, starting transfers between devices, gather_all(): return lax.all_to_all(spread, axis_name, 0, 0, tiled=True)  11.6 us
    ppermute x3, starting transfers between devices, dp_scatter_rel(): lax.ppermute(acc[b].astype(jnp.bfloat16), 'dp', dp_shift(n_y, n_z, 0, -b))  11.1 us
    ppermute x4, starting transfers between devices, dp_scatter_rel(): lax.ppermute(part.astype(jnp.bfloat16), 'dp', dp_shift(n_y, n_z, 1, 0))  10.5 us
  transfers between devices with their start and end apart: 23, of which 15 were waited for; matrix products, arithmetic and copies ran while one was open for 14% of the time, Pallas kernels for 0%

profile of v5, /device:TPU:6, one launch (start us, length us, event | category | flops | bytes accessed | tf_op | source)
XLA Modules:
  0.0 280.3 jit_solution(16946866691390441364)
XLA Ops:
  1.5 6.1 %collective-permute-start = (bf16[2,2,128,128]{3,2,1,0:T(8,128)(2,1)S(1)}, bf16[2,2,128,128]{3,2,1,0:T(8,128)(2,1)S(1)}, u32[]{:S(2)}, u32[]{:S(2)}) collective-permute-start(bf16[2,2,128,128]{3,2,1,0:T(8,128)(2,1)S(1)} %get-tuple-element.26), channel_id=1, source_target_pairs={{0,1},{1,2},{2,3},{3,0},{4,5},{5,6},{6,7},{7,4},{8,9},{9,10},{10,1... | collective-permute-start | bytes 393224 | tf_op jit(solution)/shard_map/ppermute | solution.py:42
  7.6 9.1 %collective-permute-start.1 = (bf16[2,2,128,128]{3,2,1,0:T(8,128)(2,1)S(1)}, bf16[2,2,128,128]{3,2,1,0:T(8,128)(2,1)S(1)}, u32[]{:S(2)}, u32[]{:S(2)}) collective-permute-start(bf16[2,2,128,128]{3,2,1,0:T(8,128)(2,1)S(1)} %get-tuple-element.26), channel_id=1, source_target_pairs={{0,2},{1,3},{2,0},{3,1},{4,6},{5,7},{6,4},{7,5},{8,10},{9,11},{10,... | collective-permute-start | bytes 393224 | tf_op jit(solution)/shard_map/ppermute | solution.py:42
  16.8 3.7 %collective-permute-start.2 = (bf16[2,2,128,128]{3,2,1,0:T(8,128)(2,1)S(1)}, bf16[2,2,128,128]{3,2,1,0:T(8,128)(2,1)S(1)}, u32[]{:S(2)}, u32[]{:S(2)}) collective-permute-start(bf16[2,2,128,128]{3,2,1,0:T(8,128)(2,1)S(1)} %get-tuple-element.26), channel_id=1, source_target_pairs={{0,3},{1,0},{2,1},{3,2},{4,7},{5,4},{6,5},{7,6},{8,11},{9,8},{10,9... | collective-permute-start | bytes 393224 | tf_op jit(solution)/shard_map/ppermute | solution.py:42
  23.3 5.8 %all-to-all-start = ((bf16[16,2,128,256]{2,3,1,0:T(8,128)(2,1)}), bf16[16,2,128,256]{2,3,1,0:T(8,128)(2,1)S(1)}, u32[]{:S(2)}, u32[]{:S(2)}) async-start(bf16[16,2,128,256]{2,3,1,0:T(8,128)(2,1)} %broadcast_in_dim.4), calls=%async_computation | async-start | bytes 4194304 | tf_op jit(solution)/shard_map/all_to_all | solution.py:22
  30.1 3.5 %collective-permute-start.3 = (bf16[4,2,2,128,128]{4,3,2,1,0:T(8,128)(2,1)S(1)}, bf16[4,2,2,128,128]{4,3,2,1,0:T(8,128)(2,1)S(1)}, u32[]{:S(2)}, u32[]{:S(2)}) collective-permute-start(bf16[4,2,2,128,128]{4,3,2,1,0:T(8,128)(2,1)S(1)} %pad_maximum_fusion), channel_id=1, source_target_pairs={{0,4},{1,5},{2,6},{3,7},{4,8},{5,9},{6,10},{7,11},{8,12},{9,13},{1... | collective-permute-start | bytes 1572872 | tf_op jit(solution)/shard_map/ppermute | solution.py:48
  33.7 13.9 %collective-permute-done.3 = bf16[4,2,2,128,128]{4,3,2,1,0:T(8,128)(2,1)S(1)} collective-permute-done((bf16[4,2,2,128,128]{4,3,2,1,0:T(8,128)(2,1)S(1)}, bf16[4,2,2,128,128]{4,3,2,1,0:T(8,128)(2,1)S(1)}, u32[]{:S(2)}, u32[]{:S(2)}) %collective-permute-start.3) | collective-permute-done | bytes 524320 | tf_op jit(solution)/shard_map/ppermute | solution.py:48
  51.0 5.1 %collective-permute-start.7 = (bf16[4,2,2,128,128]{4,3,2,1,0:T(8,128)(2,1)S(1)}, bf16[4,2,2,128,128]{4,3,2,1,0:T(8,128)(2,1)}, u32[]{:S(2)}, u32[]{:S(2)}) collective-permute-start(bf16[4,2,2,128,128]{4,3,2,1,0:T(8,128)(2,1)S(1)} %pad_maximum_fusion), channel_id=1, source_target_pairs={{0,28},{1,29},{2,30},{3,31},{4,0},{5,1},{6,2},{7,3},{8,4},{9,5},{1... | collective-permute-start | bytes 1572872 | tf_op jit(solution)/shard_map/ppermute | solution.py:51
  58.2 5.9 %collective-permute-done.4 = bf16[4,2,2,128,128]{4,3,2,1,0:T(8,128)(2,1)} collective-permute-done((bf16[4,2,2,128,128]{4,3,2,1,0:T(8,128)(2,1)S(1)}, bf16[4,2,2,128,128]{4,3,2,1,0:T(8,128)(2,1)}, u32[]{:S(2)}, u32[]{:S(2)}) %collective-permute-start.4) | collective-permute-done | bytes 524320 | tf_op jit(solution)/shard_map/ppermute | solution.py:48
  67.3 5.1 %collective-permute-start.8 = (bf16[4,2,2,128,128]{4,3,2,1,0:T(8,128)(2,1)}, bf16[4,2,2,128,128]{4,3,2,1,0:T(8,128)(2,1)S(1)}, u32[]{:S(2)}, u32[]{:S(2)}) collective-permute-start(bf16[4,2,2,128,128]{4,3,2,1,0:T(8,128)(2,1)} %collective-permute-done.7), channel_id=1, source_target_pairs={{0,28},{1,29},{2,30},{3,31},{4,0},{5,1},{6,2},{7,3},{8,4},{9,5},{1... | collective-permute-start | bytes 1572872 | tf_op jit(solution)/shard_map/ppermute | solution.py:51
  73.6 6.3 %collective-permute-done.5 = bf16[4,2,2,128,128]{4,3,2,1,0:T(8,128)(2,1)} collective-permute-done((bf16[4,2,2,128,128]{4,3,2,1,0:T(8,128)(2,1)}, bf16[4,2,2,128,128]{4,3,2,1,0:T(8,128)(2,1)}, u32[]{:S(2)}, u32[]{:S(2)}) %collective-permute-start.5) | collective-permute-done | bytes 524320 | tf_op jit(solution)/shard_map/ppermute | solution.py:48
  82.4 5.7 %collective-permute-start.9 = (bf16[4,2,2,128,128]{4,3,2,1,0:T(8,128)(2,1)S(1)}, bf16[4,2,2,128,128]{4,3,2,1,0:T(8,128)(2,1)S(1)}, u32[]{:S(2)}, u32[]{:S(2)}) collective-permute-start(bf16[4,2,2,128,128]{4,3,2,1,0:T(8,128)(2,1)S(1)} %collective-permute-done.8), channel_id=1, source_target_pairs={{0,28},{1,29},{2,30},{3,31},{4,0},{5,1},{6,2},{7,3},{8,4},{9,5},{1... | collective-permute-start | bytes 1572872 | tf_op jit(solution)/shard_map/ppermute | solution.py:51
  90.3 4.4 %collective-permute-done.6 = bf16[4,2,2,128,128]{4,3,2,1,0:T(8,128)(2,1)S(1)} collective-permute-done((bf16[4,2,2,128,128]{4,3,2,1,0:T(8,128)(2,1)}, bf16[4,2,2,128,128]{4,3,2,1,0:T(8,128)(2,1)S(1)}, u32[]{:S(2)}, u32[]{:S(2)}) %collective-permute-start.6) | collective-permute-done | bytes 524320 | tf_op jit(solution)/shard_map/ppermute | solution.py:48
  97.8 2.6 fusion.38
  102.7 2.2 gather_fusion.2
  104.9 3.2 %convolution_bitcast_fusion.1 = f32[128,8,128]{0,2,1:T(8,128)} fusion(bf16[8,8,128,128]{3,2,1,0:T(8,128)(2,1)} %bitcast.179, bf16[128,8,8,128]{3,0,2,1:T(8,128)(2,1)S(1)} %bitcast.177), kind=kOutput, calls=%fused_computation.16 | convolution fusion | flops 268435456 | bytes 4718592 | tf_op jit(solution)/shard_map/tgki,gkio->tgo/dot_general | solution.py:118
  108.0 2.1 gather_fusion.3
  110.2 4.6 %fusion.34 = f32[8,8,128,128]{3,2,1,0:T(8,128)} fusion(bf16[8,8,128,128]{3,2,1,0:T(8,128)(2,1)} %bitcast.188, f32[128,8,128]{0,2,1:T(8,128)} %convolution_bitcast_fusion.1), kind=kOutput, calls=%fused_computation.94 | convolution fusion | flops 269090816 | bytes 6815744 | tf_op jit(solution)/shard_map/tgh,gkho->tgko/dot_general | solution.py:120
  115.6 5.4 %copy.73 = f32[128,64,128]{2,1,0:T(8,128)} copy(f32[128,64,128]{0,2,1:T(8,128)} %bitcast.182) | data formatting | bytes 8388608 | tf_op jit(solution)/shard_map/reshape | solution.py:125
  121.0 4.8 %fusion.2 = bf16[128,32,128]{2,1,0:T(8,128)(2,1)} fusion(f32[128,64,128]{2,1,0:T(8,128)} %copy.73, s32[64]{0:T(128)S(1)} %copy-done.14), kind=kOutput, calls=%fused_computation.13 | convolution fusion | flops 403179520 | bytes 5243136 | tf_op jit(solution)/shard_map/tbo,br->tro/dot_general | solution.py:124
  125.8 2.2 stack.98
  128.0 2.7 copy.81
  130.6 2.7 fusion.41
  133.3 5.4 %copy.80 = f32[128,64,128]{2,1,0:T(8,128)} copy(f32[128,64,128]{0,2,1:T(8,128)} %bitcast.181) | data formatting | bytes 8388608 | tf_op jit(solution)/shard_map/reshape | solution.py:140
  138.8 4.8 %fusion.3 = bf16[128,32,128]{2,1,0:T(8,128)(2,1)} fusion(f32[128,64,128]{2,1,0:T(8,128)} %copy.80, s32[64]{0:T(128)S(1)} %copy-done.12), kind=kOutput, calls=%fused_computation.14 | convolution fusion | flops 403179520 | bytes 5243136 | tf_op jit(solution)/shard_map/tbi,br->tri/dot_general | solution.py:139
  143.5 2.2 stack.99
  149.0 6.1 %all-to-all-start.1 = ((bf16[16,2,128,256]{3,2,1,0:T(8,128)(2,1)}), bf16[16,2,128,256]{3,2,1,0:T(8,128)(2,1)}, u32[]{:S(2)}, u32[]{:S(2)}) async-start(bf16[16,2,128,256]{3,2,1,0:T(8,128)(2,1)} %maximum_bitcast_fusion.1), calls=%async_computation.1 | async-start | bytes 4194304 | tf_op jit(solution)/shard_map/all_to_all | solution.py:26
  155.1 2.6 copy.70
  157.7 3.0 %copy.75 = bf16[8,8,128,128]{2,3,1,0:T(8,128)(2,1)S(1)} copy(bf16[8,8,128,128]{3,2,1,0:T(8,128)(2,1)} %bitcast.183) | data formatting | bytes 4194304 | tf_op jit(solution)/shard_map/gather | solution.py:128
  160.8 2.0 multiply_convert_fusion
  162.8 4.1 %copy.87 = bf16[1,8,4,2,128,128]{5,4,3,0,2,1:T(8,128)(2,1)} copy(bf16[1,8,4,2,128,128]{4,5,3,2,1,0:T(8,128)(2,1)} %bitcast.187) | data formatting | bytes 4194304 | tf_op jit(solution)/shard_map/stack | solution.py:154
  169.8 2.7 collective-permute-start.10
  172.6 15.1 %collective-permute-done.10 = bf16[4,2,2,128,128]{4,3,2,1,0:T(8,128)(2,1)S(1)} collective-permute-done((bf16[4,2,2,128,128]{4,3,2,1,0:T(8,128)(2,1)S(1)}, bf16[4,2,2,128,128]{4,3,2,1,0:T(8,128)(2,1)S(1)}, u32[]{:S(2)}, u32[]{:S(2)}) %collective-permute-start.10) | collective-permute-done | bytes 524320 | tf_op jit(solution)/shard_map/ppermute | solution.py:64
  187.8 1.9 collective-permute-start.11
  193.2 5.7 %all-to-all-start.2 = ((bf16[16,2,128,256]{3,2,1,0:T(8,128)(2,1)}), bf16[16,2,128,256]{3,2,1,0:T(8,128)(2,1)S(1)}, u32[]{:S(2)}, u32[]{:S(2)}) async-start(bf16[16,2,128,256]{3,2,1,0:T(8,128)(2,1)} %broadcast_in_dim.5), calls=%async_computation.2 | async-start | bytes 4194304 | tf_op jit(solution)/shard_map/all_to_all | solution.py:22
  199.0 5.1 %collective-permute-start.14 = (bf16[4,2,2,128,128]{4,3,2,1,0:T(8,128)(2,1)}, bf16[4,2,2,128,128]{4,3,2,1,0:T(8,128)(2,1)S(1)}, u32[]{:S(2)}, u32[]{:S(2)}) collective-permute-start(bf16[4,2,2,128,128]{4,3,2,1,0:T(8,128)(2,1)} %get-tuple-element.13), channel_id=1, source_target_pairs={{0,28},{1,29},{2,30},{3,31},{4,0},{5,1},{6,2},{7,3},{8,4},{9,5},{1... | collective-permute-start | bytes 1572872 | tf_op jit(solution)/shard_map/ppermute | solution.py:69
  205.6 1.9 collective-permute-start.12
  207.5 8.3 %collective-permute-done.14 = bf16[4,2,2,128,128]{4,3,2,1,0:T(8,128)(2,1)S(1)} collective-permute-done((bf16[4,2,2,128,128]{4,3,2,1,0:T(8,128)(2,1)}, bf16[4,2,2,128,128]{4,3,2,1,0:T(8,128)(2,1)S(1)}, u32[]{:S(2)}, u32[]{:S(2)}) %collective-permute-start.14) | collective-permute-done | bytes 524320 | tf_op jit(solution)/shard_map/ppermute | solution.py:69
  215.9 6.3 %collective-permute-done.12 = bf16[4,2,2,128,128]{4,3,2,1,0:T(8,128)(2,1)S(1)} collective-permute-done((bf16[4,2,2,128,128]{4,3,2,1,0:T(8,128)(2,1)S(1)}, bf16[4,2,2,128,128]{4,3,2,1,0:T(8,128)(2,1)S(1)}, u32[]{:S(2)}, u32[]{:S(2)}) %collective-permute-start.12) | collective-permute-done | bytes 524320 | tf_op jit(solution)/shard_map/ppermute | solution.py:64
  225.6 3.9 %collective-permute-start.13 = (bf16[4,2,2,128,128]{4,3,2,1,0:T(8,128)(2,1)S(1)}, bf16[4,2,2,128,128]{4,3,2,1,0:T(8,128)(2,1)S(1)}, u32[]{:S(2)}, u32[]{:S(2)}) collective-permute-start(bf16[4,2,2,128,128]{4,3,2,1,0:T(8,128)(2,1)S(1)} %get-tuple-element.10), channel_id=1, source_target_pairs={{0,4},{1,5},{2,6},{3,7},{4,8},{5,9},{6,10},{7,11},{8,12},{9,13},{1... | collective-permute-start | bytes 1572872 | tf_op jit(solution)/shard_map/ppermute | solution.py:64
  229.5 8.6 %collective-permute-done.15 = bf16[4,2,2,128,128]{4,3,2,1,0:T(8,128)(2,1)S(1)} collective-permute-done((bf16[4,2,2,128,128]{4,3,2,1,0:T(8,128)(2,1)S(1)}, bf16[4,2,2,128,128]{4,3,2,1,0:T(8,128)(2,1)S(1)}, u32[]{:S(2)}, u32[]{:S(2)}) %collective-permute-start.15) | collective-permute-done | bytes 524320 | tf_op jit(solution)/shard_map/ppermute | solution.py:69
  239.3 3.4 %collective-permute-start.16 = (bf16[4,2,2,128,128]{4,3,2,1,0:T(8,128)(2,1)S(1)}, bf16[4,2,2,128,128]{4,3,2,1,0:T(8,128)(2,1)S(1)}, u32[]{:S(2)}, u32[]{:S(2)}) collective-permute-start(bf16[4,2,2,128,128]{4,3,2,1,0:T(8,128)(2,1)S(1)} %fusion.8), channel_id=1, source_target_pairs={{0,28},{1,29},{2,30},{3,31},{4,0},{5,1},{6,2},{7,3},{8,4},{9,5},{1... | collective-permute-start | bytes 1572872 | tf_op jit(solution)/shard_map/ppermute | solution.py:69
  242.8 10.1 %collective-permute-done.16 = bf16[4,2,2,128,128]{4,3,2,1,0:T(8,128)(2,1)S(1)} collective-permute-done((bf16[4,2,2,128,128]{4,3,2,1,0:T(8,128)(2,1)S(1)}, bf16[4,2,2,128,128]{4,3,2,1,0:T(8,128)(2,1)S(1)}, u32[]{:S(2)}, u32[]{:S(2)}) %collective-permute-start.16) | collective-permute-done | bytes 524320 | tf_op jit(solution)/shard_map/ppermute | solution.py:69
  254.1 4.4 %collective-permute-start.17 = (bf16[2,2,128,128]{3,2,1,0:T(8,128)(2,1)S(1)}, bf16[2,2,128,128]{3,2,1,0:T(8,128)(2,1)S(1)}, u32[]{:S(2)}, u32[]{:S(2)}) collective-permute-start(bf16[2,2,128,128]{3,2,1,0:T(8,128)(2,1)S(1)} %get-tuple-element.20), channel_id=1, source_target_pairs={{0,3},{1,0},{2,1},{3,2},{4,7},{5,4},{6,5},{7,6},{8,11},{9,8},{10,9... | collective-permute-start | bytes 393224 | tf_op jit(solution)/shard_map/ppermute | solution.py:77
  258.5 4.2 %collective-permute-start.18 = (bf16[2,2,128,128]{3,2,1,0:T(8,128)(2,1)S(1)}, bf16[2,2,128,128]{3,2,1,0:T(8,128)(2,1)S(1)}, u32[]{:S(2)}, u32[]{:S(2)}) collective-permute-start(bf16[2,2,128,128]{3,2,1,0:T(8,128)(2,1)S(1)} %get-tuple-element.22), channel_id=1, source_target_pairs={{0,2},{1,3},{2,0},{3,1},{4,6},{5,7},{6,4},{7,5},{8,10},{9,11},{10,... | collective-permute-start | bytes 393224 | tf_op jit(solution)/shard_map/ppermute | solution.py:77
  262.7 2.5 collective-permute-start.19
  265.3 5.2 %collective-permute-done.18 = bf16[2,2,128,128]{3,2,1,0:T(8,128)(2,1)S(1)} collective-permute-done((bf16[2,2,128,128]{3,2,1,0:T(8,128)(2,1)S(1)}, bf16[2,2,128,128]{3,2,1,0:T(8,128)(2,1)S(1)}, u32[]{:S(2)}, u32[]{:S(2)}) %collective-permute-start.18) | collective-permute-done | bytes 131104 | tf_op jit(solution)/shard_map/ppermute | solution.py:77
  270.5 2.4 collective-permute-done.19
  273.6 2.4 copy.83
  (98 shorter events, 47.8 us)
Async XLA Ops:
  0.6 55.5 %copy-start = (s32[64]{0:T(128)S(1)}, s32[64]{0:T(128)}, u32[]{:S(2)}) copy-start(s32[64]{0:T(128)} %param.9) | copy-start | bytes 772
  1.5 27.6 %collective-permute-start = (bf16[2,2,128,128]{3,2,1,0:T(8,128)(2,1)S(1)}, bf16[2,2,128,128]{3,2,1,0:T(8,128)(2,1)S(1)}, u32[]{:S(2)}, u32[]{:S(2)}) collective-permute-start(bf16[2,2,128,128]{3,2,1,0:T(8,128)(2,1)S(1)} %get-tuple-element.26), channel_id=1, source_target_pairs={{0,1},{1,2},{2,3},{3,0},{4,5},{5,6},{6,7},{7,4},{8,9},{9,10},{10,1... | collective-permute-start | bytes 393224 | tf_op jit(solution)/shard_map/ppermute | solution.py:42
  7.6 21.5 %collective-permute-start.1 = (bf16[2,2,128,128]{3,2,1,0:T(8,128)(2,1)S(1)}, bf16[2,2,128,128]{3,2,1,0:T(8,128)(2,1)S(1)}, u32[]{:S(2)}, u32[]{:S(2)}) collective-permute-start(bf16[2,2,128,128]{3,2,1,0:T(8,128)(2,1)S(1)} %get-tuple-element.26), channel_id=1, source_target_pairs={{0,2},{1,3},{2,0},{3,1},{4,6},{5,7},{6,4},{7,5},{8,10},{9,11},{10,... | collective-permute-start | bytes 393224 | tf_op jit(solution)/shard_map/ppermute | solution.py:42
  16.8 12.6 %collective-permute-start.2 = (bf16[2,2,128,128]{3,2,1,0:T(8,128)(2,1)S(1)}, bf16[2,2,128,128]{3,2,1,0:T(8,128)(2,1)S(1)}, u32[]{:S(2)}, u32[]{:S(2)}) collective-permute-start(bf16[2,2,128,128]{3,2,1,0:T(8,128)(2,1)S(1)} %get-tuple-element.26), channel_id=1, source_target_pairs={{0,3},{1,0},{2,1},{3,2},{4,7},{5,4},{6,5},{7,6},{8,11},{9,8},{10,9... | collective-permute-start | bytes 393224 | tf_op jit(solution)/shard_map/ppermute | solution.py:42
  23.3 42.7 %copy-start.2 = (s32[64]{0:T(128)S(1)}, s32[64]{0:T(128)}, u32[]{:S(2)}) copy-start(s32[64]{0:T(128)} %param.11) | copy-start | bytes 772
  23.3 77.1 %all-to-all-start = ((bf16[16,2,128,256]{2,3,1,0:T(8,128)(2,1)}), bf16[16,2,128,256]{2,3,1,0:T(8,128)(2,1)S(1)}, u32[]{:S(2)}, u32[]{:S(2)}) async-start(bf16[16,2,128,256]{2,3,1,0:T(8,128)(2,1)} %broadcast_in_dim.4), calls=%async_computation | async-start | bytes 4194304 | tf_op jit(solution)/shard_map/all_to_all | solution.py:22
  29.4 0.7 copy-start.11
  30.1 17.5 %collective-permute-start.3 = (bf16[4,2,2,128,128]{4,3,2,1,0:T(8,128)(2,1)S(1)}, bf16[4,2,2,128,128]{4,3,2,1,0:T(8,128)(2,1)S(1)}, u32[]{:S(2)}, u32[]{:S(2)}) collective-permute-start(bf16[4,2,2,128,128]{4,3,2,1,0:T(8,128)(2,1)S(1)} %pad_maximum_fusion), channel_id=1, source_target_pairs={{0,4},{1,5},{2,6},{3,7},{4,8},{5,9},{6,10},{7,11},{8,12},{9,13},{1... | collective-permute-start | bytes 1572872 | tf_op jit(solution)/shard_map/ppermute | solution.py:48
  47.6 16.5 %collective-permute-start.4 = (bf16[4,2,2,128,128]{4,3,2,1,0:T(8,128)(2,1)S(1)}, bf16[4,2,2,128,128]{4,3,2,1,0:T(8,128)(2,1)}, u32[]{:S(2)}, u32[]{:S(2)}) collective-permute-start(bf16[4,2,2,128,128]{4,3,2,1,0:T(8,128)(2,1)S(1)} %collective-permute-done.3), channel_id=1, source_target_pairs={{0,4},{1,5},{2,6},{3,7},{4,8},{5,9},{6,10},{7,11},{8,12},{9,13},{1... | collective-permute-start | bytes 1572872 | tf_op jit(solution)/shard_map/ppermute | solution.py:48
  51.0 15.9 %collective-permute-start.7 = (bf16[4,2,2,128,128]{4,3,2,1,0:T(8,128)(2,1)S(1)}, bf16[4,2,2,128,128]{4,3,2,1,0:T(8,128)(2,1)}, u32[]{:S(2)}, u32[]{:S(2)}) collective-permute-start(bf16[4,2,2,128,128]{4,3,2,1,0:T(8,128)(2,1)S(1)} %pad_maximum_fusion), channel_id=1, source_target_pairs={{0,28},{1,29},{2,30},{3,31},{4,0},{5,1},{6,2},{7,3},{8,4},{9,5},{1... | collective-permute-start | bytes 1572872 | tf_op jit(solution)/shard_map/ppermute | solution.py:51
  64.1 15.8 %collective-permute-start.5 = (bf16[4,2,2,128,128]{4,3,2,1,0:T(8,128)(2,1)}, bf16[4,2,2,128,128]{4,3,2,1,0:T(8,128)(2,1)}, u32[]{:S(2)}, u32[]{:S(2)}) collective-permute-start(bf16[4,2,2,128,128]{4,3,2,1,0:T(8,128)(2,1)} %collective-permute-done.4), channel_id=1, source_target_pairs={{0,4},{1,5},{2,6},{3,7},{4,8},{5,9},{6,10},{7,11},{8,12},{9,13},{1... | collective-permute-start | bytes 1572872 | tf_op jit(solution)/shard_map/ppermute | solution.py:48
  66.8 0.5 copy-start.13
  67.3 15.1 %collective-permute-start.8 = (bf16[4,2,2,128,128]{4,3,2,1,0:T(8,128)(2,1)}, bf16[4,2,2,128,128]{4,3,2,1,0:T(8,128)(2,1)S(1)}, u32[]{:S(2)}, u32[]{:S(2)}) collective-permute-start(bf16[4,2,2,128,128]{4,3,2,1,0:T(8,128)(2,1)} %collective-permute-done.7), channel_id=1, source_target_pairs={{0,28},{1,29},{2,30},{3,31},{4,0},{5,1},{6,2},{7,3},{8,4},{9,5},{1... | collective-permute-start | bytes 1572872 | tf_op jit(solution)/shard_map/ppermute | solution.py:51
  79.9 14.8 %collective-permute-start.6 = (bf16[4,2,2,128,128]{4,3,2,1,0:T(8,128)(2,1)}, bf16[4,2,2,128,128]{4,3,2,1,0:T(8,128)(2,1)S(1)}, u32[]{:S(2)}, u32[]{:S(2)}) collective-permute-start(bf16[4,2,2,128,128]{4,3,2,1,0:T(8,128)(2,1)} %collective-permute-done.5), channel_id=1, source_target_pairs={{0,4},{1,5},{2,6},{3,7},{4,8},{5,9},{6,10},{7,11},{8,12},{9,13},{1... | collective-permute-start | bytes 1572872 | tf_op jit(solution)/shard_map/ppermute | solution.py:48
  82.4 14.2 %collective-permute-start.9 = (bf16[4,2,2,128,128]{4,3,2,1,0:T(8,128)(2,1)S(1)}, bf16[4,2,2,128,128]{4,3,2,1,0:T(8,128)(2,1)S(1)}, u32[]{:S(2)}, u32[]{:S(2)}) collective-permute-start(bf16[4,2,2,128,128]{4,3,2,1,0:T(8,128)(2,1)S(1)} %collective-permute-done.8), channel_id=1, source_target_pairs={{0,28},{1,29},{2,30},{3,31},{4,0},{5,1},{6,2},{7,3},{8,4},{9,5},{1... | collective-permute-start | bytes 1572872 | tf_op jit(solution)/shard_map/ppermute | solution.py:51
  110.2 4.6 %copy-start.5 = (bf16[64,128,128]{2,1,0:T(8,128)(2,1)S(1)}, bf16[64,128,128]{2,1,0:T(8,128)(2,1)}, u32[]{:S(2)}) copy-start(bf16[64,128,128]{2,1,0:T(8,128)(2,1)} %gather_fusion.3) | copy-start | bytes 6291460
  110.2 4.6 %copy-start.7 = (bf16[1,8,4,2,128,128]{5,4,3,0,2,1:T(8,128)(2,1)S(1)}, bf16[1,8,4,2,128,128]{5,4,3,0,2,1:T(8,128)(2,1)}, u32[]{:S(2)}) copy-start(bf16[1,8,4,2,128,128]{5,4,3,0,2,1:T(8,128)(2,1)} %get-tuple-element.14) | copy-start | bytes 6291460
  110.2 4.6 %copy-start.9 = (f32[128,8,128]{0,2,1:T(8,128)S(1)}, f32[128,8,128]{0,2,1:T(8,128)}, u32[]{:S(2)}) copy-start(f32[128,8,128]{0,2,1:T(8,128)} %convolution_bitcast_fusion.1) | copy-start | bytes 1572868
  115.5 5.5 %copy-start.14 = (s32[64]{0:T(128)S(1)}, s32[64]{0:T(128)}, u32[]{:S(2)}) copy-start(s32[64]{0:T(128)} %copy-done.13) | copy-start | bytes 772
  128.0 2.7 copy-start.3
  133.3 5.4 %copy-start.12 = (s32[64]{0:T(128)S(1)}, s32[64]{0:T(128)}, u32[]{:S(2)}) copy-start(s32[64]{0:T(128)} %gather_fusion.1) | copy-start | bytes 772
  145.7 1.7 copy-start.10
  149.0 40.8 %all-to-all-start.1 = ((bf16[16,2,128,256]{3,2,1,0:T(8,128)(2,1)}), bf16[16,2,128,256]{3,2,1,0:T(8,128)(2,1)}, u32[]{:S(2)}, u32[]{:S(2)}) async-start(bf16[16,2,128,256]{3,2,1,0:T(8,128)(2,1)} %maximum_bitcast_fusion.1), calls=%async_computation.1 | async-start | bytes 4194304 | tf_op jit(solution)/shard_map/all_to_all | solution.py:26
  162.8 4.1 %copy-start.6 = (bf16[8,8,128,128]{2,3,1,0:T(8,128)(2,1)S(1)}, bf16[8,8,128,128]{2,3,1,0:T(8,128)(2,1)}, u32[]{:S(2)}) copy-start(bf16[8,8,128,128]{2,3,1,0:T(8,128)(2,1)} %copy.70) | copy-start | bytes 6291460
  166.9 1.6 copy-start.8
  168.9 18.8 %copy-start.4 = (bf16[8,4,2,2,128,128]{5,4,3,2,1,0:T(8,128)(2,1)}, bf16[8,4,2,2,128,128]{5,4,3,2,1,0:T(8,128)(2,1)S(1)}, u32[]{:S(2)}) copy-start(bf16[8,4,2,2,128,128]{5,4,3,2,1,0:T(8,128)(2,1)S(1)} %maximum_bitcast_fusion) | copy-start | bytes 12582916
  169.8 17.8 %collective-permute-start.10 = (bf16[4,2,2,128,128]{4,3,2,1,0:T(8,128)(2,1)S(1)}, bf16[4,2,2,128,128]{4,3,2,1,0:T(8,128)(2,1)S(1)}, u32[]{:S(2)}, u32[]{:S(2)}) collective-permute-start(bf16[4,2,2,128,128]{4,3,2,1,0:T(8,128)(2,1)S(1)} %get-tuple-element.12), channel_id=1, source_target_pairs={{0,4},{1,5},{2,6},{3,7},{4,8},{5,9},{6,10},{7,11},{8,12},{9,13},{1... | collective-permute-start | bytes 1572872 | tf_op jit(solution)/shard_map/ppermute | solution.py:64
  187.8 16.6 %collective-permute-start.11 = (bf16[4,2,2,128,128]{4,3,2,1,0:T(8,128)(2,1)S(1)}, bf16[4,2,2,128,128]{4,3,2,1,0:T(8,128)(2,1)S(1)}, u32[]{:S(2)}, u32[]{:S(2)}) collective-permute-start(bf16[4,2,2,128,128]{4,3,2,1,0:T(8,128)(2,1)S(1)} %fusion.9), channel_id=1, source_target_pairs={{0,4},{1,5},{2,6},{3,7},{4,8},{5,9},{6,10},{7,11},{8,12},{9,13},{1... | collective-permute-start | bytes 1572872 | tf_op jit(solution)/shard_map/ppermute | solution.py:64
  193.2 80.4 %all-to-all-start.2 = ((bf16[16,2,128,256]{3,2,1,0:T(8,128)(2,1)}), bf16[16,2,128,256]{3,2,1,0:T(8,128)(2,1)S(1)}, u32[]{:S(2)}, u32[]{:S(2)}) async-start(bf16[16,2,128,256]{3,2,1,0:T(8,128)(2,1)} %broadcast_in_dim.5), calls=%async_computation.2 | async-start | bytes 4194304 | tf_op jit(solution)/shard_map/all_to_all | solution.py:22
  199.0 16.9 %collective-permute-start.14 = (bf16[4,2,2,128,128]{4,3,2,1,0:T(8,128)(2,1)}, bf16[4,2,2,128,128]{4,3,2,1,0:T(8,128)(2,1)S(1)}, u32[]{:S(2)}, u32[]{:S(2)}) collective-permute-start(bf16[4,2,2,128,128]{4,3,2,1,0:T(8,128)(2,1)} %get-tuple-element.13), channel_id=1, source_target_pairs={{0,28},{1,29},{2,30},{3,31},{4,0},{5,1},{6,2},{7,3},{8,4},{9,5},{1... | collective-permute-start | bytes 1572872 | tf_op jit(solution)/shard_map/ppermute | solution.py:69
  205.6 16.5 %collective-permute-start.12 = (bf16[4,2,2,128,128]{4,3,2,1,0:T(8,128)(2,1)S(1)}, bf16[4,2,2,128,128]{4,3,2,1,0:T(8,128)(2,1)S(1)}, u32[]{:S(2)}, u32[]{:S(2)}) collective-permute-start(bf16[4,2,2,128,128]{4,3,2,1,0:T(8,128)(2,1)S(1)} %fusion.10), channel_id=1, source_target_pairs={{0,4},{1,5},{2,6},{3,7},{4,8},{5,9},{6,10},{7,11},{8,12},{9,13},{1... | collective-permute-start | bytes 1572872 | tf_op jit(solution)/shard_map/ppermute | solution.py:64
  223.7 14.4 %collective-permute-start.15 = (bf16[4,2,2,128,128]{4,3,2,1,0:T(8,128)(2,1)S(1)}, bf16[4,2,2,128,128]{4,3,2,1,0:T(8,128)(2,1)S(1)}, u32[]{:S(2)}, u32[]{:S(2)}) collective-permute-start(bf16[4,2,2,128,128]{4,3,2,1,0:T(8,128)(2,1)S(1)} %get-tuple-element.11), channel_id=1, source_target_pairs={{0,28},{1,29},{2,30},{3,31},{4,0},{5,1},{6,2},{7,3},{8,4},{9,5},{1... | collective-permute-start | bytes 1572872 | tf_op jit(solution)/shard_map/ppermute | solution.py:69
  225.6 17.1 %collective-permute-start.13 = (bf16[4,2,2,128,128]{4,3,2,1,0:T(8,128)(2,1)S(1)}, bf16[4,2,2,128,128]{4,3,2,1,0:T(8,128)(2,1)S(1)}, u32[]{:S(2)}, u32[]{:S(2)}) collective-permute-start(bf16[4,2,2,128,128]{4,3,2,1,0:T(8,128)(2,1)S(1)} %get-tuple-element.10), channel_id=1, source_target_pairs={{0,4},{1,5},{2,6},{3,7},{4,8},{5,9},{6,10},{7,11},{8,12},{9,13},{1... | collective-permute-start | bytes 1572872 | tf_op jit(solution)/shard_map/ppermute | solution.py:64
  239.3 13.5 %collective-permute-start.16 = (bf16[4,2,2,128,128]{4,3,2,1,0:T(8,128)(2,1)S(1)}, bf16[4,2,2,128,128]{4,3,2,1,0:T(8,128)(2,1)S(1)}, u32[]{:S(2)}, u32[]{:S(2)}) collective-permute-start(bf16[4,2,2,128,128]{4,3,2,1,0:T(8,128)(2,1)S(1)} %fusion.8), channel_id=1, source_target_pairs={{0,28},{1,29},{2,30},{3,31},{4,0},{5,1},{6,2},{7,3},{8,4},{9,5},{1... | collective-permute-start | bytes 1572872 | tf_op jit(solution)/shard_map/ppermute | solution.py:69
  254.1 11.1 %collective-permute-start.17 = (bf16[2,2,128,128]{3,2,1,0:T(8,128)(2,1)S(1)}, bf16[2,2,128,128]{3,2,1,0:T(8,128)(2,1)S(1)}, u32[]{:S(2)}, u32[]{:S(2)}) collective-permute-start(bf16[2,2,128,128]{3,2,1,0:T(8,128)(2,1)S(1)} %get-tuple-element.20), channel_id=1, source_target_pairs={{0,3},{1,0},{2,1},{3,2},{4,7},{5,4},{6,5},{7,6},{8,11},{9,8},{10,9... | collective-permute-start | bytes 393224 | tf_op jit(solution)/shard_map/ppermute | solution.py:77
  258.5 11.9 %collective-permute-start.18 = (bf16[2,2,128,128]{3,2,1,0:T(8,128)(2,1)S(1)}, bf16[2,2,128,128]{3,2,1,0:T(8,128)(2,1)S(1)}, u32[]{:S(2)}, u32[]{:S(2)}) collective-permute-start(bf16[2,2,128,128]{3,2,1,0:T(8,128)(2,1)S(1)} %get-tuple-element.22), channel_id=1, source_target_pairs={{0,2},{1,3},{2,0},{3,1},{4,6},{5,7},{6,4},{7,5},{8,10},{9,11},{10,... | collective-permute-start | bytes 393224 | tf_op jit(solution)/shard_map/ppermute | solution.py:77
  262.7 10.2 %collective-permute-start.19 = (bf16[2,2,128,128]{3,2,1,0:T(8,128)(2,1)S(1)}, bf16[2,2,128,128]{3,2,1,0:T(8,128)(2,1)S(1)}, u32[]{:S(2)}, u32[]{:S(2)}) collective-permute-start(bf16[2,2,128,128]{3,2,1,0:T(8,128)(2,1)S(1)} %get-tuple-element.21), channel_id=1, source_target_pairs={{0,1},{1,2},{2,3},{3,0},{4,5},{5,6},{6,7},{7,4},{8,9},{9,10},{10,1... | collective-permute-start | bytes 393224 | tf_op jit(solution)/shard_map/ppermute | solution.py:77
  277.7 2.6 copy-start.1

commit v6 on v5

--- a/solution.py
+++ b/solution.py
@@ -41,40 +41,71 @@
 def dp_gather_rel(x, n_y, n_z):
     by_z = [x] + [lax.ppermute(x, "dp", dp_shift(n_y, n_z, 0, b)) for b in range(1, n_z)]
     held = jnp.stack(by_z)
-    n_f, n_b = n_y // 2, (n_y - 1) // 2
-    fwd, bwd = [held], []
-    cur_f = cur_b = held
-    for k in range(1, n_f + 1):
-        cur_f = lax.ppermute(cur_f, "dp", dp_shift(n_y, n_z, 1, 0))
-        fwd.append(cur_f)
-        if k <= n_b:
-            cur_b = lax.ppermute(cur_b, "dp", dp_shift(n_y, n_z, -1, 0))
-            bwd.append(cur_b)
-    rel = fwd + [bwd[n_y - a - 1] for a in range(len(fwd), n_y)]
-    return jnp.stack(rel)
+    half = n_y // 2
+    split = n_y % 2 == 0 and held.shape[0] % 2 == 0
+    cut = held.shape[0] // 2
+    piece = {0: held}
+    cur = held
+    for k in range(1, half + 1):
+        if split and k == half:
+            fwd_tail = lax.ppermute(cur[:cut], "dp", dp_shift(n_y, n_z, 1, 0))
+        else:
+            cur = lax.ppermute(cur, "dp", dp_shift(n_y, n_z, 1, 0))
+            piece[k] = cur
+    cur = held
+    for k in range(1, (n_y - 1) // 2 + 1 + int(split)):
+        if split and k == half:
+            bwd_tail = lax.ppermute(cur[cut:], "dp", dp_shift(n_y, n_z, -1, 0))
+        else:
+            cur = lax.ppermute(cur, "dp", dp_shift(n_y, n_z, -1, 0))
+            piece[n_y - k] = cur
+    if split:
+        piece[half] = jnp.concatenate([fwd_tail, bwd_tail])
+    return jnp.stack([piece[a] for a in range(n_y)])
+
+
+def ring_chain(terms, n_y, n_z, steps, dest, direction, first):
+    got = None
+    for k in range(1, steps + 1):
+        part = terms[:, dest(k)].astype(jnp.float32)
+        if k == 1:
+            part = part[:, first]
+        elif got is not None:
+            if got.shape == part.shape:
+                part = part + got.astype(jnp.float32)
+            else:
+                part = part.at[:, first].add(got.astype(jnp.float32))
+        got = lax.ppermute(part.astype(jnp.bfloat16), "dp", dp_shift(n_y, n_z, direction, 0))
+    return got
 
 
 def dp_scatter_rel(terms, n_y, n_z):
-    n_f, n_b = n_y // 2, (n_y - 1) // 2
-    got_f = got_b = None
-    for k in range(1, n_f + 1):
-        part = terms[(n_y - n_f - 1 + k) % n_y].astype(jnp.float32)
-        if got_f is not None:
-            part = part + got_f.astype(jnp.float32)
-        got_f = lax.ppermute(part.astype(jnp.bfloat16), "dp", dp_shift(n_y, n_z, 1, 0))
-    for k in range(1, n_b + 1):
-        part = terms[n_b + 1 - k].astype(jnp.float32)
-        if got_b is not None:
-            part = part + got_b.astype(jnp.float32)
-        got_b = lax.ppermute(part.astype(jnp.bfloat16), "dp", dp_shift(n_y, n_z, -1, 0))
-    acc = terms[0].astype(jnp.float32)
-    if got_f is not None:
-        acc = acc + got_f.astype(jnp.float32)
-    if got_b is not None:
-        acc = acc + got_b.astype(jnp.float32)
-    total = acc[0]
+    half = n_y // 2
+    split = n_y % 2 == 0 and terms.shape[2] % 2 == 0
+    cut = terms.shape[2] // 2
+    n_b = half if split else (n_y - 1) // 2
+    acc = terms[:, 0].astype(jnp.float32)
+    if half > 0:
+        got_f = ring_chain(
+            terms, n_y, n_z, half, lambda k: (n_y - half - 1 + k) % n_y, 1,
+            slice(0, cut) if split else slice(None),
+        )
+        if got_f.shape[1] == acc.shape[1]:
+            acc = acc + got_f.astype(jnp.float32)
+        else:
+            acc = acc.at[:, :cut].add(got_f.astype(jnp.float32))
+    if n_b > 0:
+        got_b = ring_chain(
+            terms, n_y, n_z, n_b, lambda k: n_b + 1 - k, -1,
+            slice(cut, None) if split else slice(None),
+        )
+        if got_b.shape[1] == acc.shape[1]:
+            acc = acc + got_b.astype(jnp.float32)
+        else:
+            acc = acc.at[:, cut:].add(got_b.astype(jnp.float32))
+    total = acc[:, 0]
     for b in range(1, n_z):
-        sent = lax.ppermute(acc[b].astype(jnp.bfloat16), "dp", dp_shift(n_y, n_z, 0, -b))
+        sent = lax.ppermute(acc[:, b].astype(jnp.bfloat16), "dp", dp_shift(n_y, n_z, 0, -b))
         total = total + sent.astype(jnp.float32)
     return total.astype(jnp.bfloat16)
 
@@ -153,7 +184,7 @@
 
     terms = jnp.stack([up_term, down_term]).astype(jnp.bfloat16)
     terms = terms.reshape(2, n_y, n_z, per_dev, block_size, block_size)
-    grads = dp_scatter_rel(jnp.moveaxis(terms, 0, 2), n_y, n_z)
+    grads = dp_scatter_rel(terms, n_y, n_z)
     return (both[0], both[1], grads[0], grads[1])
 
 

time: 285 us -> 311 us (1.091)
  waiting for transfers between devices: 89.2 us -> 108 us
  starting transfers between devices: 93.7 us -> 102 us
    ppermute x3, waiting for transfers between devices: 0.24 us -> 25.4 us  [dp_gather_rel(): lax.ppermute(x, 'dp', dp_shift(n_y, n_z, 0, b))]
    ppermute x17 -> x19, waiting for transfers between devices: 88.9 us -> 70.7 us  [the longest x8 35 us: ring_chain(): lax.ppermute(part.astype(jnp.bfloat16), 'dp', dp_shift(n_y, n_z, directio...]
    all_to_all x1, waiting for transfers between devices: 0.01 us -> 11.6 us  [scatter_sum(): got = lax.all_to_all(x, axis_name, 0, 0, tiled=True)]
    ppermute x17 -> x19, starting transfers between devices: 57.2 us -> 66 us  [the longest x8 25.4 us: ring_chain(): lax.ppermute(part.astype(jnp.bfloat16), 'dp', dp_shift(n_y, n_z, directio...]
    ppermute x3, starting transfers between devices: 18.9 us -> 15.2 us  [dp_gather_rel(): lax.ppermute(x, 'dp', dp_shift(n_y, n_z, 0, b))]
    unnamed x38 -> x45, local copies, waits for them, and re-layouts: 7.16 us -> 8.07 us
  transfers between devices with their start and end apart: 23 -> 25, of which waited for: 15 -> 17; matrix products, arithmetic and copies ran while one was open for 14% -> 12% of each run, Pallas kernels for 0% -> 0%
where the time goes in v6:
time: 311 us; the launch traced here: 308 us
  waiting for transfers between devices  108 us (35%)
  starting transfers between devices  102 us (33%)
  local copies, waits for them, and re-layouts  58.7 us (19%)
  matrix products  25.2 us (8%)
  other arithmetic  13 us (4%)
    ppermute x8, waiting for transfers between devices, ring_chain(): lax.ppermute(part.astype(jnp.bfloat16), 'dp', dp_shift(n_y, n_z, directio...  35 us
    ppermute x8, starting transfers between devices, ring_chain(): lax.ppermute(part.astype(jnp.bfloat16), 'dp', dp_shift(n_y, n_z, directio...  25.4 us
    ppermute x3, waiting for transfers between devices, dp_gather_rel(): lax.ppermute(x, 'dp', dp_shift(n_y, n_z, 0, b))  25.4 us
    ppermute x3, starting transfers between devices, dp_gather_rel(): lax.ppermute(x, 'dp', dp_shift(n_y, n_z, 0, b))  15.2 us
    ppermute x3, starting transfers between devices, dp_gather_rel(): cur = lax.ppermute(cur, 'dp', dp_shift(n_y, n_z, -1, 0))  14.1 us
    all_to_all x2, starting transfers between devices, gather_all(): return lax.all_to_all(spread, axis_name, 0, 0, tiled=True)  14 us
    ppermute x3, waiting for transfers between devices, dp_gather_rel(): cur = lax.ppermute(cur, 'dp', dp_shift(n_y, n_z, 1, 0))  13.9 us
    all_to_all x1, waiting for transfers between devices, scatter_sum(): got = lax.all_to_all(x, axis_name, 0, 0, tiled=True)  11.6 us
  transfers between devices with their start and end apart: 25, of which 17 were waited for; matrix products, arithmetic and copies ran while one was open for 12% of the time, Pallas kernels for 0%

profile of v6, /device:TPU:6, one launch (start us, length us, event | category | flops | bytes accessed | tf_op | source)
XLA Modules:
  0.0 308.1 jit_solution(10094153821235882196)
XLA Ops:
  3.5 9.5 %all-to-all-start = ((bf16[16,2,128,256]{2,3,1,0:T(8,128)(2,1)}), bf16[16,2,128,256]{2,3,1,0:T(8,128)(2,1)S(1)}, u32[]{:S(2)}, u32[]{:S(2)}) async-start(bf16[16,2,128,256]{2,3,1,0:T(8,128)(2,1)} %broadcast_in_dim.4), calls=%async_computation | async-start | bytes 4194304 | tf_op jit(solution)/shard_map/all_to_all | solution.py:22
  13.1 3.3 %collective-permute-start = (bf16[2,2,128,128]{3,2,1,0:T(8,128)(2,1)S(1)}, bf16[2,2,128,128]{3,2,1,0:T(8,128)(2,1)S(1)}, u32[]{:S(2)}, u32[]{:S(2)}) collective-permute-start(bf16[2,2,128,128]{3,2,1,0:T(8,128)(2,1)S(1)} %get-tuple-element.55), channel_id=1, source_target_pairs={{0,1},{1,2},{2,3},{3,0},{4,5},{5,6},{6,7},{7,4},{8,9},{9,10},{10,1... | collective-permute-start | bytes 393224 | tf_op jit(solution)/shard_map/ppermute | solution.py:42
  16.4 8.2 %collective-permute-start.1 = (bf16[2,2,128,128]{3,2,1,0:T(8,128)(2,1)S(1)}, bf16[2,2,128,128]{3,2,1,0:T(8,128)(2,1)S(1)}, u32[]{:S(2)}, u32[]{:S(2)}) collective-permute-start(bf16[2,2,128,128]{3,2,1,0:T(8,128)(2,1)S(1)} %get-tuple-element.55), channel_id=1, source_target_pairs={{0,2},{1,3},{2,0},{3,1},{4,6},{5,7},{6,4},{7,5},{8,10},{9,11},{10,... | collective-permute-start | bytes 393224 | tf_op jit(solution)/shard_map/ppermute | solution.py:42
  24.6 3.7 %collective-permute-start.2 = (bf16[2,2,128,128]{3,2,1,0:T(8,128)(2,1)S(1)}, bf16[2,2,128,128]{3,2,1,0:T(8,128)(2,1)S(1)}, u32[]{:S(2)}, u32[]{:S(2)}) collective-permute-start(bf16[2,2,128,128]{3,2,1,0:T(8,128)(2,1)S(1)} %get-tuple-element.55), channel_id=1, source_target_pairs={{0,3},{1,0},{2,1},{3,2},{4,7},{5,4},{6,5},{7,6},{8,11},{9,8},{10,9... | collective-permute-start | bytes 393224 | tf_op jit(solution)/shard_map/ppermute | solution.py:42
  28.3 20.3 %collective-permute-done = bf16[2,2,128,128]{3,2,1,0:T(8,128)(2,1)S(1)} collective-permute-done((bf16[2,2,128,128]{3,2,1,0:T(8,128)(2,1)S(1)}, bf16[2,2,128,128]{3,2,1,0:T(8,128)(2,1)S(1)}, u32[]{:S(2)}, u32[]{:S(2)}) %collective-permute-start) | collective-permute-done | bytes 131104 | tf_op jit(solution)/shard_map/ppermute | solution.py:42
  48.6 5.2 %collective-permute-done.1 = bf16[2,2,128,128]{3,2,1,0:T(8,128)(2,1)S(1)} collective-permute-done((bf16[2,2,128,128]{3,2,1,0:T(8,128)(2,1)S(1)}, bf16[2,2,128,128]{3,2,1,0:T(8,128)(2,1)S(1)}, u32[]{:S(2)}, u32[]{:S(2)}) %collective-permute-start.1) | collective-permute-done | bytes 131104 | tf_op jit(solution)/shard_map/ppermute | solution.py:42
  54.6 3.4 %collective-permute-start.3 = (bf16[4,2,2,128,128]{4,3,2,1,0:T(8,128)(2,1)}, bf16[4,2,2,128,128]{4,3,2,1,0:T(8,128)(2,1)S(1)}, u32[]{:S(2)}, u32[]{:S(2)}) collective-permute-start(bf16[4,2,2,128,128]{4,3,2,1,0:T(8,128)(2,1)} %pad_maximum_fusion.1), channel_id=1, source_target_pairs={{0,4},{1,5},{2,6},{3,7},{4,8},{5,9},{6,10},{7,11},{8,12},{9,13},{1... | collective-permute-start | bytes 1572872 | tf_op jit(solution)/shard_map/ppermute | solution.py:53
  58.1 3.8 %collective-permute-start.7 = (bf16[4,2,2,128,128]{4,3,2,1,0:T(8,128)(2,1)}, bf16[4,2,2,128,128]{4,3,2,1,0:T(8,128)(2,1)S(1)}, u32[]{:S(2)}, u32[]{:S(2)}) collective-permute-start(bf16[4,2,2,128,128]{4,3,2,1,0:T(8,128)(2,1)} %pad_maximum_fusion.1), channel_id=1, source_target_pairs={{0,28},{1,29},{2,30},{3,31},{4,0},{5,1},{6,2},{7,3},{8,4},{9,5},{1... | collective-permute-start | bytes 1572872 | tf_op jit(solution)/shard_map/ppermute | solution.py:60
  63.5 8.4 %collective-permute-done.3 = bf16[4,2,2,128,128]{4,3,2,1,0:T(8,128)(2,1)S(1)} collective-permute-done((bf16[4,2,2,128,128]{4,3,2,1,0:T(8,128)(2,1)}, bf16[4,2,2,128,128]{4,3,2,1,0:T(8,128)(2,1)S(1)}, u32[]{:S(2)}, u32[]{:S(2)}) %collective-permute-start.3) | collective-permute-done | bytes 524320 | tf_op jit(solution)/shard_map/ppermute | solution.py:53
  73.8 5.1 %collective-permute-start.8 = (bf16[4,2,2,128,128]{4,3,2,1,0:T(8,128)(2,1)S(1)}, bf16[4,2,2,128,128]{4,3,2,1,0:T(8,128)(2,1)}, u32[]{:S(2)}, u32[]{:S(2)}) collective-permute-start(bf16[4,2,2,128,128]{4,3,2,1,0:T(8,128)(2,1)S(1)} %collective-permute-done.7), channel_id=1, source_target_pairs={{0,28},{1,29},{2,30},{3,31},{4,0},{5,1},{6,2},{7,3},{8,4},{9,5},{1... | collective-permute-start | bytes 1572872 | tf_op jit(solution)/shard_map/ppermute | solution.py:60
  82.4 5.5 %collective-permute-done.4 = bf16[4,2,2,128,128]{4,3,2,1,0:T(8,128)(2,1)} collective-permute-done((bf16[4,2,2,128,128]{4,3,2,1,0:T(8,128)(2,1)S(1)}, bf16[4,2,2,128,128]{4,3,2,1,0:T(8,128)(2,1)}, u32[]{:S(2)}, u32[]{:S(2)}) %collective-permute-start.4) | collective-permute-done | bytes 524320 | tf_op jit(solution)/shard_map/ppermute | solution.py:53
  89.8 5.1 %collective-permute-start.9 = (bf16[4,2,2,128,128]{4,3,2,1,0:T(8,128)(2,1)}, bf16[4,2,2,128,128]{4,3,2,1,0:T(8,128)(2,1)S(1)}, u32[]{:S(2)}, u32[]{:S(2)}) collective-permute-start(bf16[4,2,2,128,128]{4,3,2,1,0:T(8,128)(2,1)} %collective-permute-done.8), channel_id=1, source_target_pairs={{0,28},{1,29},{2,30},{3,31},{4,0},{5,1},{6,2},{7,3},{8,4},{9,5},{1... | collective-permute-start | bytes 1572872 | tf_op jit(solution)/shard_map/ppermute | solution.py:60
  97.3 7.2 %collective-permute-done.9 = bf16[4,2,2,128,128]{4,3,2,1,0:T(8,128)(2,1)S(1)} collective-permute-done((bf16[4,2,2,128,128]{4,3,2,1,0:T(8,128)(2,1)}, bf16[4,2,2,128,128]{4,3,2,1,0:T(8,128)(2,1)S(1)}, u32[]{:S(2)}, u32[]{:S(2)}) %collective-permute-start.9) | collective-permute-done | bytes 524320 | tf_op jit(solution)/shard_map/ppermute | solution.py:60
  104.5 5.5 %collective-permute-start.10 = (bf16[2,2,2,128,128]{4,3,2,1,0:T(8,128)(2,1)S(1)}, bf16[2,2,2,128,128]{4,3,2,1,0:T(8,128)(2,1)S(1)}, u32[]{:S(2)}, u32[]{:S(2)}) collective-permute-start(bf16[2,2,2,128,128]{4,3,2,1,0:T(8,128)(2,1)S(1)} %slice.187), channel_id=1, source_target_pairs={{0,28},{1,29},{2,30},{3,31},{4,0},{5,1},{6,2},{7,3},{8,4},{9,5},{1... | collective-permute-start | bytes 786440 | tf_op jit(solution)/shard_map/ppermute | solution.py:58
  113.9 5.6 %collective-permute-done.6 = bf16[2,2,2,128,128]{4,3,2,1,0:T(8,128)(2,1)S(1)} collective-permute-done((bf16[2,2,2,128,128]{4,3,2,1,0:T(8,128)(2,1)S(1)}, bf16[2,2,2,128,128]{4,3,2,1,0:T(8,128)(2,1)S(1)}, u32[]{:S(2)}, u32[]{:S(2)}) %collective-permute-start.6) | collective-permute-done | bytes 262176 | tf_op jit(solution)/shard_map/ppermute | solution.py:51
  120.9 2.6 fusion.50
  125.8 2.2 gather_fusion.2
  127.9 3.2 %convolution_bitcast_fusion.1 = f32[128,8,128]{0,2,1:T(8,128)} fusion(bf16[8,8,128,128]{3,2,1,0:T(8,128)(2,1)} %bitcast.174, bf16[128,8,8,128]{3,0,2,1:T(8,128)(2,1)S(1)} %bitcast.172), kind=kOutput, calls=%fused_computation.29 | convolution fusion | flops 268435456 | bytes 4718592 | tf_op jit(solution)/shard_map/tgki,gkio->tgo/dot_general | solution.py:149
  131.1 2.1 gather_fusion.3
  133.3 4.6 %fusion.46 = f32[8,8,128,128]{3,2,1,0:T(8,128)} fusion(bf16[8,8,128,128]{3,2,1,0:T(8,128)(2,1)} %bitcast.183, f32[128,8,128]{0,2,1:T(8,128)} %convolution_bitcast_fusion.1), kind=kOutput, calls=%fused_computation.114 | convolution fusion | flops 269090816 | bytes 6815744 | tf_op jit(solution)/shard_map/tgh,gkho->tgko/dot_general | solution.py:151
  138.7 5.4 %copy.73 = f32[128,64,128]{2,1,0:T(8,128)} copy(f32[128,64,128]{0,2,1:T(8,128)} %bitcast.177) | data formatting | bytes 8388608 | tf_op jit(solution)/shard_map/reshape | solution.py:156
  144.1 4.8 %fusion.2 = bf16[128,32,128]{2,1,0:T(8,128)(2,1)} fusion(f32[128,64,128]{2,1,0:T(8,128)} %copy.73, s32[64]{0:T(128)S(1)} %copy-done.18), kind=kOutput, calls=%fused_computation.26 | convolution fusion | flops 403179520 | bytes 5243136 | tf_op jit(solution)/shard_map/tbo,br->tro/dot_general | solution.py:155
  148.9 2.2 stack.98
  151.1 2.7 copy.81
  153.7 2.7 fusion.54
  156.4 5.4 %copy.80 = f32[128,64,128]{2,1,0:T(8,128)} copy(f32[128,64,128]{0,2,1:T(8,128)} %bitcast.176) | data formatting | bytes 8388608 | tf_op jit(solution)/shard_map/reshape | solution.py:171
  161.9 4.8 %fusion.3 = bf16[128,32,128]{2,1,0:T(8,128)(2,1)} fusion(f32[128,64,128]{2,1,0:T(8,128)} %copy.80, s32[64]{0:T(128)S(1)} %copy-done.16), kind=kOutput, calls=%fused_computation.27 | convolution fusion | flops 403179520 | bytes 5243136 | tf_op jit(solution)/shard_map/tbi,br->tri/dot_general | solution.py:170
  166.6 2.2 stack.99
  172.0 6.9 %all-to-all-start.1 = ((bf16[16,2,128,256]{3,2,1,0:T(8,128)(2,1)}), bf16[16,2,128,256]{3,2,1,0:T(8,128)(2,1)}, u32[]{:S(2)}, u32[]{:S(2)}) async-start(bf16[16,2,128,256]{3,2,1,0:T(8,128)(2,1)} %maximum_bitcast_fusion), calls=%async_computation.1 | async-start | bytes 4194304 | tf_op jit(solution)/shard_map/all_to_all | solution.py:26
  178.9 2.6 copy.70
  181.5 3.0 copy.75
  186.7 3.0 copy.87
  189.7 2.3 multiply_convert_fusion.1
  196.5 11.6 %all-to-all-done.1 = bf16[16,2,128,256]{3,2,1,0:T(8,128)(2,1)} async-done(((bf16[16,2,128,256]{3,2,1,0:T(8,128)(2,1)}), bf16[16,2,128,256]{3,2,1,0:T(8,128)(2,1)}, u32[]{:S(2)}, u32[]{:S(2)}) %all-to-all-start.1) | async-done | bytes 2097184 | tf_op jit(solution)/shard_map/all_to_all | solution.py:26
  211.6 4.5 %all-to-all-start.2 = ((bf16[16,2,128,256]{3,2,1,0:T(8,128)(2,1)}), bf16[16,2,128,256]{3,2,1,0:T(8,128)(2,1)}, u32[]{:S(2)}, u32[]{:S(2)}) async-start(bf16[16,2,128,256]{3,2,1,0:T(8,128)(2,1)} %broadcast_in_dim.5), calls=%async_computation.2 | async-start | bytes 4194304 | tf_op jit(solution)/shard_map/all_to_all | solution.py:22
  221.4 5.1 %collective-permute-start.16 = (bf16[2,4,2,128,128]{4,3,2,0,1:T(8,128)(2,1)S(1)}, bf16[2,4,2,128,128]{4,3,2,0,1:T(8,128)(2,1)S(1)}, u32[]{:S(2)}, u32[]{:S(2)}) collective-permute-start(bf16[2,4,2,128,128]{4,3,2,0,1:T(8,128)(2,1)S(1)} %convert_element_type.154), channel_id=1, source_target_pairs={{0,28},{1,29},{2,30},{3,31},{4,0},{5,1},{6,2},{7,3},{8,4},{9,5},{1... | collective-permute-start | bytes 1572872 | tf_op jit(solution)/shard_map/ppermute | solution.py:78
  230.0 7.8 %collective-permute-done.16 = bf16[2,4,2,128,128]{4,3,2,0,1:T(8,128)(2,1)S(1)} collective-permute-done((bf16[2,4,2,128,128]{4,3,2,0,1:T(8,128)(2,1)S(1)}, bf16[2,4,2,128,128]{4,3,2,0,1:T(8,128)(2,1)S(1)}, u32[]{:S(2)}, u32[]{:S(2)}) %collective-permute-start.16) | collective-permute-done | bytes 524320 | tf_op jit(solution)/shard_map/ppermute | solution.py:78
  237.8 6.6 %collective-permute-done.12 = bf16[2,4,2,128,128]{4,3,2,0,1:T(8,128)(2,1)S(1)} collective-permute-done((bf16[2,4,2,128,128]{4,3,2,0,1:T(8,128)(2,1)S(1)}, bf16[2,4,2,128,128]{4,3,2,0,1:T(8,128)(2,1)S(1)}, u32[]{:S(2)}, u32[]{:S(2)}) %collective-permute-start.12) | collective-permute-done | bytes 524320 | tf_op jit(solution)/shard_map/ppermute | solution.py:78
  246.7 5.1 %collective-permute-start.17 = (bf16[2,4,2,128,128]{4,3,2,0,1:T(8,128)(2,1)S(1)}, bf16[2,4,2,128,128]{4,3,2,0,1:T(8,128)(2,1)S(1)}, u32[]{:S(2)}, u32[]{:S(2)}) collective-permute-start(bf16[2,4,2,128,128]{4,3,2,0,1:T(8,128)(2,1)S(1)} %get-tuple-element.37), channel_id=1, source_target_pairs={{0,28},{1,29},{2,30},{3,31},{4,0},{5,1},{6,2},{7,3},{8,4},{9,5},{1... | collective-permute-start | bytes 1572872 | tf_op jit(solution)/shard_map/ppermute | solution.py:78
  251.9 8.5 %collective-permute-done.13 = bf16[2,4,2,128,128]{4,3,2,0,1:T(8,128)(2,1)S(1)} collective-permute-done((bf16[2,4,2,128,128]{4,3,2,0,1:T(8,128)(2,1)S(1)}, bf16[2,4,2,128,128]{4,3,2,0,1:T(8,128)(2,1)S(1)}, u32[]{:S(2)}, u32[]{:S(2)}) %collective-permute-start.13) | collective-permute-done | bytes 524320 | tf_op jit(solution)/shard_map/ppermute | solution.py:78
  263.9 5.5 %collective-permute-start.18 = (bf16[2,4,2,128,128]{4,3,2,0,1:T(8,128)(2,1)S(1)}, bf16[2,4,2,128,128]{4,3,2,0,1:T(8,128)(2,1)S(1)}, u32[]{:S(2)}, u32[]{:S(2)}) collective-permute-start(bf16[2,4,2,128,128]{4,3,2,0,1:T(8,128)(2,1)S(1)} %get-tuple-element.35), channel_id=1, source_target_pairs={{0,28},{1,29},{2,30},{3,31},{4,0},{5,1},{6,2},{7,3},{8,4},{9,5},{1... | collective-permute-start | bytes 1572872 | tf_op jit(solution)/shard_map/ppermute | solution.py:78
  269.5 7.5 %collective-permute-done.14 = bf16[2,4,2,128,128]{4,3,2,0,1:T(8,128)(2,1)S(1)} collective-permute-done((bf16[2,4,2,128,128]{4,3,2,0,1:T(8,128)(2,1)S(1)}, bf16[2,4,2,128,128]{4,3,2,0,1:T(8,128)(2,1)S(1)}, u32[]{:S(2)}, u32[]{:S(2)}) %collective-permute-start.14) | collective-permute-done | bytes 524320 | tf_op jit(solution)/shard_map/ppermute | solution.py:78
  281.3 7.1 %collective-permute-start.20 = (bf16[2,2,128,128]{3,2,1,0:T(8,128)(2,1)S(1)}, bf16[2,2,128,128]{3,2,1,0:T(8,128)(2,1)S(1)}, u32[]{:S(2)}, u32[]{:S(2)}) collective-permute-start(bf16[2,2,128,128]{3,2,1,0:T(8,128)(2,1)S(1)} %get-tuple-element.49), channel_id=1, source_target_pairs={{0,2},{1,3},{2,0},{3,1},{4,6},{5,7},{6,4},{7,5},{8,10},{9,11},{10,... | collective-permute-start | bytes 393224 | tf_op jit(solution)/shard_map/ppermute | solution.py:108
  288.5 2.5 collective-permute-start.21
  291.0 2.6 collective-permute-done.20
  293.6 5.9 %collective-permute-done.21 = bf16[2,2,128,128]{3,2,1,0:T(8,128)(2,1)S(1)} collective-permute-done((bf16[2,2,128,128]{3,2,1,0:T(8,128)(2,1)S(1)}, bf16[2,2,128,128]{3,2,1,0:T(8,128)(2,1)S(1)}, u32[]{:S(2)}, u32[]{:S(2)}) %collective-permute-start.21) | collective-permute-done | bytes 131104 | tf_op jit(solution)/shard_map/ppermute | solution.py:108
  300.3 3.0 copy.83
  304.5 2.3 copy.88
  (114 shorter events, 58.3 us)
Async XLA Ops:
  0.6 78.3 %copy-start = (s32[64]{0:T(128)S(1)}, s32[64]{0:T(128)}, u32[]{:S(2)}) copy-start(s32[64]{0:T(128)} %param.13) | copy-start | bytes 772
  3.5 9.5 %copy-start.14 = (bf16[2,128,128]{2,1,0:T(8,128)(2,1)S(1)}, bf16[2,128,128]{2,1,0:T(8,128)(2,1)}, u32[]{:S(2)}) copy-start(bf16[2,128,128]{2,1,0:T(8,128)(2,1)} %param.14) | copy-start | bytes 196612
  3.5 9.5 %copy-start.15 = (bf16[2,128,128]{2,1,0:T(8,128)(2,1)S(1)}, bf16[2,128,128]{2,1,0:T(8,128)(2,1)}, u32[]{:S(2)}) copy-start(bf16[2,128,128]{2,1,0:T(8,128)(2,1)} %param.12) | copy-start | bytes 196612
  3.5 77.5 %copy-start.2 = (s32[64]{0:T(128)S(1)}, s32[64]{0:T(128)}, u32[]{:S(2)}) copy-start(s32[64]{0:T(128)} %param.15) | copy-start | bytes 772
  3.5 120.0 %all-to-all-start = ((bf16[16,2,128,256]{2,3,1,0:T(8,128)(2,1)}), bf16[16,2,128,256]{2,3,1,0:T(8,128)(2,1)S(1)}, u32[]{:S(2)}, u32[]{:S(2)}) async-start(bf16[16,2,128,256]{2,3,1,0:T(8,128)(2,1)} %broadcast_in_dim.4), calls=%async_computation | async-start | bytes 4194304 | tf_op jit(solution)/shard_map/all_to_all | solution.py:22
  13.1 35.5 %collective-permute-start = (bf16[2,2,128,128]{3,2,1,0:T(8,128)(2,1)S(1)}, bf16[2,2,128,128]{3,2,1,0:T(8,128)(2,1)S(1)}, u32[]{:S(2)}, u32[]{:S(2)}) collective-permute-start(bf16[2,2,128,128]{3,2,1,0:T(8,128)(2,1)S(1)} %get-tuple-element.55), channel_id=1, source_target_pairs={{0,1},{1,2},{2,3},{3,0},{4,5},{5,6},{6,7},{7,4},{8,9},{9,10},{10,1... | collective-permute-start | bytes 393224 | tf_op jit(solution)/shard_map/ppermute | solution.py:42
  16.4 37.4 %collective-permute-start.1 = (bf16[2,2,128,128]{3,2,1,0:T(8,128)(2,1)S(1)}, bf16[2,2,128,128]{3,2,1,0:T(8,128)(2,1)S(1)}, u32[]{:S(2)}, u32[]{:S(2)}) collective-permute-start(bf16[2,2,128,128]{3,2,1,0:T(8,128)(2,1)S(1)} %get-tuple-element.55), channel_id=1, source_target_pairs={{0,2},{1,3},{2,0},{3,1},{4,6},{5,7},{6,4},{7,5},{8,10},{9,11},{10,... | collective-permute-start | bytes 393224 | tf_op jit(solution)/shard_map/ppermute | solution.py:42
  24.6 29.1 %collective-permute-start.2 = (bf16[2,2,128,128]{3,2,1,0:T(8,128)(2,1)S(1)}, bf16[2,2,128,128]{3,2,1,0:T(8,128)(2,1)S(1)}, u32[]{:S(2)}, u32[]{:S(2)}) collective-permute-start(bf16[2,2,128,128]{3,2,1,0:T(8,128)(2,1)S(1)} %get-tuple-element.55), channel_id=1, source_target_pairs={{0,3},{1,0},{2,1},{3,2},{4,7},{5,4},{6,5},{7,6},{8,11},{9,8},{10,9... | collective-permute-start | bytes 393224 | tf_op jit(solution)/shard_map/ppermute | solution.py:42
  53.7 0.9 copy-start.13
  54.6 17.2 %collective-permute-start.3 = (bf16[4,2,2,128,128]{4,3,2,1,0:T(8,128)(2,1)}, bf16[4,2,2,128,128]{4,3,2,1,0:T(8,128)(2,1)S(1)}, u32[]{:S(2)}, u32[]{:S(2)}) collective-permute-start(bf16[4,2,2,128,128]{4,3,2,1,0:T(8,128)(2,1)} %pad_maximum_fusion.1), channel_id=1, source_target_pairs={{0,4},{1,5},{2,6},{3,7},{4,8},{5,9},{6,10},{7,11},{8,12},{9,13},{1... | collective-permute-start | bytes 1572872 | tf_op jit(solution)/shard_map/ppermute | solution.py:53
  58.1 15.7 %collective-permute-start.7 = (bf16[4,2,2,128,128]{4,3,2,1,0:T(8,128)(2,1)}, bf16[4,2,2,128,128]{4,3,2,1,0:T(8,128)(2,1)S(1)}, u32[]{:S(2)}, u32[]{:S(2)}) collective-permute-start(bf16[4,2,2,128,128]{4,3,2,1,0:T(8,128)(2,1)} %pad_maximum_fusion.1), channel_id=1, source_target_pairs={{0,28},{1,29},{2,30},{3,31},{4,0},{5,1},{6,2},{7,3},{8,4},{9,5},{1... | collective-permute-start | bytes 1572872 | tf_op jit(solution)/shard_map/ppermute | solution.py:60
  71.8 10.5 %copy-start.12 = (bf16[4,2,2,128,128]{4,3,2,1,0:T(8,128)(2,1)}, bf16[4,2,2,128,128]{4,3,2,1,0:T(8,128)(2,1)S(1)}, u32[]{:S(2)}) copy-start(bf16[4,2,2,128,128]{4,3,2,1,0:T(8,128)(2,1)S(1)} %collective-permute-done.3) | copy-start | bytes 1572868
  71.8 16.1 %collective-permute-start.4 = (bf16[4,2,2,128,128]{4,3,2,1,0:T(8,128)(2,1)S(1)}, bf16[4,2,2,128,128]{4,3,2,1,0:T(8,128)(2,1)}, u32[]{:S(2)}, u32[]{:S(2)}) collective-permute-start(bf16[4,2,2,128,128]{4,3,2,1,0:T(8,128)(2,1)S(1)} %collective-permute-done.3), channel_id=1, source_target_pairs={{0,4},{1,5},{2,6},{3,7},{4,8},{5,9},{6,10},{7,11},{8,12},{9,13},{1... | collective-permute-start | bytes 1572872 | tf_op jit(solution)/shard_map/ppermute | solution.py:53
  73.8 16.1 %copy-start.10 = (bf16[4,2,2,128,128]{4,3,2,1,0:T(8,128)(2,1)}, bf16[4,2,2,128,128]{4,3,2,1,0:T(8,128)(2,1)S(1)}, u32[]{:S(2)}) copy-start(bf16[4,2,2,128,128]{4,3,2,1,0:T(8,128)(2,1)S(1)} %collective-permute-done.7) | copy-start | bytes 1572868
  73.8 16.1 %collective-permute-start.8 = (bf16[4,2,2,128,128]{4,3,2,1,0:T(8,128)(2,1)S(1)}, bf16[4,2,2,128,128]{4,3,2,1,0:T(8,128)(2,1)}, u32[]{:S(2)}, u32[]{:S(2)}) collective-permute-start(bf16[4,2,2,128,128]{4,3,2,1,0:T(8,128)(2,1)S(1)} %collective-permute-done.7), channel_id=1, source_target_pairs={{0,28},{1,29},{2,30},{3,31},{4,0},{5,1},{6,2},{7,3},{8,4},{9,5},{1... | collective-permute-start | bytes 1572872 | tf_op jit(solution)/shard_map/ppermute | solution.py:60
  81.8 0.5 copy-start.17
  87.9 22.1 %collective-permute-start.5 = (bf16[4,2,2,128,128]{4,3,2,1,0:T(8,128)(2,1)}, bf16[4,2,2,128,128]{4,3,2,1,0:T(8,128)(2,1)S(1)}, u32[]{:S(2)}, u32[]{:S(2)}) collective-permute-start(bf16[4,2,2,128,128]{4,3,2,1,0:T(8,128)(2,1)} %collective-permute-done.4), channel_id=1, source_target_pairs={{0,4},{1,5},{2,6},{3,7},{4,8},{5,9},{6,10},{7,11},{8,12},{9,13},{1... | collective-permute-start | bytes 1572872 | tf_op jit(solution)/shard_map/ppermute | solution.py:53
  89.8 14.6 %collective-permute-start.9 = (bf16[4,2,2,128,128]{4,3,2,1,0:T(8,128)(2,1)}, bf16[4,2,2,128,128]{4,3,2,1,0:T(8,128)(2,1)S(1)}, u32[]{:S(2)}, u32[]{:S(2)}) collective-permute-start(bf16[4,2,2,128,128]{4,3,2,1,0:T(8,128)(2,1)} %collective-permute-done.8), channel_id=1, source_target_pairs={{0,28},{1,29},{2,30},{3,31},{4,0},{5,1},{6,2},{7,3},{8,4},{9,5},{1... | collective-permute-start | bytes 1572872 | tf_op jit(solution)/shard_map/ppermute | solution.py:60
  104.5 9.4 %collective-permute-start.10 = (bf16[2,2,2,128,128]{4,3,2,1,0:T(8,128)(2,1)S(1)}, bf16[2,2,2,128,128]{4,3,2,1,0:T(8,128)(2,1)S(1)}, u32[]{:S(2)}, u32[]{:S(2)}) collective-permute-start(bf16[2,2,2,128,128]{4,3,2,1,0:T(8,128)(2,1)S(1)} %slice.187), channel_id=1, source_target_pairs={{0,28},{1,29},{2,30},{3,31},{4,0},{5,1},{6,2},{7,3},{8,4},{9,5},{1... | collective-permute-start | bytes 786440 | tf_op jit(solution)/shard_map/ppermute | solution.py:58
  110.0 9.5 %collective-permute-start.6 = (bf16[2,2,2,128,128]{4,3,2,1,0:T(8,128)(2,1)S(1)}, bf16[2,2,2,128,128]{4,3,2,1,0:T(8,128)(2,1)S(1)}, u32[]{:S(2)}, u32[]{:S(2)}) collective-permute-start(bf16[2,2,2,128,128]{4,3,2,1,0:T(8,128)(2,1)S(1)} %slice.186), channel_id=1, source_target_pairs={{0,4},{1,5},{2,6},{3,7},{4,8},{5,9},{6,10},{7,11},{8,12},{9,13},{1... | collective-permute-start | bytes 786440 | tf_op jit(solution)/shard_map/ppermute | solution.py:51
  113.3 7.5 %copy-start.11 = (bf16[4,2,2,128,128]{4,3,2,1,0:T(8,128)(2,1)S(1)}, bf16[4,2,2,128,128]{4,3,2,1,0:T(8,128)(2,1)}, u32[]{:S(2)}) copy-start(bf16[4,2,2,128,128]{4,3,2,1,0:T(8,128)(2,1)} %copy-done.10) | copy-start | bytes 1572868
  133.3 4.6 %copy-start.6 = (bf16[64,128,128]{2,1,0:T(8,128)(2,1)S(1)}, bf16[64,128,128]{2,1,0:T(8,128)(2,1)}, u32[]{:S(2)}) copy-start(bf16[64,128,128]{2,1,0:T(8,128)(2,1)} %gather_fusion.3) | copy-start | bytes 6291460
  133.3 4.6 %copy-start.7 = (bf16[1,8,4,2,128,128]{5,4,3,0,2,1:T(8,128)(2,1)S(1)}, bf16[1,8,4,2,128,128]{5,4,3,0,2,1:T(8,128)(2,1)}, u32[]{:S(2)}) copy-start(bf16[1,8,4,2,128,128]{5,4,3,0,2,1:T(8,128)(2,1)} %get-tuple-element.41) | copy-start | bytes 6291460
  133.3 4.6 %copy-start.8 = (f32[128,8,128]{0,2,1:T(8,128)S(1)}, f32[128,8,128]{0,2,1:T(8,128)}, u32[]{:S(2)}) copy-start(f32[128,8,128]{0,2,1:T(8,128)} %convolution_bitcast_fusion.1) | copy-start | bytes 1572868
  138.6 5.4 %copy-start.18 = (s32[64]{0:T(128)S(1)}, s32[64]{0:T(128)}, u32[]{:S(2)}) copy-start(s32[64]{0:T(128)} %copy-done.17) | copy-start | bytes 772
  151.1 2.7 copy-start.5
  156.4 5.4 %copy-start.16 = (s32[64]{0:T(128)S(1)}, s32[64]{0:T(128)}, u32[]{:S(2)}) copy-start(s32[64]{0:T(128)} %gather_fusion.1) | copy-start | bytes 772
  168.8 1.7 copy-start.9
  172.0 36.1 %all-to-all-start.1 = ((bf16[16,2,128,256]{3,2,1,0:T(8,128)(2,1)}), bf16[16,2,128,256]{3,2,1,0:T(8,128)(2,1)}, u32[]{:S(2)}, u32[]{:S(2)}) async-start(bf16[16,2,128,256]{3,2,1,0:T(8,128)(2,1)} %maximum_bitcast_fusion), calls=%async_computation.1 | async-start | bytes 4194304 | tf_op jit(solution)/shard_map/all_to_all | solution.py:26
  192.0 1.7 copy-start.3
  194.6 23.5 %collective-permute-start.15 = (bf16[2,2,2,128,128]{4,3,2,0,1:T(8,128)(2,1)}, bf16[2,2,2,128,128]{4,3,2,0,1:T(8,128)(2,1)S(1)}, u32[]{:S(2)}, u32[]{:S(2)}) collective-permute-start(bf16[2,2,2,128,128]{4,3,2,0,1:T(8,128)(2,1)} %get-tuple-element.51), channel_id=1, source_target_pairs={{0,28},{1,29},{2,30},{3,31},{4,0},{5,1},{6,2},{7,3},{8,4},{9,5},{1... | collective-permute-start | bytes 786440 | tf_op jit(solution)/shard_map/ppermute | solution.py:78
  211.6 88.7 %all-to-all-start.2 = ((bf16[16,2,128,256]{3,2,1,0:T(8,128)(2,1)}), bf16[16,2,128,256]{3,2,1,0:T(8,128)(2,1)}, u32[]{:S(2)}, u32[]{:S(2)}) async-start(bf16[16,2,128,256]{3,2,1,0:T(8,128)(2,1)} %broadcast_in_dim.5), calls=%async_computation.2 | async-start | bytes 4194304 | tf_op jit(solution)/shard_map/all_to_all | solution.py:22
  216.1 11.7 %collective-permute-start.11 = (bf16[2,2,2,128,128]{4,3,2,0,1:T(8,128)(2,1)}, bf16[2,2,2,128,128]{4,3,2,0,1:T(8,128)(2,1)S(1)}, u32[]{:S(2)}, u32[]{:S(2)}) collective-permute-start(bf16[2,2,2,128,128]{4,3,2,0,1:T(8,128)(2,1)} %get-tuple-element.50), channel_id=1, source_target_pairs={{0,4},{1,5},{2,6},{3,7},{4,8},{5,9},{6,10},{7,11},{8,12},{9,13},{1... | collective-permute-start | bytes 786440 | tf_op jit(solution)/shard_map/ppermute | solution.py:78
  220.0 24.4 %copy-start.4 = (bf16[8,8,128,128]{3,2,1,0:T(8,128)(2,1)S(1)}, bf16[8,8,128,128]{3,2,1,0:T(8,128)(2,1)}, u32[]{:S(2)}) copy-start(bf16[8,8,128,128]{3,2,1,0:T(8,128)(2,1)} %copy-done.3) | copy-start | bytes 6291460
  221.4 16.3 %collective-permute-start.16 = (bf16[2,4,2,128,128]{4,3,2,0,1:T(8,128)(2,1)S(1)}, bf16[2,4,2,128,128]{4,3,2,0,1:T(8,128)(2,1)S(1)}, u32[]{:S(2)}, u32[]{:S(2)}) collective-permute-start(bf16[2,4,2,128,128]{4,3,2,0,1:T(8,128)(2,1)S(1)} %convert_element_type.154), channel_id=1, source_target_pairs={{0,28},{1,29},{2,30},{3,31},{4,0},{5,1},{6,2},{7,3},{8,4},{9,5},{1... | collective-permute-start | bytes 1572872 | tf_op jit(solution)/shard_map/ppermute | solution.py:78
  228.0 16.4 %collective-permute-start.12 = (bf16[2,4,2,128,128]{4,3,2,0,1:T(8,128)(2,1)S(1)}, bf16[2,4,2,128,128]{4,3,2,0,1:T(8,128)(2,1)S(1)}, u32[]{:S(2)}, u32[]{:S(2)}) collective-permute-start(bf16[2,4,2,128,128]{4,3,2,0,1:T(8,128)(2,1)S(1)} %convert_element_type.141), channel_id=1, source_target_pairs={{0,4},{1,5},{2,6},{3,7},{4,8},{5,9},{6,10},{7,11},{8,12},{9,13},{1... | collective-permute-start | bytes 1572872 | tf_op jit(solution)/shard_map/ppermute | solution.py:78
  244.8 15.5 %collective-permute-start.13 = (bf16[2,4,2,128,128]{4,3,2,0,1:T(8,128)(2,1)S(1)}, bf16[2,4,2,128,128]{4,3,2,0,1:T(8,128)(2,1)S(1)}, u32[]{:S(2)}, u32[]{:S(2)}) collective-permute-start(bf16[2,4,2,128,128]{4,3,2,0,1:T(8,128)(2,1)S(1)} %get-tuple-element.36), channel_id=1, source_target_pairs={{0,4},{1,5},{2,6},{3,7},{4,8},{5,9},{6,10},{7,11},{8,12},{9,13},{1... | collective-permute-start | bytes 1572872 | tf_op jit(solution)/shard_map/ppermute | solution.py:78
  246.7 14.8 %collective-permute-start.17 = (bf16[2,4,2,128,128]{4,3,2,0,1:T(8,128)(2,1)S(1)}, bf16[2,4,2,128,128]{4,3,2,0,1:T(8,128)(2,1)S(1)}, u32[]{:S(2)}, u32[]{:S(2)}) collective-permute-start(bf16[2,4,2,128,128]{4,3,2,0,1:T(8,128)(2,1)S(1)} %get-tuple-element.37), channel_id=1, source_target_pairs={{0,28},{1,29},{2,30},{3,31},{4,0},{5,1},{6,2},{7,3},{8,4},{9,5},{1... | collective-permute-start | bytes 1572872 | tf_op jit(solution)/shard_map/ppermute | solution.py:78
  262.0 15.1 %collective-permute-start.14 = (bf16[2,4,2,128,128]{4,3,2,0,1:T(8,128)(2,1)S(1)}, bf16[2,4,2,128,128]{4,3,2,0,1:T(8,128)(2,1)S(1)}, u32[]{:S(2)}, u32[]{:S(2)}) collective-permute-start(bf16[2,4,2,128,128]{4,3,2,0,1:T(8,128)(2,1)S(1)} %get-tuple-element.34), channel_id=1, source_target_pairs={{0,4},{1,5},{2,6},{3,7},{4,8},{5,9},{6,10},{7,11},{8,12},{9,13},{1... | collective-permute-start | bytes 1572872 | tf_op jit(solution)/shard_map/ppermute | solution.py:78
  263.9 15.2 %collective-permute-start.18 = (bf16[2,4,2,128,128]{4,3,2,0,1:T(8,128)(2,1)S(1)}, bf16[2,4,2,128,128]{4,3,2,0,1:T(8,128)(2,1)S(1)}, u32[]{:S(2)}, u32[]{:S(2)}) collective-permute-start(bf16[2,4,2,128,128]{4,3,2,0,1:T(8,128)(2,1)S(1)} %get-tuple-element.35), channel_id=1, source_target_pairs={{0,28},{1,29},{2,30},{3,31},{4,0},{5,1},{6,2},{7,3},{8,4},{9,5},{1... | collective-permute-start | bytes 1572872 | tf_op jit(solution)/shard_map/ppermute | solution.py:78
  279.4 11.6 %collective-permute-start.19 = (bf16[2,2,128,128]{3,2,1,0:T(8,128)(2,1)S(1)}, bf16[2,2,128,128]{3,2,1,0:T(8,128)(2,1)S(1)}, u32[]{:S(2)}, u32[]{:S(2)}) collective-permute-start(bf16[2,2,128,128]{3,2,1,0:T(8,128)(2,1)S(1)} %get-tuple-element.47), channel_id=1, source_target_pairs={{0,3},{1,0},{2,1},{3,2},{4,7},{5,4},{6,5},{7,6},{8,11},{9,8},{10,9... | collective-permute-start | bytes 393224 | tf_op jit(solution)/shard_map/ppermute | solution.py:108
  281.3 12.3 %collective-permute-start.20 = (bf16[2,2,128,128]{3,2,1,0:T(8,128)(2,1)S(1)}, bf16[2,2,128,128]{3,2,1,0:T(8,128)(2,1)S(1)}, u32[]{:S(2)}, u32[]{:S(2)}) collective-permute-start(bf16[2,2,128,128]{3,2,1,0:T(8,128)(2,1)S(1)} %get-tuple-element.49), channel_id=1, source_target_pairs={{0,2},{1,3},{2,0},{3,1},{4,6},{5,7},{6,4},{7,5},{8,10},{9,11},{10,... | collective-permute-start | bytes 393224 | tf_op jit(solution)/shard_map/ppermute | solution.py:108
  288.5 11.1 %collective-permute-start.21 = (bf16[2,2,128,128]{3,2,1,0:T(8,128)(2,1)S(1)}, bf16[2,2,128,128]{3,2,1,0:T(8,128)(2,1)S(1)}, u32[]{:S(2)}, u32[]{:S(2)}) collective-permute-start(bf16[2,2,128,128]{3,2,1,0:T(8,128)(2,1)S(1)} %get-tuple-element.48), channel_id=1, source_target_pairs={{0,1},{1,2},{2,3},{3,0},{4,5},{5,6},{6,7},{7,4},{8,9},{9,10},{10,1... | collective-permute-start | bytes 393224 | tf_op jit(solution)/shard_map/ppermute | solution.py:108
  304.5 3.6 %copy-start.1 = (s32[64]{0:T(128)S(1)}, s32[64]{0:T(128)}, u32[]{:S(2)}) copy-start(s32[64]{0:T(128)} %param.13) | copy-start | bytes 772

commit v7 on v5

--- a/solution.py
+++ b/solution.py
@@ -117,13 +117,12 @@
     picked_in = full_input.reshape(tokens, row_blocks, block_size)[:, up_index]
     preact = jnp.einsum("tgki,gkio->tgo", picked_in, up_tiles, preferred_element_type=jnp.float32)
     hidden = (preact * normal_cdf(preact)).astype(jnp.bfloat16)
-    product = jnp.einsum("tgh,gkho->tgko", hidden, down_tiles, preferred_element_type=jnp.float32)
+    product = jnp.einsum("gkho,tgh->gkot", down_tiles, hidden, preferred_element_type=jnp.float32)
     span = jnp.arange(row_blocks, dtype=jnp.int32)
     highest = lax.Precision.HIGHEST
-    down_hot = (down_rows[:, None] == span).astype(jnp.float32)
-    out_part = jnp.einsum(
-        "tbo,br->tro", product.reshape(tokens, groups * K, block_size), down_hot,
-        precision=highest, preferred_element_type=jnp.float32,
+    down_hot = (down_index[..., None] == span).astype(jnp.float32)
+    out_t = jnp.einsum(
+        "gkr,gkot->rot", down_hot, product, precision=highest, preferred_element_type=jnp.float32
     )
     picked_grad = full_grad.reshape(tokens, row_blocks, block_size)[:, down_index]
     down_term = (
@@ -134,20 +133,20 @@
         "tgko,gkho->tgh", picked_grad, down_tiles, preferred_element_type=jnp.float32
     )
     preact_grad = (hidden_grad * gelu_slope(preact)).astype(jnp.bfloat16)
-    back = jnp.einsum("tgo,gkio->tgki", preact_grad, up_tiles, preferred_element_type=jnp.float32)
-    up_hot = (up_rows[:, None] == span).astype(jnp.float32)
-    in_part = jnp.einsum(
-        "tbi,br->tri", back.reshape(tokens, groups * K, block_size), up_hot,
-        precision=highest, preferred_element_type=jnp.float32,
+    back = jnp.einsum("gkio,tgo->gkit", up_tiles, preact_grad, preferred_element_type=jnp.float32)
+    up_hot = (up_index[..., None] == span).astype(jnp.float32)
+    in_t = jnp.einsum(
+        "gkr,gkit->rit", up_hot, back, precision=highest, preferred_element_type=jnp.float32
     )
     up_term = (
         jnp.einsum("tgki,tgo->gkio", picked_in, preact_grad, preferred_element_type=jnp.float32)
         * scale
     )
 
-    parts = jnp.stack([out_part, in_part]).astype(jnp.bfloat16)
-    parts = parts.reshape(2, tokens, n_tensor, shard_width)
-    mine = scatter_sum(jnp.moveaxis(parts, 2, 0), "tensor")
+    parts = jnp.stack([out_t, in_t]).astype(jnp.bfloat16)
+    parts = parts.reshape(2, n_tensor, shard_width // block_size, block_size, tokens)
+    parts = jnp.transpose(parts, (1, 0, 4, 2, 3)).reshape(n_tensor, 2, tokens, shard_width)
+    mine = scatter_sum(parts, "tensor")
     both = gather_all(mine, "tensor")
     both = jnp.moveaxis(both, 0, 2).reshape(2, tokens, width)
 

time: 285 us -> 274 us (0.961)
  matrix products: 23.5 us -> 13.5 us
  waiting for transfers between devices: 89.2 us -> 94.5 us
  local copies, waits for them, and re-layouts: 59.8 us -> 55.1 us
    dot_general x4, matrix products: 16.8 us -> 4.74 us  [the longest x1 1.67 us: per_device(): jnp.einsum('gkr,gkot->rot', down_hot, product, precision=highest, preferr...]
    reshape x2 -> x0, local copies, waits for them, and re-layouts: 10.9 us -> none  [the longest x1 5.44 us: per_device(): back.reshape(tokens, groups * K, block_size)]
    slice x1 -> x3, local copies, waits for them, and re-layouts: 2.57 us -> 10.9 us  [per_device(): up_all, down_all = (weights[0], weights[1])]
    ppermute x4, waiting for transfers between devices: 30.4 us -> 36.2 us  [dp_gather_rel(): cur_f = lax.ppermute(cur_f, 'dp', dp_shift(n_y, n_z, 1, 0))]
    another operation x4 -> x3, local copies, waits for them, and re-layouts: 8.71 us -> 4.99 us  [the longest x1 4.17 us: per_device(): up_tiles = up_all.reshape(groups, K, block_size, block_size)]
    gather x2 -> x3, local copies, waits for them, and re-layouts: 5.16 us -> 7.72 us  [per_device(): full_grad.reshape(tokens, row_blocks, block_size)[:, down_index]]
    unnamed x38 -> x28, local copies, waits for them, and re-layouts: 7.16 us -> 5.99 us
  transfers between devices with their start and end apart: 23 -> 23, of which waited for: 15 -> 16; matrix products, arithmetic and copies ran while one was open for 14% -> 17% of each run, Pallas kernels for 0% -> 0%
where the time goes in v7:
time: 274 us; the launch traced here: 270 us
  waiting for transfers between devices  94.5 us (34%)
  starting transfers between devices  94.1 us (34%)
  local copies, waits for them, and re-layouts  55.1 us (20%)
  matrix products  13.5 us (5%)
  other arithmetic  11.4 us (4%)
    ppermute x4, waiting for transfers between devices, dp_gather_rel(): cur_f = lax.ppermute(cur_f, 'dp', dp_shift(n_y, n_z, 1, 0))  36.2 us
    ppermute x3, waiting for transfers between devices, dp_scatter_rel(): lax.ppermute(part.astype(jnp.bfloat16), 'dp', dp_shift(n_y, n_z, -1, 0))  27.4 us
    ppermute x4, waiting for transfers between devices, dp_scatter_rel(): lax.ppermute(part.astype(jnp.bfloat16), 'dp', dp_shift(n_y, n_z, 1, 0))  21.5 us
    ppermute x3, starting transfers between devices, dp_gather_rel(): lax.ppermute(x, 'dp', dp_shift(n_y, n_z, 0, b))  18.9 us
    ppermute x3, starting transfers between devices, dp_gather_rel(): cur_b = lax.ppermute(cur_b, 'dp', dp_shift(n_y, n_z, -1, 0))  16 us
    ppermute x3, starting transfers between devices, dp_scatter_rel(): lax.ppermute(acc[b].astype(jnp.bfloat16), 'dp', dp_shift(n_y, n_z, 0, -b))  11.7 us
    all_to_all x2, starting transfers between devices, gather_all(): return lax.all_to_all(spread, axis_name, 0, 0, tiled=True)  11.6 us
    slice x3, local copies, waits for them, and re-layouts, per_device(): up_all, down_all = (weights[0], weights[1])  10.9 us
  transfers between devices with their start and end apart: 23, of which 16 were waited for; matrix products, arithmetic and copies ran while one was open for 17% of the time, Pallas kernels for 0%

profile of v7, /device:TPU:6, one launch (start us, length us, event | category | flops | bytes accessed | tf_op | source)
XLA Modules:
  0.0 270.0 jit_solution(17780438193729533824)
XLA Ops:
  1.5 6.1 %collective-permute-start = (bf16[2,2,128,128]{3,2,1,0:T(8,128)(2,1)S(1)}, bf16[2,2,128,128]{3,2,1,0:T(8,128)(2,1)S(1)}, u32[]{:S(2)}, u32[]{:S(2)}) collective-permute-start(bf16[2,2,128,128]{3,2,1,0:T(8,128)(2,1)S(1)} %get-tuple-element.26), channel_id=1, source_target_pairs={{0,1},{1,2},{2,3},{3,0},{4,5},{5,6},{6,7},{7,4},{8,9},{9,10},{10,1... | collective-permute-start | bytes 393224 | tf_op jit(solution)/shard_map/ppermute | solution.py:42
  7.6 9.1 %collective-permute-start.1 = (bf16[2,2,128,128]{3,2,1,0:T(8,128)(2,1)S(1)}, bf16[2,2,128,128]{3,2,1,0:T(8,128)(2,1)S(1)}, u32[]{:S(2)}, u32[]{:S(2)}) collective-permute-start(bf16[2,2,128,128]{3,2,1,0:T(8,128)(2,1)S(1)} %get-tuple-element.26), channel_id=1, source_target_pairs={{0,2},{1,3},{2,0},{3,1},{4,6},{5,7},{6,4},{7,5},{8,10},{9,11},{10,... | collective-permute-start | bytes 393224 | tf_op jit(solution)/shard_map/ppermute | solution.py:42
  16.8 3.7 %collective-permute-start.2 = (bf16[2,2,128,128]{3,2,1,0:T(8,128)(2,1)S(1)}, bf16[2,2,128,128]{3,2,1,0:T(8,128)(2,1)S(1)}, u32[]{:S(2)}, u32[]{:S(2)}) collective-permute-start(bf16[2,2,128,128]{3,2,1,0:T(8,128)(2,1)S(1)} %get-tuple-element.26), channel_id=1, source_target_pairs={{0,3},{1,0},{2,1},{3,2},{4,7},{5,4},{6,5},{7,6},{8,11},{9,8},{10,9... | collective-permute-start | bytes 393224 | tf_op jit(solution)/shard_map/ppermute | solution.py:42
  23.3 5.8 %all-to-all-start = ((bf16[16,2,128,256]{2,3,1,0:T(8,128)(2,1)}), bf16[16,2,128,256]{2,3,1,0:T(8,128)(2,1)}, u32[]{:S(2)}, u32[]{:S(2)}) async-start(bf16[16,2,128,256]{2,3,1,0:T(8,128)(2,1)} %broadcast_in_dim.4), calls=%async_computation | async-start | bytes 4194304 | tf_op jit(solution)/shard_map/all_to_all | solution.py:22
  29.4 3.5 %collective-permute-start.3 = (bf16[4,2,2,128,128]{4,3,2,1,0:T(8,128)(2,1)S(1)}, bf16[4,2,2,128,128]{4,3,2,1,0:T(8,128)(2,1)S(1)}, u32[]{:S(2)}, u32[]{:S(2)}) collective-permute-start(bf16[4,2,2,128,128]{4,3,2,1,0:T(8,128)(2,1)S(1)} %pad_maximum_fusion.1), channel_id=1, source_target_pairs={{0,4},{1,5},{2,6},{3,7},{4,8},{5,9},{6,10},{7,11},{8,12},{9,13},{1... | collective-permute-start | bytes 1572872 | tf_op jit(solution)/shard_map/ppermute | solution.py:48
  33.0 13.9 %collective-permute-done.3 = bf16[4,2,2,128,128]{4,3,2,1,0:T(8,128)(2,1)S(1)} collective-permute-done((bf16[4,2,2,128,128]{4,3,2,1,0:T(8,128)(2,1)S(1)}, bf16[4,2,2,128,128]{4,3,2,1,0:T(8,128)(2,1)S(1)}, u32[]{:S(2)}, u32[]{:S(2)}) %collective-permute-start.3) | collective-permute-done | bytes 524320 | tf_op jit(solution)/shard_map/ppermute | solution.py:48
  46.9 1.9 collective-permute-start.4
  49.0 5.1 %collective-permute-start.7 = (bf16[4,2,2,128,128]{4,3,2,1,0:T(8,128)(2,1)S(1)}, bf16[4,2,2,128,128]{4,3,2,1,0:T(8,128)(2,1)S(1)}, u32[]{:S(2)}, u32[]{:S(2)}) collective-permute-start(bf16[4,2,2,128,128]{4,3,2,1,0:T(8,128)(2,1)S(1)} %pad_maximum_fusion.1), channel_id=1, source_target_pairs={{0,28},{1,29},{2,30},{3,31},{4,0},{5,1},{6,2},{7,3},{8,4},{9,5},{1... | collective-permute-start | bytes 1572872 | tf_op jit(solution)/shard_map/ppermute | solution.py:51
  55.0 8.4 %collective-permute-done.4 = bf16[4,2,2,128,128]{4,3,2,1,0:T(8,128)(2,1)S(1)} collective-permute-done((bf16[4,2,2,128,128]{4,3,2,1,0:T(8,128)(2,1)S(1)}, bf16[4,2,2,128,128]{4,3,2,1,0:T(8,128)(2,1)S(1)}, u32[]{:S(2)}, u32[]{:S(2)}) %collective-permute-start.4) | collective-permute-done | bytes 524320 | tf_op jit(solution)/shard_map/ppermute | solution.py:48
  63.4 1.9 collective-permute-start.5
  66.2 5.1 %collective-permute-start.8 = (bf16[4,2,2,128,128]{4,3,2,1,0:T(8,128)(2,1)S(1)}, bf16[4,2,2,128,128]{4,3,2,1,0:T(8,128)(2,1)S(1)}, u32[]{:S(2)}, u32[]{:S(2)}) collective-permute-start(bf16[4,2,2,128,128]{4,3,2,1,0:T(8,128)(2,1)S(1)} %collective-permute-done.7), channel_id=1, source_target_pairs={{0,28},{1,29},{2,30},{3,31},{4,0},{5,1},{6,2},{7,3},{8,4},{9,5},{1... | collective-permute-start | bytes 1572872 | tf_op jit(solution)/shard_map/ppermute | solution.py:51
  71.7 7.3 %collective-permute-done.5 = bf16[4,2,2,128,128]{4,3,2,1,0:T(8,128)(2,1)S(1)} collective-permute-done((bf16[4,2,2,128,128]{4,3,2,1,0:T(8,128)(2,1)S(1)}, bf16[4,2,2,128,128]{4,3,2,1,0:T(8,128)(2,1)S(1)}, u32[]{:S(2)}, u32[]{:S(2)}) %collective-permute-start.5) | collective-permute-done | bytes 524320 | tf_op jit(solution)/shard_map/ppermute | solution.py:48
  79.0 1.9 collective-permute-start.6
  81.1 5.8 %collective-permute-start.9 = (bf16[4,2,2,128,128]{4,3,2,1,0:T(8,128)(2,1)S(1)}, bf16[4,2,2,128,128]{4,3,2,1,0:T(8,128)(2,1)S(1)}, u32[]{:S(2)}, u32[]{:S(2)}) collective-permute-start(bf16[4,2,2,128,128]{4,3,2,1,0:T(8,128)(2,1)S(1)} %collective-permute-done.8), channel_id=1, source_target_pairs={{0,28},{1,29},{2,30},{3,31},{4,0},{5,1},{6,2},{7,3},{8,4},{9,5},{1... | collective-permute-start | bytes 1572872 | tf_op jit(solution)/shard_map/ppermute | solution.py:51
  87.0 6.7 %collective-permute-done.6 = bf16[4,2,2,128,128]{4,3,2,1,0:T(8,128)(2,1)S(1)} collective-permute-done((bf16[4,2,2,128,128]{4,3,2,1,0:T(8,128)(2,1)S(1)}, bf16[4,2,2,128,128]{4,3,2,1,0:T(8,128)(2,1)S(1)}, u32[]{:S(2)}, u32[]{:S(2)}) %collective-permute-start.6) | collective-permute-done | bytes 524320 | tf_op jit(solution)/shard_map/ppermute | solution.py:48
  97.6 6.4 %copy.52 = bf16[1,8,4,2,128,128]{4,3,2,1,5,0:T(2,128)(2,1)} copy(bf16[1,8,4,2,128,128]{5,4,3,0,2,1:T(8,128)(2,1)} %get-tuple-element.14) | data formatting | bytes 4194304 | tf_op jit(solution)/shard_map/slice | solution.py:102
  104.0 2.6 copy.53
  106.6 4.2 %copy.63 = bf16[8,8,128,128]{3,1,0,2:T(8,128)(2,1)} copy(bf16[8,8,128,128]{2,3,1,0:T(8,128)(2,1)} %bitcast.183) | data formatting | bytes 4194304 | tf_op jit(solution)/shard_map/reshape;squeeze | solution.py:113
  114.7 2.2 gather_fusion.3
  116.8 2.9 %copy.62 = bf16[128,8,8,128]{0,2,1,3:T(8,128)(2,1)} copy(bf16[128,8,8,128]{3,0,2,1:T(8,128)(2,1)S(1)} %bitcast.172) | data formatting | bytes 4194304 | tf_op jit(solution)/shard_map/gather | solution.py:127
  119.7 2.2 gather_fusion.2
  121.9 3.2 %convolution_bitcast_fusion = f32[128,8,128]{0,2,1:T(8,128)S(1)} fusion(bf16[8,8,128,128]{3,2,1,0:T(8,128)(2,1)} %bitcast.176, bf16[128,8,8,128]{3,0,2,1:T(8,128)(2,1)} %bitcast.174), kind=kOutput, calls=%fused_computation.13 | convolution fusion | flops 268435456 | bytes 4718592 | tf_op jit(solution)/shard_map/tgki,gkio->tgo/dot_general | solution.py:118
  135.6 5.9 %all-to-all-start.1 = ((bf16[16,2,128,256]{2,3,1,0:T(8,128)(2,1)}), bf16[16,2,128,256]{2,3,1,0:T(8,128)(2,1)}, u32[]{:S(2)}, u32[]{:S(2)}) async-start(bf16[16,2,128,256]{2,3,1,0:T(8,128)(2,1)} %bitcast.177), calls=%async_computation.1 | async-start | bytes 4194304 | tf_op jit(solution)/shard_map/all_to_all | solution.py:26
  141.5 3.9 %copy.57 = bf16[8,8,128,128]{2,3,1,0:T(8,128)(2,1)} copy(bf16[8,8,128,128]{3,2,1,0:T(8,128)(2,1)} %bitcast.175) | data formatting | bytes 4194304 | tf_op jit(solution)/shard_map/gather | solution.py:117
  145.4 2.6 copy.61
  148.0 3.6 %multiply_convert_fusion = bf16[8,8,128,128]{3,2,1,0:T(8,128)(2,1)} fusion(bf16[8,8,128,128]{2,3,1,0:T(8,128)(2,1)} %copy.61, f32[128,8,128]{0,2,1:T(8,128)S(1)} %convolution_bitcast_fusion), kind=kOutput, calls=%fused_computation.5 | convolution fusion | flops 271187968 | bytes 4718592 | tf_op jit(solution)/shard_map/tgh,tgko->gkho/dot_general | solution.py:129
  151.7 4.1 %copy.72 = bf16[1,8,4,2,128,128]{5,4,3,0,2,1:T(8,128)(2,1)} copy(bf16[1,8,4,2,128,128]{4,5,3,2,1,0:T(8,128)(2,1)} %bitcast.182) | data formatting | bytes 4194304 | tf_op jit(solution)/shard_map/stack | solution.py:153
  158.7 2.7 %collective-permute-start.10 = (bf16[4,2,2,128,128]{4,3,2,1,0:T(8,128)(2,1)S(1)}, bf16[4,2,2,128,128]{4,3,2,1,0:T(8,128)(2,1)S(1)}, u32[]{:S(2)}, u32[]{:S(2)}) collective-permute-start(bf16[4,2,2,128,128]{4,3,2,1,0:T(8,128)(2,1)S(1)} %get-tuple-element.12), channel_id=1, source_target_pairs={{0,4},{1,5},{2,6},{3,7},{4,8},{5,9},{6,10},{7,11},{8,12},{9,13},{1... | collective-permute-start | bytes 1572872 | tf_op jit(solution)/shard_map/ppermute | solution.py:64
  161.4 15.1 %collective-permute-done.10 = bf16[4,2,2,128,128]{4,3,2,1,0:T(8,128)(2,1)S(1)} collective-permute-done((bf16[4,2,2,128,128]{4,3,2,1,0:T(8,128)(2,1)S(1)}, bf16[4,2,2,128,128]{4,3,2,1,0:T(8,128)(2,1)S(1)}, u32[]{:S(2)}, u32[]{:S(2)}) %collective-permute-start.10) | collective-permute-done | bytes 524320 | tf_op jit(solution)/shard_map/ppermute | solution.py:64
  176.7 1.9 collective-permute-start.11
  178.6 1.9 reduce_sum.12
  182.3 5.7 %all-to-all-start.2 = ((bf16[16,2,128,256]{3,2,1,0:T(8,128)(2,1)}), bf16[16,2,128,256]{3,2,1,0:T(8,128)(2,1)S(1)}, u32[]{:S(2)}, u32[]{:S(2)}) async-start(bf16[16,2,128,256]{3,2,1,0:T(8,128)(2,1)} %broadcast_in_dim.5), calls=%async_computation.2 | async-start | bytes 4194304 | tf_op jit(solution)/shard_map/all_to_all | solution.py:22
  188.0 5.1 %collective-permute-start.14 = (bf16[4,2,2,128,128]{4,3,2,1,0:T(8,128)(2,1)}, bf16[4,2,2,128,128]{4,3,2,1,0:T(8,128)(2,1)S(1)}, u32[]{:S(2)}, u32[]{:S(2)}) collective-permute-start(bf16[4,2,2,128,128]{4,3,2,1,0:T(8,128)(2,1)} %get-tuple-element.13), channel_id=1, source_target_pairs={{0,28},{1,29},{2,30},{3,31},{4,0},{5,1},{6,2},{7,3},{8,4},{9,5},{1... | collective-permute-start | bytes 1572872 | tf_op jit(solution)/shard_map/ppermute | solution.py:69
  194.5 1.9 collective-permute-start.12
  196.4 8.5 %collective-permute-done.14 = bf16[4,2,2,128,128]{4,3,2,1,0:T(8,128)(2,1)S(1)} collective-permute-done((bf16[4,2,2,128,128]{4,3,2,1,0:T(8,128)(2,1)}, bf16[4,2,2,128,128]{4,3,2,1,0:T(8,128)(2,1)S(1)}, u32[]{:S(2)}, u32[]{:S(2)}) %collective-permute-start.14) | collective-permute-done | bytes 524320 | tf_op jit(solution)/shard_map/ppermute | solution.py:69
  204.9 6.3 %collective-permute-done.12 = bf16[4,2,2,128,128]{4,3,2,1,0:T(8,128)(2,1)S(1)} collective-permute-done((bf16[4,2,2,128,128]{4,3,2,1,0:T(8,128)(2,1)S(1)}, bf16[4,2,2,128,128]{4,3,2,1,0:T(8,128)(2,1)S(1)}, u32[]{:S(2)}, u32[]{:S(2)}) %collective-permute-start.12) | collective-permute-done | bytes 524320 | tf_op jit(solution)/shard_map/ppermute | solution.py:64
  212.7 1.9 collective-permute-start.15
  214.6 3.9 %collective-permute-start.13 = (bf16[4,2,2,128,128]{4,3,2,1,0:T(8,128)(2,1)S(1)}, bf16[4,2,2,128,128]{4,3,2,1,0:T(8,128)(2,1)S(1)}, u32[]{:S(2)}, u32[]{:S(2)}) collective-permute-start(bf16[4,2,2,128,128]{4,3,2,1,0:T(8,128)(2,1)S(1)} %get-tuple-element.10), channel_id=1, source_target_pairs={{0,4},{1,5},{2,6},{3,7},{4,8},{5,9},{6,10},{7,11},{8,12},{9,13},{1... | collective-permute-start | bytes 1572872 | tf_op jit(solution)/shard_map/ppermute | solution.py:64
  218.6 8.7 %collective-permute-done.15 = bf16[4,2,2,128,128]{4,3,2,1,0:T(8,128)(2,1)S(1)} collective-permute-done((bf16[4,2,2,128,128]{4,3,2,1,0:T(8,128)(2,1)S(1)}, bf16[4,2,2,128,128]{4,3,2,1,0:T(8,128)(2,1)S(1)}, u32[]{:S(2)}, u32[]{:S(2)}) %collective-permute-start.15) | collective-permute-done | bytes 524320 | tf_op jit(solution)/shard_map/ppermute | solution.py:69
  228.5 3.4 %collective-permute-start.16 = (bf16[4,2,2,128,128]{4,3,2,1,0:T(8,128)(2,1)S(1)}, bf16[4,2,2,128,128]{4,3,2,1,0:T(8,128)(2,1)S(1)}, u32[]{:S(2)}, u32[]{:S(2)}) collective-permute-start(bf16[4,2,2,128,128]{4,3,2,1,0:T(8,128)(2,1)S(1)} %fusion.5), channel_id=1, source_target_pairs={{0,28},{1,29},{2,30},{3,31},{4,0},{5,1},{6,2},{7,3},{8,4},{9,5},{1... | collective-permute-start | bytes 1572872 | tf_op jit(solution)/shard_map/ppermute | solution.py:69
  232.0 10.2 %collective-permute-done.16 = bf16[4,2,2,128,128]{4,3,2,1,0:T(8,128)(2,1)S(1)} collective-permute-done((bf16[4,2,2,128,128]{4,3,2,1,0:T(8,128)(2,1)S(1)}, bf16[4,2,2,128,128]{4,3,2,1,0:T(8,128)(2,1)S(1)}, u32[]{:S(2)}, u32[]{:S(2)}) %collective-permute-start.16) | collective-permute-done | bytes 524320 | tf_op jit(solution)/shard_map/ppermute | solution.py:69
  243.5 4.7 %collective-permute-start.17 = (bf16[2,2,128,128]{3,2,1,0:T(8,128)(2,1)S(1)}, bf16[2,2,128,128]{3,2,1,0:T(8,128)(2,1)S(1)}, u32[]{:S(2)}, u32[]{:S(2)}) collective-permute-start(bf16[2,2,128,128]{3,2,1,0:T(8,128)(2,1)S(1)} %get-tuple-element.20), channel_id=1, source_target_pairs={{0,3},{1,0},{2,1},{3,2},{4,7},{5,4},{6,5},{7,6},{8,11},{9,8},{10,9... | collective-permute-start | bytes 393224 | tf_op jit(solution)/shard_map/ppermute | solution.py:77
  248.2 3.9 %collective-permute-start.18 = (bf16[2,2,128,128]{3,2,1,0:T(8,128)(2,1)S(1)}, bf16[2,2,128,128]{3,2,1,0:T(8,128)(2,1)S(1)}, u32[]{:S(2)}, u32[]{:S(2)}) collective-permute-start(bf16[2,2,128,128]{3,2,1,0:T(8,128)(2,1)S(1)} %get-tuple-element.22), channel_id=1, source_target_pairs={{0,2},{1,3},{2,0},{3,1},{4,6},{5,7},{6,4},{7,5},{8,10},{9,11},{10,... | collective-permute-start | bytes 393224 | tf_op jit(solution)/shard_map/ppermute | solution.py:77
  252.1 3.1 %collective-permute-start.19 = (bf16[2,2,128,128]{3,2,1,0:T(8,128)(2,1)S(1)}, bf16[2,2,128,128]{3,2,1,0:T(8,128)(2,1)S(1)}, u32[]{:S(2)}, u32[]{:S(2)}) collective-permute-start(bf16[2,2,128,128]{3,2,1,0:T(8,128)(2,1)S(1)} %get-tuple-element.21), channel_id=1, source_target_pairs={{0,1},{1,2},{2,3},{3,0},{4,5},{5,6},{6,7},{7,4},{8,9},{9,10},{10,1... | collective-permute-start | bytes 393224 | tf_op jit(solution)/shard_map/ppermute | solution.py:77
  255.2 2.5 collective-permute-done.17
  257.7 2.3 collective-permute-done.18
  260.0 2.5 collective-permute-done.19
  263.3 2.3 copy.68
  (91 shorter events, 40.1 us)
Async XLA Ops:
  0.6 53.5 %copy-start = (s32[64]{0:T(128)S(1)}, s32[64]{0:T(128)}, u32[]{:S(2)}) copy-start(s32[64]{0:T(128)} %param.9) | copy-start | bytes 772
  1.5 27.6 %collective-permute-start = (bf16[2,2,128,128]{3,2,1,0:T(8,128)(2,1)S(1)}, bf16[2,2,128,128]{3,2,1,0:T(8,128)(2,1)S(1)}, u32[]{:S(2)}, u32[]{:S(2)}) collective-permute-start(bf16[2,2,128,128]{3,2,1,0:T(8,128)(2,1)S(1)} %get-tuple-element.26), channel_id=1, source_target_pairs={{0,1},{1,2},{2,3},{3,0},{4,5},{5,6},{6,7},{7,4},{8,9},{9,10},{10,1... | collective-permute-start | bytes 393224 | tf_op jit(solution)/shard_map/ppermute | solution.py:42
  7.6 21.5 %collective-permute-start.1 = (bf16[2,2,128,128]{3,2,1,0:T(8,128)(2,1)S(1)}, bf16[2,2,128,128]{3,2,1,0:T(8,128)(2,1)S(1)}, u32[]{:S(2)}, u32[]{:S(2)}) collective-permute-start(bf16[2,2,128,128]{3,2,1,0:T(8,128)(2,1)S(1)} %get-tuple-element.26), channel_id=1, source_target_pairs={{0,2},{1,3},{2,0},{3,1},{4,6},{5,7},{6,4},{7,5},{8,10},{9,11},{10,... | collective-permute-start | bytes 393224 | tf_op jit(solution)/shard_map/ppermute | solution.py:42
  16.8 12.6 %collective-permute-start.2 = (bf16[2,2,128,128]{3,2,1,0:T(8,128)(2,1)S(1)}, bf16[2,2,128,128]{3,2,1,0:T(8,128)(2,1)S(1)}, u32[]{:S(2)}, u32[]{:S(2)}) collective-permute-start(bf16[2,2,128,128]{3,2,1,0:T(8,128)(2,1)S(1)} %get-tuple-element.26), channel_id=1, source_target_pairs={{0,3},{1,0},{2,1},{3,2},{4,7},{5,4},{6,5},{7,6},{8,11},{9,8},{10,9... | collective-permute-start | bytes 393224 | tf_op jit(solution)/shard_map/ppermute | solution.py:42
  23.3 42.1 %copy-start.2 = (s32[64]{0:T(128)S(1)}, s32[64]{0:T(128)}, u32[]{:S(2)}) copy-start(s32[64]{0:T(128)} %param.11) | copy-start | bytes 772
  23.3 87.5 %all-to-all-start = ((bf16[16,2,128,256]{2,3,1,0:T(8,128)(2,1)}), bf16[16,2,128,256]{2,3,1,0:T(8,128)(2,1)}, u32[]{:S(2)}, u32[]{:S(2)}) async-start(bf16[16,2,128,256]{2,3,1,0:T(8,128)(2,1)} %broadcast_in_dim.4), calls=%async_computation | async-start | bytes 4194304 | tf_op jit(solution)/shard_map/all_to_all | solution.py:22
  29.4 17.5 %collective-permute-start.3 = (bf16[4,2,2,128,128]{4,3,2,1,0:T(8,128)(2,1)S(1)}, bf16[4,2,2,128,128]{4,3,2,1,0:T(8,128)(2,1)S(1)}, u32[]{:S(2)}, u32[]{:S(2)}) collective-permute-start(bf16[4,2,2,128,128]{4,3,2,1,0:T(8,128)(2,1)S(1)} %pad_maximum_fusion.1), channel_id=1, source_target_pairs={{0,4},{1,5},{2,6},{3,7},{4,8},{5,9},{6,10},{7,11},{8,12},{9,13},{1... | collective-permute-start | bytes 1572872 | tf_op jit(solution)/shard_map/ppermute | solution.py:48
  46.9 16.5 %collective-permute-start.4 = (bf16[4,2,2,128,128]{4,3,2,1,0:T(8,128)(2,1)S(1)}, bf16[4,2,2,128,128]{4,3,2,1,0:T(8,128)(2,1)S(1)}, u32[]{:S(2)}, u32[]{:S(2)}) collective-permute-start(bf16[4,2,2,128,128]{4,3,2,1,0:T(8,128)(2,1)S(1)} %collective-permute-done.3), channel_id=1, source_target_pairs={{0,4},{1,5},{2,6},{3,7},{4,8},{5,9},{6,10},{7,11},{8,12},{9,13},{1... | collective-permute-start | bytes 1572872 | tf_op jit(solution)/shard_map/ppermute | solution.py:48
  49.0 17.2 %collective-permute-start.7 = (bf16[4,2,2,128,128]{4,3,2,1,0:T(8,128)(2,1)S(1)}, bf16[4,2,2,128,128]{4,3,2,1,0:T(8,128)(2,1)S(1)}, u32[]{:S(2)}, u32[]{:S(2)}) collective-permute-start(bf16[4,2,2,128,128]{4,3,2,1,0:T(8,128)(2,1)S(1)} %pad_maximum_fusion.1), channel_id=1, source_target_pairs={{0,28},{1,29},{2,30},{3,31},{4,0},{5,1},{6,2},{7,3},{8,4},{9,5},{1... | collective-permute-start | bytes 1572872 | tf_op jit(solution)/shard_map/ppermute | solution.py:51
  63.4 15.6 %collective-permute-start.5 = (bf16[4,2,2,128,128]{4,3,2,1,0:T(8,128)(2,1)S(1)}, bf16[4,2,2,128,128]{4,3,2,1,0:T(8,128)(2,1)S(1)}, u32[]{:S(2)}, u32[]{:S(2)}) collective-permute-start(bf16[4,2,2,128,128]{4,3,2,1,0:T(8,128)(2,1)S(1)} %collective-permute-done.4), channel_id=1, source_target_pairs={{0,4},{1,5},{2,6},{3,7},{4,8},{5,9},{6,10},{7,11},{8,12},{9,13},{1... | collective-permute-start | bytes 1572872 | tf_op jit(solution)/shard_map/ppermute | solution.py:48
  66.2 14.9 %collective-permute-start.8 = (bf16[4,2,2,128,128]{4,3,2,1,0:T(8,128)(2,1)S(1)}, bf16[4,2,2,128,128]{4,3,2,1,0:T(8,128)(2,1)S(1)}, u32[]{:S(2)}, u32[]{:S(2)}) collective-permute-start(bf16[4,2,2,128,128]{4,3,2,1,0:T(8,128)(2,1)S(1)} %collective-permute-done.7), channel_id=1, source_target_pairs={{0,28},{1,29},{2,30},{3,31},{4,0},{5,1},{6,2},{7,3},{8,4},{9,5},{1... | collective-permute-start | bytes 1572872 | tf_op jit(solution)/shard_map/ppermute | solution.py:51
  79.0 14.7 %collective-permute-start.6 = (bf16[4,2,2,128,128]{4,3,2,1,0:T(8,128)(2,1)S(1)}, bf16[4,2,2,128,128]{4,3,2,1,0:T(8,128)(2,1)S(1)}, u32[]{:S(2)}, u32[]{:S(2)}) collective-permute-start(bf16[4,2,2,128,128]{4,3,2,1,0:T(8,128)(2,1)S(1)} %collective-permute-done.5), channel_id=1, source_target_pairs={{0,4},{1,5},{2,6},{3,7},{4,8},{5,9},{6,10},{7,11},{8,12},{9,13},{1... | collective-permute-start | bytes 1572872 | tf_op jit(solution)/shard_map/ppermute | solution.py:48
  81.1 14.4 %collective-permute-start.9 = (bf16[4,2,2,128,128]{4,3,2,1,0:T(8,128)(2,1)S(1)}, bf16[4,2,2,128,128]{4,3,2,1,0:T(8,128)(2,1)S(1)}, u32[]{:S(2)}, u32[]{:S(2)}) collective-permute-start(bf16[4,2,2,128,128]{4,3,2,1,0:T(8,128)(2,1)S(1)} %collective-permute-done.8), channel_id=1, source_target_pairs={{0,28},{1,29},{2,30},{3,31},{4,0},{5,1},{6,2},{7,3},{8,4},{9,5},{1... | collective-permute-start | bytes 1572872 | tf_op jit(solution)/shard_map/ppermute | solution.py:51
  97.6 6.5 %copy-start.3 = (bf16[1,8,4,2,128,128]{5,4,3,0,2,1:T(8,128)(2,1)}, bf16[1,8,4,2,128,128]{5,4,3,0,2,1:T(8,128)(2,1)S(1)}, u32[]{:S(2)}) copy-start(bf16[1,8,4,2,128,128]{5,4,3,0,2,1:T(8,128)(2,1)S(1)} %get-tuple-element.15) | copy-start | bytes 6291460
  121.9 3.2 %copy-start.6 = (bf16[1,8,4,2,128,128]{4,3,2,1,5,0:T(2,128)(2,1)S(1)}, bf16[1,8,4,2,128,128]{4,3,2,1,5,0:T(2,128)(2,1)}, u32[]{:S(2)}) copy-start(bf16[1,8,4,2,128,128]{4,3,2,1,5,0:T(2,128)(2,1)} %copy.52) | copy-start | bytes 6291460
  125.1 1.6 copy-start.9
  129.7 1.6 copy-start.5
  135.6 43.0 %all-to-all-start.1 = ((bf16[16,2,128,256]{2,3,1,0:T(8,128)(2,1)}), bf16[16,2,128,256]{2,3,1,0:T(8,128)(2,1)}, u32[]{:S(2)}, u32[]{:S(2)}) async-start(bf16[16,2,128,256]{2,3,1,0:T(8,128)(2,1)} %bitcast.177), calls=%async_computation.1 | async-start | bytes 4194304 | tf_op jit(solution)/shard_map/all_to_all | solution.py:26
  151.7 4.1 %copy-start.7 = (bf16[8,8,128,128]{2,3,1,0:T(8,128)(2,1)S(1)}, bf16[8,8,128,128]{2,3,1,0:T(8,128)(2,1)}, u32[]{:S(2)}) copy-start(bf16[8,8,128,128]{2,3,1,0:T(8,128)(2,1)} %copy.57) | copy-start | bytes 6291460
  155.8 1.6 copy-start.8
  157.7 18.8 %copy-start.4 = (bf16[8,4,2,2,128,128]{5,4,3,2,1,0:T(8,128)(2,1)}, bf16[8,4,2,2,128,128]{5,4,3,2,1,0:T(8,128)(2,1)S(1)}, u32[]{:S(2)}) copy-start(bf16[8,4,2,2,128,128]{5,4,3,2,1,0:T(8,128)(2,1)S(1)} %maximum_bitcast_fusion) | copy-start | bytes 12582916
  158.7 17.8 %collective-permute-start.10 = (bf16[4,2,2,128,128]{4,3,2,1,0:T(8,128)(2,1)S(1)}, bf16[4,2,2,128,128]{4,3,2,1,0:T(8,128)(2,1)S(1)}, u32[]{:S(2)}, u32[]{:S(2)}) collective-permute-start(bf16[4,2,2,128,128]{4,3,2,1,0:T(8,128)(2,1)S(1)} %get-tuple-element.12), channel_id=1, source_target_pairs={{0,4},{1,5},{2,6},{3,7},{4,8},{5,9},{6,10},{7,11},{8,12},{9,13},{1... | collective-permute-start | bytes 1572872 | tf_op jit(solution)/shard_map/ppermute | solution.py:64
  176.7 16.6 %collective-permute-start.11 = (bf16[4,2,2,128,128]{4,3,2,1,0:T(8,128)(2,1)S(1)}, bf16[4,2,2,128,128]{4,3,2,1,0:T(8,128)(2,1)S(1)}, u32[]{:S(2)}, u32[]{:S(2)}) collective-permute-start(bf16[4,2,2,128,128]{4,3,2,1,0:T(8,128)(2,1)S(1)} %fusion.6), channel_id=1, source_target_pairs={{0,4},{1,5},{2,6},{3,7},{4,8},{5,9},{6,10},{7,11},{8,12},{9,13},{1... | collective-permute-start | bytes 1572872 | tf_op jit(solution)/shard_map/ppermute | solution.py:64
  182.3 81.0 %all-to-all-start.2 = ((bf16[16,2,128,256]{3,2,1,0:T(8,128)(2,1)}), bf16[16,2,128,256]{3,2,1,0:T(8,128)(2,1)S(1)}, u32[]{:S(2)}, u32[]{:S(2)}) async-start(bf16[16,2,128,256]{3,2,1,0:T(8,128)(2,1)} %broadcast_in_dim.5), calls=%async_computation.2 | async-start | bytes 4194304 | tf_op jit(solution)/shard_map/all_to_all | solution.py:22
  188.0 16.9 %collective-permute-start.14 = (bf16[4,2,2,128,128]{4,3,2,1,0:T(8,128)(2,1)}, bf16[4,2,2,128,128]{4,3,2,1,0:T(8,128)(2,1)S(1)}, u32[]{:S(2)}, u32[]{:S(2)}) collective-permute-start(bf16[4,2,2,128,128]{4,3,2,1,0:T(8,128)(2,1)} %get-tuple-element.13), channel_id=1, source_target_pairs={{0,28},{1,29},{2,30},{3,31},{4,0},{5,1},{6,2},{7,3},{8,4},{9,5},{1... | collective-permute-start | bytes 1572872 | tf_op jit(solution)/shard_map/ppermute | solution.py:69
  194.5 16.7 %collective-permute-start.12 = (bf16[4,2,2,128,128]{4,3,2,1,0:T(8,128)(2,1)S(1)}, bf16[4,2,2,128,128]{4,3,2,1,0:T(8,128)(2,1)S(1)}, u32[]{:S(2)}, u32[]{:S(2)}) collective-permute-start(bf16[4,2,2,128,128]{4,3,2,1,0:T(8,128)(2,1)S(1)} %fusion.7), channel_id=1, source_target_pairs={{0,4},{1,5},{2,6},{3,7},{4,8},{5,9},{6,10},{7,11},{8,12},{9,13},{1... | collective-permute-start | bytes 1572872 | tf_op jit(solution)/shard_map/ppermute | solution.py:64
  212.7 14.6 %collective-permute-start.15 = (bf16[4,2,2,128,128]{4,3,2,1,0:T(8,128)(2,1)S(1)}, bf16[4,2,2,128,128]{4,3,2,1,0:T(8,128)(2,1)S(1)}, u32[]{:S(2)}, u32[]{:S(2)}) collective-permute-start(bf16[4,2,2,128,128]{4,3,2,1,0:T(8,128)(2,1)S(1)} %get-tuple-element.11), channel_id=1, source_target_pairs={{0,28},{1,29},{2,30},{3,31},{4,0},{5,1},{6,2},{7,3},{8,4},{9,5},{1... | collective-permute-start | bytes 1572872 | tf_op jit(solution)/shard_map/ppermute | solution.py:69
  214.6 17.3 %collective-permute-start.13 = (bf16[4,2,2,128,128]{4,3,2,1,0:T(8,128)(2,1)S(1)}, bf16[4,2,2,128,128]{4,3,2,1,0:T(8,128)(2,1)S(1)}, u32[]{:S(2)}, u32[]{:S(2)}) collective-permute-start(bf16[4,2,2,128,128]{4,3,2,1,0:T(8,128)(2,1)S(1)} %get-tuple-element.10), channel_id=1, source_target_pairs={{0,4},{1,5},{2,6},{3,7},{4,8},{5,9},{6,10},{7,11},{8,12},{9,13},{1... | collective-permute-start | bytes 1572872 | tf_op jit(solution)/shard_map/ppermute | solution.py:64
  228.5 13.7 %collective-permute-start.16 = (bf16[4,2,2,128,128]{4,3,2,1,0:T(8,128)(2,1)S(1)}, bf16[4,2,2,128,128]{4,3,2,1,0:T(8,128)(2,1)S(1)}, u32[]{:S(2)}, u32[]{:S(2)}) collective-permute-start(bf16[4,2,2,128,128]{4,3,2,1,0:T(8,128)(2,1)S(1)} %fusion.5), channel_id=1, source_target_pairs={{0,28},{1,29},{2,30},{3,31},{4,0},{5,1},{6,2},{7,3},{8,4},{9,5},{1... | collective-permute-start | bytes 1572872 | tf_op jit(solution)/shard_map/ppermute | solution.py:69
  243.5 14.2 %collective-permute-start.17 = (bf16[2,2,128,128]{3,2,1,0:T(8,128)(2,1)S(1)}, bf16[2,2,128,128]{3,2,1,0:T(8,128)(2,1)S(1)}, u32[]{:S(2)}, u32[]{:S(2)}) collective-permute-start(bf16[2,2,128,128]{3,2,1,0:T(8,128)(2,1)S(1)} %get-tuple-element.20), channel_id=1, source_target_pairs={{0,3},{1,0},{2,1},{3,2},{4,7},{5,4},{6,5},{7,6},{8,11},{9,8},{10,9... | collective-permute-start | bytes 393224 | tf_op jit(solution)/shard_map/ppermute | solution.py:77
  248.2 11.9 %collective-permute-start.18 = (bf16[2,2,128,128]{3,2,1,0:T(8,128)(2,1)S(1)}, bf16[2,2,128,128]{3,2,1,0:T(8,128)(2,1)S(1)}, u32[]{:S(2)}, u32[]{:S(2)}) collective-permute-start(bf16[2,2,128,128]{3,2,1,0:T(8,128)(2,1)S(1)} %get-tuple-element.22), channel_id=1, source_target_pairs={{0,2},{1,3},{2,0},{3,1},{4,6},{5,7},{6,4},{7,5},{8,10},{9,11},{10,... | collective-permute-start | bytes 393224 | tf_op jit(solution)/shard_map/ppermute | solution.py:77
  252.1 10.5 %collective-permute-start.19 = (bf16[2,2,128,128]{3,2,1,0:T(8,128)(2,1)S(1)}, bf16[2,2,128,128]{3,2,1,0:T(8,128)(2,1)S(1)}, u32[]{:S(2)}, u32[]{:S(2)}) collective-permute-start(bf16[2,2,128,128]{3,2,1,0:T(8,128)(2,1)S(1)} %get-tuple-element.21), channel_id=1, source_target_pairs={{0,1},{1,2},{2,3},{3,0},{4,5},{5,6},{6,7},{7,4},{8,9},{9,10},{10,1... | collective-permute-start | bytes 393224 | tf_op jit(solution)/shard_map/ppermute | solution.py:77
  267.3 2.6 copy-start.1

commit v8 on v7

--- a/solution.py
+++ b/solution.py
@@ -117,12 +117,13 @@
     picked_in = full_input.reshape(tokens, row_blocks, block_size)[:, up_index]
     preact = jnp.einsum("tgki,gkio->tgo", picked_in, up_tiles, preferred_element_type=jnp.float32)
     hidden = (preact * normal_cdf(preact)).astype(jnp.bfloat16)
-    product = jnp.einsum("gkho,tgh->gkot", down_tiles, hidden, preferred_element_type=jnp.float32)
+    spread = jnp.broadcast_to(hidden[:, :, None, :], (tokens, groups, K, block_size))
+    product = jnp.einsum("tgkh,gkho->gkto", spread, down_tiles, preferred_element_type=jnp.float32)
     span = jnp.arange(row_blocks, dtype=jnp.int32)
     highest = lax.Precision.HIGHEST
     down_hot = (down_index[..., None] == span).astype(jnp.float32)
     out_t = jnp.einsum(
-        "gkr,gkot->rot", down_hot, product, precision=highest, preferred_element_type=jnp.float32
+        "gkr,gkto->rto", down_hot, product, precision=highest, preferred_element_type=jnp.float32
     )
     picked_grad = full_grad.reshape(tokens, row_blocks, block_size)[:, down_index]
     down_term = (
@@ -143,9 +144,9 @@
         * scale
     )
 
-    parts = jnp.stack([out_t, in_t]).astype(jnp.bfloat16)
-    parts = parts.reshape(2, n_tensor, shard_width // block_size, block_size, tokens)
-    parts = jnp.transpose(parts, (1, 0, 4, 2, 3)).reshape(n_tensor, 2, tokens, shard_width)
+    parts = jnp.stack([out_t, jnp.transpose(in_t, (0, 2, 1))]).astype(jnp.bfloat16)
+    parts = parts.reshape(2, n_tensor, shard_width // block_size, tokens, block_size)
+    parts = jnp.transpose(parts, (1, 0, 3, 2, 4)).reshape(n_tensor, 2, tokens, shard_width)
     mine = scatter_sum(parts, "tensor")
     both = gather_all(mine, "tensor")
     both = jnp.moveaxis(both, 0, 2).reshape(2, tokens, width)

time: 274 us -> 281 us (1.026)
  matrix products: 13.5 us -> 19.3 us
  other arithmetic: 11.4 us -> 14.3 us
    reshape x0 -> x2, local copies, waits for them, and re-layouts: none -> 8.05 us  [per_device(): jnp.transpose(parts, (1, 0, 3, 2, 4))]
    slice x3 -> x2, local copies, waits for them, and re-layouts: 10.9 us -> 4.43 us  [per_device(): up_all, down_all = (weights[0], weights[1])]
    transpose x0 -> x1, other arithmetic: none -> 4.43 us  [per_device(): jnp.transpose(parts, (1, 0, 3, 2, 4))]
    dot_general x2, matrix products: 2.38 us -> 6.5 us  [the longest x1 4.12 us: per_device(): jnp.einsum('gkr,gkto->rto', down_hot, product, precision=highest, preferr...]
    another operation x2 -> x1, local copies, waits for them, and re-layouts: 0.82 us -> 4.11 us  [per_device(): jnp.stack([out_t, jnp.transpose(in_t, (0, 2, 1))]).astype(jnp.bfloat16)]
    unnamed x28 -> x30, local copies, waits for them, and re-layouts: 5.99 us -> 4.16 us
    gather x3 -> x2, local copies, waits for them, and re-layouts: 7.72 us -> 6.08 us  [per_device(): full_grad.reshape(tokens, row_blocks, block_size)[:, down_index]]
  transfers between devices with their start and end apart: 23 -> 23, of which waited for: 16 -> 14; matrix products, arithmetic and copies ran while one was open for 17% -> 15% of each run, Pallas kernels for 0% -> 0%
where the time goes in v8:
time: 281 us; the launch traced here: 278 us
  waiting for transfers between devices  95.5 us (34%)
  starting transfers between devices  93.9 us (33%)
  local copies, waits for them, and re-layouts  53.9 us (19%)
  matrix products  19.3 us (7%)
  other arithmetic  14.3 us (5%)
    ppermute x4, waiting for transfers between devices, dp_gather_rel(): cur_f = lax.ppermute(cur_f, 'dp', dp_shift(n_y, n_z, 1, 0))  37 us
    ppermute x3, waiting for transfers between devices, dp_scatter_rel(): lax.ppermute(part.astype(jnp.bfloat16), 'dp', dp_shift(n_y, n_z, -1, 0))  27 us
    ppermute x4, waiting for transfers between devices, dp_scatter_rel(): lax.ppermute(part.astype(jnp.bfloat16), 'dp', dp_shift(n_y, n_z, 1, 0))  21.6 us
    ppermute x3, starting transfers between devices, dp_gather_rel(): lax.ppermute(x, 'dp', dp_shift(n_y, n_z, 0, b))  17.7 us
    ppermute x3, starting transfers between devices, dp_gather_rel(): cur_b = lax.ppermute(cur_b, 'dp', dp_shift(n_y, n_z, -1, 0))  15.9 us
    ppermute x3, starting transfers between devices, dp_scatter_rel(): lax.ppermute(acc[b].astype(jnp.bfloat16), 'dp', dp_shift(n_y, n_z, 0, -b))  12.9 us
    all_to_all x2, starting transfers between devices, gather_all(): return lax.all_to_all(spread, axis_name, 0, 0, tiled=True)  11.6 us
    ppermute x4, starting transfers between devices, dp_scatter_rel(): lax.ppermute(part.astype(jnp.bfloat16), 'dp', dp_shift(n_y, n_z, 1, 0))  10.5 us
  transfers between devices with their start and end apart: 23, of which 14 were waited for; matrix products, arithmetic and copies ran while one was open for 15% of the time, Pallas kernels for 0%

profile of v8, /device:TPU:6, one launch (start us, length us, event | category | flops | bytes accessed | tf_op | source)
XLA Modules:
  0.0 278.2 jit_solution(2229835208391693057)
XLA Ops:
  1.5 10.9 %collective-permute-start.2 = (bf16[2,2,128,128]{3,2,1,0:T(8,128)(2,1)S(1)}, bf16[2,2,128,128]{3,2,1,0:T(8,128)(2,1)S(1)}, u32[]{:S(2)}, u32[]{:S(2)}) collective-permute-start(bf16[2,2,128,128]{3,2,1,0:T(8,128)(2,1)S(1)} %get-tuple-element.26), channel_id=1, source_target_pairs={{0,3},{1,0},{2,1},{3,2},{4,7},{5,4},{6,5},{7,6},{8,11},{9,8},{10,9... | collective-permute-start | bytes 393224 | tf_op jit(solution)/shard_map/ppermute | solution.py:42
  12.5 1.9 collective-permute-start.1
  14.4 4.8 %collective-permute-start = (bf16[2,2,128,128]{3,2,1,0:T(8,128)(2,1)S(1)}, bf16[2,2,128,128]{3,2,1,0:T(8,128)(2,1)S(1)}, u32[]{:S(2)}, u32[]{:S(2)}) collective-permute-start(bf16[2,2,128,128]{3,2,1,0:T(8,128)(2,1)S(1)} %get-tuple-element.26), channel_id=1, source_target_pairs={{0,1},{1,2},{2,3},{3,0},{4,5},{5,6},{6,7},{7,4},{8,9},{9,10},{10,1... | collective-permute-start | bytes 393224 | tf_op jit(solution)/shard_map/ppermute | solution.py:42
  22.1 5.8 %all-to-all-start = ((bf16[16,2,128,256]{2,3,1,0:T(8,128)(2,1)}), bf16[16,2,128,256]{2,3,1,0:T(8,128)(2,1)}, u32[]{:S(2)}, u32[]{:S(2)}) async-start(bf16[16,2,128,256]{2,3,1,0:T(8,128)(2,1)} %broadcast_in_dim.6), calls=%async_computation | async-start | bytes 4194304 | tf_op jit(solution)/shard_map/all_to_all | solution.py:22
  28.0 3.5 %collective-permute-start.3 = (bf16[4,2,2,128,128]{4,3,2,1,0:T(8,128)(2,1)S(1)}, bf16[4,2,2,128,128]{4,3,2,1,0:T(8,128)(2,1)S(1)}, u32[]{:S(2)}, u32[]{:S(2)}) collective-permute-start(bf16[4,2,2,128,128]{4,3,2,1,0:T(8,128)(2,1)S(1)} %pad_maximum_fusion), channel_id=1, source_target_pairs={{0,4},{1,5},{2,6},{3,7},{4,8},{5,9},{6,10},{7,11},{8,12},{9,13},{1... | collective-permute-start | bytes 1572872 | tf_op jit(solution)/shard_map/ppermute | solution.py:48
  31.7 14.0 %collective-permute-done.3 = bf16[4,2,2,128,128]{4,3,2,1,0:T(8,128)(2,1)S(1)} collective-permute-done((bf16[4,2,2,128,128]{4,3,2,1,0:T(8,128)(2,1)S(1)}, bf16[4,2,2,128,128]{4,3,2,1,0:T(8,128)(2,1)S(1)}, u32[]{:S(2)}, u32[]{:S(2)}) %collective-permute-start.3) | collective-permute-done | bytes 524320 | tf_op jit(solution)/shard_map/ppermute | solution.py:48
  47.8 5.1 %collective-permute-start.7 = (bf16[4,2,2,128,128]{4,3,2,1,0:T(8,128)(2,1)S(1)}, bf16[4,2,2,128,128]{4,3,2,1,0:T(8,128)(2,1)S(1)}, u32[]{:S(2)}, u32[]{:S(2)}) collective-permute-start(bf16[4,2,2,128,128]{4,3,2,1,0:T(8,128)(2,1)S(1)} %pad_maximum_fusion), channel_id=1, source_target_pairs={{0,28},{1,29},{2,30},{3,31},{4,0},{5,1},{6,2},{7,3},{8,4},{9,5},{1... | collective-permute-start | bytes 1572872 | tf_op jit(solution)/shard_map/ppermute | solution.py:51
  53.8 8.5 %collective-permute-done.4 = bf16[4,2,2,128,128]{4,3,2,1,0:T(8,128)(2,1)S(1)} collective-permute-done((bf16[4,2,2,128,128]{4,3,2,1,0:T(8,128)(2,1)S(1)}, bf16[4,2,2,128,128]{4,3,2,1,0:T(8,128)(2,1)S(1)}, u32[]{:S(2)}, u32[]{:S(2)}) %collective-permute-start.4) | collective-permute-done | bytes 524320 | tf_op jit(solution)/shard_map/ppermute | solution.py:48
  65.1 5.1 %collective-permute-start.8 = (bf16[4,2,2,128,128]{4,3,2,1,0:T(8,128)(2,1)S(1)}, bf16[4,2,2,128,128]{4,3,2,1,0:T(8,128)(2,1)S(1)}, u32[]{:S(2)}, u32[]{:S(2)}) collective-permute-start(bf16[4,2,2,128,128]{4,3,2,1,0:T(8,128)(2,1)S(1)} %collective-permute-done.7), channel_id=1, source_target_pairs={{0,28},{1,29},{2,30},{3,31},{4,0},{5,1},{6,2},{7,3},{8,4},{9,5},{1... | collective-permute-start | bytes 1572872 | tf_op jit(solution)/shard_map/ppermute | solution.py:51
  70.6 7.5 %collective-permute-done.5 = bf16[4,2,2,128,128]{4,3,2,1,0:T(8,128)(2,1)S(1)} collective-permute-done((bf16[4,2,2,128,128]{4,3,2,1,0:T(8,128)(2,1)S(1)}, bf16[4,2,2,128,128]{4,3,2,1,0:T(8,128)(2,1)S(1)}, u32[]{:S(2)}, u32[]{:S(2)}) %collective-permute-start.5) | collective-permute-done | bytes 524320 | tf_op jit(solution)/shard_map/ppermute | solution.py:48
  80.2 5.6 %collective-permute-start.9 = (bf16[4,2,2,128,128]{4,3,2,1,0:T(8,128)(2,1)S(1)}, bf16[4,2,2,128,128]{4,3,2,1,0:T(8,128)(2,1)S(1)}, u32[]{:S(2)}, u32[]{:S(2)}) collective-permute-start(bf16[4,2,2,128,128]{4,3,2,1,0:T(8,128)(2,1)S(1)} %collective-permute-done.8), channel_id=1, source_target_pairs={{0,28},{1,29},{2,30},{3,31},{4,0},{5,1},{6,2},{7,3},{8,4},{9,5},{1... | collective-permute-start | bytes 1572872 | tf_op jit(solution)/shard_map/ppermute | solution.py:51
  85.9 7.0 %collective-permute-done.6 = bf16[4,2,2,128,128]{4,3,2,1,0:T(8,128)(2,1)S(1)} collective-permute-done((bf16[4,2,2,128,128]{4,3,2,1,0:T(8,128)(2,1)S(1)}, bf16[4,2,2,128,128]{4,3,2,1,0:T(8,128)(2,1)S(1)}, u32[]{:S(2)}, u32[]{:S(2)}) %collective-permute-start.6) | collective-permute-done | bytes 524320 | tf_op jit(solution)/shard_map/ppermute | solution.py:48
  96.7 2.7 copy.52
  99.4 4.1 %copy.63 = bf16[8,8,128,128]{3,1,0,2:T(8,128)(2,1)} copy(bf16[8,8,128,128]{2,3,1,0:T(8,128)(2,1)} %bitcast.182) | data formatting | bytes 4194304 | tf_op jit(solution)/shard_map/reshape;squeeze | solution.py:113
  106.8 2.2 gather_fusion.3
  109.9 2.6 multiply_convert_fusion.2
  115.1 2.7 bitcast_convert_fusion
  117.7 4.1 %copy.65 = bf16[1,16,2,128,128]{4,2,1,3,0:T(2,128)(2,1)S(1)} copy(bf16[1,16,2,128,128]{3,2,1,4,0:T(2,128)(2,1)} %bitcast.189) | data formatting | bytes 2097152 | tf_op jit(solution)/shard_map/stack | solution.py:147
  122.7 2.4 fusion.14
  125.1 4.1 %bitcast_convert_fusion.1 = bf16[32,128,128]{2,0,1:T(8,128)(2,1)S(1)} fusion(f32[8,8,128,128]{3,2,1,0:T(8,128)S(1)} %fusion.14, s32[8,8]{1,0:T(8,128)S(1)} %eq.36), kind=kOutput, calls=%fused_computation.12 | convolution fusion | flops 403179520 | bytes 5243136 | tf_op jit(solution)/shard_map/gkr,gkto->rto/dot_general | solution.py:125
  129.2 4.4 %maximum_bitcast_fusion.1 = bf16[16,2,128,2,128]{4,3,0,2,1:T(2,128)(2,1)} fusion(bf16[1,16,2,128,128]{4,2,1,3,0:T(2,128)(2,1)S(1)} %copy.65, bf16[1,16,2,128,128]{4,2,1,3,0:T(2,128)(2,1)S(1)} %bitcast.190), kind=kLoop, calls=%fused_computation.9 | loop fusion | flops 1048576 | bytes 4194304 | tf_op jit(solution)/shard_map/transpose | solution.py:149
  133.7 4.4 %reshape.284 = bf16[16,2,128,256]{3,0,2,1:T(8,128)(2,1)} reshape(bf16[16,2,128,2,128]{4,3,0,2,1:T(2,128)(2,1)} %maximum_bitcast_fusion.1) | data formatting | bytes 4194304 | tf_op jit(solution)/shard_map/reshape | solution.py:149
  138.0 3.7 %copy.88 = bf16[16,2,128,256]{3,2,1,0:T(8,128)(2,1)} copy(bf16[16,2,128,256]{3,0,2,1:T(8,128)(2,1)} %reshape.284) | data formatting | bytes 4194304 | tf_op jit(solution)/shard_map/reshape | solution.py:149
  141.7 5.7 %all-to-all-start.1 = ((bf16[16,2,128,256]{3,2,1,0:T(8,128)(2,1)}), bf16[16,2,128,256]{3,2,1,0:T(8,128)(2,1)}, u32[]{:S(2)}, u32[]{:S(2)}) async-start(bf16[16,2,128,256]{3,2,1,0:T(8,128)(2,1)} %copy.88), calls=%async_computation.1 | async-start | bytes 4194304 | tf_op jit(solution)/shard_map/all_to_all | solution.py:26
  147.4 3.9 %copy.61 = bf16[8,8,128,128]{2,3,1,0:T(8,128)(2,1)} copy(bf16[8,8,128,128]{3,2,1,0:T(8,128)(2,1)} %bitcast.175) | data formatting | bytes 4194304 | tf_op jit(solution)/shard_map/gather | solution.py:128
  151.3 3.6 %multiply_convert_fusion = bf16[8,8,128,128]{3,2,1,0:T(8,128)(2,1)} fusion(bf16[8,8,128,128]{2,3,1,0:T(8,128)(2,1)} %copy.61, bf16[128,8,128]{0,2,1:T(8,128)(2,1)S(1)} %get-tuple-element.27), kind=kOutput, calls=%fused_computation.7 | convolution fusion | flops 270532608 | bytes 4456448 | tf_op jit(solution)/shard_map/tgh,tgko->gkho/dot_general | solution.py:130
  155.0 3.9 %copy.71 = bf16[1,8,4,2,128,128]{5,4,3,0,2,1:T(8,128)(2,1)} copy(bf16[1,8,4,2,128,128]{4,5,3,2,1,0:T(8,128)(2,1)} %bitcast.181) | data formatting | bytes 4194304 | tf_op jit(solution)/shard_map/stack | solution.py:154
  158.9 2.6 copy.56
  161.5 2.4 multiply_convert_fusion.1
  165.3 2.8 collective-permute-start.10
  168.1 15.1 %collective-permute-done.10 = bf16[4,2,2,128,128]{4,3,2,1,0:T(8,128)(2,1)S(1)} collective-permute-done((bf16[4,2,2,128,128]{4,3,2,1,0:T(8,128)(2,1)S(1)}, bf16[4,2,2,128,128]{4,3,2,1,0:T(8,128)(2,1)S(1)}, u32[]{:S(2)}, u32[]{:S(2)}) %collective-permute-start.10) | collective-permute-done | bytes 524320 | tf_op jit(solution)/shard_map/ppermute | solution.py:64
  183.3 1.9 collective-permute-start.11
  188.7 5.7 %all-to-all-start.2 = ((bf16[16,2,128,256]{3,2,1,0:T(8,128)(2,1)}), bf16[16,2,128,256]{3,2,1,0:T(8,128)(2,1)S(1)}, u32[]{:S(2)}, u32[]{:S(2)}) async-start(bf16[16,2,128,256]{3,2,1,0:T(8,128)(2,1)} %broadcast_in_dim.8), calls=%async_computation.2 | async-start | bytes 4194304 | tf_op jit(solution)/shard_map/all_to_all | solution.py:22
  194.5 5.1 %collective-permute-start.14 = (bf16[4,2,2,128,128]{4,3,2,1,0:T(8,128)(2,1)}, bf16[4,2,2,128,128]{4,3,2,1,0:T(8,128)(2,1)S(1)}, u32[]{:S(2)}, u32[]{:S(2)}) collective-permute-start(bf16[4,2,2,128,128]{4,3,2,1,0:T(8,128)(2,1)} %get-tuple-element.13), channel_id=1, source_target_pairs={{0,28},{1,29},{2,30},{3,31},{4,0},{5,1},{6,2},{7,3},{8,4},{9,5},{1... | collective-permute-start | bytes 1572872 | tf_op jit(solution)/shard_map/ppermute | solution.py:69
  201.1 1.9 collective-permute-start.12
  203.0 8.3 %collective-permute-done.14 = bf16[4,2,2,128,128]{4,3,2,1,0:T(8,128)(2,1)S(1)} collective-permute-done((bf16[4,2,2,128,128]{4,3,2,1,0:T(8,128)(2,1)}, bf16[4,2,2,128,128]{4,3,2,1,0:T(8,128)(2,1)S(1)}, u32[]{:S(2)}, u32[]{:S(2)}) %collective-permute-start.14) | collective-permute-done | bytes 524320 | tf_op jit(solution)/shard_map/ppermute | solution.py:69
  211.4 6.3 %collective-permute-done.12 = bf16[4,2,2,128,128]{4,3,2,1,0:T(8,128)(2,1)S(1)} collective-permute-done((bf16[4,2,2,128,128]{4,3,2,1,0:T(8,128)(2,1)S(1)}, bf16[4,2,2,128,128]{4,3,2,1,0:T(8,128)(2,1)S(1)}, u32[]{:S(2)}, u32[]{:S(2)}) %collective-permute-start.12) | collective-permute-done | bytes 524320 | tf_op jit(solution)/shard_map/ppermute | solution.py:64
  219.2 1.9 collective-permute-start.15
  221.1 3.9 %collective-permute-start.13 = (bf16[4,2,2,128,128]{4,3,2,1,0:T(8,128)(2,1)S(1)}, bf16[4,2,2,128,128]{4,3,2,1,0:T(8,128)(2,1)S(1)}, u32[]{:S(2)}, u32[]{:S(2)}) collective-permute-start(bf16[4,2,2,128,128]{4,3,2,1,0:T(8,128)(2,1)S(1)} %get-tuple-element.10), channel_id=1, source_target_pairs={{0,4},{1,5},{2,6},{3,7},{4,8},{5,9},{6,10},{7,11},{8,12},{9,13},{1... | collective-permute-start | bytes 1572872 | tf_op jit(solution)/shard_map/ppermute | solution.py:64
  225.0 8.6 %collective-permute-done.15 = bf16[4,2,2,128,128]{4,3,2,1,0:T(8,128)(2,1)S(1)} collective-permute-done((bf16[4,2,2,128,128]{4,3,2,1,0:T(8,128)(2,1)S(1)}, bf16[4,2,2,128,128]{4,3,2,1,0:T(8,128)(2,1)S(1)}, u32[]{:S(2)}, u32[]{:S(2)}) %collective-permute-start.15) | collective-permute-done | bytes 524320 | tf_op jit(solution)/shard_map/ppermute | solution.py:69
  234.8 3.4 %collective-permute-start.16 = (bf16[4,2,2,128,128]{4,3,2,1,0:T(8,128)(2,1)S(1)}, bf16[4,2,2,128,128]{4,3,2,1,0:T(8,128)(2,1)S(1)}, u32[]{:S(2)}, u32[]{:S(2)}) collective-permute-start(bf16[4,2,2,128,128]{4,3,2,1,0:T(8,128)(2,1)S(1)} %fusion.9), channel_id=1, source_target_pairs={{0,28},{1,29},{2,30},{3,31},{4,0},{5,1},{6,2},{7,3},{8,4},{9,5},{1... | collective-permute-start | bytes 1572872 | tf_op jit(solution)/shard_map/ppermute | solution.py:69
  238.3 10.1 %collective-permute-done.16 = bf16[4,2,2,128,128]{4,3,2,1,0:T(8,128)(2,1)S(1)} collective-permute-done((bf16[4,2,2,128,128]{4,3,2,1,0:T(8,128)(2,1)S(1)}, bf16[4,2,2,128,128]{4,3,2,1,0:T(8,128)(2,1)S(1)}, u32[]{:S(2)}, u32[]{:S(2)}) %collective-permute-start.16) | collective-permute-done | bytes 524320 | tf_op jit(solution)/shard_map/ppermute | solution.py:69
  249.6 5.2 %collective-permute-start.19 = (bf16[2,2,128,128]{3,2,1,0:T(8,128)(2,1)S(1)}, bf16[2,2,128,128]{3,2,1,0:T(8,128)(2,1)S(1)}, u32[]{:S(2)}, u32[]{:S(2)}) collective-permute-start(bf16[2,2,128,128]{3,2,1,0:T(8,128)(2,1)S(1)} %get-tuple-element.21), channel_id=1, source_target_pairs={{0,1},{1,2},{2,3},{3,0},{4,5},{5,6},{6,7},{7,4},{8,9},{9,10},{10,1... | collective-permute-start | bytes 393224 | tf_op jit(solution)/shard_map/ppermute | solution.py:77
  254.9 4.3 %collective-permute-start.18 = (bf16[2,2,128,128]{3,2,1,0:T(8,128)(2,1)S(1)}, bf16[2,2,128,128]{3,2,1,0:T(8,128)(2,1)S(1)}, u32[]{:S(2)}, u32[]{:S(2)}) collective-permute-start(bf16[2,2,128,128]{3,2,1,0:T(8,128)(2,1)S(1)} %get-tuple-element.22), channel_id=1, source_target_pairs={{0,2},{1,3},{2,0},{3,1},{4,6},{5,7},{6,4},{7,5},{8,10},{9,11},{10,... | collective-permute-start | bytes 393224 | tf_op jit(solution)/shard_map/ppermute | solution.py:77
  259.2 3.4 %collective-permute-start.17 = (bf16[2,2,128,128]{3,2,1,0:T(8,128)(2,1)S(1)}, bf16[2,2,128,128]{3,2,1,0:T(8,128)(2,1)S(1)}, u32[]{:S(2)}, u32[]{:S(2)}) collective-permute-start(bf16[2,2,128,128]{3,2,1,0:T(8,128)(2,1)S(1)} %get-tuple-element.20), channel_id=1, source_target_pairs={{0,3},{1,0},{2,1},{3,2},{4,7},{5,4},{6,5},{7,6},{8,11},{9,8},{10,9... | collective-permute-start | bytes 393224 | tf_op jit(solution)/shard_map/ppermute | solution.py:77
  262.6 4.4 %collective-permute-done.18 = bf16[2,2,128,128]{3,2,1,0:T(8,128)(2,1)S(1)} collective-permute-done((bf16[2,2,128,128]{3,2,1,0:T(8,128)(2,1)S(1)}, bf16[2,2,128,128]{3,2,1,0:T(8,128)(2,1)S(1)}, u32[]{:S(2)}, u32[]{:S(2)}) %collective-permute-start.18) | collective-permute-done | bytes 131104 | tf_op jit(solution)/shard_map/ppermute | solution.py:77
  267.0 3.7 %collective-permute-done.17 = bf16[2,2,128,128]{3,2,1,0:T(8,128)(2,1)S(1)} collective-permute-done((bf16[2,2,128,128]{3,2,1,0:T(8,128)(2,1)S(1)}, bf16[2,2,128,128]{3,2,1,0:T(8,128)(2,1)S(1)}, u32[]{:S(2)}, u32[]{:S(2)}) %collective-permute-start.17) | collective-permute-done | bytes 131104 | tf_op jit(solution)/shard_map/ppermute | solution.py:77
  271.5 2.4 copy.67
  (92 shorter events, 39.1 us)
Async XLA Ops:
  0.6 52.3 %copy-start = (s32[64]{0:T(128)S(1)}, s32[64]{0:T(128)}, u32[]{:S(2)}) copy-start(s32[64]{0:T(128)} %param.11) | copy-start | bytes 772
  1.5 26.4 %collective-permute-start.2 = (bf16[2,2,128,128]{3,2,1,0:T(8,128)(2,1)S(1)}, bf16[2,2,128,128]{3,2,1,0:T(8,128)(2,1)S(1)}, u32[]{:S(2)}, u32[]{:S(2)}) collective-permute-start(bf16[2,2,128,128]{3,2,1,0:T(8,128)(2,1)S(1)} %get-tuple-element.26), channel_id=1, source_target_pairs={{0,3},{1,0},{2,1},{3,2},{4,7},{5,4},{6,5},{7,6},{8,11},{9,8},{10,9... | collective-permute-start | bytes 393224 | tf_op jit(solution)/shard_map/ppermute | solution.py:42
  12.5 15.5 %collective-permute-start.1 = (bf16[2,2,128,128]{3,2,1,0:T(8,128)(2,1)S(1)}, bf16[2,2,128,128]{3,2,1,0:T(8,128)(2,1)S(1)}, u32[]{:S(2)}, u32[]{:S(2)}) collective-permute-start(bf16[2,2,128,128]{3,2,1,0:T(8,128)(2,1)S(1)} %get-tuple-element.26), channel_id=1, source_target_pairs={{0,2},{1,3},{2,0},{3,1},{4,6},{5,7},{6,4},{7,5},{8,10},{9,11},{10,... | collective-permute-start | bytes 393224 | tf_op jit(solution)/shard_map/ppermute | solution.py:42
  14.4 13.5 %collective-permute-start = (bf16[2,2,128,128]{3,2,1,0:T(8,128)(2,1)S(1)}, bf16[2,2,128,128]{3,2,1,0:T(8,128)(2,1)S(1)}, u32[]{:S(2)}, u32[]{:S(2)}) collective-permute-start(bf16[2,2,128,128]{3,2,1,0:T(8,128)(2,1)S(1)} %get-tuple-element.26), channel_id=1, source_target_pairs={{0,1},{1,2},{2,3},{3,0},{4,5},{5,6},{6,7},{7,4},{8,9},{9,10},{10,1... | collective-permute-start | bytes 393224 | tf_op jit(solution)/shard_map/ppermute | solution.py:42
  22.1 42.1 %copy-start.2 = (s32[64]{0:T(128)S(1)}, s32[64]{0:T(128)}, u32[]{:S(2)}) copy-start(s32[64]{0:T(128)} %param.9) | copy-start | bytes 772
  22.1 81.4 %all-to-all-start = ((bf16[16,2,128,256]{2,3,1,0:T(8,128)(2,1)}), bf16[16,2,128,256]{2,3,1,0:T(8,128)(2,1)}, u32[]{:S(2)}, u32[]{:S(2)}) async-start(bf16[16,2,128,256]{2,3,1,0:T(8,128)(2,1)} %broadcast_in_dim.6), calls=%async_computation | async-start | bytes 4194304 | tf_op jit(solution)/shard_map/all_to_all | solution.py:22
  28.0 17.6 %collective-permute-start.3 = (bf16[4,2,2,128,128]{4,3,2,1,0:T(8,128)(2,1)S(1)}, bf16[4,2,2,128,128]{4,3,2,1,0:T(8,128)(2,1)S(1)}, u32[]{:S(2)}, u32[]{:S(2)}) collective-permute-start(bf16[4,2,2,128,128]{4,3,2,1,0:T(8,128)(2,1)S(1)} %pad_maximum_fusion), channel_id=1, source_target_pairs={{0,4},{1,5},{2,6},{3,7},{4,8},{5,9},{6,10},{7,11},{8,12},{9,13},{1... | collective-permute-start | bytes 1572872 | tf_op jit(solution)/shard_map/ppermute | solution.py:48
  45.7 16.7 %collective-permute-start.4 = (bf16[4,2,2,128,128]{4,3,2,1,0:T(8,128)(2,1)S(1)}, bf16[4,2,2,128,128]{4,3,2,1,0:T(8,128)(2,1)S(1)}, u32[]{:S(2)}, u32[]{:S(2)}) collective-permute-start(bf16[4,2,2,128,128]{4,3,2,1,0:T(8,128)(2,1)S(1)} %collective-permute-done.3), channel_id=1, source_target_pairs={{0,4},{1,5},{2,6},{3,7},{4,8},{5,9},{6,10},{7,11},{8,12},{9,13},{1... | collective-permute-start | bytes 1572872 | tf_op jit(solution)/shard_map/ppermute | solution.py:48
  47.8 17.4 %collective-permute-start.7 = (bf16[4,2,2,128,128]{4,3,2,1,0:T(8,128)(2,1)S(1)}, bf16[4,2,2,128,128]{4,3,2,1,0:T(8,128)(2,1)S(1)}, u32[]{:S(2)}, u32[]{:S(2)}) collective-permute-start(bf16[4,2,2,128,128]{4,3,2,1,0:T(8,128)(2,1)S(1)} %pad_maximum_fusion), channel_id=1, source_target_pairs={{0,28},{1,29},{2,30},{3,31},{4,0},{5,1},{6,2},{7,3},{8,4},{9,5},{1... | collective-permute-start | bytes 1572872 | tf_op jit(solution)/shard_map/ppermute | solution.py:51
  62.3 15.8 %collective-permute-start.5 = (bf16[4,2,2,128,128]{4,3,2,1,0:T(8,128)(2,1)S(1)}, bf16[4,2,2,128,128]{4,3,2,1,0:T(8,128)(2,1)S(1)}, u32[]{:S(2)}, u32[]{:S(2)}) collective-permute-start(bf16[4,2,2,128,128]{4,3,2,1,0:T(8,128)(2,1)S(1)} %collective-permute-done.4), channel_id=1, source_target_pairs={{0,4},{1,5},{2,6},{3,7},{4,8},{5,9},{6,10},{7,11},{8,12},{9,13},{1... | collective-permute-start | bytes 1572872 | tf_op jit(solution)/shard_map/ppermute | solution.py:48
  65.1 15.0 %collective-permute-start.8 = (bf16[4,2,2,128,128]{4,3,2,1,0:T(8,128)(2,1)S(1)}, bf16[4,2,2,128,128]{4,3,2,1,0:T(8,128)(2,1)S(1)}, u32[]{:S(2)}, u32[]{:S(2)}) collective-permute-start(bf16[4,2,2,128,128]{4,3,2,1,0:T(8,128)(2,1)S(1)} %collective-permute-done.7), channel_id=1, source_target_pairs={{0,28},{1,29},{2,30},{3,31},{4,0},{5,1},{6,2},{7,3},{8,4},{9,5},{1... | collective-permute-start | bytes 1572872 | tf_op jit(solution)/shard_map/ppermute | solution.py:51
  78.1 14.9 %collective-permute-start.6 = (bf16[4,2,2,128,128]{4,3,2,1,0:T(8,128)(2,1)S(1)}, bf16[4,2,2,128,128]{4,3,2,1,0:T(8,128)(2,1)S(1)}, u32[]{:S(2)}, u32[]{:S(2)}) collective-permute-start(bf16[4,2,2,128,128]{4,3,2,1,0:T(8,128)(2,1)S(1)} %collective-permute-done.5), channel_id=1, source_target_pairs={{0,4},{1,5},{2,6},{3,7},{4,8},{5,9},{6,10},{7,11},{8,12},{9,13},{1... | collective-permute-start | bytes 1572872 | tf_op jit(solution)/shard_map/ppermute | solution.py:48
  80.2 14.6 %collective-permute-start.9 = (bf16[4,2,2,128,128]{4,3,2,1,0:T(8,128)(2,1)S(1)}, bf16[4,2,2,128,128]{4,3,2,1,0:T(8,128)(2,1)S(1)}, u32[]{:S(2)}, u32[]{:S(2)}) collective-permute-start(bf16[4,2,2,128,128]{4,3,2,1,0:T(8,128)(2,1)S(1)} %collective-permute-done.8), channel_id=1, source_target_pairs={{0,28},{1,29},{2,30},{3,31},{4,0},{5,1},{6,2},{7,3},{8,4},{9,5},{1... | collective-permute-start | bytes 1572872 | tf_op jit(solution)/shard_map/ppermute | solution.py:51
  96.7 2.7 copy-start.3
  109.9 2.6 copy-start.6
  109.9 2.8 %copy-start.7 = (bf16[1,8,4,2,128,128]{5,4,3,0,2,1:T(8,128)(2,1)S(1)}, bf16[1,8,4,2,128,128]{5,4,3,0,2,1:T(8,128)(2,1)}, u32[]{:S(2)}) copy-start(bf16[1,8,4,2,128,128]{5,4,3,0,2,1:T(8,128)(2,1)} %get-tuple-element.14) | copy-start | bytes 6291460
  112.8 1.6 copy-start.5
  114.4 0.7 copy-start.9
  141.7 43.5 %all-to-all-start.1 = ((bf16[16,2,128,256]{3,2,1,0:T(8,128)(2,1)}), bf16[16,2,128,256]{3,2,1,0:T(8,128)(2,1)}, u32[]{:S(2)}, u32[]{:S(2)}) async-start(bf16[16,2,128,256]{3,2,1,0:T(8,128)(2,1)} %copy.88), calls=%async_computation.1 | async-start | bytes 4194304 | tf_op jit(solution)/shard_map/all_to_all | solution.py:26
  158.9 2.6 copy-start.10
  161.5 2.5 copy-start.8
  164.3 18.8 %copy-start.4 = (bf16[8,4,2,2,128,128]{5,4,3,2,1,0:T(8,128)(2,1)}, bf16[8,4,2,2,128,128]{5,4,3,2,1,0:T(8,128)(2,1)S(1)}, u32[]{:S(2)}) copy-start(bf16[8,4,2,2,128,128]{5,4,3,2,1,0:T(8,128)(2,1)S(1)} %maximum_bitcast_fusion) | copy-start | bytes 12582916
  165.3 17.8 %collective-permute-start.10 = (bf16[4,2,2,128,128]{4,3,2,1,0:T(8,128)(2,1)S(1)}, bf16[4,2,2,128,128]{4,3,2,1,0:T(8,128)(2,1)S(1)}, u32[]{:S(2)}, u32[]{:S(2)}) collective-permute-start(bf16[4,2,2,128,128]{4,3,2,1,0:T(8,128)(2,1)S(1)} %get-tuple-element.12), channel_id=1, source_target_pairs={{0,4},{1,5},{2,6},{3,7},{4,8},{5,9},{6,10},{7,11},{8,12},{9,13},{1... | collective-permute-start | bytes 1572872 | tf_op jit(solution)/shard_map/ppermute | solution.py:64
  183.3 16.6 %collective-permute-start.11 = (bf16[4,2,2,128,128]{4,3,2,1,0:T(8,128)(2,1)S(1)}, bf16[4,2,2,128,128]{4,3,2,1,0:T(8,128)(2,1)S(1)}, u32[]{:S(2)}, u32[]{:S(2)}) collective-permute-start(bf16[4,2,2,128,128]{4,3,2,1,0:T(8,128)(2,1)S(1)} %fusion.10), channel_id=1, source_target_pairs={{0,4},{1,5},{2,6},{3,7},{4,8},{5,9},{6,10},{7,11},{8,12},{9,13},{1... | collective-permute-start | bytes 1572872 | tf_op jit(solution)/shard_map/ppermute | solution.py:64
  188.7 82.7 %all-to-all-start.2 = ((bf16[16,2,128,256]{3,2,1,0:T(8,128)(2,1)}), bf16[16,2,128,256]{3,2,1,0:T(8,128)(2,1)S(1)}, u32[]{:S(2)}, u32[]{:S(2)}) async-start(bf16[16,2,128,256]{3,2,1,0:T(8,128)(2,1)} %broadcast_in_dim.8), calls=%async_computation.2 | async-start | bytes 4194304 | tf_op jit(solution)/shard_map/all_to_all | solution.py:22
  194.5 16.9 %collective-permute-start.14 = (bf16[4,2,2,128,128]{4,3,2,1,0:T(8,128)(2,1)}, bf16[4,2,2,128,128]{4,3,2,1,0:T(8,128)(2,1)S(1)}, u32[]{:S(2)}, u32[]{:S(2)}) collective-permute-start(bf16[4,2,2,128,128]{4,3,2,1,0:T(8,128)(2,1)} %get-tuple-element.13), channel_id=1, source_target_pairs={{0,28},{1,29},{2,30},{3,31},{4,0},{5,1},{6,2},{7,3},{8,4},{9,5},{1... | collective-permute-start | bytes 1572872 | tf_op jit(solution)/shard_map/ppermute | solution.py:69
  201.1 16.5 %collective-permute-start.12 = (bf16[4,2,2,128,128]{4,3,2,1,0:T(8,128)(2,1)S(1)}, bf16[4,2,2,128,128]{4,3,2,1,0:T(8,128)(2,1)S(1)}, u32[]{:S(2)}, u32[]{:S(2)}) collective-permute-start(bf16[4,2,2,128,128]{4,3,2,1,0:T(8,128)(2,1)S(1)} %fusion.11), channel_id=1, source_target_pairs={{0,4},{1,5},{2,6},{3,7},{4,8},{5,9},{6,10},{7,11},{8,12},{9,13},{1... | collective-permute-start | bytes 1572872 | tf_op jit(solution)/shard_map/ppermute | solution.py:64
  219.2 14.4 %collective-permute-start.15 = (bf16[4,2,2,128,128]{4,3,2,1,0:T(8,128)(2,1)S(1)}, bf16[4,2,2,128,128]{4,3,2,1,0:T(8,128)(2,1)S(1)}, u32[]{:S(2)}, u32[]{:S(2)}) collective-permute-start(bf16[4,2,2,128,128]{4,3,2,1,0:T(8,128)(2,1)S(1)} %get-tuple-element.11), channel_id=1, source_target_pairs={{0,28},{1,29},{2,30},{3,31},{4,0},{5,1},{6,2},{7,3},{8,4},{9,5},{1... | collective-permute-start | bytes 1572872 | tf_op jit(solution)/shard_map/ppermute | solution.py:69
  221.1 17.2 %collective-permute-start.13 = (bf16[4,2,2,128,128]{4,3,2,1,0:T(8,128)(2,1)S(1)}, bf16[4,2,2,128,128]{4,3,2,1,0:T(8,128)(2,1)S(1)}, u32[]{:S(2)}, u32[]{:S(2)}) collective-permute-start(bf16[4,2,2,128,128]{4,3,2,1,0:T(8,128)(2,1)S(1)} %get-tuple-element.10), channel_id=1, source_target_pairs={{0,4},{1,5},{2,6},{3,7},{4,8},{5,9},{6,10},{7,11},{8,12},{9,13},{1... | collective-permute-start | bytes 1572872 | tf_op jit(solution)/shard_map/ppermute | solution.py:64
  234.8 13.5 %collective-permute-start.16 = (bf16[4,2,2,128,128]{4,3,2,1,0:T(8,128)(2,1)S(1)}, bf16[4,2,2,128,128]{4,3,2,1,0:T(8,128)(2,1)S(1)}, u32[]{:S(2)}, u32[]{:S(2)}) collective-permute-start(bf16[4,2,2,128,128]{4,3,2,1,0:T(8,128)(2,1)S(1)} %fusion.9), channel_id=1, source_target_pairs={{0,28},{1,29},{2,30},{3,31},{4,0},{5,1},{6,2},{7,3},{8,4},{9,5},{1... | collective-permute-start | bytes 1572872 | tf_op jit(solution)/shard_map/ppermute | solution.py:69
  249.6 13.0 %collective-permute-start.19 = (bf16[2,2,128,128]{3,2,1,0:T(8,128)(2,1)S(1)}, bf16[2,2,128,128]{3,2,1,0:T(8,128)(2,1)S(1)}, u32[]{:S(2)}, u32[]{:S(2)}) collective-permute-start(bf16[2,2,128,128]{3,2,1,0:T(8,128)(2,1)S(1)} %get-tuple-element.21), channel_id=1, source_target_pairs={{0,1},{1,2},{2,3},{3,0},{4,5},{5,6},{6,7},{7,4},{8,9},{9,10},{10,1... | collective-permute-start | bytes 393224 | tf_op jit(solution)/shard_map/ppermute | solution.py:77
  254.9 12.2 %collective-permute-start.18 = (bf16[2,2,128,128]{3,2,1,0:T(8,128)(2,1)S(1)}, bf16[2,2,128,128]{3,2,1,0:T(8,128)(2,1)S(1)}, u32[]{:S(2)}, u32[]{:S(2)}) collective-permute-start(bf16[2,2,128,128]{3,2,1,0:T(8,128)(2,1)S(1)} %get-tuple-element.22), channel_id=1, source_target_pairs={{0,2},{1,3},{2,0},{3,1},{4,6},{5,7},{6,4},{7,5},{8,10},{9,11},{10,... | collective-permute-start | bytes 393224 | tf_op jit(solution)/shard_map/ppermute | solution.py:77
  259.2 11.5 %collective-permute-start.17 = (bf16[2,2,128,128]{3,2,1,0:T(8,128)(2,1)S(1)}, bf16[2,2,128,128]{3,2,1,0:T(8,128)(2,1)S(1)}, u32[]{:S(2)}, u32[]{:S(2)}) collective-permute-start(bf16[2,2,128,128]{3,2,1,0:T(8,128)(2,1)S(1)} %get-tuple-element.20), channel_id=1, source_target_pairs={{0,3},{1,0},{2,1},{3,2},{4,7},{5,4},{6,5},{7,6},{8,11},{9,8},{10,9... | collective-permute-start | bytes 393224 | tf_op jit(solution)/shard_map/ppermute | solution.py:77
  275.5 2.6 copy-start.1

commit v9 on v7

--- a/solution.py
+++ b/solution.py
@@ -54,7 +54,7 @@
     return jnp.stack(rel)
 
 
-def dp_scatter_rel(terms, n_y, n_z):
+def dp_scatter_rel(terms, n_y, n_z, ready=None):
     n_f, n_b = n_y // 2, (n_y - 1) // 2
     got_f = got_b = None
     for k in range(1, n_f + 1):
@@ -72,11 +72,13 @@
         acc = acc + got_f.astype(jnp.float32)
     if got_b is not None:
         acc = acc + got_b.astype(jnp.float32)
+    if ready is not None:
+        acc, ready = lax.optimization_barrier((acc, ready))
     total = acc[0]
     for b in range(1, n_z):
         sent = lax.ppermute(acc[b].astype(jnp.bfloat16), "dp", dp_shift(n_y, n_z, 0, -b))
         total = total + sent.astype(jnp.float32)
-    return total.astype(jnp.bfloat16)
+    return total.astype(jnp.bfloat16), ready
 
 
 def per_device(activations, out_grad, up_blocks, up_rows, down_blocks, down_rows):
@@ -149,11 +151,12 @@
     mine = scatter_sum(parts, "tensor")
     both = gather_all(mine, "tensor")
     both = jnp.moveaxis(both, 0, 2).reshape(2, tokens, width)
+    outs = (both[0], both[1])
 
     terms = jnp.stack([up_term, down_term]).astype(jnp.bfloat16)
     terms = terms.reshape(2, n_y, n_z, per_dev, block_size, block_size)
-    grads = dp_scatter_rel(jnp.moveaxis(terms, 0, 2), n_y, n_z)
-    return (both[0], both[1], grads[0], grads[1])
+    grads, outs = dp_scatter_rel(jnp.moveaxis(terms, 0, 2), n_y, n_z, outs)
+    return (outs[0], outs[1], grads[0], grads[1])
 
 
 def solution(mesh):

time: 274 us -> 274 us (level)
  local copies, waits for them, and re-layouts: 55.1 us -> 52 us
  waiting for transfers between devices: 94.5 us -> 97.3 us
    all_to_all x1, waiting for transfers between devices: 0.01 us -> 10.1 us  [scatter_sum(): got = lax.all_to_all(x, axis_name, 0, 0, tiled=True)]
    ppermute x3, waiting for transfers between devices: 27.4 us -> 18.7 us  [dp_scatter_rel(): lax.ppermute(part.astype(jnp.bfloat16), 'dp', dp_shift(n_y, n_z, -1, 0))]
    slice x3 -> x2, local copies, waits for them, and re-layouts: 10.9 us -> 4.38 us  [per_device(): up_all, down_all = (weights[0], weights[1])]
    another operation x0 -> x1, local copies, waits for them, and re-layouts: none -> 4.67 us  [per_device(): down_tiles = down_all.reshape(groups, K, block_size, block_size)]
    ppermute x4, waiting for transfers between devices: 21.5 us -> 24.9 us  [dp_scatter_rel(): lax.ppermute(part.astype(jnp.bfloat16), 'dp', dp_shift(n_y, n_z, 1, 0))]
    gather x3 -> x2, local copies, waits for them, and re-layouts: 7.72 us -> 5.25 us  [per_device(): full_grad.reshape(tokens, row_blocks, block_size)[:, down_index]]
    unnamed x28 -> x32, local copies, waits for them, and re-layouts: 5.99 us -> 6.78 us
  transfers between devices with their start and end apart: 23 -> 23, of which waited for: 16 -> 15; matrix products, arithmetic and copies ran while one was open for 17% -> 17% of each run, Pallas kernels for 0% -> 0%
where the time goes in v9:
time: 274 us; the launch traced here: 271 us
  waiting for transfers between devices  97.3 us (36%)
  starting transfers between devices  93.6 us (34%)
  local copies, waits for them, and re-layouts  52 us (19%)
  other arithmetic  13.5 us (5%)
  matrix products  13.2 us (5%)
    ppermute x4, waiting for transfers between devices, dp_gather_rel(): cur_f = lax.ppermute(cur_f, 'dp', dp_shift(n_y, n_z, 1, 0))  36.2 us
    ppermute x4, waiting for transfers between devices, dp_scatter_rel(): lax.ppermute(part.astype(jnp.bfloat16), 'dp', dp_shift(n_y, n_z, 1, 0))  24.9 us
    ppermute x3, starting transfers between devices, dp_gather_rel(): lax.ppermute(x, 'dp', dp_shift(n_y, n_z, 0, b))  18.9 us
    ppermute x3, waiting for transfers between devices, dp_scatter_rel(): lax.ppermute(part.astype(jnp.bfloat16), 'dp', dp_shift(n_y, n_z, -1, 0))  18.7 us
    ppermute x3, starting transfers between devices, dp_gather_rel(): cur_b = lax.ppermute(cur_b, 'dp', dp_shift(n_y, n_z, -1, 0))  16 us
    ppermute x3, starting transfers between devices, dp_scatter_rel(): lax.ppermute(acc[b].astype(jnp.bfloat16), 'dp', dp_shift(n_y, n_z, 0, -b))  11.5 us
    ppermute x4, starting transfers between devices, dp_scatter_rel(): lax.ppermute(part.astype(jnp.bfloat16), 'dp', dp_shift(n_y, n_z, 1, 0))  11.1 us
    all_to_all x2, starting transfers between devices, gather_all(): return lax.all_to_all(spread, axis_name, 0, 0, tiled=True)  10.7 us
  transfers between devices with their start and end apart: 23, of which 15 were waited for; matrix products, arithmetic and copies ran while one was open for 17% of the time, Pallas kernels for 0%

profile of v9, /device:TPU:6, one launch (start us, length us, event | category | flops | bytes accessed | tf_op | source)
XLA Modules:
  0.0 270.9 jit_solution(7970588070629181838)
XLA Ops:
  1.5 6.1 %collective-permute-start = (bf16[2,2,128,128]{3,2,1,0:T(8,128)(2,1)S(1)}, bf16[2,2,128,128]{3,2,1,0:T(8,128)(2,1)S(1)}, u32[]{:S(2)}, u32[]{:S(2)}) collective-permute-start(bf16[2,2,128,128]{3,2,1,0:T(8,128)(2,1)S(1)} %get-tuple-element.30), channel_id=1, source_target_pairs={{0,1},{1,2},{2,3},{3,0},{4,5},{5,6},{6,7},{7,4},{8,9},{9,10},{10,1... | collective-permute-start | bytes 393224 | tf_op jit(solution)/shard_map/ppermute | solution.py:42
  7.6 9.1 %collective-permute-start.1 = (bf16[2,2,128,128]{3,2,1,0:T(8,128)(2,1)S(1)}, bf16[2,2,128,128]{3,2,1,0:T(8,128)(2,1)S(1)}, u32[]{:S(2)}, u32[]{:S(2)}) collective-permute-start(bf16[2,2,128,128]{3,2,1,0:T(8,128)(2,1)S(1)} %get-tuple-element.30), channel_id=1, source_target_pairs={{0,2},{1,3},{2,0},{3,1},{4,6},{5,7},{6,4},{7,5},{8,10},{9,11},{10,... | collective-permute-start | bytes 393224 | tf_op jit(solution)/shard_map/ppermute | solution.py:42
  16.8 3.7 %collective-permute-start.2 = (bf16[2,2,128,128]{3,2,1,0:T(8,128)(2,1)S(1)}, bf16[2,2,128,128]{3,2,1,0:T(8,128)(2,1)S(1)}, u32[]{:S(2)}, u32[]{:S(2)}) collective-permute-start(bf16[2,2,128,128]{3,2,1,0:T(8,128)(2,1)S(1)} %get-tuple-element.30), channel_id=1, source_target_pairs={{0,3},{1,0},{2,1},{3,2},{4,7},{5,4},{6,5},{7,6},{8,11},{9,8},{10,9... | collective-permute-start | bytes 393224 | tf_op jit(solution)/shard_map/ppermute | solution.py:42
  21.5 1.9 broadcast_in_dim.4
  23.3 5.8 %all-to-all-start = ((bf16[16,2,128,256]{2,3,1,0:T(8,128)(2,1)}), bf16[16,2,128,256]{2,3,1,0:T(8,128)(2,1)}, u32[]{:S(2)}, u32[]{:S(2)}) async-start(bf16[16,2,128,256]{2,3,1,0:T(8,128)(2,1)} %broadcast_in_dim.4), calls=%async_computation | async-start | bytes 4194304 | tf_op jit(solution)/shard_map/all_to_all | solution.py:22
  29.4 3.5 %collective-permute-start.3 = (bf16[4,2,2,128,128]{4,3,2,1,0:T(8,128)(2,1)S(1)}, bf16[4,2,2,128,128]{4,3,2,1,0:T(8,128)(2,1)S(1)}, u32[]{:S(2)}, u32[]{:S(2)}) collective-permute-start(bf16[4,2,2,128,128]{4,3,2,1,0:T(8,128)(2,1)S(1)} %pad_maximum_fusion.1), channel_id=1, source_target_pairs={{0,4},{1,5},{2,6},{3,7},{4,8},{5,9},{6,10},{7,11},{8,12},{9,13},{1... | collective-permute-start | bytes 1572872 | tf_op jit(solution)/shard_map/ppermute | solution.py:48
  33.0 13.9 %collective-permute-done.3 = bf16[4,2,2,128,128]{4,3,2,1,0:T(8,128)(2,1)S(1)} collective-permute-done((bf16[4,2,2,128,128]{4,3,2,1,0:T(8,128)(2,1)S(1)}, bf16[4,2,2,128,128]{4,3,2,1,0:T(8,128)(2,1)S(1)}, u32[]{:S(2)}, u32[]{:S(2)}) %collective-permute-start.3) | collective-permute-done | bytes 524320 | tf_op jit(solution)/shard_map/ppermute | solution.py:48
  46.9 1.9 collective-permute-start.4
  49.0 5.1 %collective-permute-start.7 = (bf16[4,2,2,128,128]{4,3,2,1,0:T(8,128)(2,1)S(1)}, bf16[4,2,2,128,128]{4,3,2,1,0:T(8,128)(2,1)S(1)}, u32[]{:S(2)}, u32[]{:S(2)}) collective-permute-start(bf16[4,2,2,128,128]{4,3,2,1,0:T(8,128)(2,1)S(1)} %pad_maximum_fusion.1), channel_id=1, source_target_pairs={{0,28},{1,29},{2,30},{3,31},{4,0},{5,1},{6,2},{7,3},{8,4},{9,5},{1... | collective-permute-start | bytes 1572872 | tf_op jit(solution)/shard_map/ppermute | solution.py:51
  55.0 8.4 %collective-permute-done.4 = bf16[4,2,2,128,128]{4,3,2,1,0:T(8,128)(2,1)S(1)} collective-permute-done((bf16[4,2,2,128,128]{4,3,2,1,0:T(8,128)(2,1)S(1)}, bf16[4,2,2,128,128]{4,3,2,1,0:T(8,128)(2,1)S(1)}, u32[]{:S(2)}, u32[]{:S(2)}) %collective-permute-start.4) | collective-permute-done | bytes 524320 | tf_op jit(solution)/shard_map/ppermute | solution.py:48
  63.4 1.9 collective-permute-start.5
  66.2 5.1 %collective-permute-start.8 = (bf16[4,2,2,128,128]{4,3,2,1,0:T(8,128)(2,1)S(1)}, bf16[4,2,2,128,128]{4,3,2,1,0:T(8,128)(2,1)S(1)}, u32[]{:S(2)}, u32[]{:S(2)}) collective-permute-start(bf16[4,2,2,128,128]{4,3,2,1,0:T(8,128)(2,1)S(1)} %collective-permute-done.7), channel_id=1, source_target_pairs={{0,28},{1,29},{2,30},{3,31},{4,0},{5,1},{6,2},{7,3},{8,4},{9,5},{1... | collective-permute-start | bytes 1572872 | tf_op jit(solution)/shard_map/ppermute | solution.py:51
  71.7 7.3 %collective-permute-done.5 = bf16[4,2,2,128,128]{4,3,2,1,0:T(8,128)(2,1)S(1)} collective-permute-done((bf16[4,2,2,128,128]{4,3,2,1,0:T(8,128)(2,1)S(1)}, bf16[4,2,2,128,128]{4,3,2,1,0:T(8,128)(2,1)S(1)}, u32[]{:S(2)}, u32[]{:S(2)}) %collective-permute-start.5) | collective-permute-done | bytes 524320 | tf_op jit(solution)/shard_map/ppermute | solution.py:48
  79.0 1.9 collective-permute-start.6
  81.1 5.8 %collective-permute-start.9 = (bf16[4,2,2,128,128]{4,3,2,1,0:T(8,128)(2,1)S(1)}, bf16[4,2,2,128,128]{4,3,2,1,0:T(8,128)(2,1)S(1)}, u32[]{:S(2)}, u32[]{:S(2)}) collective-permute-start(bf16[4,2,2,128,128]{4,3,2,1,0:T(8,128)(2,1)S(1)} %collective-permute-done.8), channel_id=1, source_target_pairs={{0,28},{1,29},{2,30},{3,31},{4,0},{5,1},{6,2},{7,3},{8,4},{9,5},{1... | collective-permute-start | bytes 1572872 | tf_op jit(solution)/shard_map/ppermute | solution.py:51
  87.0 6.7 %collective-permute-done.6 = bf16[4,2,2,128,128]{4,3,2,1,0:T(8,128)(2,1)S(1)} collective-permute-done((bf16[4,2,2,128,128]{4,3,2,1,0:T(8,128)(2,1)S(1)}, bf16[4,2,2,128,128]{4,3,2,1,0:T(8,128)(2,1)S(1)}, u32[]{:S(2)}, u32[]{:S(2)}) %collective-permute-start.6) | collective-permute-done | bytes 524320 | tf_op jit(solution)/shard_map/ppermute | solution.py:48
  97.5 4.7 %copy.64 = bf16[8,8,128,128]{2,1,0,3:T(8,128)(2,1)} copy(bf16[8,8,128,128]{3,2,1,0:T(8,128)(2,1)} %bitcast.180) | data formatting | bytes 4194304 | tf_op jit(solution)/shard_map/reshape;squeeze | solution.py:116
  102.2 2.6 copy.58
  104.8 4.1 %copy.66 = bf16[8,8,128,128]{3,1,0,2:T(8,128)(2,1)} copy(bf16[8,8,128,128]{2,3,1,0:T(8,128)(2,1)} %bitcast.179) | data formatting | bytes 4194304 | tf_op jit(solution)/shard_map/reshape;squeeze | solution.py:115
  113.4 2.5 convolution_bitcast_fusion
  121.4 2.2 gather_fusion.3
  123.6 3.2 %fusion.3 = bf16[128,8,128]{0,2,1:T(8,128)(2,1)S(1)} fusion(bf16[8,8,128,128]{3,2,1,0:T(8,128)(2,1)} %bitcast.181, bf16[128,8,8,128]{3,0,2,1:T(8,128)(2,1)} %bitcast.173, f32[128,8,128]{0,2,1:T(8,128)} %copy-done.9), kind=kOutput, calls=%fused_computation.16 | convolution fusion | flops 269746176 | bytes 4980736 | tf_op jit(solution)/shard_map/tgko,gkho->tgh/dot_general | solution.py:134
  132.0 5.9 %all-to-all-start.1 = ((bf16[16,2,128,256]{2,3,1,0:T(8,128)(2,1)}), bf16[16,2,128,256]{2,3,1,0:T(8,128)(2,1)}, u32[]{:S(2)}, u32[]{:S(2)}) async-start(bf16[16,2,128,256]{2,3,1,0:T(8,128)(2,1)} %bitcast.175), calls=%async_computation.1 | async-start | bytes 4194304 | tf_op jit(solution)/shard_map/all_to_all | solution.py:26
  137.9 2.6 copy.54
  140.5 3.1 %copy.56 = bf16[8,8,128,128]{2,3,1,0:T(8,128)(2,1)S(1)} copy(bf16[8,8,128,128]{3,2,1,0:T(8,128)(2,1)} %bitcast.174) | data formatting | bytes 4194304 | tf_op jit(solution)/shard_map/gather | solution.py:129
  143.6 2.1 multiply_convert_fusion
  145.7 4.1 %copy.63 = bf16[1,8,4,2,128,128]{5,4,3,0,2,1:T(8,128)(2,1)} copy(bf16[1,8,4,2,128,128]{4,5,3,2,1,0:T(8,128)(2,1)} %bitcast.178) | data formatting | bytes 4194304 | tf_op jit(solution)/shard_map/stack | solution.py:156
  151.7 2.0 copy-done.4
  154.6 2.7 %collective-permute-start.10 = (bf16[4,2,2,128,128]{4,3,2,1,0:T(8,128)(2,1)}, bf16[4,2,2,128,128]{4,3,2,1,0:T(8,128)(2,1)S(1)}, u32[]{:S(2)}, u32[]{:S(2)}) collective-permute-start(bf16[4,2,2,128,128]{4,3,2,1,0:T(8,128)(2,1)} %get-tuple-element.16), channel_id=1, source_target_pairs={{0,4},{1,5},{2,6},{3,7},{4,8},{5,9},{6,10},{7,11},{8,12},{9,13},{1... | collective-permute-start | bytes 1572872 | tf_op jit(solution)/shard_map/ppermute | solution.py:64
  157.3 10.1 %all-to-all-done.1 = bf16[16,2,128,256]{2,3,1,0:T(8,128)(2,1)} async-done(((bf16[16,2,128,256]{2,3,1,0:T(8,128)(2,1)}), bf16[16,2,128,256]{2,3,1,0:T(8,128)(2,1)}, u32[]{:S(2)}, u32[]{:S(2)}) %all-to-all-start.1) | async-done | bytes 2097184 | tf_op jit(solution)/shard_map/all_to_all | solution.py:26
  167.4 1.9 reduce_sum.12
  171.0 4.9 %all-to-all-start.2 = ((bf16[16,2,128,256]{3,2,1,0:T(8,128)(2,1)}), bf16[16,2,128,256]{3,2,1,0:T(8,128)(2,1)S(1)}, u32[]{:S(2)}, u32[]{:S(2)}) async-start(bf16[16,2,128,256]{3,2,1,0:T(8,128)(2,1)} %broadcast_in_dim.5), calls=%async_computation.2 | async-start | bytes 4194304 | tf_op jit(solution)/shard_map/all_to_all | solution.py:22
  177.1 2.7 %collective-permute-start.11 = (bf16[4,2,2,128,128]{4,3,2,1,0:T(8,128)(2,1)S(1)}, bf16[4,2,2,128,128]{4,3,2,1,0:T(8,128)(2,1)S(1)}, u32[]{:S(2)}, u32[]{:S(2)}) collective-permute-start(bf16[4,2,2,128,128]{4,3,2,1,0:T(8,128)(2,1)S(1)} %fusion.6), channel_id=1, source_target_pairs={{0,4},{1,5},{2,6},{3,7},{4,8},{5,9},{6,10},{7,11},{8,12},{9,13},{1... | collective-permute-start | bytes 1572872 | tf_op jit(solution)/shard_map/ppermute | solution.py:64
  179.9 4.8 %collective-permute-start.14 = (bf16[4,2,2,128,128]{4,3,2,1,0:T(8,128)(2,1)S(1)}, bf16[4,2,2,128,128]{4,3,2,1,0:T(8,128)(2,1)S(1)}, u32[]{:S(2)}, u32[]{:S(2)}) collective-permute-start(bf16[4,2,2,128,128]{4,3,2,1,0:T(8,128)(2,1)S(1)} %get-tuple-element.17), channel_id=1, source_target_pairs={{0,28},{1,29},{2,30},{3,31},{4,0},{5,1},{6,2},{7,3},{8,4},{9,5},{1... | collective-permute-start | bytes 1572872 | tf_op jit(solution)/shard_map/ppermute | solution.py:69
  184.7 10.3 %collective-permute-done.11 = bf16[4,2,2,128,128]{4,3,2,1,0:T(8,128)(2,1)S(1)} collective-permute-done((bf16[4,2,2,128,128]{4,3,2,1,0:T(8,128)(2,1)S(1)}, bf16[4,2,2,128,128]{4,3,2,1,0:T(8,128)(2,1)S(1)}, u32[]{:S(2)}, u32[]{:S(2)}) %collective-permute-start.11) | collective-permute-done | bytes 524320 | tf_op jit(solution)/shard_map/ppermute | solution.py:64
  196.2 1.9 collective-permute-start.12
  198.2 14.6 %collective-permute-done.12 = bf16[4,2,2,128,128]{4,3,2,1,0:T(8,128)(2,1)S(1)} collective-permute-done((bf16[4,2,2,128,128]{4,3,2,1,0:T(8,128)(2,1)S(1)}, bf16[4,2,2,128,128]{4,3,2,1,0:T(8,128)(2,1)S(1)}, u32[]{:S(2)}, u32[]{:S(2)}) %collective-permute-start.12) | collective-permute-done | bytes 524320 | tf_op jit(solution)/shard_map/ppermute | solution.py:64
  214.3 2.1 collective-permute-start.15
  216.5 3.7 %collective-permute-start.13 = (bf16[4,2,2,128,128]{4,3,2,1,0:T(8,128)(2,1)S(1)}, bf16[4,2,2,128,128]{4,3,2,1,0:T(8,128)(2,1)S(1)}, u32[]{:S(2)}, u32[]{:S(2)}) collective-permute-start(bf16[4,2,2,128,128]{4,3,2,1,0:T(8,128)(2,1)S(1)} %get-tuple-element.14), channel_id=1, source_target_pairs={{0,4},{1,5},{2,6},{3,7},{4,8},{5,9},{6,10},{7,11},{8,12},{9,13},{1... | collective-permute-start | bytes 1572872 | tf_op jit(solution)/shard_map/ppermute | solution.py:64
  220.2 8.6 %collective-permute-done.15 = bf16[4,2,2,128,128]{4,3,2,1,0:T(8,128)(2,1)S(1)} collective-permute-done((bf16[4,2,2,128,128]{4,3,2,1,0:T(8,128)(2,1)S(1)}, bf16[4,2,2,128,128]{4,3,2,1,0:T(8,128)(2,1)S(1)}, u32[]{:S(2)}, u32[]{:S(2)}) %collective-permute-start.15) | collective-permute-done | bytes 524320 | tf_op jit(solution)/shard_map/ppermute | solution.py:69
  230.0 3.4 %collective-permute-start.16 = (bf16[4,2,2,128,128]{4,3,2,1,0:T(8,128)(2,1)S(1)}, bf16[4,2,2,128,128]{4,3,2,1,0:T(8,128)(2,1)S(1)}, u32[]{:S(2)}, u32[]{:S(2)}) collective-permute-start(bf16[4,2,2,128,128]{4,3,2,1,0:T(8,128)(2,1)S(1)} %fusion.5), channel_id=1, source_target_pairs={{0,28},{1,29},{2,30},{3,31},{4,0},{5,1},{6,2},{7,3},{8,4},{9,5},{1... | collective-permute-start | bytes 1572872 | tf_op jit(solution)/shard_map/ppermute | solution.py:69
  233.5 10.1 %collective-permute-done.16 = bf16[4,2,2,128,128]{4,3,2,1,0:T(8,128)(2,1)S(1)} collective-permute-done((bf16[4,2,2,128,128]{4,3,2,1,0:T(8,128)(2,1)S(1)}, bf16[4,2,2,128,128]{4,3,2,1,0:T(8,128)(2,1)S(1)}, u32[]{:S(2)}, u32[]{:S(2)}) %collective-permute-start.16) | collective-permute-done | bytes 524320 | tf_op jit(solution)/shard_map/ppermute | solution.py:69
  244.9 2.4 copy.71
  249.7 4.6 %collective-permute-start.17 = (bf16[2,2,128,128]{3,2,1,0:T(8,128)(2,1)}, bf16[2,2,128,128]{3,2,1,0:T(8,128)(2,1)S(1)}, u32[]{:S(2)}, u32[]{:S(2)}) collective-permute-start(bf16[2,2,128,128]{3,2,1,0:T(8,128)(2,1)} %get-tuple-element.24), channel_id=1, source_target_pairs={{0,3},{1,0},{2,1},{3,2},{4,7},{5,4},{6,5},{7,6},{8,11},{9,8},{10,9... | collective-permute-start | bytes 393224 | tf_op jit(solution)/shard_map/ppermute | solution.py:79
  254.3 3.9 %collective-permute-start.18 = (bf16[2,2,128,128]{3,2,1,0:T(8,128)(2,1)}, bf16[2,2,128,128]{3,2,1,0:T(8,128)(2,1)S(1)}, u32[]{:S(2)}, u32[]{:S(2)}) collective-permute-start(bf16[2,2,128,128]{3,2,1,0:T(8,128)(2,1)} %get-tuple-element.26), channel_id=1, source_target_pairs={{0,2},{1,3},{2,0},{3,1},{4,6},{5,7},{6,4},{7,5},{8,10},{9,11},{10,... | collective-permute-start | bytes 393224 | tf_op jit(solution)/shard_map/ppermute | solution.py:79
  258.3 2.9 %collective-permute-start.19 = (bf16[2,2,128,128]{3,2,1,0:T(8,128)(2,1)S(1)}, bf16[2,2,128,128]{3,2,1,0:T(8,128)(2,1)}, u32[]{:S(2)}, u32[]{:S(2)}) collective-permute-start(bf16[2,2,128,128]{3,2,1,0:T(8,128)(2,1)S(1)} %get-tuple-element.25), channel_id=1, source_target_pairs={{0,1},{1,2},{2,3},{3,0},{4,5},{5,6},{6,7},{7,4},{8,9},{9,10},{10,1... | collective-permute-start | bytes 393224 | tf_op jit(solution)/shard_map/ppermute | solution.py:79
  264.2 2.1 collective-permute-done.18
  266.3 3.0 %collective-permute-done.19 = bf16[2,2,128,128]{3,2,1,0:T(8,128)(2,1)} collective-permute-done((bf16[2,2,128,128]{3,2,1,0:T(8,128)(2,1)S(1)}, bf16[2,2,128,128]{3,2,1,0:T(8,128)(2,1)}, u32[]{:S(2)}, u32[]{:S(2)}) %collective-permute-start.19) | collective-permute-done | bytes 131104 | tf_op jit(solution)/shard_map/ppermute | solution.py:79
  (95 shorter events, 41.8 us)
Async XLA Ops:
  0.6 53.5 %copy-start = (s32[64]{0:T(128)S(1)}, s32[64]{0:T(128)}, u32[]{:S(2)}) copy-start(s32[64]{0:T(128)} %param.9) | copy-start | bytes 772
  1.5 27.6 %collective-permute-start = (bf16[2,2,128,128]{3,2,1,0:T(8,128)(2,1)S(1)}, bf16[2,2,128,128]{3,2,1,0:T(8,128)(2,1)S(1)}, u32[]{:S(2)}, u32[]{:S(2)}) collective-permute-start(bf16[2,2,128,128]{3,2,1,0:T(8,128)(2,1)S(1)} %get-tuple-element.30), channel_id=1, source_target_pairs={{0,1},{1,2},{2,3},{3,0},{4,5},{5,6},{6,7},{7,4},{8,9},{9,10},{10,1... | collective-permute-start | bytes 393224 | tf_op jit(solution)/shard_map/ppermute | solution.py:42
  7.6 21.5 %collective-permute-start.1 = (bf16[2,2,128,128]{3,2,1,0:T(8,128)(2,1)S(1)}, bf16[2,2,128,128]{3,2,1,0:T(8,128)(2,1)S(1)}, u32[]{:S(2)}, u32[]{:S(2)}) collective-permute-start(bf16[2,2,128,128]{3,2,1,0:T(8,128)(2,1)S(1)} %get-tuple-element.30), channel_id=1, source_target_pairs={{0,2},{1,3},{2,0},{3,1},{4,6},{5,7},{6,4},{7,5},{8,10},{9,11},{10,... | collective-permute-start | bytes 393224 | tf_op jit(solution)/shard_map/ppermute | solution.py:42
  16.8 12.6 %collective-permute-start.2 = (bf16[2,2,128,128]{3,2,1,0:T(8,128)(2,1)S(1)}, bf16[2,2,128,128]{3,2,1,0:T(8,128)(2,1)S(1)}, u32[]{:S(2)}, u32[]{:S(2)}) collective-permute-start(bf16[2,2,128,128]{3,2,1,0:T(8,128)(2,1)S(1)} %get-tuple-element.30), channel_id=1, source_target_pairs={{0,3},{1,0},{2,1},{3,2},{4,7},{5,4},{6,5},{7,6},{8,11},{9,8},{10,9... | collective-permute-start | bytes 393224 | tf_op jit(solution)/shard_map/ppermute | solution.py:42
  23.3 42.0 %copy-start.2 = (s32[64]{0:T(128)S(1)}, s32[64]{0:T(128)}, u32[]{:S(2)}) copy-start(s32[64]{0:T(128)} %param.11) | copy-start | bytes 772
  23.3 85.6 %all-to-all-start = ((bf16[16,2,128,256]{2,3,1,0:T(8,128)(2,1)}), bf16[16,2,128,256]{2,3,1,0:T(8,128)(2,1)}, u32[]{:S(2)}, u32[]{:S(2)}) async-start(bf16[16,2,128,256]{2,3,1,0:T(8,128)(2,1)} %broadcast_in_dim.4), calls=%async_computation | async-start | bytes 4194304 | tf_op jit(solution)/shard_map/all_to_all | solution.py:22
  29.4 17.5 %collective-permute-start.3 = (bf16[4,2,2,128,128]{4,3,2,1,0:T(8,128)(2,1)S(1)}, bf16[4,2,2,128,128]{4,3,2,1,0:T(8,128)(2,1)S(1)}, u32[]{:S(2)}, u32[]{:S(2)}) collective-permute-start(bf16[4,2,2,128,128]{4,3,2,1,0:T(8,128)(2,1)S(1)} %pad_maximum_fusion.1), channel_id=1, source_target_pairs={{0,4},{1,5},{2,6},{3,7},{4,8},{5,9},{6,10},{7,11},{8,12},{9,13},{1... | collective-permute-start | bytes 1572872 | tf_op jit(solution)/shard_map/ppermute | solution.py:48
  46.9 16.5 %collective-permute-start.4 = (bf16[4,2,2,128,128]{4,3,2,1,0:T(8,128)(2,1)S(1)}, bf16[4,2,2,128,128]{4,3,2,1,0:T(8,128)(2,1)S(1)}, u32[]{:S(2)}, u32[]{:S(2)}) collective-permute-start(bf16[4,2,2,128,128]{4,3,2,1,0:T(8,128)(2,1)S(1)} %collective-permute-done.3), channel_id=1, source_target_pairs={{0,4},{1,5},{2,6},{3,7},{4,8},{5,9},{6,10},{7,11},{8,12},{9,13},{1... | collective-permute-start | bytes 1572872 | tf_op jit(solution)/shard_map/ppermute | solution.py:48
  49.0 17.2 %collective-permute-start.7 = (bf16[4,2,2,128,128]{4,3,2,1,0:T(8,128)(2,1)S(1)}, bf16[4,2,2,128,128]{4,3,2,1,0:T(8,128)(2,1)S(1)}, u32[]{:S(2)}, u32[]{:S(2)}) collective-permute-start(bf16[4,2,2,128,128]{4,3,2,1,0:T(8,128)(2,1)S(1)} %pad_maximum_fusion.1), channel_id=1, source_target_pairs={{0,28},{1,29},{2,30},{3,31},{4,0},{5,1},{6,2},{7,3},{8,4},{9,5},{1... | collective-permute-start | bytes 1572872 | tf_op jit(solution)/shard_map/ppermute | solution.py:51
  63.4 15.6 %collective-permute-start.5 = (bf16[4,2,2,128,128]{4,3,2,1,0:T(8,128)(2,1)S(1)}, bf16[4,2,2,128,128]{4,3,2,1,0:T(8,128)(2,1)S(1)}, u32[]{:S(2)}, u32[]{:S(2)}) collective-permute-start(bf16[4,2,2,128,128]{4,3,2,1,0:T(8,128)(2,1)S(1)} %collective-permute-done.4), channel_id=1, source_target_pairs={{0,4},{1,5},{2,6},{3,7},{4,8},{5,9},{6,10},{7,11},{8,12},{9,13},{1... | collective-permute-start | bytes 1572872 | tf_op jit(solution)/shard_map/ppermute | solution.py:48
  66.2 14.9 %collective-permute-start.8 = (bf16[4,2,2,128,128]{4,3,2,1,0:T(8,128)(2,1)S(1)}, bf16[4,2,2,128,128]{4,3,2,1,0:T(8,128)(2,1)S(1)}, u32[]{:S(2)}, u32[]{:S(2)}) collective-permute-start(bf16[4,2,2,128,128]{4,3,2,1,0:T(8,128)(2,1)S(1)} %collective-permute-done.7), channel_id=1, source_target_pairs={{0,28},{1,29},{2,30},{3,31},{4,0},{5,1},{6,2},{7,3},{8,4},{9,5},{1... | collective-permute-start | bytes 1572872 | tf_op jit(solution)/shard_map/ppermute | solution.py:51
  79.0 14.7 %collective-permute-start.6 = (bf16[4,2,2,128,128]{4,3,2,1,0:T(8,128)(2,1)S(1)}, bf16[4,2,2,128,128]{4,3,2,1,0:T(8,128)(2,1)S(1)}, u32[]{:S(2)}, u32[]{:S(2)}) collective-permute-start(bf16[4,2,2,128,128]{4,3,2,1,0:T(8,128)(2,1)S(1)} %collective-permute-done.5), channel_id=1, source_target_pairs={{0,4},{1,5},{2,6},{3,7},{4,8},{5,9},{6,10},{7,11},{8,12},{9,13},{1... | collective-permute-start | bytes 1572872 | tf_op jit(solution)/shard_map/ppermute | solution.py:48
  81.1 14.4 %collective-permute-start.9 = (bf16[4,2,2,128,128]{4,3,2,1,0:T(8,128)(2,1)S(1)}, bf16[4,2,2,128,128]{4,3,2,1,0:T(8,128)(2,1)S(1)}, u32[]{:S(2)}, u32[]{:S(2)}) collective-permute-start(bf16[4,2,2,128,128]{4,3,2,1,0:T(8,128)(2,1)S(1)} %collective-permute-done.8), channel_id=1, source_target_pairs={{0,28},{1,29},{2,30},{3,31},{4,0},{5,1},{6,2},{7,3},{8,4},{9,5},{1... | collective-permute-start | bytes 1572872 | tf_op jit(solution)/shard_map/ppermute | solution.py:51
  97.5 4.7 %copy-start.3 = (bf16[1,8,4,2,128,128]{5,4,3,0,2,1:T(8,128)(2,1)}, bf16[1,8,4,2,128,128]{5,4,3,0,2,1:T(8,128)(2,1)S(1)}, u32[]{:S(2)}) copy-start(bf16[1,8,4,2,128,128]{5,4,3,0,2,1:T(8,128)(2,1)S(1)} %get-tuple-element.19) | copy-start | bytes 6291460
  113.4 2.5 copy-start.6
  115.9 0.8 copy-start.9
  123.6 3.2 %copy-start.5 = (bf16[8,8,128,128]{3,1,0,2:T(8,128)(2,1)S(1)}, bf16[8,8,128,128]{3,1,0,2:T(8,128)(2,1)}, u32[]{:S(2)}) copy-start(bf16[8,8,128,128]{3,1,0,2:T(8,128)(2,1)} %copy.66) | copy-start | bytes 6291460
  129.2 1.2 copy-start.11
  132.0 35.4 %all-to-all-start.1 = ((bf16[16,2,128,256]{2,3,1,0:T(8,128)(2,1)}), bf16[16,2,128,256]{2,3,1,0:T(8,128)(2,1)}, u32[]{:S(2)}, u32[]{:S(2)}) async-start(bf16[16,2,128,256]{2,3,1,0:T(8,128)(2,1)} %bitcast.175), calls=%async_computation.1 | async-start | bytes 4194304 | tf_op jit(solution)/shard_map/all_to_all | solution.py:26
  140.5 3.1 %copy-start.10 = (f32[128,8,128]{0,2,1:T(8,128)S(1)}, f32[128,8,128]{0,2,1:T(8,128)}, u32[]{:S(2)}) copy-start(f32[128,8,128]{0,2,1:T(8,128)} %copy-done.9) | copy-start | bytes 1572868
  145.7 4.1 %copy-start.7 = (bf16[8,8,128,128]{2,3,1,0:T(8,128)(2,1)S(1)}, bf16[8,8,128,128]{2,3,1,0:T(8,128)(2,1)}, u32[]{:S(2)}) copy-start(bf16[8,8,128,128]{2,3,1,0:T(8,128)(2,1)} %copy.54) | copy-start | bytes 6291460
  149.8 1.6 copy-start.8
  151.7 2.0 copy-start.4
  154.6 21.3 %collective-permute-start.10 = (bf16[4,2,2,128,128]{4,3,2,1,0:T(8,128)(2,1)}, bf16[4,2,2,128,128]{4,3,2,1,0:T(8,128)(2,1)S(1)}, u32[]{:S(2)}, u32[]{:S(2)}) collective-permute-start(bf16[4,2,2,128,128]{4,3,2,1,0:T(8,128)(2,1)} %get-tuple-element.16), channel_id=1, source_target_pairs={{0,4},{1,5},{2,6},{3,7},{4,8},{5,9},{6,10},{7,11},{8,12},{9,13},{1... | collective-permute-start | bytes 1572872 | tf_op jit(solution)/shard_map/ppermute | solution.py:64
  171.0 73.9 %all-to-all-start.2 = ((bf16[16,2,128,256]{3,2,1,0:T(8,128)(2,1)}), bf16[16,2,128,256]{3,2,1,0:T(8,128)(2,1)S(1)}, u32[]{:S(2)}, u32[]{:S(2)}) async-start(bf16[16,2,128,256]{3,2,1,0:T(8,128)(2,1)} %broadcast_in_dim.5), calls=%async_computation.2 | async-start | bytes 4194304 | tf_op jit(solution)/shard_map/all_to_all | solution.py:22
  177.1 17.8 %collective-permute-start.11 = (bf16[4,2,2,128,128]{4,3,2,1,0:T(8,128)(2,1)S(1)}, bf16[4,2,2,128,128]{4,3,2,1,0:T(8,128)(2,1)S(1)}, u32[]{:S(2)}, u32[]{:S(2)}) collective-permute-start(bf16[4,2,2,128,128]{4,3,2,1,0:T(8,128)(2,1)S(1)} %fusion.6), channel_id=1, source_target_pairs={{0,4},{1,5},{2,6},{3,7},{4,8},{5,9},{6,10},{7,11},{8,12},{9,13},{1... | collective-permute-start | bytes 1572872 | tf_op jit(solution)/shard_map/ppermute | solution.py:64
  179.9 18.3 %collective-permute-start.14 = (bf16[4,2,2,128,128]{4,3,2,1,0:T(8,128)(2,1)S(1)}, bf16[4,2,2,128,128]{4,3,2,1,0:T(8,128)(2,1)S(1)}, u32[]{:S(2)}, u32[]{:S(2)}) collective-permute-start(bf16[4,2,2,128,128]{4,3,2,1,0:T(8,128)(2,1)S(1)} %get-tuple-element.17), channel_id=1, source_target_pairs={{0,28},{1,29},{2,30},{3,31},{4,0},{5,1},{6,2},{7,3},{8,4},{9,5},{1... | collective-permute-start | bytes 1572872 | tf_op jit(solution)/shard_map/ppermute | solution.py:69
  196.2 16.6 %collective-permute-start.12 = (bf16[4,2,2,128,128]{4,3,2,1,0:T(8,128)(2,1)S(1)}, bf16[4,2,2,128,128]{4,3,2,1,0:T(8,128)(2,1)S(1)}, u32[]{:S(2)}, u32[]{:S(2)}) collective-permute-start(bf16[4,2,2,128,128]{4,3,2,1,0:T(8,128)(2,1)S(1)} %fusion.7), channel_id=1, source_target_pairs={{0,4},{1,5},{2,6},{3,7},{4,8},{5,9},{6,10},{7,11},{8,12},{9,13},{1... | collective-permute-start | bytes 1572872 | tf_op jit(solution)/shard_map/ppermute | solution.py:64
  214.3 14.5 %collective-permute-start.15 = (bf16[4,2,2,128,128]{4,3,2,1,0:T(8,128)(2,1)S(1)}, bf16[4,2,2,128,128]{4,3,2,1,0:T(8,128)(2,1)S(1)}, u32[]{:S(2)}, u32[]{:S(2)}) collective-permute-start(bf16[4,2,2,128,128]{4,3,2,1,0:T(8,128)(2,1)S(1)} %get-tuple-element.15), channel_id=1, source_target_pairs={{0,28},{1,29},{2,30},{3,31},{4,0},{5,1},{6,2},{7,3},{8,4},{9,5},{1... | collective-permute-start | bytes 1572872 | tf_op jit(solution)/shard_map/ppermute | solution.py:69
  216.5 17.0 %collective-permute-start.13 = (bf16[4,2,2,128,128]{4,3,2,1,0:T(8,128)(2,1)S(1)}, bf16[4,2,2,128,128]{4,3,2,1,0:T(8,128)(2,1)S(1)}, u32[]{:S(2)}, u32[]{:S(2)}) collective-permute-start(bf16[4,2,2,128,128]{4,3,2,1,0:T(8,128)(2,1)S(1)} %get-tuple-element.14), channel_id=1, source_target_pairs={{0,4},{1,5},{2,6},{3,7},{4,8},{5,9},{6,10},{7,11},{8,12},{9,13},{1... | collective-permute-start | bytes 1572872 | tf_op jit(solution)/shard_map/ppermute | solution.py:64
  230.0 13.5 %collective-permute-start.16 = (bf16[4,2,2,128,128]{4,3,2,1,0:T(8,128)(2,1)S(1)}, bf16[4,2,2,128,128]{4,3,2,1,0:T(8,128)(2,1)S(1)}, u32[]{:S(2)}, u32[]{:S(2)}) collective-permute-start(bf16[4,2,2,128,128]{4,3,2,1,0:T(8,128)(2,1)S(1)} %fusion.5), channel_id=1, source_target_pairs={{0,28},{1,29},{2,30},{3,31},{4,0},{5,1},{6,2},{7,3},{8,4},{9,5},{1... | collective-permute-start | bytes 1572872 | tf_op jit(solution)/shard_map/ppermute | solution.py:69
  249.7 14.4 %collective-permute-start.17 = (bf16[2,2,128,128]{3,2,1,0:T(8,128)(2,1)}, bf16[2,2,128,128]{3,2,1,0:T(8,128)(2,1)S(1)}, u32[]{:S(2)}, u32[]{:S(2)}) collective-permute-start(bf16[2,2,128,128]{3,2,1,0:T(8,128)(2,1)} %get-tuple-element.24), channel_id=1, source_target_pairs={{0,3},{1,0},{2,1},{3,2},{4,7},{5,4},{6,5},{7,6},{8,11},{9,8},{10,9... | collective-permute-start | bytes 393224 | tf_op jit(solution)/shard_map/ppermute | solution.py:79
  254.3 12.0 %collective-permute-start.18 = (bf16[2,2,128,128]{3,2,1,0:T(8,128)(2,1)}, bf16[2,2,128,128]{3,2,1,0:T(8,128)(2,1)S(1)}, u32[]{:S(2)}, u32[]{:S(2)}) collective-permute-start(bf16[2,2,128,128]{3,2,1,0:T(8,128)(2,1)} %get-tuple-element.26), channel_id=1, source_target_pairs={{0,2},{1,3},{2,0},{3,1},{4,6},{5,7},{6,4},{7,5},{8,10},{9,11},{10,... | collective-permute-start | bytes 393224 | tf_op jit(solution)/shard_map/ppermute | solution.py:79
  258.3 11.0 %collective-permute-start.19 = (bf16[2,2,128,128]{3,2,1,0:T(8,128)(2,1)S(1)}, bf16[2,2,128,128]{3,2,1,0:T(8,128)(2,1)}, u32[]{:S(2)}, u32[]{:S(2)}) collective-permute-start(bf16[2,2,128,128]{3,2,1,0:T(8,128)(2,1)S(1)} %get-tuple-element.25), channel_id=1, source_target_pairs={{0,1},{1,2},{2,3},{3,0},{4,5},{5,6},{6,7},{7,4},{8,9},{9,10},{10,1... | collective-permute-start | bytes 393224 | tf_op jit(solution)/shard_map/ppermute | solution.py:79
  261.2 9.7 %copy-start.1 = (s32[64]{0:T(128)S(1)}, s32[64]{0:T(128)}, u32[]{:S(2)}) copy-start(s32[64]{0:T(128)} %param.9) | copy-start | bytes 772

commit v10 on v7

--- a/solution.py
+++ b/solution.py
@@ -38,20 +38,21 @@
     ]
 
 
-def dp_gather_rel(x, n_y, n_z):
+def dp_gather_rel(x, n_y, n_z, tie=None, tie_step=2):
     by_z = [x] + [lax.ppermute(x, "dp", dp_shift(n_y, n_z, 0, b)) for b in range(1, n_z)]
     held = jnp.stack(by_z)
     n_f, n_b = n_y // 2, (n_y - 1) // 2
     fwd, bwd = [held], []
     cur_f = cur_b = held
     for k in range(1, n_f + 1):
+        if tie is not None and k == min(tie_step + 1, n_f):
+            cur_f, cur_b, tie = lax.optimization_barrier((cur_f, cur_b, tie))
         cur_f = lax.ppermute(cur_f, "dp", dp_shift(n_y, n_z, 1, 0))
         fwd.append(cur_f)
         if k <= n_b:
             cur_b = lax.ppermute(cur_b, "dp", dp_shift(n_y, n_z, -1, 0))
             bwd.append(cur_b)
-    rel = fwd + [bwd[n_y - a - 1] for a in range(len(fwd), n_y)]
-    return jnp.stack(rel)
+    return fwd + [bwd[n_y - a - 1] for a in range(len(fwd), n_y)], tie
 
 
 def dp_scatter_rel(terms, n_y, n_z):
@@ -79,42 +80,15 @@
     return total.astype(jnp.bfloat16)
 
 
-def per_device(activations, out_grad, up_blocks, up_rows, down_blocks, down_rows):
-    block_size = up_blocks.shape[1]
-    groups = up_rows.shape[0] // K
-    n_tensor = lax.axis_size("tensor")
-    n_dp = lax.axis_size("dp")
-    tokens = activations.shape[0]
-    shard_width = activations.shape[1]
-    width = shard_width * n_tensor
-    row_blocks = width // block_size
-
-    feats = gather_all(jnp.stack([activations, out_grad]), "tensor")
-    feats = jnp.moveaxis(feats, 0, 2).reshape(2, tokens, width)
-    full_input, full_grad = feats[0], feats[1]
-    per_dev = up_blocks.shape[0]
-    n_z = Z_HI
-    n_y = n_dp // n_z
-    if n_z * per_dev != K:
-        raise ValueError("layout")
-    weights = dp_gather_rel(jnp.stack([up_blocks, down_blocks]), n_y, n_z)
-    weights = jnp.moveaxis(weights, 2, 0).reshape(2, -1, block_size, block_size)
-    up_all, down_all = weights[0], weights[1]
-    me = lax.axis_index("dp")
-    my_y, my_z = me // n_z, me % n_z
-    a = jnp.arange(n_y, dtype=jnp.int32)[:, None, None]
-    b = jnp.arange(n_z, dtype=jnp.int32)[None, :, None]
-    r = jnp.arange(per_dev, dtype=jnp.int32)[None, None, :]
-    order = ((((my_y - a) % n_y) * n_z + (my_z - b) % n_z) * per_dev + r).reshape(-1)
-    up_rows = up_rows[order]
-    down_rows = down_rows[order]
-
-    scale = 1.0 / math.sqrt(tokens * n_dp)
-    up_tiles = up_all.reshape(groups, K, block_size, block_size)
-    down_tiles = down_all.reshape(groups, K, block_size, block_size)
-    up_index = up_rows.reshape(groups, K)
-    down_index = down_rows.reshape(groups, K)
-    picked_in = full_input.reshape(tokens, row_blocks, block_size)[:, up_index]
+def chunk_compute(x_rows, g_rows, pieces, up_rows, down_rows, order_of, scale):
+    tokens, row_blocks, block_size = x_rows.shape
+    w = jnp.stack(pieces)
+    groups = w.shape[0]
+    up_tiles = w[:, :, 0].reshape(groups, K, block_size, block_size)
+    down_tiles = w[:, :, 1].reshape(groups, K, block_size, block_size)
+    up_index = up_rows[order_of].reshape(groups, K)
+    down_index = down_rows[order_of].reshape(groups, K)
+    picked_in = x_rows[:, up_index]
     preact = jnp.einsum("tgki,gkio->tgo", picked_in, up_tiles, preferred_element_type=jnp.float32)
     hidden = (preact * normal_cdf(preact)).astype(jnp.bfloat16)
     product = jnp.einsum("gkho,tgh->gkot", down_tiles, hidden, preferred_element_type=jnp.float32)
@@ -124,7 +98,7 @@
     out_t = jnp.einsum(
         "gkr,gkot->rot", down_hot, product, precision=highest, preferred_element_type=jnp.float32
     )
-    picked_grad = full_grad.reshape(tokens, row_blocks, block_size)[:, down_index]
+    picked_grad = g_rows[:, down_index]
     down_term = (
         jnp.einsum("tgh,tgko->gkho", hidden, picked_grad, preferred_element_type=jnp.float32)
         * scale
@@ -142,6 +116,51 @@
         jnp.einsum("tgki,tgo->gkio", picked_in, preact_grad, preferred_element_type=jnp.float32)
         * scale
     )
+    return out_t, in_t, up_term, down_term
+
+
+def per_device(activations, out_grad, up_blocks, up_rows, down_blocks, down_rows):
+    block_size = up_blocks.shape[1]
+    n_tensor = lax.axis_size("tensor")
+    n_dp = lax.axis_size("dp")
+    tokens = activations.shape[0]
+    shard_width = activations.shape[1]
+    width = shard_width * n_tensor
+    row_blocks = width // block_size
+
+    feats = gather_all(jnp.stack([activations, out_grad]), "tensor")
+    per_dev = up_blocks.shape[0]
+    n_z = Z_HI
+    n_y = n_dp // n_z
+    if n_z * per_dev != K:
+        raise ValueError("layout")
+    pieces, feats = dp_gather_rel(jnp.stack([up_blocks, down_blocks]), n_y, n_z, feats)
+    feats = jnp.moveaxis(feats, 0, 2).reshape(2, tokens, width)
+    x_rows = feats[0].reshape(tokens, row_blocks, block_size)
+    g_rows = feats[1].reshape(tokens, row_blocks, block_size)
+    me = lax.axis_index("dp")
+    my_y, my_z = me // n_z, me % n_z
+    b = jnp.arange(n_z, dtype=jnp.int32)[:, None]
+    r = jnp.arange(per_dev, dtype=jnp.int32)[None, :]
+    scale = 1.0 / math.sqrt(tokens * n_dp)
+
+    late = [a for a in range(n_y) if min(a, n_y - a) >= n_y // 2 - 1]
+    early = [a for a in range(n_y) if a not in late]
+    chunks = [c for c in (early, late) if c]
+    out_t = in_t = None
+    term_of = {}
+    for chunk in chunks:
+        a = jnp.array(chunk, dtype=jnp.int32)[:, None, None]
+        order_of = ((((my_y - a) % n_y) * n_z + (my_z - b) % n_z) * per_dev + r).reshape(-1)
+        got = chunk_compute(
+            x_rows, g_rows, [pieces[i] for i in chunk], up_rows, down_rows, order_of, scale
+        )
+        out_t = got[0] if out_t is None else out_t + got[0]
+        in_t = got[1] if in_t is None else in_t + got[1]
+        up_term = got[2].astype(jnp.bfloat16).reshape(len(chunk), n_z, per_dev, block_size, block_size)
+        down_term = got[3].astype(jnp.bfloat16).reshape(len(chunk), n_z, per_dev, block_size, block_size)
+        for i, blk in enumerate(chunk):
+            term_of[blk] = jnp.stack([up_term[i], down_term[i]], axis=1)
 
     parts = jnp.stack([out_t, in_t]).astype(jnp.bfloat16)
     parts = parts.reshape(2, n_tensor, shard_width // block_size, block_size, tokens)
@@ -150,9 +169,7 @@
     both = gather_all(mine, "tensor")
     both = jnp.moveaxis(both, 0, 2).reshape(2, tokens, width)
 
-    terms = jnp.stack([up_term, down_term]).astype(jnp.bfloat16)
-    terms = terms.reshape(2, n_y, n_z, per_dev, block_size, block_size)
-    grads = dp_scatter_rel(jnp.moveaxis(terms, 0, 2), n_y, n_z)
+    grads = dp_scatter_rel([term_of[i] for i in range(n_y)], n_y, n_z)
     return (both[0], both[1], grads[0], grads[1])
 
 

time: 274 us -> 285 us (1.040)
  waiting for transfers between devices: 94.5 us -> 71.3 us
  local copies, waits for them, and re-layouts: 55.1 us -> 77.5 us
  other arithmetic: 11.4 us -> 21.6 us
  matrix products: 13.5 us -> 16.7 us
    ppermute x3, waiting for transfers between devices: 27.4 us -> 9.58 us  [dp_scatter_rel(): lax.ppermute(part.astype(jnp.bfloat16), 'dp', dp_shift(n_y, n_z, -1, 0))]
    all_to_all x1, waiting for transfers between devices: 0.01 us -> 15.8 us  [scatter_sum(): got = lax.all_to_all(x, axis_name, 0, 0, tiled=True)]
    ppermute x4, waiting for transfers between devices: 21.5 us -> 10.9 us  [dp_scatter_rel(): lax.ppermute(part.astype(jnp.bfloat16), 'dp', dp_shift(n_y, n_z, 1, 0))]
    ppermute x4, waiting for transfers between devices: 36.2 us -> 27.6 us  [dp_gather_rel(): cur_f = lax.ppermute(cur_f, 'dp', dp_shift(n_y, n_z, 1, 0))]
    another operation x5 -> x13, local copies, waits for them, and re-layouts: 10.3 us -> 17.3 us  [the longest x8 8.58 us: per_device(): term_of[blk] = jnp.stack([up_term[i], down_term[i]], axis=1)]
    convert_element_type x4 -> x5, other arithmetic: 4.13 us -> 10.4 us  [dp_scatter_rel(): part.astype(jnp.bfloat16)]
    gather x7 -> x14, local copies, waits for them, and re-layouts: 15.3 us -> 21.3 us  [the longest x6 9.8 us: chunk_compute(): picked_grad = g_rows[:, down_index]]
    slice x4 -> x11, local copies, waits for them, and re-layouts: 11 us -> 16.6 us  [the longest x4 7.44 us: chunk_compute(): down_tiles = w[:, :, 1].reshape(groups, K, block_size, block_size)]
  transfers between devices with their start and end apart: 23 -> 23, of which waited for: 16 -> 14; matrix products, arithmetic and copies ran while one was open for 17% -> 26% of each run, Pallas kernels for 0% -> 0%
where the time goes in v10:
time: 285 us; the launch traced here: 282 us
  starting transfers between devices  93.3 us (33%)
  local copies, waits for them, and re-layouts  77.5 us (27%)
  waiting for transfers between devices  71.3 us (25%)
  other arithmetic  21.6 us (8%)
  matrix products  16.7 us (6%)
    ppermute x4, waiting for transfers between devices, dp_gather_rel(): cur_f = lax.ppermute(cur_f, 'dp', dp_shift(n_y, n_z, 1, 0))  27.6 us
    ppermute x3, starting transfers between devices, dp_gather_rel(): lax.ppermute(x, 'dp', dp_shift(n_y, n_z, 0, b))  17.7 us
    all_to_all x1, waiting for transfers between devices, scatter_sum(): got = lax.all_to_all(x, axis_name, 0, 0, tiled=True)  15.8 us
    ppermute x3, starting transfers between devices, dp_gather_rel(): cur_b = lax.ppermute(cur_b, 'dp', dp_shift(n_y, n_z, -1, 0))  14.6 us
    ppermute x3, starting transfers between devices, dp_scatter_rel(): lax.ppermute(part.astype(jnp.bfloat16), 'dp', dp_shift(n_y, n_z, -1, 0))  14.1 us
    ppermute x3, starting transfers between devices, dp_scatter_rel(): lax.ppermute(acc[b].astype(jnp.bfloat16), 'dp', dp_shift(n_y, n_z, 0, -b))  12.9 us
    ppermute x4, waiting for transfers between devices, dp_scatter_rel(): lax.ppermute(part.astype(jnp.bfloat16), 'dp', dp_shift(n_y, n_z, 1, 0))  10.9 us
    all_to_all x2, starting transfers between devices, gather_all(): return lax.all_to_all(spread, axis_name, 0, 0, tiled=True)  10.7 us
  transfers between devices with their start and end apart: 23, of which 14 were waited for; matrix products, arithmetic and copies ran while one was open for 26% of the time, Pallas kernels for 0%

profile of v10, /device:TPU:6, one launch (start us, length us, event | category | flops | bytes accessed | tf_op | source)
XLA Modules:
  0.0 281.8 jit_solution(16998716624517687522)
XLA Ops:
  1.5 10.9 %collective-permute-start.2 = (bf16[2,2,128,128]{3,2,1,0:T(8,128)(2,1)S(1)}, bf16[2,2,128,128]{3,2,1,0:T(8,128)(2,1)S(1)}, u32[]{:S(2)}, u32[]{:S(2)}) collective-permute-start(bf16[2,2,128,128]{3,2,1,0:T(8,128)(2,1)S(1)} %get-tuple-element.46), channel_id=1, source_target_pairs={{0,3},{1,0},{2,1},{3,2},{4,7},{5,4},{6,5},{7,6},{8,11},{9,8},{10,9... | collective-permute-start | bytes 393224 | tf_op jit(solution)/shard_map/ppermute | solution.py:42
  12.5 1.9 collective-permute-start.1
  14.4 4.8 %collective-permute-start = (bf16[2,2,128,128]{3,2,1,0:T(8,128)(2,1)S(1)}, bf16[2,2,128,128]{3,2,1,0:T(8,128)(2,1)S(1)}, u32[]{:S(2)}, u32[]{:S(2)}) collective-permute-start(bf16[2,2,128,128]{3,2,1,0:T(8,128)(2,1)S(1)} %get-tuple-element.46), channel_id=1, source_target_pairs={{0,1},{1,2},{2,3},{3,0},{4,5},{5,6},{6,7},{7,4},{8,9},{9,10},{10,1... | collective-permute-start | bytes 393224 | tf_op jit(solution)/shard_map/ppermute | solution.py:42
  22.1 5.8 %all-to-all-start = ((bf16[16,2,128,256]{2,3,1,0:T(8,128)(2,1)}), bf16[16,2,128,256]{2,3,1,0:T(8,128)(2,1)}, u32[]{:S(2)}, u32[]{:S(2)}) async-start(bf16[16,2,128,256]{2,3,1,0:T(8,128)(2,1)} %broadcast_in_dim.4), calls=%async_computation | async-start | bytes 4194304 | tf_op jit(solution)/shard_map/all_to_all | solution.py:22
  30.3 3.5 %collective-permute-start.3 = (bf16[4,2,2,128,128]{4,3,2,1,0:T(8,128)(2,1)S(1)}, bf16[4,2,2,128,128]{4,3,2,1,0:T(8,128)(2,1)S(1)}, u32[]{:S(2)}, u32[]{:S(2)}) collective-permute-start(bf16[4,2,2,128,128]{4,3,2,1,0:T(8,128)(2,1)S(1)} %pad_maximum_fusion.2), channel_id=1, source_target_pairs={{0,4},{1,5},{2,6},{3,7},{4,8},{5,9},{6,10},{7,11},{8,12},{9,13},{1... | collective-permute-start | bytes 1572872 | tf_op jit(solution)/shard_map/ppermute | solution.py:50
  34.6 3.8 %collective-permute-start.5 = (bf16[4,2,2,128,128]{4,3,2,1,0:T(8,128)(2,1)S(1)}, bf16[4,2,2,128,128]{4,3,2,1,0:T(8,128)(2,1)S(1)}, u32[]{:S(2)}, u32[]{:S(2)}) collective-permute-start(bf16[4,2,2,128,128]{4,3,2,1,0:T(8,128)(2,1)S(1)} %pad_maximum_fusion.2), channel_id=1, source_target_pairs={{0,28},{1,29},{2,30},{3,31},{4,0},{5,1},{6,2},{7,3},{8,4},{9,5},{1... | collective-permute-start | bytes 1572872 | tf_op jit(solution)/shard_map/ppermute | solution.py:53
  39.5 8.5 %collective-permute-done.3 = bf16[4,2,2,128,128]{4,3,2,1,0:T(8,128)(2,1)S(1)} collective-permute-done((bf16[4,2,2,128,128]{4,3,2,1,0:T(8,128)(2,1)S(1)}, bf16[4,2,2,128,128]{4,3,2,1,0:T(8,128)(2,1)S(1)}, u32[]{:S(2)}, u32[]{:S(2)}) %collective-permute-start.3) | collective-permute-done | bytes 524320 | tf_op jit(solution)/shard_map/ppermute | solution.py:50
  47.9 1.9 collective-permute-start.4
  50.4 5.1 %collective-permute-start.6 = (bf16[4,2,2,128,128]{4,3,2,1,0:T(8,128)(2,1)S(1)}, bf16[4,2,2,128,128]{4,3,2,1,0:T(8,128)(2,1)}, u32[]{:S(2)}, u32[]{:S(2)}) collective-permute-start(bf16[4,2,2,128,128]{4,3,2,1,0:T(8,128)(2,1)S(1)} %collective-permute-done.5), channel_id=1, source_target_pairs={{0,28},{1,29},{2,30},{3,31},{4,0},{5,1},{6,2},{7,3},{8,4},{9,5},{1... | collective-permute-start | bytes 1572872 | tf_op jit(solution)/shard_map/ppermute | solution.py:53
  55.6 9.1 %collective-permute-done.4 = bf16[4,2,2,128,128]{4,3,2,1,0:T(8,128)(2,1)} collective-permute-done((bf16[4,2,2,128,128]{4,3,2,1,0:T(8,128)(2,1)S(1)}, bf16[4,2,2,128,128]{4,3,2,1,0:T(8,128)(2,1)}, u32[]{:S(2)}, u32[]{:S(2)}) %collective-permute-start.4) | collective-permute-done | bytes 524320 | tf_op jit(solution)/shard_map/ppermute | solution.py:50
  69.3 2.7 copy.141
  72.0 2.8 %copy.124 = bf16[5,4,1,2,128,128]{4,3,1,0,5,2:T(2,128)(2,1)} copy(bf16[5,4,1,2,128,128]{5,4,3,2,1,0:T(8,128)(2,1)S(1)} %get-tuple-element.16) | data formatting | bytes 2621440 | tf_op jit(solution)/shard_map/slice | solution.py:88
  79.0 2.0 gather_fusion.6
  82.9 2.3 copy.128
  85.2 5.7 %collective-permute-start.9 = (bf16[4,2,2,128,128]{4,3,2,1,0:T(8,128)(2,1)}, bf16[4,2,2,128,128]{4,3,2,1,0:T(8,128)(2,1)}, u32[]{:S(2)}, u32[]{:S(2)}) collective-permute-start(bf16[4,2,2,128,128]{4,3,2,1,0:T(8,128)(2,1)} %collective-permute-done.6), channel_id=1, source_target_pairs={{0,28},{1,29},{2,30},{3,31},{4,0},{5,1},{6,2},{7,3},{8,4},{9,5},{1... | collective-permute-start | bytes 1572872 | tf_op jit(solution)/shard_map/ppermute | solution.py:53
  90.9 1.9 collective-permute-start.7
  92.9 1.9 gather_fusion.7
  96.1 2.0 gather_fusion.2
  98.1 2.8 gather_fusion.5
  106.4 2.2 collective-permute-start.8
  109.2 2.6 fusion.37
  111.8 9.6 %collective-permute-done.8 = bf16[4,2,2,128,128]{4,3,2,1,0:T(8,128)(2,1)S(1)} collective-permute-done((bf16[4,2,2,128,128]{4,3,2,1,0:T(8,128)(2,1)}, bf16[4,2,2,128,128]{4,3,2,1,0:T(8,128)(2,1)S(1)}, u32[]{:S(2)}, u32[]{:S(2)}) %collective-permute-start.8) | collective-permute-done | bytes 524320 | tf_op jit(solution)/shard_map/ppermute | solution.py:50
  124.1 2.3 copy.133
  126.4 2.4 copy.146
  128.8 3.1 %copy.132 = bf16[3,4,1,2,128,128]{4,3,1,0,5,2:T(2,128)(2,1)} copy(bf16[3,4,1,2,128,128]{5,4,3,2,1,0:T(8,128)(2,1)} %get-tuple-element.22) | data formatting | bytes 1572864 | tf_op jit(solution)/shard_map/slice | solution.py:88
  142.5 5.9 %all-to-all-start.1 = ((bf16[16,2,128,256]{2,3,1,0:T(8,128)(2,1)}), bf16[16,2,128,256]{2,3,1,0:T(8,128)(2,1)}, u32[]{:S(2)}, u32[]{:S(2)}) async-start(bf16[16,2,128,256]{2,3,1,0:T(8,128)(2,1)} %bitcast.68), calls=%async_computation.1 | async-start | bytes 4194304 | tf_op jit(solution)/shard_map/all_to_all | solution.py:26
  149.5 2.3 copy.135
  162.0 15.8 %all-to-all-done.1 = bf16[16,2,128,256]{2,3,1,0:T(8,128)(2,1)} async-done(((bf16[16,2,128,256]{2,3,1,0:T(8,128)(2,1)}), bf16[16,2,128,256]{2,3,1,0:T(8,128)(2,1)}, u32[]{:S(2)}, u32[]{:S(2)}) %all-to-all-start.1) | async-done | bytes 2097184 | tf_op jit(solution)/shard_map/all_to_all | solution.py:26
  181.4 4.9 %all-to-all-start.2 = ((bf16[16,2,128,256]{3,2,1,0:T(8,128)(2,1)}), bf16[16,2,128,256]{3,2,1,0:T(8,128)(2,1)S(1)}, u32[]{:S(2)}, u32[]{:S(2)}) async-start(bf16[16,2,128,256]{3,2,1,0:T(8,128)(2,1)} %broadcast_in_dim.5), calls=%async_computation.2 | async-start | bytes 4194304 | tf_op jit(solution)/shard_map/all_to_all | solution.py:22
  186.3 2.9 %multiply_convert_fusion.1 = bf16[5,8,128,128]{3,2,1,0:T(8,128)(2,1)} fusion(bf16[5,8,128,128]{2,3,1,0:T(8,128)(2,1)} %copy.129, bf16[128,5,128]{0,2,1:T(8,128)(2,1)} %copy-done.25), kind=kOutput, calls=%fused_computation.9 | convolution fusion | flops 169082880 | bytes 2785280 | tf_op jit(solution)/shard_map/tgki,tgo->gkio/dot_general | solution.py:116
  192.9 3.6 %collective-permute-start.14 = (bf16[4,2,2,128,128]{4,3,2,1,0:T(8,128)(2,1)}, bf16[4,2,2,128,128]{4,3,2,1,0:T(8,128)(2,1)}, u32[]{:S(2)}, u32[]{:S(2)}) collective-permute-start(bf16[4,2,2,128,128]{4,3,2,1,0:T(8,128)(2,1)} %pad_maximum_fusion.4), channel_id=1, source_target_pairs={{0,28},{1,29},{2,30},{3,31},{4,0},{5,1},{6,2},{7,3},{8,4},{9,5},{1... | collective-permute-start | bytes 1572872 | tf_op jit(solution)/shard_map/ppermute | solution.py:70
  198.3 2.1 add_convert_fusion.4
  200.5 2.2 collective-permute-start.11
  209.1 2.1 add_convert_fusion.1
  211.2 4.8 %collective-permute-start.15 = (bf16[4,2,2,128,128]{4,3,2,1,0:T(8,128)(2,1)}, bf16[4,2,2,128,128]{4,3,2,1,0:T(8,128)(2,1)}, u32[]{:S(2)}, u32[]{:S(2)}) collective-permute-start(bf16[4,2,2,128,128]{4,3,2,1,0:T(8,128)(2,1)} %add_convert_fusion.1), channel_id=1, source_target_pairs={{0,28},{1,29},{2,30},{3,31},{4,0},{5,1},{6,2},{7,3},{8,4},{9,5},{1... | collective-permute-start | bytes 1572872 | tf_op jit(solution)/shard_map/ppermute | solution.py:70
  217.6 2.0 add_convert_fusion.3
  222.6 4.5 %collective-permute-done.15 = bf16[4,2,2,128,128]{4,3,2,1,0:T(8,128)(2,1)} collective-permute-done((bf16[4,2,2,128,128]{4,3,2,1,0:T(8,128)(2,1)}, bf16[4,2,2,128,128]{4,3,2,1,0:T(8,128)(2,1)}, u32[]{:S(2)}, u32[]{:S(2)}) %collective-permute-start.15) | collective-permute-done | bytes 524320 | tf_op jit(solution)/shard_map/ppermute | solution.py:70
  227.0 2.1 add_convert_fusion
  229.1 5.6 %collective-permute-start.16 = (bf16[4,2,2,128,128]{4,3,2,1,0:T(8,128)(2,1)}, bf16[4,2,2,128,128]{4,3,2,1,0:T(8,128)(2,1)}, u32[]{:S(2)}, u32[]{:S(2)}) collective-permute-start(bf16[4,2,2,128,128]{4,3,2,1,0:T(8,128)(2,1)} %add_convert_fusion), channel_id=1, source_target_pairs={{0,28},{1,29},{2,30},{3,31},{4,0},{5,1},{6,2},{7,3},{8,4},{9,5},{1... | collective-permute-start | bytes 1572872 | tf_op jit(solution)/shard_map/ppermute | solution.py:70
  235.8 2.0 add_convert_fusion.2
  240.0 4.9 %collective-permute-done.16 = bf16[4,2,2,128,128]{4,3,2,1,0:T(8,128)(2,1)} collective-permute-done((bf16[4,2,2,128,128]{4,3,2,1,0:T(8,128)(2,1)}, bf16[4,2,2,128,128]{4,3,2,1,0:T(8,128)(2,1)}, u32[]{:S(2)}, u32[]{:S(2)}) %collective-permute-start.16) | collective-permute-done | bytes 524320 | tf_op jit(solution)/shard_map/ppermute | solution.py:70
  244.8 8.2 %collective-permute-done.13 = bf16[4,2,2,128,128]{4,3,2,1,0:T(8,128)(2,1)S(1)} collective-permute-done((bf16[4,2,2,128,128]{4,3,2,1,0:T(8,128)(2,1)}, bf16[4,2,2,128,128]{4,3,2,1,0:T(8,128)(2,1)S(1)}, u32[]{:S(2)}, u32[]{:S(2)}) %collective-permute-start.13) | collective-permute-done | bytes 524320 | tf_op jit(solution)/shard_map/ppermute | solution.py:65
  254.4 5.5 %collective-permute-start.19 = (bf16[2,2,128,128]{3,2,1,0:T(8,128)(2,1)S(1)}, bf16[2,2,128,128]{3,2,1,0:T(8,128)(2,1)S(1)}, u32[]{:S(2)}, u32[]{:S(2)}) collective-permute-start(bf16[2,2,128,128]{3,2,1,0:T(8,128)(2,1)S(1)} %get-tuple-element.41), channel_id=1, source_target_pairs={{0,1},{1,2},{2,3},{3,0},{4,5},{5,6},{6,7},{7,4},{8,9},{9,10},{10,1... | collective-permute-start | bytes 393224 | tf_op jit(solution)/shard_map/ppermute | solution.py:78
  259.9 2.1 collective-permute-start.18
  262.0 5.3 %collective-permute-start.17 = (bf16[2,2,128,128]{3,2,1,0:T(8,128)(2,1)S(1)}, bf16[2,2,128,128]{3,2,1,0:T(8,128)(2,1)S(1)}, u32[]{:S(2)}, u32[]{:S(2)}) collective-permute-start(bf16[2,2,128,128]{3,2,1,0:T(8,128)(2,1)S(1)} %get-tuple-element.40), channel_id=1, source_target_pairs={{0,3},{1,0},{2,1},{3,2},{4,7},{5,4},{6,5},{7,6},{8,11},{9,8},{10,9... | collective-permute-start | bytes 393224 | tf_op jit(solution)/shard_map/ppermute | solution.py:78
  267.4 4.4 %collective-permute-done.18 = bf16[2,2,128,128]{3,2,1,0:T(8,128)(2,1)S(1)} collective-permute-done((bf16[2,2,128,128]{3,2,1,0:T(8,128)(2,1)S(1)}, bf16[2,2,128,128]{3,2,1,0:T(8,128)(2,1)S(1)}, u32[]{:S(2)}, u32[]{:S(2)}) %collective-permute-start.18) | collective-permute-done | bytes 131104 | tf_op jit(solution)/shard_map/ppermute | solution.py:78
  271.8 2.5 collective-permute-done.17
  275.1 2.4 copy.151
  (171 shorter events, 80.3 us)
Async XLA Ops:
  0.6 27.6 %copy-start = (s32[64]{0:T(128)S(1)}, s32[64]{0:T(128)}, u32[]{:S(2)}) copy-start(s32[64]{0:T(128)} %param.13) | copy-start | bytes 772
  1.5 28.7 %collective-permute-start.2 = (bf16[2,2,128,128]{3,2,1,0:T(8,128)(2,1)S(1)}, bf16[2,2,128,128]{3,2,1,0:T(8,128)(2,1)S(1)}, u32[]{:S(2)}, u32[]{:S(2)}) collective-permute-start(bf16[2,2,128,128]{3,2,1,0:T(8,128)(2,1)S(1)} %get-tuple-element.46), channel_id=1, source_target_pairs={{0,3},{1,0},{2,1},{3,2},{4,7},{5,4},{6,5},{7,6},{8,11},{9,8},{10,9... | collective-permute-start | bytes 393224 | tf_op jit(solution)/shard_map/ppermute | solution.py:42
  12.5 17.7 %collective-permute-start.1 = (bf16[2,2,128,128]{3,2,1,0:T(8,128)(2,1)S(1)}, bf16[2,2,128,128]{3,2,1,0:T(8,128)(2,1)S(1)}, u32[]{:S(2)}, u32[]{:S(2)}) collective-permute-start(bf16[2,2,128,128]{3,2,1,0:T(8,128)(2,1)S(1)} %get-tuple-element.46), channel_id=1, source_target_pairs={{0,2},{1,3},{2,0},{3,1},{4,6},{5,7},{6,4},{7,5},{8,10},{9,11},{10,... | collective-permute-start | bytes 393224 | tf_op jit(solution)/shard_map/ppermute | solution.py:42
  14.4 15.8 %collective-permute-start = (bf16[2,2,128,128]{3,2,1,0:T(8,128)(2,1)S(1)}, bf16[2,2,128,128]{3,2,1,0:T(8,128)(2,1)S(1)}, u32[]{:S(2)}, u32[]{:S(2)}) collective-permute-start(bf16[2,2,128,128]{3,2,1,0:T(8,128)(2,1)S(1)} %get-tuple-element.46), channel_id=1, source_target_pairs={{0,1},{1,2},{2,3},{3,0},{4,5},{5,6},{6,7},{7,4},{8,9},{9,10},{10,1... | collective-permute-start | bytes 393224 | tf_op jit(solution)/shard_map/ppermute | solution.py:42
  22.1 5.9 %copy-start.27 = (s32[3]{0:T(128)S(1)}, s32[3]{0:T(128)}, u32[]{:S(2)}) copy-start(s32[3]{0:T(128)} %constant.107) | copy-start | bytes 40
  22.1 7.0 %copy-start.26 = (s32[5]{0:T(128)S(1)}, s32[5]{0:T(128)}, u32[]{:S(2)}) copy-start(s32[5]{0:T(128)} %constant.106) | copy-start | bytes 64
  22.1 52.8 %all-to-all-start = ((bf16[16,2,128,256]{2,3,1,0:T(8,128)(2,1)}), bf16[16,2,128,256]{2,3,1,0:T(8,128)(2,1)}, u32[]{:S(2)}, u32[]{:S(2)}) async-start(bf16[16,2,128,256]{2,3,1,0:T(8,128)(2,1)} %broadcast_in_dim.4), calls=%async_computation | async-start | bytes 4194304 | tf_op jit(solution)/shard_map/all_to_all | solution.py:22
  27.9 5.9 %copy-start.2 = (s32[64]{0:T(128)S(1)}, s32[64]{0:T(128)}, u32[]{:S(2)}) copy-start(s32[64]{0:T(128)} %param.11) | copy-start | bytes 772
  30.3 17.6 %collective-permute-start.3 = (bf16[4,2,2,128,128]{4,3,2,1,0:T(8,128)(2,1)S(1)}, bf16[4,2,2,128,128]{4,3,2,1,0:T(8,128)(2,1)S(1)}, u32[]{:S(2)}, u32[]{:S(2)}) collective-permute-start(bf16[4,2,2,128,128]{4,3,2,1,0:T(8,128)(2,1)S(1)} %pad_maximum_fusion.2), channel_id=1, source_target_pairs={{0,4},{1,5},{2,6},{3,7},{4,8},{5,9},{6,10},{7,11},{8,12},{9,13},{1... | collective-permute-start | bytes 1572872 | tf_op jit(solution)/shard_map/ppermute | solution.py:50
  34.6 15.7 %collective-permute-start.5 = (bf16[4,2,2,128,128]{4,3,2,1,0:T(8,128)(2,1)S(1)}, bf16[4,2,2,128,128]{4,3,2,1,0:T(8,128)(2,1)S(1)}, u32[]{:S(2)}, u32[]{:S(2)}) collective-permute-start(bf16[4,2,2,128,128]{4,3,2,1,0:T(8,128)(2,1)S(1)} %pad_maximum_fusion.2), channel_id=1, source_target_pairs={{0,28},{1,29},{2,30},{3,31},{4,0},{5,1},{6,2},{7,3},{8,4},{9,5},{1... | collective-permute-start | bytes 1572872 | tf_op jit(solution)/shard_map/ppermute | solution.py:53
  47.9 16.8 %collective-permute-start.4 = (bf16[4,2,2,128,128]{4,3,2,1,0:T(8,128)(2,1)S(1)}, bf16[4,2,2,128,128]{4,3,2,1,0:T(8,128)(2,1)}, u32[]{:S(2)}, u32[]{:S(2)}) collective-permute-start(bf16[4,2,2,128,128]{4,3,2,1,0:T(8,128)(2,1)S(1)} %collective-permute-done.3), channel_id=1, source_target_pairs={{0,4},{1,5},{2,6},{3,7},{4,8},{5,9},{6,10},{7,11},{8,12},{9,13},{1... | collective-permute-start | bytes 1572872 | tf_op jit(solution)/shard_map/ppermute | solution.py:50
  50.4 15.9 %collective-permute-start.6 = (bf16[4,2,2,128,128]{4,3,2,1,0:T(8,128)(2,1)S(1)}, bf16[4,2,2,128,128]{4,3,2,1,0:T(8,128)(2,1)}, u32[]{:S(2)}, u32[]{:S(2)}) collective-permute-start(bf16[4,2,2,128,128]{4,3,2,1,0:T(8,128)(2,1)S(1)} %collective-permute-done.5), channel_id=1, source_target_pairs={{0,28},{1,29},{2,30},{3,31},{4,0},{5,1},{6,2},{7,3},{8,4},{9,5},{1... | collective-permute-start | bytes 1572872 | tf_op jit(solution)/shard_map/ppermute | solution.py:53
  81.0 4.2 %copy-start.3 = (bf16[40,128,128]{2,1,0:T(8,128)(2,1)}, bf16[40,128,128]{2,1,0:T(8,128)(2,1)S(1)}, u32[]{:S(2)}) copy-start(bf16[40,128,128]{2,1,0:T(8,128)(2,1)S(1)} %gather_fusion.6) | copy-start | bytes 3932164
  85.2 26.6 %collective-permute-start.9 = (bf16[4,2,2,128,128]{4,3,2,1,0:T(8,128)(2,1)}, bf16[4,2,2,128,128]{4,3,2,1,0:T(8,128)(2,1)}, u32[]{:S(2)}, u32[]{:S(2)}) collective-permute-start(bf16[4,2,2,128,128]{4,3,2,1,0:T(8,128)(2,1)} %collective-permute-done.6), channel_id=1, source_target_pairs={{0,28},{1,29},{2,30},{3,31},{4,0},{5,1},{6,2},{7,3},{8,4},{9,5},{1... | collective-permute-start | bytes 1572872 | tf_op jit(solution)/shard_map/ppermute | solution.py:53
  90.9 15.5 %collective-permute-start.7 = (bf16[4,2,2,128,128]{4,3,2,1,0:T(8,128)(2,1)}, bf16[4,2,2,128,128]{4,3,2,1,0:T(8,128)(2,1)}, u32[]{:S(2)}, u32[]{:S(2)}) collective-permute-start(bf16[4,2,2,128,128]{4,3,2,1,0:T(8,128)(2,1)} %collective-permute-done.4), channel_id=1, source_target_pairs={{0,4},{1,5},{2,6},{3,7},{4,8},{5,9},{6,10},{7,11},{8,12},{9,13},{1... | collective-permute-start | bytes 1572872 | tf_op jit(solution)/shard_map/ppermute | solution.py:50
  94.8 1.3 copy-start.6
  100.9 1.3 copy-start.8
  100.9 1.8 copy-start.18
  101.5 7.1 %copy-start.15 = (f32[128,5,128]{0,2,1:T(8,128)}, f32[128,5,128]{0,2,1:T(8,128)S(1)}, u32[]{:S(2)}) copy-start(f32[128,5,128]{0,2,1:T(8,128)S(1)} %convolution_bitcast_fusion) | copy-start | bytes 983044
  102.8 1.3 copy-start.9
  106.4 15.0 %collective-permute-start.8 = (bf16[4,2,2,128,128]{4,3,2,1,0:T(8,128)(2,1)}, bf16[4,2,2,128,128]{4,3,2,1,0:T(8,128)(2,1)S(1)}, u32[]{:S(2)}, u32[]{:S(2)}) collective-permute-start(bf16[4,2,2,128,128]{4,3,2,1,0:T(8,128)(2,1)} %collective-permute-done.7), channel_id=1, source_target_pairs={{0,4},{1,5},{2,6},{3,7},{4,8},{5,9},{6,10},{7,11},{8,12},{9,13},{1... | collective-permute-start | bytes 1572872 | tf_op jit(solution)/shard_map/ppermute | solution.py:50
  131.9 1.9 copy-start.14
  133.7 1.6 copy-start.17
  137.7 1.6 copy-start.5
  142.5 5.9 %copy-start.7 = (bf16[24,128,128]{2,1,0:T(8,128)(2,1)S(1)}, bf16[24,128,128]{2,1,0:T(8,128)(2,1)}, u32[]{:S(2)}) copy-start(bf16[24,128,128]{2,1,0:T(8,128)(2,1)} %copy-done.6) | copy-start | bytes 2359300
  142.5 35.3 %all-to-all-start.1 = ((bf16[16,2,128,256]{2,3,1,0:T(8,128)(2,1)}), bf16[16,2,128,256]{2,3,1,0:T(8,128)(2,1)}, u32[]{:S(2)}, u32[]{:S(2)}) async-start(bf16[16,2,128,256]{2,3,1,0:T(8,128)(2,1)} %bitcast.68), calls=%async_computation.1 | async-start | bytes 4194304 | tf_op jit(solution)/shard_map/all_to_all | solution.py:26
  148.3 3.5 %copy-start.4 = (bf16[40,128,128]{2,1,0:T(8,128)(2,1)S(1)}, bf16[40,128,128]{2,1,0:T(8,128)(2,1)}, u32[]{:S(2)}) copy-start(bf16[40,128,128]{2,1,0:T(8,128)(2,1)} %copy-done.3) | copy-start | bytes 3932164
  151.8 1.5 copy-start.11
  154.6 1.3 copy-start.12
  156.3 3.6 %copy-start.10 = (bf16[5,8,128,128]{2,3,1,0:T(8,128)(2,1)S(1)}, bf16[5,8,128,128]{2,3,1,0:T(8,128)(2,1)}, u32[]{:S(2)}) copy-start(bf16[5,8,128,128]{2,3,1,0:T(8,128)(2,1)} %copy.139) | copy-start | bytes 3932164
  156.3 3.6 %copy-start.16 = (f32[128,5,128]{0,2,1:T(8,128)S(1)}, f32[128,5,128]{0,2,1:T(8,128)}, u32[]{:S(2)}) copy-start(f32[128,5,128]{0,2,1:T(8,128)} %copy-done.15) | copy-start | bytes 983044
  158.0 40.3 %collective-permute-start.10 = (bf16[4,2,2,128,128]{4,3,2,1,0:T(8,128)(2,1)}, bf16[4,2,2,128,128]{4,3,2,1,0:T(8,128)(2,1)}, u32[]{:S(2)}, u32[]{:S(2)}) collective-permute-start(bf16[4,2,2,128,128]{4,3,2,1,0:T(8,128)(2,1)} %pad_maximum_fusion.3), channel_id=1, source_target_pairs={{0,4},{1,5},{2,6},{3,7},{4,8},{5,9},{6,10},{7,11},{8,12},{9,13},{1... | collective-permute-start | bytes 1572872 | tf_op jit(solution)/shard_map/ppermute | solution.py:65
  181.4 93.6 %all-to-all-start.2 = ((bf16[16,2,128,256]{3,2,1,0:T(8,128)(2,1)}), bf16[16,2,128,256]{3,2,1,0:T(8,128)(2,1)S(1)}, u32[]{:S(2)}, u32[]{:S(2)}) async-start(bf16[16,2,128,256]{3,2,1,0:T(8,128)(2,1)} %broadcast_in_dim.5), calls=%async_computation.2 | async-start | bytes 4194304 | tf_op jit(solution)/shard_map/all_to_all | solution.py:22
  192.9 16.2 %collective-permute-start.14 = (bf16[4,2,2,128,128]{4,3,2,1,0:T(8,128)(2,1)}, bf16[4,2,2,128,128]{4,3,2,1,0:T(8,128)(2,1)}, u32[]{:S(2)}, u32[]{:S(2)}) collective-permute-start(bf16[4,2,2,128,128]{4,3,2,1,0:T(8,128)(2,1)} %pad_maximum_fusion.4), channel_id=1, source_target_pairs={{0,28},{1,29},{2,30},{3,31},{4,0},{5,1},{6,2},{7,3},{8,4},{9,5},{1... | collective-permute-start | bytes 1572872 | tf_op jit(solution)/shard_map/ppermute | solution.py:70
  200.5 17.1 %collective-permute-start.11 = (bf16[4,2,2,128,128]{4,3,2,1,0:T(8,128)(2,1)}, bf16[4,2,2,128,128]{4,3,2,1,0:T(8,128)(2,1)}, u32[]{:S(2)}, u32[]{:S(2)}) collective-permute-start(bf16[4,2,2,128,128]{4,3,2,1,0:T(8,128)(2,1)} %add_convert_fusion.4), channel_id=1, source_target_pairs={{0,4},{1,5},{2,6},{3,7},{4,8},{5,9},{6,10},{7,11},{8,12},{9,13},{1... | collective-permute-start | bytes 1572872 | tf_op jit(solution)/shard_map/ppermute | solution.py:65
  207.4 1.7 copy-start.23
  207.4 10.2 %copy-start.22 = (bf16[4,1,2,128,128]{4,3,2,1,0:T(8,128)(2,1)S(1)}, bf16[4,1,2,128,128]{4,3,2,1,0:T(8,128)(2,1)}, u32[]{:S(2)}) copy-start(bf16[4,1,2,128,128]{4,3,2,1,0:T(8,128)(2,1)} %copy.159) | copy-start | bytes 786436
  209.1 12.4 %copy-start.21 = (bf16[1,8,128,128]{2,3,1,0:T(8,128)(2,1)S(1)}, bf16[1,8,128,128]{2,3,1,0:T(8,128)(2,1)}, u32[]{:S(2)}) copy-start(bf16[1,8,128,128]{2,3,1,0:T(8,128)(2,1)} %get-tuple-element.31) | copy-start | bytes 786436
  209.1 13.3 %copy-start.20 = (bf16[1,8,128,128]{2,3,1,0:T(8,128)(2,1)S(1)}, bf16[1,8,128,128]{2,3,1,0:T(8,128)(2,1)}, u32[]{:S(2)}) copy-start(bf16[1,8,128,128]{2,3,1,0:T(8,128)(2,1)} %get-tuple-element.33) | copy-start | bytes 786436
  211.2 15.9 %collective-permute-start.15 = (bf16[4,2,2,128,128]{4,3,2,1,0:T(8,128)(2,1)}, bf16[4,2,2,128,128]{4,3,2,1,0:T(8,128)(2,1)}, u32[]{:S(2)}, u32[]{:S(2)}) collective-permute-start(bf16[4,2,2,128,128]{4,3,2,1,0:T(8,128)(2,1)} %add_convert_fusion.1), channel_id=1, source_target_pairs={{0,28},{1,29},{2,30},{3,31},{4,0},{5,1},{6,2},{7,3},{8,4},{9,5},{1... | collective-permute-start | bytes 1572872 | tf_op jit(solution)/shard_map/ppermute | solution.py:70
  219.6 16.2 %collective-permute-start.12 = (bf16[4,2,2,128,128]{4,3,2,1,0:T(8,128)(2,1)}, bf16[4,2,2,128,128]{4,3,2,1,0:T(8,128)(2,1)}, u32[]{:S(2)}, u32[]{:S(2)}) collective-permute-start(bf16[4,2,2,128,128]{4,3,2,1,0:T(8,128)(2,1)} %add_convert_fusion.3), channel_id=1, source_target_pairs={{0,4},{1,5},{2,6},{3,7},{4,8},{5,9},{6,10},{7,11},{8,12},{9,13},{1... | collective-permute-start | bytes 1572872 | tf_op jit(solution)/shard_map/ppermute | solution.py:65
  227.0 12.7 %copy-start.19 = (bf16[1,8,128,128]{2,3,1,0:T(8,128)(2,1)S(1)}, bf16[1,8,128,128]{2,3,1,0:T(8,128)(2,1)}, u32[]{:S(2)}) copy-start(bf16[1,8,128,128]{2,3,1,0:T(8,128)(2,1)} %get-tuple-element.29) | copy-start | bytes 786436
  229.1 15.7 %collective-permute-start.16 = (bf16[4,2,2,128,128]{4,3,2,1,0:T(8,128)(2,1)}, bf16[4,2,2,128,128]{4,3,2,1,0:T(8,128)(2,1)}, u32[]{:S(2)}, u32[]{:S(2)}) collective-permute-start(bf16[4,2,2,128,128]{4,3,2,1,0:T(8,128)(2,1)} %add_convert_fusion), channel_id=1, source_target_pairs={{0,28},{1,29},{2,30},{3,31},{4,0},{5,1},{6,2},{7,3},{8,4},{9,5},{1... | collective-permute-start | bytes 1572872 | tf_op jit(solution)/shard_map/ppermute | solution.py:70
  237.9 15.2 %collective-permute-start.13 = (bf16[4,2,2,128,128]{4,3,2,1,0:T(8,128)(2,1)}, bf16[4,2,2,128,128]{4,3,2,1,0:T(8,128)(2,1)S(1)}, u32[]{:S(2)}, u32[]{:S(2)}) collective-permute-start(bf16[4,2,2,128,128]{4,3,2,1,0:T(8,128)(2,1)} %add_convert_fusion.2), channel_id=1, source_target_pairs={{0,4},{1,5},{2,6},{3,7},{4,8},{5,9},{6,10},{7,11},{8,12},{9,13},{1... | collective-permute-start | bytes 1572872 | tf_op jit(solution)/shard_map/ppermute | solution.py:65
  254.4 12.9 %collective-permute-start.19 = (bf16[2,2,128,128]{3,2,1,0:T(8,128)(2,1)S(1)}, bf16[2,2,128,128]{3,2,1,0:T(8,128)(2,1)S(1)}, u32[]{:S(2)}, u32[]{:S(2)}) collective-permute-start(bf16[2,2,128,128]{3,2,1,0:T(8,128)(2,1)S(1)} %get-tuple-element.41), channel_id=1, source_target_pairs={{0,1},{1,2},{2,3},{3,0},{4,5},{5,6},{6,7},{7,4},{8,9},{9,10},{10,1... | collective-permute-start | bytes 393224 | tf_op jit(solution)/shard_map/ppermute | solution.py:78
  259.9 11.8 %collective-permute-start.18 = (bf16[2,2,128,128]{3,2,1,0:T(8,128)(2,1)S(1)}, bf16[2,2,128,128]{3,2,1,0:T(8,128)(2,1)S(1)}, u32[]{:S(2)}, u32[]{:S(2)}) collective-permute-start(bf16[2,2,128,128]{3,2,1,0:T(8,128)(2,1)S(1)} %get-tuple-element.42), channel_id=1, source_target_pairs={{0,2},{1,3},{2,0},{3,1},{4,6},{5,7},{6,4},{7,5},{8,10},{9,11},{10,... | collective-permute-start | bytes 393224 | tf_op jit(solution)/shard_map/ppermute | solution.py:78
  262.0 12.3 %collective-permute-start.17 = (bf16[2,2,128,128]{3,2,1,0:T(8,128)(2,1)S(1)}, bf16[2,2,128,128]{3,2,1,0:T(8,128)(2,1)S(1)}, u32[]{:S(2)}, u32[]{:S(2)}) collective-permute-start(bf16[2,2,128,128]{3,2,1,0:T(8,128)(2,1)S(1)} %get-tuple-element.40), channel_id=1, source_target_pairs={{0,3},{1,0},{2,1},{3,2},{4,7},{5,4},{6,5},{7,6},{8,11},{9,8},{10,9... | collective-permute-start | bytes 393224 | tf_op jit(solution)/shard_map/ppermute | solution.py:78
  279.2 2.6 copy-start.1
  (3 other events, 3.0 us)

commit v11 on v7

--- a/solution.py
+++ b/solution.py
@@ -54,7 +54,7 @@
     return jnp.stack(rel)
 
 
-def dp_scatter_rel(terms, n_y, n_z):
+def dp_scatter_rel(terms, n_y, n_z, tie=None):
     n_f, n_b = n_y // 2, (n_y - 1) // 2
     got_f = got_b = None
     for k in range(1, n_f + 1):
@@ -67,6 +67,8 @@
         if got_b is not None:
             part = part + got_b.astype(jnp.float32)
         got_b = lax.ppermute(part.astype(jnp.bfloat16), "dp", dp_shift(n_y, n_z, -1, 0))
+        if k == 1 and tie is not None:
+            got_b, tie = lax.optimization_barrier((got_b, tie))
     acc = terms[0].astype(jnp.float32)
     if got_f is not None:
         acc = acc + got_f.astype(jnp.float32)
@@ -76,7 +78,7 @@
     for b in range(1, n_z):
         sent = lax.ppermute(acc[b].astype(jnp.bfloat16), "dp", dp_shift(n_y, n_z, 0, -b))
         total = total + sent.astype(jnp.float32)
-    return total.astype(jnp.bfloat16)
+    return total.astype(jnp.bfloat16), tie
 
 
 def per_device(activations, out_grad, up_blocks, up_rows, down_blocks, down_rows):
@@ -147,12 +149,11 @@
     parts = parts.reshape(2, n_tensor, shard_width // block_size, block_size, tokens)
     parts = jnp.transpose(parts, (1, 0, 4, 2, 3)).reshape(n_tensor, 2, tokens, shard_width)
     mine = scatter_sum(parts, "tensor")
+    terms = jnp.stack([up_term, down_term]).astype(jnp.bfloat16)
+    terms = terms.reshape(2, n_y, n_z, per_dev, block_size, block_size)
+    grads, mine = dp_scatter_rel(jnp.moveaxis(terms, 0, 2), n_y, n_z, mine)
     both = gather_all(mine, "tensor")
     both = jnp.moveaxis(both, 0, 2).reshape(2, tokens, width)
-
-    terms = jnp.stack([up_term, down_term]).astype(jnp.bfloat16)
-    terms = terms.reshape(2, n_y, n_z, per_dev, block_size, block_size)
-    grads = dp_scatter_rel(jnp.moveaxis(terms, 0, 2), n_y, n_z)
     return (both[0], both[1], grads[0], grads[1])
 
 

time: 274 us -> 265 us (0.967)
  local copies, waits for them, and re-layouts: 55.1 us -> 47.7 us
    ppermute x3, waiting for transfers between devices: 27.4 us -> 16.9 us  [dp_scatter_rel(): lax.ppermute(part.astype(jnp.bfloat16), 'dp', dp_shift(n_y, n_z, -1, 0))]
    ppermute x4, waiting for transfers between devices: 21.5 us -> 29.3 us  [dp_scatter_rel(): lax.ppermute(part.astype(jnp.bfloat16), 'dp', dp_shift(n_y, n_z, 1, 0))]
    slice x3 -> x2, local copies, waits for them, and re-layouts: 10.9 us -> 4.39 us  [per_device(): up_all, down_all = (weights[0], weights[1])]
    another operation x0 -> x1, local copies, waits for them, and re-layouts: none -> 4.64 us  [per_device(): down_tiles = down_all.reshape(groups, K, block_size, block_size)]
    gather x3 -> x2, local copies, waits for them, and re-layouts: 7.72 us -> 5.2 us  [per_device(): full_grad.reshape(tokens, row_blocks, block_size)[:, down_index]]
  transfers between devices with their start and end apart: 23 -> 23, of which waited for: 16 -> 15; matrix products, arithmetic and copies ran while one was open for 17% -> 16% of each run, Pallas kernels for 0% -> 0%
where the time goes in v11:
time: 265 us; the launch traced here: 260 us
  starting transfers between devices  93.5 us (35%)
  waiting for transfers between devices  91.8 us (35%)
  local copies, waits for them, and re-layouts  47.7 us (18%)
  matrix products  13.9 us (5%)
  other arithmetic  11.7 us (4%)
    ppermute x4, waiting for transfers between devices, dp_gather_rel(): cur_f = lax.ppermute(cur_f, 'dp', dp_shift(n_y, n_z, 1, 0))  36.2 us
    ppermute x4, waiting for transfers between devices, dp_scatter_rel(): lax.ppermute(part.astype(jnp.bfloat16), 'dp', dp_shift(n_y, n_z, 1, 0))  29.3 us
    ppermute x3, starting transfers between devices, dp_gather_rel(): lax.ppermute(x, 'dp', dp_shift(n_y, n_z, 0, b))  18.9 us
    ppermute x3, waiting for transfers between devices, dp_scatter_rel(): lax.ppermute(part.astype(jnp.bfloat16), 'dp', dp_shift(n_y, n_z, -1, 0))  16.9 us
    ppermute x3, starting transfers between devices, dp_gather_rel(): cur_b = lax.ppermute(cur_b, 'dp', dp_shift(n_y, n_z, -1, 0))  16 us
    all_to_all x2, starting transfers between devices, gather_all(): return lax.all_to_all(spread, axis_name, 0, 0, tiled=True)  11.6 us
    ppermute x3, starting transfers between devices, dp_scatter_rel(): lax.ppermute(acc[b].astype(jnp.bfloat16), 'dp', dp_shift(n_y, n_z, 0, -b))  11.4 us
    ppermute x4, starting transfers between devices, dp_scatter_rel(): lax.ppermute(part.astype(jnp.bfloat16), 'dp', dp_shift(n_y, n_z, 1, 0))  10.5 us
  transfers between devices with their start and end apart: 23, of which 15 were waited for; matrix products, arithmetic and copies ran while one was open for 16% of the time, Pallas kernels for 0%

profile of v11, /device:TPU:6, one launch (start us, length us, event | category | flops | bytes accessed | tf_op | source)
XLA Modules:
  0.0 259.8 jit_solution(718346991928728917)
XLA Ops:
  1.5 6.1 %collective-permute-start = (bf16[2,2,128,128]{3,2,1,0:T(8,128)(2,1)S(1)}, bf16[2,2,128,128]{3,2,1,0:T(8,128)(2,1)S(1)}, u32[]{:S(2)}, u32[]{:S(2)}) collective-permute-start(bf16[2,2,128,128]{3,2,1,0:T(8,128)(2,1)S(1)} %get-tuple-element.30), channel_id=1, source_target_pairs={{0,1},{1,2},{2,3},{3,0},{4,5},{5,6},{6,7},{7,4},{8,9},{9,10},{10,1... | collective-permute-start | bytes 393224 | tf_op jit(solution)/shard_map/ppermute | solution.py:42
  7.6 9.1 %collective-permute-start.1 = (bf16[2,2,128,128]{3,2,1,0:T(8,128)(2,1)S(1)}, bf16[2,2,128,128]{3,2,1,0:T(8,128)(2,1)S(1)}, u32[]{:S(2)}, u32[]{:S(2)}) collective-permute-start(bf16[2,2,128,128]{3,2,1,0:T(8,128)(2,1)S(1)} %get-tuple-element.30), channel_id=1, source_target_pairs={{0,2},{1,3},{2,0},{3,1},{4,6},{5,7},{6,4},{7,5},{8,10},{9,11},{10,... | collective-permute-start | bytes 393224 | tf_op jit(solution)/shard_map/ppermute | solution.py:42
  16.8 3.7 %collective-permute-start.2 = (bf16[2,2,128,128]{3,2,1,0:T(8,128)(2,1)S(1)}, bf16[2,2,128,128]{3,2,1,0:T(8,128)(2,1)S(1)}, u32[]{:S(2)}, u32[]{:S(2)}) collective-permute-start(bf16[2,2,128,128]{3,2,1,0:T(8,128)(2,1)S(1)} %get-tuple-element.30), channel_id=1, source_target_pairs={{0,3},{1,0},{2,1},{3,2},{4,7},{5,4},{6,5},{7,6},{8,11},{9,8},{10,9... | collective-permute-start | bytes 393224 | tf_op jit(solution)/shard_map/ppermute | solution.py:42
  23.3 5.8 %all-to-all-start = ((bf16[16,2,128,256]{2,3,1,0:T(8,128)(2,1)}), bf16[16,2,128,256]{2,3,1,0:T(8,128)(2,1)}, u32[]{:S(2)}, u32[]{:S(2)}) async-start(bf16[16,2,128,256]{2,3,1,0:T(8,128)(2,1)} %broadcast_in_dim.4), calls=%async_computation | async-start | bytes 4194304 | tf_op jit(solution)/shard_map/all_to_all | solution.py:22
  29.4 3.5 %collective-permute-start.3 = (bf16[4,2,2,128,128]{4,3,2,1,0:T(8,128)(2,1)S(1)}, bf16[4,2,2,128,128]{4,3,2,1,0:T(8,128)(2,1)S(1)}, u32[]{:S(2)}, u32[]{:S(2)}) collective-permute-start(bf16[4,2,2,128,128]{4,3,2,1,0:T(8,128)(2,1)S(1)} %pad_maximum_fusion.1), channel_id=1, source_target_pairs={{0,4},{1,5},{2,6},{3,7},{4,8},{5,9},{6,10},{7,11},{8,12},{9,13},{1... | collective-permute-start | bytes 1572872 | tf_op jit(solution)/shard_map/ppermute | solution.py:48
  33.0 13.9 %collective-permute-done.3 = bf16[4,2,2,128,128]{4,3,2,1,0:T(8,128)(2,1)S(1)} collective-permute-done((bf16[4,2,2,128,128]{4,3,2,1,0:T(8,128)(2,1)S(1)}, bf16[4,2,2,128,128]{4,3,2,1,0:T(8,128)(2,1)S(1)}, u32[]{:S(2)}, u32[]{:S(2)}) %collective-permute-start.3) | collective-permute-done | bytes 524320 | tf_op jit(solution)/shard_map/ppermute | solution.py:48
  46.9 1.9 collective-permute-start.4
  49.0 5.1 %collective-permute-start.7 = (bf16[4,2,2,128,128]{4,3,2,1,0:T(8,128)(2,1)S(1)}, bf16[4,2,2,128,128]{4,3,2,1,0:T(8,128)(2,1)S(1)}, u32[]{:S(2)}, u32[]{:S(2)}) collective-permute-start(bf16[4,2,2,128,128]{4,3,2,1,0:T(8,128)(2,1)S(1)} %pad_maximum_fusion.1), channel_id=1, source_target_pairs={{0,28},{1,29},{2,30},{3,31},{4,0},{5,1},{6,2},{7,3},{8,4},{9,5},{1... | collective-permute-start | bytes 1572872 | tf_op jit(solution)/shard_map/ppermute | solution.py:51
  55.0 8.4 %collective-permute-done.4 = bf16[4,2,2,128,128]{4,3,2,1,0:T(8,128)(2,1)S(1)} collective-permute-done((bf16[4,2,2,128,128]{4,3,2,1,0:T(8,128)(2,1)S(1)}, bf16[4,2,2,128,128]{4,3,2,1,0:T(8,128)(2,1)S(1)}, u32[]{:S(2)}, u32[]{:S(2)}) %collective-permute-start.4) | collective-permute-done | bytes 524320 | tf_op jit(solution)/shard_map/ppermute | solution.py:48
  63.4 1.9 collective-permute-start.5
  66.2 5.1 %collective-permute-start.8 = (bf16[4,2,2,128,128]{4,3,2,1,0:T(8,128)(2,1)S(1)}, bf16[4,2,2,128,128]{4,3,2,1,0:T(8,128)(2,1)S(1)}, u32[]{:S(2)}, u32[]{:S(2)}) collective-permute-start(bf16[4,2,2,128,128]{4,3,2,1,0:T(8,128)(2,1)S(1)} %collective-permute-done.7), channel_id=1, source_target_pairs={{0,28},{1,29},{2,30},{3,31},{4,0},{5,1},{6,2},{7,3},{8,4},{9,5},{1... | collective-permute-start | bytes 1572872 | tf_op jit(solution)/shard_map/ppermute | solution.py:51
  71.7 7.3 %collective-permute-done.5 = bf16[4,2,2,128,128]{4,3,2,1,0:T(8,128)(2,1)S(1)} collective-permute-done((bf16[4,2,2,128,128]{4,3,2,1,0:T(8,128)(2,1)S(1)}, bf16[4,2,2,128,128]{4,3,2,1,0:T(8,128)(2,1)S(1)}, u32[]{:S(2)}, u32[]{:S(2)}) %collective-permute-start.5) | collective-permute-done | bytes 524320 | tf_op jit(solution)/shard_map/ppermute | solution.py:48
  79.0 1.9 collective-permute-start.6
  81.1 5.8 %collective-permute-start.9 = (bf16[4,2,2,128,128]{4,3,2,1,0:T(8,128)(2,1)S(1)}, bf16[4,2,2,128,128]{4,3,2,1,0:T(8,128)(2,1)S(1)}, u32[]{:S(2)}, u32[]{:S(2)}) collective-permute-start(bf16[4,2,2,128,128]{4,3,2,1,0:T(8,128)(2,1)S(1)} %collective-permute-done.8), channel_id=1, source_target_pairs={{0,28},{1,29},{2,30},{3,31},{4,0},{5,1},{6,2},{7,3},{8,4},{9,5},{1... | collective-permute-start | bytes 1572872 | tf_op jit(solution)/shard_map/ppermute | solution.py:51
  87.0 6.7 %collective-permute-done.6 = bf16[4,2,2,128,128]{4,3,2,1,0:T(8,128)(2,1)S(1)} collective-permute-done((bf16[4,2,2,128,128]{4,3,2,1,0:T(8,128)(2,1)S(1)}, bf16[4,2,2,128,128]{4,3,2,1,0:T(8,128)(2,1)S(1)}, u32[]{:S(2)}, u32[]{:S(2)}) %collective-permute-start.6) | collective-permute-done | bytes 524320 | tf_op jit(solution)/shard_map/ppermute | solution.py:48
  97.5 4.6 %copy.64 = bf16[8,8,128,128]{2,1,0,3:T(8,128)(2,1)} copy(bf16[8,8,128,128]{3,2,1,0:T(8,128)(2,1)} %bitcast.183) | data formatting | bytes 4194304 | tf_op jit(solution)/shard_map/reshape;squeeze | solution.py:116
  102.2 2.6 %copy.58 = bf16[1,8,4,2,128,128]{4,5,3,2,1,0:T(8,128)(2,1)} copy(bf16[1,8,4,2,128,128]{5,4,3,0,2,1:T(8,128)(2,1)S(1)} %get-tuple-element.19) | data formatting | bytes 4194304 | tf_op jit(solution)/shard_map/slice | solution.py:104
  104.8 4.2 %copy.66 = bf16[8,8,128,128]{3,1,0,2:T(8,128)(2,1)} copy(bf16[8,8,128,128]{2,3,1,0:T(8,128)(2,1)} %bitcast.182) | data formatting | bytes 4194304 | tf_op jit(solution)/shard_map/reshape;squeeze | solution.py:115
  112.8 2.2 gather_fusion.1
  115.0 3.2 %convolution_bitcast_fusion = f32[128,8,128]{0,2,1:T(8,128)} fusion(bf16[8,8,128,128]{3,2,1,0:T(8,128)(2,1)} %bitcast.175, bf16[128,8,8,128]{3,0,2,1:T(8,128)(2,1)S(1)} %bitcast.173), kind=kOutput, calls=%fused_computation.13 | convolution fusion | flops 268435456 | bytes 4718592 | tf_op jit(solution)/shard_map/tgki,gkio->tgo/dot_general | solution.py:120
  118.2 2.2 gather_fusion.3
  120.3 3.2 %fusion.3 = bf16[128,8,128]{0,2,1:T(8,128)(2,1)S(1)} fusion(bf16[8,8,128,128]{3,2,1,0:T(8,128)(2,1)} %bitcast.184, bf16[128,8,8,128]{3,0,2,1:T(8,128)(2,1)} %bitcast.176, f32[128,8,128]{0,2,1:T(8,128)} %convolution_bitcast_fusion), kind=kOutput, calls=%fused_computation.16 | convolution fusion | flops 269746176 | bytes 4980736 | tf_op jit(solution)/shard_map/tgko,gkho->tgh/dot_general | solution.py:134
  131.9 5.9 %all-to-all-start.1 = ((bf16[16,2,128,256]{2,3,1,0:T(8,128)(2,1)}), bf16[16,2,128,256]{2,3,1,0:T(8,128)(2,1)}, u32[]{:S(2)}, u32[]{:S(2)}) async-start(bf16[16,2,128,256]{2,3,1,0:T(8,128)(2,1)} %bitcast.178), calls=%async_computation.1 | async-start | bytes 4194304 | tf_op jit(solution)/shard_map/all_to_all | solution.py:26
  137.8 2.6 %copy.54 = bf16[8,8,128,128]{2,3,1,0:T(8,128)(2,1)} copy(bf16[8,8,128,128]{3,2,1,0:T(8,128)(2,1)S(1)} %bitcast.174) | data formatting | bytes 4194304 | tf_op jit(solution)/shard_map/gather | solution.py:119
  140.4 3.0 %copy.56 = bf16[8,8,128,128]{2,3,1,0:T(8,128)(2,1)S(1)} copy(bf16[8,8,128,128]{3,2,1,0:T(8,128)(2,1)} %bitcast.177) | data formatting | bytes 4194304 | tf_op jit(solution)/shard_map/gather | solution.py:129
  143.5 2.1 multiply_convert_fusion
  145.5 4.1 %copy.63 = bf16[1,8,4,2,128,128]{5,4,3,0,2,1:T(8,128)(2,1)} copy(bf16[1,8,4,2,128,128]{4,5,3,2,1,0:T(8,128)(2,1)} %bitcast.181) | data formatting | bytes 4194304 | tf_op jit(solution)/shard_map/stack | solution.py:152
  151.7 2.7 %collective-permute-start.11 = (bf16[4,2,2,128,128]{4,3,2,1,0:T(8,128)(2,1)S(1)}, bf16[4,2,2,128,128]{4,3,2,1,0:T(8,128)(2,1)S(1)}, u32[]{:S(2)}, u32[]{:S(2)}) collective-permute-start(bf16[4,2,2,128,128]{4,3,2,1,0:T(8,128)(2,1)S(1)} %get-tuple-element.16), channel_id=1, source_target_pairs={{0,4},{1,5},{2,6},{3,7},{4,8},{5,9},{6,10},{7,11},{8,12},{9,13},{1... | collective-permute-start | bytes 1572872 | tf_op jit(solution)/shard_map/ppermute | solution.py:64
  154.4 4.8 %collective-permute-start.10 = (bf16[4,2,2,128,128]{4,3,2,1,0:T(8,128)(2,1)S(1)}, bf16[4,2,2,128,128]{4,3,2,1,0:T(8,128)(2,1)}, u32[]{:S(2)}, u32[]{:S(2)}) collective-permute-start(bf16[4,2,2,128,128]{4,3,2,1,0:T(8,128)(2,1)S(1)} %get-tuple-element.17), channel_id=1, source_target_pairs={{0,28},{1,29},{2,30},{3,31},{4,0},{5,1},{6,2},{7,3},{8,4},{9,5},{1... | collective-permute-start | bytes 1572872 | tf_op jit(solution)/shard_map/ppermute | solution.py:69
  159.2 10.3 %collective-permute-done.11 = bf16[4,2,2,128,128]{4,3,2,1,0:T(8,128)(2,1)S(1)} collective-permute-done((bf16[4,2,2,128,128]{4,3,2,1,0:T(8,128)(2,1)S(1)}, bf16[4,2,2,128,128]{4,3,2,1,0:T(8,128)(2,1)S(1)}, u32[]{:S(2)}, u32[]{:S(2)}) %collective-permute-start.11) | collective-permute-done | bytes 524320 | tf_op jit(solution)/shard_map/ppermute | solution.py:64
  169.7 1.9 collective-permute-start.12
  171.6 1.9 reduce_sum.12
  175.3 5.7 %all-to-all-start.2 = ((bf16[16,2,128,256]{3,2,1,0:T(8,128)(2,1)}), bf16[16,2,128,256]{3,2,1,0:T(8,128)(2,1)S(1)}, u32[]{:S(2)}, u32[]{:S(2)}) async-start(bf16[16,2,128,256]{3,2,1,0:T(8,128)(2,1)} %broadcast_in_dim.5), calls=%async_computation.2 | async-start | bytes 4194304 | tf_op jit(solution)/shard_map/all_to_all | solution.py:22
  181.0 5.3 %collective-permute-done.12 = bf16[4,2,2,128,128]{4,3,2,1,0:T(8,128)(2,1)S(1)} collective-permute-done((bf16[4,2,2,128,128]{4,3,2,1,0:T(8,128)(2,1)S(1)}, bf16[4,2,2,128,128]{4,3,2,1,0:T(8,128)(2,1)S(1)}, u32[]{:S(2)}, u32[]{:S(2)}) %collective-permute-start.12) | collective-permute-done | bytes 524320 | tf_op jit(solution)/shard_map/ppermute | solution.py:64
  187.5 1.9 collective-permute-start.13
  189.4 13.7 %collective-permute-done.13 = bf16[4,2,2,128,128]{4,3,2,1,0:T(8,128)(2,1)S(1)} collective-permute-done((bf16[4,2,2,128,128]{4,3,2,1,0:T(8,128)(2,1)S(1)}, bf16[4,2,2,128,128]{4,3,2,1,0:T(8,128)(2,1)S(1)}, u32[]{:S(2)}, u32[]{:S(2)}) %collective-permute-start.13) | collective-permute-done | bytes 524320 | tf_op jit(solution)/shard_map/ppermute | solution.py:64
  204.9 1.9 collective-permute-start.15
  206.8 3.9 %collective-permute-start.14 = (bf16[4,2,2,128,128]{4,3,2,1,0:T(8,128)(2,1)S(1)}, bf16[4,2,2,128,128]{4,3,2,1,0:T(8,128)(2,1)S(1)}, u32[]{:S(2)}, u32[]{:S(2)}) collective-permute-start(bf16[4,2,2,128,128]{4,3,2,1,0:T(8,128)(2,1)S(1)} %get-tuple-element.14), channel_id=1, source_target_pairs={{0,4},{1,5},{2,6},{3,7},{4,8},{5,9},{6,10},{7,11},{8,12},{9,13},{1... | collective-permute-start | bytes 1572872 | tf_op jit(solution)/shard_map/ppermute | solution.py:64
  210.7 7.7 %collective-permute-done.15 = bf16[4,2,2,128,128]{4,3,2,1,0:T(8,128)(2,1)S(1)} collective-permute-done((bf16[4,2,2,128,128]{4,3,2,1,0:T(8,128)(2,1)S(1)}, bf16[4,2,2,128,128]{4,3,2,1,0:T(8,128)(2,1)S(1)}, u32[]{:S(2)}, u32[]{:S(2)}) %collective-permute-start.15) | collective-permute-done | bytes 524320 | tf_op jit(solution)/shard_map/ppermute | solution.py:69
  219.6 3.4 %collective-permute-start.16 = (bf16[4,2,2,128,128]{4,3,2,1,0:T(8,128)(2,1)S(1)}, bf16[4,2,2,128,128]{4,3,2,1,0:T(8,128)(2,1)S(1)}, u32[]{:S(2)}, u32[]{:S(2)}) collective-permute-start(bf16[4,2,2,128,128]{4,3,2,1,0:T(8,128)(2,1)S(1)} %fusion.5), channel_id=1, source_target_pairs={{0,28},{1,29},{2,30},{3,31},{4,0},{5,1},{6,2},{7,3},{8,4},{9,5},{1... | collective-permute-start | bytes 1572872 | tf_op jit(solution)/shard_map/ppermute | solution.py:69
  223.1 9.2 %collective-permute-done.16 = bf16[4,2,2,128,128]{4,3,2,1,0:T(8,128)(2,1)S(1)} collective-permute-done((bf16[4,2,2,128,128]{4,3,2,1,0:T(8,128)(2,1)S(1)}, bf16[4,2,2,128,128]{4,3,2,1,0:T(8,128)(2,1)S(1)}, u32[]{:S(2)}, u32[]{:S(2)}) %collective-permute-start.16) | collective-permute-done | bytes 524320 | tf_op jit(solution)/shard_map/ppermute | solution.py:69
  233.6 4.7 %collective-permute-start.17 = (bf16[2,2,128,128]{3,2,1,0:T(8,128)(2,1)S(1)}, bf16[2,2,128,128]{3,2,1,0:T(8,128)(2,1)S(1)}, u32[]{:S(2)}, u32[]{:S(2)}) collective-permute-start(bf16[2,2,128,128]{3,2,1,0:T(8,128)(2,1)S(1)} %get-tuple-element.24), channel_id=1, source_target_pairs={{0,3},{1,0},{2,1},{3,2},{4,7},{5,4},{6,5},{7,6},{8,11},{9,8},{10,9... | collective-permute-start | bytes 393224 | tf_op jit(solution)/shard_map/ppermute | solution.py:79
  238.3 3.9 %collective-permute-start.18 = (bf16[2,2,128,128]{3,2,1,0:T(8,128)(2,1)S(1)}, bf16[2,2,128,128]{3,2,1,0:T(8,128)(2,1)S(1)}, u32[]{:S(2)}, u32[]{:S(2)}) collective-permute-start(bf16[2,2,128,128]{3,2,1,0:T(8,128)(2,1)S(1)} %get-tuple-element.26), channel_id=1, source_target_pairs={{0,2},{1,3},{2,0},{3,1},{4,6},{5,7},{6,4},{7,5},{8,10},{9,11},{10,... | collective-permute-start | bytes 393224 | tf_op jit(solution)/shard_map/ppermute | solution.py:79
  242.2 2.8 %collective-permute-start.19 = (bf16[2,2,128,128]{3,2,1,0:T(8,128)(2,1)S(1)}, bf16[2,2,128,128]{3,2,1,0:T(8,128)(2,1)S(1)}, u32[]{:S(2)}, u32[]{:S(2)}) collective-permute-start(bf16[2,2,128,128]{3,2,1,0:T(8,128)(2,1)S(1)} %get-tuple-element.25), channel_id=1, source_target_pairs={{0,1},{1,2},{2,3},{3,0},{4,5},{5,6},{6,7},{7,4},{8,9},{9,10},{10,1... | collective-permute-start | bytes 393224 | tf_op jit(solution)/shard_map/ppermute | solution.py:79
  245.0 2.6 collective-permute-done.17
  247.6 2.9 %collective-permute-done.18 = bf16[2,2,128,128]{3,2,1,0:T(8,128)(2,1)S(1)} collective-permute-done((bf16[2,2,128,128]{3,2,1,0:T(8,128)(2,1)S(1)}, bf16[2,2,128,128]{3,2,1,0:T(8,128)(2,1)S(1)}, u32[]{:S(2)}, u32[]{:S(2)}) %collective-permute-start.18) | collective-permute-done | bytes 131104 | tf_op jit(solution)/shard_map/ppermute | solution.py:79
  250.6 1.9 collective-permute-done.19
  253.2 2.3 copy.71
  (90 shorter events, 37.1 us)
Async XLA Ops:
  0.6 53.5 %copy-start = (s32[64]{0:T(128)S(1)}, s32[64]{0:T(128)}, u32[]{:S(2)}) copy-start(s32[64]{0:T(128)} %param.9) | copy-start | bytes 772
  1.5 27.6 %collective-permute-start = (bf16[2,2,128,128]{3,2,1,0:T(8,128)(2,1)S(1)}, bf16[2,2,128,128]{3,2,1,0:T(8,128)(2,1)S(1)}, u32[]{:S(2)}, u32[]{:S(2)}) collective-permute-start(bf16[2,2,128,128]{3,2,1,0:T(8,128)(2,1)S(1)} %get-tuple-element.30), channel_id=1, source_target_pairs={{0,1},{1,2},{2,3},{3,0},{4,5},{5,6},{6,7},{7,4},{8,9},{9,10},{10,1... | collective-permute-start | bytes 393224 | tf_op jit(solution)/shard_map/ppermute | solution.py:42
  7.6 21.5 %collective-permute-start.1 = (bf16[2,2,128,128]{3,2,1,0:T(8,128)(2,1)S(1)}, bf16[2,2,128,128]{3,2,1,0:T(8,128)(2,1)S(1)}, u32[]{:S(2)}, u32[]{:S(2)}) collective-permute-start(bf16[2,2,128,128]{3,2,1,0:T(8,128)(2,1)S(1)} %get-tuple-element.30), channel_id=1, source_target_pairs={{0,2},{1,3},{2,0},{3,1},{4,6},{5,7},{6,4},{7,5},{8,10},{9,11},{10,... | collective-permute-start | bytes 393224 | tf_op jit(solution)/shard_map/ppermute | solution.py:42
  16.8 12.6 %collective-permute-start.2 = (bf16[2,2,128,128]{3,2,1,0:T(8,128)(2,1)S(1)}, bf16[2,2,128,128]{3,2,1,0:T(8,128)(2,1)S(1)}, u32[]{:S(2)}, u32[]{:S(2)}) collective-permute-start(bf16[2,2,128,128]{3,2,1,0:T(8,128)(2,1)S(1)} %get-tuple-element.30), channel_id=1, source_target_pairs={{0,3},{1,0},{2,1},{3,2},{4,7},{5,4},{6,5},{7,6},{8,11},{9,8},{10,9... | collective-permute-start | bytes 393224 | tf_op jit(solution)/shard_map/ppermute | solution.py:42
  23.3 42.1 %copy-start.2 = (s32[64]{0:T(128)S(1)}, s32[64]{0:T(128)}, u32[]{:S(2)}) copy-start(s32[64]{0:T(128)} %param.11) | copy-start | bytes 772
  23.3 85.6 %all-to-all-start = ((bf16[16,2,128,256]{2,3,1,0:T(8,128)(2,1)}), bf16[16,2,128,256]{2,3,1,0:T(8,128)(2,1)}, u32[]{:S(2)}, u32[]{:S(2)}) async-start(bf16[16,2,128,256]{2,3,1,0:T(8,128)(2,1)} %broadcast_in_dim.4), calls=%async_computation | async-start | bytes 4194304 | tf_op jit(solution)/shard_map/all_to_all | solution.py:22
  29.4 17.5 %collective-permute-start.3 = (bf16[4,2,2,128,128]{4,3,2,1,0:T(8,128)(2,1)S(1)}, bf16[4,2,2,128,128]{4,3,2,1,0:T(8,128)(2,1)S(1)}, u32[]{:S(2)}, u32[]{:S(2)}) collective-permute-start(bf16[4,2,2,128,128]{4,3,2,1,0:T(8,128)(2,1)S(1)} %pad_maximum_fusion.1), channel_id=1, source_target_pairs={{0,4},{1,5},{2,6},{3,7},{4,8},{5,9},{6,10},{7,11},{8,12},{9,13},{1... | collective-permute-start | bytes 1572872 | tf_op jit(solution)/shard_map/ppermute | solution.py:48
  46.9 16.5 %collective-permute-start.4 = (bf16[4,2,2,128,128]{4,3,2,1,0:T(8,128)(2,1)S(1)}, bf16[4,2,2,128,128]{4,3,2,1,0:T(8,128)(2,1)S(1)}, u32[]{:S(2)}, u32[]{:S(2)}) collective-permute-start(bf16[4,2,2,128,128]{4,3,2,1,0:T(8,128)(2,1)S(1)} %collective-permute-done.3), channel_id=1, source_target_pairs={{0,4},{1,5},{2,6},{3,7},{4,8},{5,9},{6,10},{7,11},{8,12},{9,13},{1... | collective-permute-start | bytes 1572872 | tf_op jit(solution)/shard_map/ppermute | solution.py:48
  49.0 17.2 %collective-permute-start.7 = (bf16[4,2,2,128,128]{4,3,2,1,0:T(8,128)(2,1)S(1)}, bf16[4,2,2,128,128]{4,3,2,1,0:T(8,128)(2,1)S(1)}, u32[]{:S(2)}, u32[]{:S(2)}) collective-permute-start(bf16[4,2,2,128,128]{4,3,2,1,0:T(8,128)(2,1)S(1)} %pad_maximum_fusion.1), channel_id=1, source_target_pairs={{0,28},{1,29},{2,30},{3,31},{4,0},{5,1},{6,2},{7,3},{8,4},{9,5},{1... | collective-permute-start | bytes 1572872 | tf_op jit(solution)/shard_map/ppermute | solution.py:51
  63.4 15.6 %collective-permute-start.5 = (bf16[4,2,2,128,128]{4,3,2,1,0:T(8,128)(2,1)S(1)}, bf16[4,2,2,128,128]{4,3,2,1,0:T(8,128)(2,1)S(1)}, u32[]{:S(2)}, u32[]{:S(2)}) collective-permute-start(bf16[4,2,2,128,128]{4,3,2,1,0:T(8,128)(2,1)S(1)} %collective-permute-done.4), channel_id=1, source_target_pairs={{0,4},{1,5},{2,6},{3,7},{4,8},{5,9},{6,10},{7,11},{8,12},{9,13},{1... | collective-permute-start | bytes 1572872 | tf_op jit(solution)/shard_map/ppermute | solution.py:48
  66.2 14.9 %collective-permute-start.8 = (bf16[4,2,2,128,128]{4,3,2,1,0:T(8,128)(2,1)S(1)}, bf16[4,2,2,128,128]{4,3,2,1,0:T(8,128)(2,1)S(1)}, u32[]{:S(2)}, u32[]{:S(2)}) collective-permute-start(bf16[4,2,2,128,128]{4,3,2,1,0:T(8,128)(2,1)S(1)} %collective-permute-done.7), channel_id=1, source_target_pairs={{0,28},{1,29},{2,30},{3,31},{4,0},{5,1},{6,2},{7,3},{8,4},{9,5},{1... | collective-permute-start | bytes 1572872 | tf_op jit(solution)/shard_map/ppermute | solution.py:51
  79.0 14.7 %collective-permute-start.6 = (bf16[4,2,2,128,128]{4,3,2,1,0:T(8,128)(2,1)S(1)}, bf16[4,2,2,128,128]{4,3,2,1,0:T(8,128)(2,1)S(1)}, u32[]{:S(2)}, u32[]{:S(2)}) collective-permute-start(bf16[4,2,2,128,128]{4,3,2,1,0:T(8,128)(2,1)S(1)} %collective-permute-done.5), channel_id=1, source_target_pairs={{0,4},{1,5},{2,6},{3,7},{4,8},{5,9},{6,10},{7,11},{8,12},{9,13},{1... | collective-permute-start | bytes 1572872 | tf_op jit(solution)/shard_map/ppermute | solution.py:48
  81.1 14.4 %collective-permute-start.9 = (bf16[4,2,2,128,128]{4,3,2,1,0:T(8,128)(2,1)S(1)}, bf16[4,2,2,128,128]{4,3,2,1,0:T(8,128)(2,1)S(1)}, u32[]{:S(2)}, u32[]{:S(2)}) collective-permute-start(bf16[4,2,2,128,128]{4,3,2,1,0:T(8,128)(2,1)S(1)} %collective-permute-done.8), channel_id=1, source_target_pairs={{0,28},{1,29},{2,30},{3,31},{4,0},{5,1},{6,2},{7,3},{8,4},{9,5},{1... | collective-permute-start | bytes 1572872 | tf_op jit(solution)/shard_map/ppermute | solution.py:51
  97.5 4.6 %copy-start.3 = (bf16[1,8,4,2,128,128]{5,4,3,0,2,1:T(8,128)(2,1)}, bf16[1,8,4,2,128,128]{5,4,3,0,2,1:T(8,128)(2,1)S(1)}, u32[]{:S(2)}) copy-start(bf16[1,8,4,2,128,128]{5,4,3,0,2,1:T(8,128)(2,1)S(1)} %get-tuple-element.19) | copy-start | bytes 6291460
  120.3 3.2 %copy-start.6 = (bf16[8,8,128,128]{2,1,0,3:T(8,128)(2,1)S(1)}, bf16[8,8,128,128]{2,1,0,3:T(8,128)(2,1)}, u32[]{:S(2)}) copy-start(bf16[8,8,128,128]{2,1,0,3:T(8,128)(2,1)} %copy.64) | copy-start | bytes 6291460
  120.3 3.2 %copy-start.9 = (f32[128,8,128]{0,2,1:T(8,128)S(1)}, f32[128,8,128]{0,2,1:T(8,128)}, u32[]{:S(2)}) copy-start(f32[128,8,128]{0,2,1:T(8,128)} %convolution_bitcast_fusion) | copy-start | bytes 1572868
  126.0 1.6 copy-start.5
  131.9 39.6 %all-to-all-start.1 = ((bf16[16,2,128,256]{2,3,1,0:T(8,128)(2,1)}), bf16[16,2,128,256]{2,3,1,0:T(8,128)(2,1)}, u32[]{:S(2)}, u32[]{:S(2)}) async-start(bf16[16,2,128,256]{2,3,1,0:T(8,128)(2,1)} %bitcast.178), calls=%async_computation.1 | async-start | bytes 4194304 | tf_op jit(solution)/shard_map/all_to_all | solution.py:26
  145.5 4.1 %copy-start.7 = (bf16[8,8,128,128]{2,3,1,0:T(8,128)(2,1)S(1)}, bf16[8,8,128,128]{2,3,1,0:T(8,128)(2,1)}, u32[]{:S(2)}) copy-start(bf16[8,8,128,128]{2,3,1,0:T(8,128)(2,1)} %copy.54) | copy-start | bytes 6291460
  149.6 1.6 copy-start.8
  151.6 17.9 %copy-start.4 = (bf16[8,4,2,2,128,128]{5,4,3,2,1,0:T(8,128)(2,1)}, bf16[8,4,2,2,128,128]{5,4,3,2,1,0:T(8,128)(2,1)S(1)}, u32[]{:S(2)}) copy-start(bf16[8,4,2,2,128,128]{5,4,3,2,1,0:T(8,128)(2,1)S(1)} %maximum_bitcast_fusion) | copy-start | bytes 12582916
  151.7 17.8 %collective-permute-start.11 = (bf16[4,2,2,128,128]{4,3,2,1,0:T(8,128)(2,1)S(1)}, bf16[4,2,2,128,128]{4,3,2,1,0:T(8,128)(2,1)S(1)}, u32[]{:S(2)}, u32[]{:S(2)}) collective-permute-start(bf16[4,2,2,128,128]{4,3,2,1,0:T(8,128)(2,1)S(1)} %get-tuple-element.16), channel_id=1, source_target_pairs={{0,4},{1,5},{2,6},{3,7},{4,8},{5,9},{6,10},{7,11},{8,12},{9,13},{1... | collective-permute-start | bytes 1572872 | tf_op jit(solution)/shard_map/ppermute | solution.py:64
  154.4 19.1 %collective-permute-start.10 = (bf16[4,2,2,128,128]{4,3,2,1,0:T(8,128)(2,1)S(1)}, bf16[4,2,2,128,128]{4,3,2,1,0:T(8,128)(2,1)}, u32[]{:S(2)}, u32[]{:S(2)}) collective-permute-start(bf16[4,2,2,128,128]{4,3,2,1,0:T(8,128)(2,1)S(1)} %get-tuple-element.17), channel_id=1, source_target_pairs={{0,28},{1,29},{2,30},{3,31},{4,0},{5,1},{6,2},{7,3},{8,4},{9,5},{1... | collective-permute-start | bytes 1572872 | tf_op jit(solution)/shard_map/ppermute | solution.py:69
  169.7 16.6 %collective-permute-start.12 = (bf16[4,2,2,128,128]{4,3,2,1,0:T(8,128)(2,1)S(1)}, bf16[4,2,2,128,128]{4,3,2,1,0:T(8,128)(2,1)S(1)}, u32[]{:S(2)}, u32[]{:S(2)}) collective-permute-start(bf16[4,2,2,128,128]{4,3,2,1,0:T(8,128)(2,1)S(1)} %fusion.6), channel_id=1, source_target_pairs={{0,4},{1,5},{2,6},{3,7},{4,8},{5,9},{6,10},{7,11},{8,12},{9,13},{1... | collective-permute-start | bytes 1572872 | tf_op jit(solution)/shard_map/ppermute | solution.py:64
  175.3 77.9 %all-to-all-start.2 = ((bf16[16,2,128,256]{3,2,1,0:T(8,128)(2,1)}), bf16[16,2,128,256]{3,2,1,0:T(8,128)(2,1)S(1)}, u32[]{:S(2)}, u32[]{:S(2)}) async-start(bf16[16,2,128,256]{3,2,1,0:T(8,128)(2,1)} %broadcast_in_dim.5), calls=%async_computation.2 | async-start | bytes 4194304 | tf_op jit(solution)/shard_map/all_to_all | solution.py:22
  187.5 15.7 %collective-permute-start.13 = (bf16[4,2,2,128,128]{4,3,2,1,0:T(8,128)(2,1)S(1)}, bf16[4,2,2,128,128]{4,3,2,1,0:T(8,128)(2,1)S(1)}, u32[]{:S(2)}, u32[]{:S(2)}) collective-permute-start(bf16[4,2,2,128,128]{4,3,2,1,0:T(8,128)(2,1)S(1)} %fusion.7), channel_id=1, source_target_pairs={{0,4},{1,5},{2,6},{3,7},{4,8},{5,9},{6,10},{7,11},{8,12},{9,13},{1... | collective-permute-start | bytes 1572872 | tf_op jit(solution)/shard_map/ppermute | solution.py:64
  204.9 13.5 %collective-permute-start.15 = (bf16[4,2,2,128,128]{4,3,2,1,0:T(8,128)(2,1)S(1)}, bf16[4,2,2,128,128]{4,3,2,1,0:T(8,128)(2,1)S(1)}, u32[]{:S(2)}, u32[]{:S(2)}) collective-permute-start(bf16[4,2,2,128,128]{4,3,2,1,0:T(8,128)(2,1)S(1)} %get-tuple-element.15), channel_id=1, source_target_pairs={{0,28},{1,29},{2,30},{3,31},{4,0},{5,1},{6,2},{7,3},{8,4},{9,5},{1... | collective-permute-start | bytes 1572872 | tf_op jit(solution)/shard_map/ppermute | solution.py:69
  206.8 16.3 %collective-permute-start.14 = (bf16[4,2,2,128,128]{4,3,2,1,0:T(8,128)(2,1)S(1)}, bf16[4,2,2,128,128]{4,3,2,1,0:T(8,128)(2,1)S(1)}, u32[]{:S(2)}, u32[]{:S(2)}) collective-permute-start(bf16[4,2,2,128,128]{4,3,2,1,0:T(8,128)(2,1)S(1)} %get-tuple-element.14), channel_id=1, source_target_pairs={{0,4},{1,5},{2,6},{3,7},{4,8},{5,9},{6,10},{7,11},{8,12},{9,13},{1... | collective-permute-start | bytes 1572872 | tf_op jit(solution)/shard_map/ppermute | solution.py:64
  219.6 12.6 %collective-permute-start.16 = (bf16[4,2,2,128,128]{4,3,2,1,0:T(8,128)(2,1)S(1)}, bf16[4,2,2,128,128]{4,3,2,1,0:T(8,128)(2,1)S(1)}, u32[]{:S(2)}, u32[]{:S(2)}) collective-permute-start(bf16[4,2,2,128,128]{4,3,2,1,0:T(8,128)(2,1)S(1)} %fusion.5), channel_id=1, source_target_pairs={{0,28},{1,29},{2,30},{3,31},{4,0},{5,1},{6,2},{7,3},{8,4},{9,5},{1... | collective-permute-start | bytes 1572872 | tf_op jit(solution)/shard_map/ppermute | solution.py:69
  233.6 14.0 %collective-permute-start.17 = (bf16[2,2,128,128]{3,2,1,0:T(8,128)(2,1)S(1)}, bf16[2,2,128,128]{3,2,1,0:T(8,128)(2,1)S(1)}, u32[]{:S(2)}, u32[]{:S(2)}) collective-permute-start(bf16[2,2,128,128]{3,2,1,0:T(8,128)(2,1)S(1)} %get-tuple-element.24), channel_id=1, source_target_pairs={{0,3},{1,0},{2,1},{3,2},{4,7},{5,4},{6,5},{7,6},{8,11},{9,8},{10,9... | collective-permute-start | bytes 393224 | tf_op jit(solution)/shard_map/ppermute | solution.py:79
  238.3 12.3 %collective-permute-start.18 = (bf16[2,2,128,128]{3,2,1,0:T(8,128)(2,1)S(1)}, bf16[2,2,128,128]{3,2,1,0:T(8,128)(2,1)S(1)}, u32[]{:S(2)}, u32[]{:S(2)}) collective-permute-start(bf16[2,2,128,128]{3,2,1,0:T(8,128)(2,1)S(1)} %get-tuple-element.26), channel_id=1, source_target_pairs={{0,2},{1,3},{2,0},{3,1},{4,6},{5,7},{6,4},{7,5},{8,10},{9,11},{10,... | collective-permute-start | bytes 393224 | tf_op jit(solution)/shard_map/ppermute | solution.py:79
  242.2 10.2 %collective-permute-start.19 = (bf16[2,2,128,128]{3,2,1,0:T(8,128)(2,1)S(1)}, bf16[2,2,128,128]{3,2,1,0:T(8,128)(2,1)S(1)}, u32[]{:S(2)}, u32[]{:S(2)}) collective-permute-start(bf16[2,2,128,128]{3,2,1,0:T(8,128)(2,1)S(1)} %get-tuple-element.25), channel_id=1, source_target_pairs={{0,1},{1,2},{2,3},{3,0},{4,5},{5,6},{6,7},{7,4},{8,9},{9,10},{10,1... | collective-permute-start | bytes 393224 | tf_op jit(solution)/shard_map/ppermute | solution.py:79
  257.2 2.6 %copy-start.1 = (s32[64]{0:T(128)S(1)}, s32[64]{0:T(128)}, u32[]{:S(2)}) copy-start(s32[64]{0:T(128)} %param.9) | copy-start | bytes 772

commit v12 on v11

--- a/solution.py
+++ b/solution.py
@@ -54,26 +54,43 @@
     return jnp.stack(rel)
 
 
+def ring_chain(terms, n_y, n_z, steps, dest, direction, first, tie=None):
+    got = None
+    for k in range(1, steps + 1):
+        part = terms[dest(k)].astype(jnp.float32)
+        if k == 1:
+            part = part[first]
+        elif got.shape == part.shape:
+            part = part + got.astype(jnp.float32)
+        else:
+            part = part.at[first].add(got.astype(jnp.float32))
+        got = lax.ppermute(part.astype(jnp.bfloat16), "dp", dp_shift(n_y, n_z, direction, 0))
+        if k == 1 and tie is not None:
+            got, tie = lax.optimization_barrier((got, tie))
+    return got, tie
+
+
 def dp_scatter_rel(terms, n_y, n_z, tie=None):
-    n_f, n_b = n_y // 2, (n_y - 1) // 2
-    got_f = got_b = None
-    for k in range(1, n_f + 1):
-        part = terms[(n_y - n_f - 1 + k) % n_y].astype(jnp.float32)
-        if got_f is not None:
-            part = part + got_f.astype(jnp.float32)
-        got_f = lax.ppermute(part.astype(jnp.bfloat16), "dp", dp_shift(n_y, n_z, 1, 0))
-    for k in range(1, n_b + 1):
-        part = terms[n_b + 1 - k].astype(jnp.float32)
-        if got_b is not None:
-            part = part + got_b.astype(jnp.float32)
-        got_b = lax.ppermute(part.astype(jnp.bfloat16), "dp", dp_shift(n_y, n_z, -1, 0))
-        if k == 1 and tie is not None:
-            got_b, tie = lax.optimization_barrier((got_b, tie))
+    half = n_y // 2
+    split = n_y % 2 == 0 and terms.shape[1] % 2 == 0
+    cut = terms.shape[1] // 2
+    n_b = half if split else (n_y - 1) // 2
     acc = terms[0].astype(jnp.float32)
-    if got_f is not None:
-        acc = acc + got_f.astype(jnp.float32)
-    if got_b is not None:
-        acc = acc + got_b.astype(jnp.float32)
+    for steps, dest, direction, first in (
+        (half, lambda k: (n_y - half - 1 + k) % n_y, 1, slice(0, cut) if split else slice(None)),
+        (n_b, lambda k: n_b + 1 - k, -1, slice(cut, None) if split else slice(None)),
+    ):
+        if steps == 0:
+            continue
+        got, tied = ring_chain(
+            terms, n_y, n_z, steps, dest, direction, first, tie if direction < 0 else None
+        )
+        if direction < 0:
+            tie = tied
+        if got.shape == acc.shape:
+            acc = acc + got.astype(jnp.float32)
+        else:
+            acc = acc.at[first].add(got.astype(jnp.float32))
     total = acc[0]
     for b in range(1, n_z):
         sent = lax.ppermute(acc[b].astype(jnp.bfloat16), "dp", dp_shift(n_y, n_z, 0, -b))

time: 265 us -> 273 us (1.030)
  starting transfers between devices: 93.5 us -> 103 us
  waiting for transfers between devices: 91.8 us -> 88 us
    ppermute x7 -> x8, starting transfers between devices: 20.6 us -> 29.9 us  [ring_chain(): lax.ppermute(part.astype(jnp.bfloat16), 'dp', dp_shift(n_y, n_z, directio...]
    ppermute x7 -> x8, waiting for transfers between devices: 46.2 us -> 42 us  [ring_chain(): lax.ppermute(part.astype(jnp.bfloat16), 'dp', dp_shift(n_y, n_z, directio...]
  transfers between devices with their start and end apart: 23 -> 24, of which waited for: 15 -> 15; matrix products, arithmetic and copies ran while one was open for 16% -> 17% of each run, Pallas kernels for 0% -> 0%
where the time goes in v12:
time: 273 us; the launch traced here: 268 us
  starting transfers between devices  103 us (38%)
  waiting for transfers between devices  88 us (32%)
  local copies, waits for them, and re-layouts  48.5 us (18%)
  other arithmetic  14.4 us (5%)
  matrix products  13.2 us (5%)
    ppermute x8, waiting for transfers between devices, ring_chain(): lax.ppermute(part.astype(jnp.bfloat16), 'dp', dp_shift(n_y, n_z, directio...  42 us
    ppermute x4, waiting for transfers between devices, dp_gather_rel(): cur_f = lax.ppermute(cur_f, 'dp', dp_shift(n_y, n_z, 1, 0))  36.2 us
    ppermute x8, starting transfers between devices, ring_chain(): lax.ppermute(part.astype(jnp.bfloat16), 'dp', dp_shift(n_y, n_z, directio...  29.9 us
    ppermute x3, starting transfers between devices, dp_gather_rel(): lax.ppermute(x, 'dp', dp_shift(n_y, n_z, 0, b))  18.9 us
    ppermute x3, starting transfers between devices, dp_gather_rel(): cur_b = lax.ppermute(cur_b, 'dp', dp_shift(n_y, n_z, -1, 0))  16 us
    ppermute x3, starting transfers between devices, dp_scatter_rel(): lax.ppermute(acc[b].astype(jnp.bfloat16), 'dp', dp_shift(n_y, n_z, 0, -b))  11.5 us
    all_to_all x2, starting transfers between devices, gather_all(): return lax.all_to_all(spread, axis_name, 0, 0, tiled=True)  11.4 us
    ppermute x4, starting transfers between devices, dp_gather_rel(): cur_f = lax.ppermute(cur_f, 'dp', dp_shift(n_y, n_z, 1, 0))  9.21 us
  transfers between devices with their start and end apart: 24, of which 15 were waited for; matrix products, arithmetic and copies ran while one was open for 17% of the time, Pallas kernels for 0%

profile of v12, /device:TPU:6, one launch (start us, length us, event | category | flops | bytes accessed | tf_op | source)
XLA Modules:
  0.0 268.2 jit_solution(491215384163198881)
XLA Ops:
  1.5 6.1 %collective-permute-start = (bf16[2,2,128,128]{3,2,1,0:T(8,128)(2,1)S(1)}, bf16[2,2,128,128]{3,2,1,0:T(8,128)(2,1)S(1)}, u32[]{:S(2)}, u32[]{:S(2)}) collective-permute-start(bf16[2,2,128,128]{3,2,1,0:T(8,128)(2,1)S(1)} %get-tuple-element.58), channel_id=1, source_target_pairs={{0,1},{1,2},{2,3},{3,0},{4,5},{5,6},{6,7},{7,4},{8,9},{9,10},{10,1... | collective-permute-start | bytes 393224 | tf_op jit(solution)/shard_map/ppermute | solution.py:42
  7.6 9.1 %collective-permute-start.1 = (bf16[2,2,128,128]{3,2,1,0:T(8,128)(2,1)S(1)}, bf16[2,2,128,128]{3,2,1,0:T(8,128)(2,1)S(1)}, u32[]{:S(2)}, u32[]{:S(2)}) collective-permute-start(bf16[2,2,128,128]{3,2,1,0:T(8,128)(2,1)S(1)} %get-tuple-element.58), channel_id=1, source_target_pairs={{0,2},{1,3},{2,0},{3,1},{4,6},{5,7},{6,4},{7,5},{8,10},{9,11},{10,... | collective-permute-start | bytes 393224 | tf_op jit(solution)/shard_map/ppermute | solution.py:42
  16.8 3.7 %collective-permute-start.2 = (bf16[2,2,128,128]{3,2,1,0:T(8,128)(2,1)S(1)}, bf16[2,2,128,128]{3,2,1,0:T(8,128)(2,1)S(1)}, u32[]{:S(2)}, u32[]{:S(2)}) collective-permute-start(bf16[2,2,128,128]{3,2,1,0:T(8,128)(2,1)S(1)} %get-tuple-element.58), channel_id=1, source_target_pairs={{0,3},{1,0},{2,1},{3,2},{4,7},{5,4},{6,5},{7,6},{8,11},{9,8},{10,9... | collective-permute-start | bytes 393224 | tf_op jit(solution)/shard_map/ppermute | solution.py:42
  23.3 5.8 %all-to-all-start = ((bf16[16,2,128,256]{2,3,1,0:T(8,128)(2,1)}), bf16[16,2,128,256]{2,3,1,0:T(8,128)(2,1)}, u32[]{:S(2)}, u32[]{:S(2)}) async-start(bf16[16,2,128,256]{2,3,1,0:T(8,128)(2,1)} %broadcast_in_dim.4), calls=%async_computation | async-start | bytes 4194304 | tf_op jit(solution)/shard_map/all_to_all | solution.py:22
  29.4 3.5 %collective-permute-start.3 = (bf16[4,2,2,128,128]{4,3,2,1,0:T(8,128)(2,1)S(1)}, bf16[4,2,2,128,128]{4,3,2,1,0:T(8,128)(2,1)S(1)}, u32[]{:S(2)}, u32[]{:S(2)}) collective-permute-start(bf16[4,2,2,128,128]{4,3,2,1,0:T(8,128)(2,1)S(1)} %pad_maximum_fusion.1), channel_id=1, source_target_pairs={{0,4},{1,5},{2,6},{3,7},{4,8},{5,9},{6,10},{7,11},{8,12},{9,13},{1... | collective-permute-start | bytes 1572872 | tf_op jit(solution)/shard_map/ppermute | solution.py:48
  33.0 13.9 %collective-permute-done.3 = bf16[4,2,2,128,128]{4,3,2,1,0:T(8,128)(2,1)S(1)} collective-permute-done((bf16[4,2,2,128,128]{4,3,2,1,0:T(8,128)(2,1)S(1)}, bf16[4,2,2,128,128]{4,3,2,1,0:T(8,128)(2,1)S(1)}, u32[]{:S(2)}, u32[]{:S(2)}) %collective-permute-start.3) | collective-permute-done | bytes 524320 | tf_op jit(solution)/shard_map/ppermute | solution.py:48
  46.9 1.9 collective-permute-start.4
  49.0 5.1 %collective-permute-start.7 = (bf16[4,2,2,128,128]{4,3,2,1,0:T(8,128)(2,1)S(1)}, bf16[4,2,2,128,128]{4,3,2,1,0:T(8,128)(2,1)S(1)}, u32[]{:S(2)}, u32[]{:S(2)}) collective-permute-start(bf16[4,2,2,128,128]{4,3,2,1,0:T(8,128)(2,1)S(1)} %pad_maximum_fusion.1), channel_id=1, source_target_pairs={{0,28},{1,29},{2,30},{3,31},{4,0},{5,1},{6,2},{7,3},{8,4},{9,5},{1... | collective-permute-start | bytes 1572872 | tf_op jit(solution)/shard_map/ppermute | solution.py:51
  55.0 8.4 %collective-permute-done.4 = bf16[4,2,2,128,128]{4,3,2,1,0:T(8,128)(2,1)S(1)} collective-permute-done((bf16[4,2,2,128,128]{4,3,2,1,0:T(8,128)(2,1)S(1)}, bf16[4,2,2,128,128]{4,3,2,1,0:T(8,128)(2,1)S(1)}, u32[]{:S(2)}, u32[]{:S(2)}) %collective-permute-start.4) | collective-permute-done | bytes 524320 | tf_op jit(solution)/shard_map/ppermute | solution.py:48
  63.4 1.9 collective-permute-start.5
  66.2 5.1 %collective-permute-start.8 = (bf16[4,2,2,128,128]{4,3,2,1,0:T(8,128)(2,1)S(1)}, bf16[4,2,2,128,128]{4,3,2,1,0:T(8,128)(2,1)S(1)}, u32[]{:S(2)}, u32[]{:S(2)}) collective-permute-start(bf16[4,2,2,128,128]{4,3,2,1,0:T(8,128)(2,1)S(1)} %collective-permute-done.7), channel_id=1, source_target_pairs={{0,28},{1,29},{2,30},{3,31},{4,0},{5,1},{6,2},{7,3},{8,4},{9,5},{1... | collective-permute-start | bytes 1572872 | tf_op jit(solution)/shard_map/ppermute | solution.py:51
  71.7 7.3 %collective-permute-done.5 = bf16[4,2,2,128,128]{4,3,2,1,0:T(8,128)(2,1)S(1)} collective-permute-done((bf16[4,2,2,128,128]{4,3,2,1,0:T(8,128)(2,1)S(1)}, bf16[4,2,2,128,128]{4,3,2,1,0:T(8,128)(2,1)S(1)}, u32[]{:S(2)}, u32[]{:S(2)}) %collective-permute-start.5) | collective-permute-done | bytes 524320 | tf_op jit(solution)/shard_map/ppermute | solution.py:48
  79.0 1.9 collective-permute-start.6
  81.1 5.8 %collective-permute-start.9 = (bf16[4,2,2,128,128]{4,3,2,1,0:T(8,128)(2,1)S(1)}, bf16[4,2,2,128,128]{4,3,2,1,0:T(8,128)(2,1)S(1)}, u32[]{:S(2)}, u32[]{:S(2)}) collective-permute-start(bf16[4,2,2,128,128]{4,3,2,1,0:T(8,128)(2,1)S(1)} %collective-permute-done.8), channel_id=1, source_target_pairs={{0,28},{1,29},{2,30},{3,31},{4,0},{5,1},{6,2},{7,3},{8,4},{9,5},{1... | collective-permute-start | bytes 1572872 | tf_op jit(solution)/shard_map/ppermute | solution.py:51
  87.0 6.7 %collective-permute-done.6 = bf16[4,2,2,128,128]{4,3,2,1,0:T(8,128)(2,1)S(1)} collective-permute-done((bf16[4,2,2,128,128]{4,3,2,1,0:T(8,128)(2,1)S(1)}, bf16[4,2,2,128,128]{4,3,2,1,0:T(8,128)(2,1)S(1)}, u32[]{:S(2)}, u32[]{:S(2)}) %collective-permute-start.6) | collective-permute-done | bytes 524320 | tf_op jit(solution)/shard_map/ppermute | solution.py:48
  97.5 4.7 %copy.64 = bf16[8,8,128,128]{2,1,0,3:T(8,128)(2,1)} copy(bf16[8,8,128,128]{3,2,1,0:T(8,128)(2,1)} %bitcast.194) | data formatting | bytes 4194304 | tf_op jit(solution)/shard_map/reshape;squeeze | solution.py:133
  102.2 2.6 copy.58
  104.8 4.1 %copy.66 = bf16[8,8,128,128]{3,1,0,2:T(8,128)(2,1)} copy(bf16[8,8,128,128]{2,3,1,0:T(8,128)(2,1)} %bitcast.193) | data formatting | bytes 4194304 | tf_op jit(solution)/shard_map/reshape;squeeze | solution.py:132
  113.4 2.5 convolution_bitcast_fusion
  121.4 2.1 gather_fusion.3
  123.5 3.2 %fusion.3 = bf16[128,8,128]{0,2,1:T(8,128)(2,1)S(1)} fusion(bf16[8,8,128,128]{3,2,1,0:T(8,128)(2,1)} %bitcast.195, bf16[128,8,8,128]{3,0,2,1:T(8,128)(2,1)} %bitcast.187, f32[128,8,128]{0,2,1:T(8,128)} %copy-done.9), kind=kOutput, calls=%fused_computation.16 | convolution fusion | flops 269746176 | bytes 4980736 | tf_op jit(solution)/shard_map/tgko,gkho->tgh/dot_general | solution.py:151
  132.0 5.9 %all-to-all-start.1 = ((bf16[16,2,128,256]{2,3,1,0:T(8,128)(2,1)}), bf16[16,2,128,256]{2,3,1,0:T(8,128)(2,1)}, u32[]{:S(2)}, u32[]{:S(2)}) async-start(bf16[16,2,128,256]{2,3,1,0:T(8,128)(2,1)} %bitcast.189), calls=%async_computation.1 | async-start | bytes 4194304 | tf_op jit(solution)/shard_map/all_to_all | solution.py:26
  137.9 2.6 copy.54
  140.5 3.1 %copy.56 = bf16[8,8,128,128]{2,3,1,0:T(8,128)(2,1)S(1)} copy(bf16[8,8,128,128]{3,2,1,0:T(8,128)(2,1)} %bitcast.188) | data formatting | bytes 4194304 | tf_op jit(solution)/shard_map/gather | solution.py:146
  143.6 2.0 multiply_convert_fusion
  145.7 4.1 %copy.63 = bf16[1,8,4,2,128,128]{5,4,3,0,2,1:T(8,128)(2,1)} copy(bf16[1,8,4,2,128,128]{4,5,3,2,1,0:T(8,128)(2,1)} %bitcast.192) | data formatting | bytes 4194304 | tf_op jit(solution)/shard_map/stack | solution.py:169
  151.8 2.7 %collective-permute-start.11 = (bf16[2,2,2,128,128]{4,3,2,1,0:T(8,128)(2,1)S(1)}, bf16[2,2,2,128,128]{4,3,2,1,0:T(8,128)(2,1)S(1)}, u32[]{:S(2)}, u32[]{:S(2)}) collective-permute-start(bf16[2,2,2,128,128]{4,3,2,1,0:T(8,128)(2,1)S(1)} %get-tuple-element.40), channel_id=1, source_target_pairs={{0,4},{1,5},{2,6},{3,7},{4,8},{5,9},{6,10},{7,11},{8,12},{9,13},{1... | collective-permute-start | bytes 786440 | tf_op jit(solution)/shard_map/ppermute | solution.py:67
  155.8 8.1 %collective-permute-done.11 = bf16[2,2,2,128,128]{4,3,2,1,0:T(8,128)(2,1)S(1)} collective-permute-done((bf16[2,2,2,128,128]{4,3,2,1,0:T(8,128)(2,1)S(1)}, bf16[2,2,2,128,128]{4,3,2,1,0:T(8,128)(2,1)S(1)}, u32[]{:S(2)}, u32[]{:S(2)}) %collective-permute-start.11) | collective-permute-done | bytes 262176 | tf_op jit(solution)/shard_map/ppermute | solution.py:67
  164.7 1.9 collective-permute-start.12
  166.7 5.1 %collective-permute-start.10 = (bf16[2,2,2,128,128]{4,3,2,1,0:T(8,128)(2,1)S(1)}, bf16[2,2,2,128,128]{4,3,2,1,0:T(8,128)(2,1)S(1)}, u32[]{:S(2)}, u32[]{:S(2)}) collective-permute-start(bf16[2,2,2,128,128]{4,3,2,1,0:T(8,128)(2,1)S(1)} %get-tuple-element.41), channel_id=1, source_target_pairs={{0,28},{1,29},{2,30},{3,31},{4,0},{5,1},{6,2},{7,3},{8,4},{9,5},{1... | collective-permute-start | bytes 786440 | tf_op jit(solution)/shard_map/ppermute | solution.py:67
  171.8 1.9 reduce_sum.12
  173.7 3.3 %collective-permute-done.10 = bf16[2,2,2,128,128]{4,3,2,1,0:T(8,128)(2,1)S(1)} collective-permute-done((bf16[2,2,2,128,128]{4,3,2,1,0:T(8,128)(2,1)S(1)}, bf16[2,2,2,128,128]{4,3,2,1,0:T(8,128)(2,1)S(1)}, u32[]{:S(2)}, u32[]{:S(2)}) %collective-permute-start.10) | collective-permute-done | bytes 262176 | tf_op jit(solution)/shard_map/ppermute | solution.py:67
  178.7 5.6 %all-to-all-start.2 = ((bf16[16,2,128,256]{3,2,1,0:T(8,128)(2,1)}), bf16[16,2,128,256]{3,2,1,0:T(8,128)(2,1)S(1)}, u32[]{:S(2)}, u32[]{:S(2)}) async-start(bf16[16,2,128,256]{3,2,1,0:T(8,128)(2,1)} %broadcast_in_dim.5), calls=%async_computation.2 | async-start | bytes 4194304 | tf_op jit(solution)/shard_map/all_to_all | solution.py:22
  185.7 3.7 %collective-permute-start.13 = (bf16[4,2,2,128,128]{4,3,2,1,0:T(8,128)(2,1)S(1)}, bf16[4,2,2,128,128]{4,3,2,1,0:T(8,128)(2,1)S(1)}, u32[]{:S(2)}, u32[]{:S(2)}) collective-permute-start(bf16[4,2,2,128,128]{4,3,2,1,0:T(8,128)(2,1)S(1)} %fusion.6), channel_id=1, source_target_pairs={{0,4},{1,5},{2,6},{3,7},{4,8},{5,9},{6,10},{7,11},{8,12},{9,13},{1... | collective-permute-start | bytes 1572872 | tf_op jit(solution)/shard_map/ppermute | solution.py:67
  190.1 3.8 %collective-permute-start.15 = (bf16[4,2,2,128,128]{4,3,2,1,0:T(8,128)(2,1)}, bf16[4,2,2,128,128]{4,3,2,1,0:T(8,128)(2,1)S(1)}, u32[]{:S(2)}, u32[]{:S(2)}) collective-permute-start(bf16[4,2,2,128,128]{4,3,2,1,0:T(8,128)(2,1)} %fusion.14), channel_id=1, source_target_pairs={{0,28},{1,29},{2,30},{3,31},{4,0},{5,1},{6,2},{7,3},{8,4},{9,5},{1... | collective-permute-start | bytes 1572872 | tf_op jit(solution)/shard_map/ppermute | solution.py:67
  194.0 9.5 %collective-permute-done.13 = bf16[4,2,2,128,128]{4,3,2,1,0:T(8,128)(2,1)S(1)} collective-permute-done((bf16[4,2,2,128,128]{4,3,2,1,0:T(8,128)(2,1)S(1)}, bf16[4,2,2,128,128]{4,3,2,1,0:T(8,128)(2,1)S(1)}, u32[]{:S(2)}, u32[]{:S(2)}) %collective-permute-start.13) | collective-permute-done | bytes 524320 | tf_op jit(solution)/shard_map/ppermute | solution.py:67
  203.5 2.4 collective-permute-done.15
  207.5 5.4 %collective-permute-start.16 = (bf16[4,2,2,128,128]{4,3,2,1,0:T(8,128)(2,1)S(1)}, bf16[4,2,2,128,128]{4,3,2,1,0:T(8,128)(2,1)S(1)}, u32[]{:S(2)}, u32[]{:S(2)}) collective-permute-start(bf16[4,2,2,128,128]{4,3,2,1,0:T(8,128)(2,1)S(1)} %get-tuple-element.39), channel_id=1, source_target_pairs={{0,28},{1,29},{2,30},{3,31},{4,0},{5,1},{6,2},{7,3},{8,4},{9,5},{1... | collective-permute-start | bytes 1572872 | tf_op jit(solution)/shard_map/ppermute | solution.py:67
  212.8 1.9 collective-permute-start.14
  214.8 8.9 %collective-permute-done.16 = bf16[4,2,2,128,128]{4,3,2,1,0:T(8,128)(2,1)S(1)} collective-permute-done((bf16[4,2,2,128,128]{4,3,2,1,0:T(8,128)(2,1)S(1)}, bf16[4,2,2,128,128]{4,3,2,1,0:T(8,128)(2,1)S(1)}, u32[]{:S(2)}, u32[]{:S(2)}) %collective-permute-start.16) | collective-permute-done | bytes 524320 | tf_op jit(solution)/shard_map/ppermute | solution.py:67
  225.0 5.4 %collective-permute-start.17 = (bf16[4,2,2,128,128]{4,3,2,1,0:T(8,128)(2,1)S(1)}, bf16[4,2,2,128,128]{4,3,2,1,0:T(8,128)(2,1)S(1)}, u32[]{:S(2)}, u32[]{:S(2)}) collective-permute-start(bf16[4,2,2,128,128]{4,3,2,1,0:T(8,128)(2,1)S(1)} %fusion.5), channel_id=1, source_target_pairs={{0,28},{1,29},{2,30},{3,31},{4,0},{5,1},{6,2},{7,3},{8,4},{9,5},{1... | collective-permute-start | bytes 1572872 | tf_op jit(solution)/shard_map/ppermute | solution.py:67
  230.3 9.7 %collective-permute-done.17 = bf16[4,2,2,128,128]{4,3,2,1,0:T(8,128)(2,1)S(1)} collective-permute-done((bf16[4,2,2,128,128]{4,3,2,1,0:T(8,128)(2,1)S(1)}, bf16[4,2,2,128,128]{4,3,2,1,0:T(8,128)(2,1)S(1)}, u32[]{:S(2)}, u32[]{:S(2)}) %collective-permute-start.17) | collective-permute-done | bytes 524320 | tf_op jit(solution)/shard_map/ppermute | solution.py:67
  241.4 4.6 %collective-permute-start.18 = (bf16[2,2,128,128]{3,2,1,0:T(8,128)(2,1)S(1)}, bf16[2,2,128,128]{3,2,1,0:T(8,128)(2,1)S(1)}, u32[]{:S(2)}, u32[]{:S(2)}) collective-permute-start(bf16[2,2,128,128]{3,2,1,0:T(8,128)(2,1)S(1)} %get-tuple-element.52), channel_id=1, source_target_pairs={{0,3},{1,0},{2,1},{3,2},{4,7},{5,4},{6,5},{7,6},{8,11},{9,8},{10,9... | collective-permute-start | bytes 393224 | tf_op jit(solution)/shard_map/ppermute | solution.py:96
  246.0 3.9 %collective-permute-start.19 = (bf16[2,2,128,128]{3,2,1,0:T(8,128)(2,1)S(1)}, bf16[2,2,128,128]{3,2,1,0:T(8,128)(2,1)S(1)}, u32[]{:S(2)}, u32[]{:S(2)}) collective-permute-start(bf16[2,2,128,128]{3,2,1,0:T(8,128)(2,1)S(1)} %get-tuple-element.54), channel_id=1, source_target_pairs={{0,2},{1,3},{2,0},{3,1},{4,6},{5,7},{6,4},{7,5},{8,10},{9,11},{10,... | collective-permute-start | bytes 393224 | tf_op jit(solution)/shard_map/ppermute | solution.py:96
  250.0 3.0 %collective-permute-start.20 = (bf16[2,2,128,128]{3,2,1,0:T(8,128)(2,1)S(1)}, bf16[2,2,128,128]{3,2,1,0:T(8,128)(2,1)S(1)}, u32[]{:S(2)}, u32[]{:S(2)}) collective-permute-start(bf16[2,2,128,128]{3,2,1,0:T(8,128)(2,1)S(1)} %get-tuple-element.53), channel_id=1, source_target_pairs={{0,1},{1,2},{2,3},{3,0},{4,5},{5,6},{6,7},{7,4},{8,9},{9,10},{10,1... | collective-permute-start | bytes 393224 | tf_op jit(solution)/shard_map/ppermute | solution.py:96
  253.0 5.9 %collective-permute-done.19 = bf16[2,2,128,128]{3,2,1,0:T(8,128)(2,1)S(1)} collective-permute-done((bf16[2,2,128,128]{3,2,1,0:T(8,128)(2,1)S(1)}, bf16[2,2,128,128]{3,2,1,0:T(8,128)(2,1)S(1)}, u32[]{:S(2)}, u32[]{:S(2)}) %collective-permute-start.19) | collective-permute-done | bytes 131104 | tf_op jit(solution)/shard_map/ppermute | solution.py:96
  258.8 2.0 collective-permute-done.20
  261.6 2.4 copy.71
  (98 shorter events, 42.7 us)
Async XLA Ops:
  0.6 53.5 %copy-start = (s32[64]{0:T(128)S(1)}, s32[64]{0:T(128)}, u32[]{:S(2)}) copy-start(s32[64]{0:T(128)} %param.13) | copy-start | bytes 772
  1.5 27.6 %collective-permute-start = (bf16[2,2,128,128]{3,2,1,0:T(8,128)(2,1)S(1)}, bf16[2,2,128,128]{3,2,1,0:T(8,128)(2,1)S(1)}, u32[]{:S(2)}, u32[]{:S(2)}) collective-permute-start(bf16[2,2,128,128]{3,2,1,0:T(8,128)(2,1)S(1)} %get-tuple-element.58), channel_id=1, source_target_pairs={{0,1},{1,2},{2,3},{3,0},{4,5},{5,6},{6,7},{7,4},{8,9},{9,10},{10,1... | collective-permute-start | bytes 393224 | tf_op jit(solution)/shard_map/ppermute | solution.py:42
  7.6 21.5 %collective-permute-start.1 = (bf16[2,2,128,128]{3,2,1,0:T(8,128)(2,1)S(1)}, bf16[2,2,128,128]{3,2,1,0:T(8,128)(2,1)S(1)}, u32[]{:S(2)}, u32[]{:S(2)}) collective-permute-start(bf16[2,2,128,128]{3,2,1,0:T(8,128)(2,1)S(1)} %get-tuple-element.58), channel_id=1, source_target_pairs={{0,2},{1,3},{2,0},{3,1},{4,6},{5,7},{6,4},{7,5},{8,10},{9,11},{10,... | collective-permute-start | bytes 393224 | tf_op jit(solution)/shard_map/ppermute | solution.py:42
  16.8 12.6 %collective-permute-start.2 = (bf16[2,2,128,128]{3,2,1,0:T(8,128)(2,1)S(1)}, bf16[2,2,128,128]{3,2,1,0:T(8,128)(2,1)S(1)}, u32[]{:S(2)}, u32[]{:S(2)}) collective-permute-start(bf16[2,2,128,128]{3,2,1,0:T(8,128)(2,1)S(1)} %get-tuple-element.58), channel_id=1, source_target_pairs={{0,3},{1,0},{2,1},{3,2},{4,7},{5,4},{6,5},{7,6},{8,11},{9,8},{10,9... | collective-permute-start | bytes 393224 | tf_op jit(solution)/shard_map/ppermute | solution.py:42
  23.3 42.0 %copy-start.2 = (s32[64]{0:T(128)S(1)}, s32[64]{0:T(128)}, u32[]{:S(2)}) copy-start(s32[64]{0:T(128)} %param.15) | copy-start | bytes 772
  23.3 85.6 %all-to-all-start = ((bf16[16,2,128,256]{2,3,1,0:T(8,128)(2,1)}), bf16[16,2,128,256]{2,3,1,0:T(8,128)(2,1)}, u32[]{:S(2)}, u32[]{:S(2)}) async-start(bf16[16,2,128,256]{2,3,1,0:T(8,128)(2,1)} %broadcast_in_dim.4), calls=%async_computation | async-start | bytes 4194304 | tf_op jit(solution)/shard_map/all_to_all | solution.py:22
  29.4 17.5 %collective-permute-start.3 = (bf16[4,2,2,128,128]{4,3,2,1,0:T(8,128)(2,1)S(1)}, bf16[4,2,2,128,128]{4,3,2,1,0:T(8,128)(2,1)S(1)}, u32[]{:S(2)}, u32[]{:S(2)}) collective-permute-start(bf16[4,2,2,128,128]{4,3,2,1,0:T(8,128)(2,1)S(1)} %pad_maximum_fusion.1), channel_id=1, source_target_pairs={{0,4},{1,5},{2,6},{3,7},{4,8},{5,9},{6,10},{7,11},{8,12},{9,13},{1... | collective-permute-start | bytes 1572872 | tf_op jit(solution)/shard_map/ppermute | solution.py:48
  46.9 16.5 %collective-permute-start.4 = (bf16[4,2,2,128,128]{4,3,2,1,0:T(8,128)(2,1)S(1)}, bf16[4,2,2,128,128]{4,3,2,1,0:T(8,128)(2,1)S(1)}, u32[]{:S(2)}, u32[]{:S(2)}) collective-permute-start(bf16[4,2,2,128,128]{4,3,2,1,0:T(8,128)(2,1)S(1)} %collective-permute-done.3), channel_id=1, source_target_pairs={{0,4},{1,5},{2,6},{3,7},{4,8},{5,9},{6,10},{7,11},{8,12},{9,13},{1... | collective-permute-start | bytes 1572872 | tf_op jit(solution)/shard_map/ppermute | solution.py:48
  49.0 17.2 %collective-permute-start.7 = (bf16[4,2,2,128,128]{4,3,2,1,0:T(8,128)(2,1)S(1)}, bf16[4,2,2,128,128]{4,3,2,1,0:T(8,128)(2,1)S(1)}, u32[]{:S(2)}, u32[]{:S(2)}) collective-permute-start(bf16[4,2,2,128,128]{4,3,2,1,0:T(8,128)(2,1)S(1)} %pad_maximum_fusion.1), channel_id=1, source_target_pairs={{0,28},{1,29},{2,30},{3,31},{4,0},{5,1},{6,2},{7,3},{8,4},{9,5},{1... | collective-permute-start | bytes 1572872 | tf_op jit(solution)/shard_map/ppermute | solution.py:51
  63.4 15.6 %collective-permute-start.5 = (bf16[4,2,2,128,128]{4,3,2,1,0:T(8,128)(2,1)S(1)}, bf16[4,2,2,128,128]{4,3,2,1,0:T(8,128)(2,1)S(1)}, u32[]{:S(2)}, u32[]{:S(2)}) collective-permute-start(bf16[4,2,2,128,128]{4,3,2,1,0:T(8,128)(2,1)S(1)} %collective-permute-done.4), channel_id=1, source_target_pairs={{0,4},{1,5},{2,6},{3,7},{4,8},{5,9},{6,10},{7,11},{8,12},{9,13},{1... | collective-permute-start | bytes 1572872 | tf_op jit(solution)/shard_map/ppermute | solution.py:48
  66.2 14.9 %collective-permute-start.8 = (bf16[4,2,2,128,128]{4,3,2,1,0:T(8,128)(2,1)S(1)}, bf16[4,2,2,128,128]{4,3,2,1,0:T(8,128)(2,1)S(1)}, u32[]{:S(2)}, u32[]{:S(2)}) collective-permute-start(bf16[4,2,2,128,128]{4,3,2,1,0:T(8,128)(2,1)S(1)} %collective-permute-done.7), channel_id=1, source_target_pairs={{0,28},{1,29},{2,30},{3,31},{4,0},{5,1},{6,2},{7,3},{8,4},{9,5},{1... | collective-permute-start | bytes 1572872 | tf_op jit(solution)/shard_map/ppermute | solution.py:51
  79.0 14.7 %collective-permute-start.6 = (bf16[4,2,2,128,128]{4,3,2,1,0:T(8,128)(2,1)S(1)}, bf16[4,2,2,128,128]{4,3,2,1,0:T(8,128)(2,1)S(1)}, u32[]{:S(2)}, u32[]{:S(2)}) collective-permute-start(bf16[4,2,2,128,128]{4,3,2,1,0:T(8,128)(2,1)S(1)} %collective-permute-done.5), channel_id=1, source_target_pairs={{0,4},{1,5},{2,6},{3,7},{4,8},{5,9},{6,10},{7,11},{8,12},{9,13},{1... | collective-permute-start | bytes 1572872 | tf_op jit(solution)/shard_map/ppermute | solution.py:48
  81.1 14.4 %collective-permute-start.9 = (bf16[4,2,2,128,128]{4,3,2,1,0:T(8,128)(2,1)S(1)}, bf16[4,2,2,128,128]{4,3,2,1,0:T(8,128)(2,1)S(1)}, u32[]{:S(2)}, u32[]{:S(2)}) collective-permute-start(bf16[4,2,2,128,128]{4,3,2,1,0:T(8,128)(2,1)S(1)} %collective-permute-done.8), channel_id=1, source_target_pairs={{0,28},{1,29},{2,30},{3,31},{4,0},{5,1},{6,2},{7,3},{8,4},{9,5},{1... | collective-permute-start | bytes 1572872 | tf_op jit(solution)/shard_map/ppermute | solution.py:51
  97.5 4.7 %copy-start.3 = (bf16[1,8,4,2,128,128]{5,4,3,0,2,1:T(8,128)(2,1)}, bf16[1,8,4,2,128,128]{5,4,3,0,2,1:T(8,128)(2,1)S(1)}, u32[]{:S(2)}) copy-start(bf16[1,8,4,2,128,128]{5,4,3,0,2,1:T(8,128)(2,1)S(1)} %get-tuple-element.47) | copy-start | bytes 6291460
  113.4 2.5 copy-start.6
  115.9 0.8 copy-start.9
  123.5 3.2 %copy-start.5 = (bf16[8,8,128,128]{3,1,0,2:T(8,128)(2,1)S(1)}, bf16[8,8,128,128]{3,1,0,2:T(8,128)(2,1)}, u32[]{:S(2)}) copy-start(bf16[8,8,128,128]{3,1,0,2:T(8,128)(2,1)} %copy.66) | copy-start | bytes 6291460
  129.1 1.2 copy-start.11
  132.0 39.8 %all-to-all-start.1 = ((bf16[16,2,128,256]{2,3,1,0:T(8,128)(2,1)}), bf16[16,2,128,256]{2,3,1,0:T(8,128)(2,1)}, u32[]{:S(2)}, u32[]{:S(2)}) async-start(bf16[16,2,128,256]{2,3,1,0:T(8,128)(2,1)} %bitcast.189), calls=%async_computation.1 | async-start | bytes 4194304 | tf_op jit(solution)/shard_map/all_to_all | solution.py:26
  140.5 3.1 %copy-start.10 = (f32[128,8,128]{0,2,1:T(8,128)S(1)}, f32[128,8,128]{0,2,1:T(8,128)}, u32[]{:S(2)}) copy-start(f32[128,8,128]{0,2,1:T(8,128)} %copy-done.9) | copy-start | bytes 1572868
  145.7 4.1 %copy-start.7 = (bf16[8,8,128,128]{2,3,1,0:T(8,128)(2,1)S(1)}, bf16[8,8,128,128]{2,3,1,0:T(8,128)(2,1)}, u32[]{:S(2)}) copy-start(bf16[8,8,128,128]{2,3,1,0:T(8,128)(2,1)} %copy.54) | copy-start | bytes 6291460
  149.7 1.6 copy-start.8
  151.7 4.1 %copy-start.4 = (bf16[8,4,2,2,128,128]{5,4,3,2,1,0:T(8,128)(2,1)}, bf16[8,4,2,2,128,128]{5,4,3,2,1,0:T(8,128)(2,1)S(1)}, u32[]{:S(2)}) copy-start(bf16[8,4,2,2,128,128]{5,4,3,2,1,0:T(8,128)(2,1)S(1)} %maximum_bitcast_fusion) | copy-start | bytes 12582916
  151.8 12.2 %collective-permute-start.11 = (bf16[2,2,2,128,128]{4,3,2,1,0:T(8,128)(2,1)S(1)}, bf16[2,2,2,128,128]{4,3,2,1,0:T(8,128)(2,1)S(1)}, u32[]{:S(2)}, u32[]{:S(2)}) collective-permute-start(bf16[2,2,2,128,128]{4,3,2,1,0:T(8,128)(2,1)S(1)} %get-tuple-element.40), channel_id=1, source_target_pairs={{0,4},{1,5},{2,6},{3,7},{4,8},{5,9},{6,10},{7,11},{8,12},{9,13},{1... | collective-permute-start | bytes 786440 | tf_op jit(solution)/shard_map/ppermute | solution.py:67
  164.7 19.6 %collective-permute-start.12 = (bf16[4,2,2,128,128]{4,3,2,1,0:T(8,128)(2,1)}, bf16[4,2,2,128,128]{4,3,2,1,0:T(8,128)(2,1)}, u32[]{:S(2)}, u32[]{:S(2)}) collective-permute-start(bf16[4,2,2,128,128]{4,3,2,1,0:T(8,128)(2,1)} %fusion.16), channel_id=1, source_target_pairs={{0,4},{1,5},{2,6},{3,7},{4,8},{5,9},{6,10},{7,11},{8,12},{9,13},{1... | collective-permute-start | bytes 1572872 | tf_op jit(solution)/shard_map/ppermute | solution.py:67
  166.7 10.3 %collective-permute-start.10 = (bf16[2,2,2,128,128]{4,3,2,1,0:T(8,128)(2,1)S(1)}, bf16[2,2,2,128,128]{4,3,2,1,0:T(8,128)(2,1)S(1)}, u32[]{:S(2)}, u32[]{:S(2)}) collective-permute-start(bf16[2,2,2,128,128]{4,3,2,1,0:T(8,128)(2,1)S(1)} %get-tuple-element.41), channel_id=1, source_target_pairs={{0,28},{1,29},{2,30},{3,31},{4,0},{5,1},{6,2},{7,3},{8,4},{9,5},{1... | collective-permute-start | bytes 786440 | tf_op jit(solution)/shard_map/ppermute | solution.py:67
  178.7 82.9 %all-to-all-start.2 = ((bf16[16,2,128,256]{3,2,1,0:T(8,128)(2,1)}), bf16[16,2,128,256]{3,2,1,0:T(8,128)(2,1)S(1)}, u32[]{:S(2)}, u32[]{:S(2)}) async-start(bf16[16,2,128,256]{3,2,1,0:T(8,128)(2,1)} %broadcast_in_dim.5), calls=%async_computation.2 | async-start | bytes 4194304 | tf_op jit(solution)/shard_map/all_to_all | solution.py:22
  185.7 17.8 %collective-permute-start.13 = (bf16[4,2,2,128,128]{4,3,2,1,0:T(8,128)(2,1)S(1)}, bf16[4,2,2,128,128]{4,3,2,1,0:T(8,128)(2,1)S(1)}, u32[]{:S(2)}, u32[]{:S(2)}) collective-permute-start(bf16[4,2,2,128,128]{4,3,2,1,0:T(8,128)(2,1)S(1)} %fusion.6), channel_id=1, source_target_pairs={{0,4},{1,5},{2,6},{3,7},{4,8},{5,9},{6,10},{7,11},{8,12},{9,13},{1... | collective-permute-start | bytes 1572872 | tf_op jit(solution)/shard_map/ppermute | solution.py:67
  190.1 15.8 %collective-permute-start.15 = (bf16[4,2,2,128,128]{4,3,2,1,0:T(8,128)(2,1)}, bf16[4,2,2,128,128]{4,3,2,1,0:T(8,128)(2,1)S(1)}, u32[]{:S(2)}, u32[]{:S(2)}) collective-permute-start(bf16[4,2,2,128,128]{4,3,2,1,0:T(8,128)(2,1)} %fusion.14), channel_id=1, source_target_pairs={{0,28},{1,29},{2,30},{3,31},{4,0},{5,1},{6,2},{7,3},{8,4},{9,5},{1... | collective-permute-start | bytes 1572872 | tf_op jit(solution)/shard_map/ppermute | solution.py:67
  207.5 16.2 %collective-permute-start.16 = (bf16[4,2,2,128,128]{4,3,2,1,0:T(8,128)(2,1)S(1)}, bf16[4,2,2,128,128]{4,3,2,1,0:T(8,128)(2,1)S(1)}, u32[]{:S(2)}, u32[]{:S(2)}) collective-permute-start(bf16[4,2,2,128,128]{4,3,2,1,0:T(8,128)(2,1)S(1)} %get-tuple-element.39), channel_id=1, source_target_pairs={{0,28},{1,29},{2,30},{3,31},{4,0},{5,1},{6,2},{7,3},{8,4},{9,5},{1... | collective-permute-start | bytes 1572872 | tf_op jit(solution)/shard_map/ppermute | solution.py:67
  212.8 17.5 %collective-permute-start.14 = (bf16[4,2,2,128,128]{4,3,2,1,0:T(8,128)(2,1)S(1)}, bf16[4,2,2,128,128]{4,3,2,1,0:T(8,128)(2,1)S(1)}, u32[]{:S(2)}, u32[]{:S(2)}) collective-permute-start(bf16[4,2,2,128,128]{4,3,2,1,0:T(8,128)(2,1)S(1)} %get-tuple-element.38), channel_id=1, source_target_pairs={{0,4},{1,5},{2,6},{3,7},{4,8},{5,9},{6,10},{7,11},{8,12},{9,13},{1... | collective-permute-start | bytes 1572872 | tf_op jit(solution)/shard_map/ppermute | solution.py:67
  225.0 15.1 %collective-permute-start.17 = (bf16[4,2,2,128,128]{4,3,2,1,0:T(8,128)(2,1)S(1)}, bf16[4,2,2,128,128]{4,3,2,1,0:T(8,128)(2,1)S(1)}, u32[]{:S(2)}, u32[]{:S(2)}) collective-permute-start(bf16[4,2,2,128,128]{4,3,2,1,0:T(8,128)(2,1)S(1)} %fusion.5), channel_id=1, source_target_pairs={{0,28},{1,29},{2,30},{3,31},{4,0},{5,1},{6,2},{7,3},{8,4},{9,5},{1... | collective-permute-start | bytes 1572872 | tf_op jit(solution)/shard_map/ppermute | solution.py:67
  241.4 11.6 %collective-permute-start.18 = (bf16[2,2,128,128]{3,2,1,0:T(8,128)(2,1)S(1)}, bf16[2,2,128,128]{3,2,1,0:T(8,128)(2,1)S(1)}, u32[]{:S(2)}, u32[]{:S(2)}) collective-permute-start(bf16[2,2,128,128]{3,2,1,0:T(8,128)(2,1)S(1)} %get-tuple-element.52), channel_id=1, source_target_pairs={{0,3},{1,0},{2,1},{3,2},{4,7},{5,4},{6,5},{7,6},{8,11},{9,8},{10,9... | collective-permute-start | bytes 393224 | tf_op jit(solution)/shard_map/ppermute | solution.py:96
  246.0 12.8 %collective-permute-start.19 = (bf16[2,2,128,128]{3,2,1,0:T(8,128)(2,1)S(1)}, bf16[2,2,128,128]{3,2,1,0:T(8,128)(2,1)S(1)}, u32[]{:S(2)}, u32[]{:S(2)}) collective-permute-start(bf16[2,2,128,128]{3,2,1,0:T(8,128)(2,1)S(1)} %get-tuple-element.54), channel_id=1, source_target_pairs={{0,2},{1,3},{2,0},{3,1},{4,6},{5,7},{6,4},{7,5},{8,10},{9,11},{10,... | collective-permute-start | bytes 393224 | tf_op jit(solution)/shard_map/ppermute | solution.py:96
  250.0 10.8 %collective-permute-start.20 = (bf16[2,2,128,128]{3,2,1,0:T(8,128)(2,1)S(1)}, bf16[2,2,128,128]{3,2,1,0:T(8,128)(2,1)S(1)}, u32[]{:S(2)}, u32[]{:S(2)}) collective-permute-start(bf16[2,2,128,128]{3,2,1,0:T(8,128)(2,1)S(1)} %get-tuple-element.53), channel_id=1, source_target_pairs={{0,1},{1,2},{2,3},{3,0},{4,5},{5,6},{6,7},{7,4},{8,9},{9,10},{10,1... | collective-permute-start | bytes 393224 | tf_op jit(solution)/shard_map/ppermute | solution.py:96
  265.6 2.6 copy-start.1

commit v13 on v2

--- a/solution.py
+++ b/solution.py
@@ -54,19 +54,22 @@
     return jnp.stack(rel)
 
 
-def dp_scatter_rel(terms, n_y, n_z):
+def dp_scatter_rel(terms, n_y, n_z, late=None):
     n_f, n_b = n_y // 2, (n_y - 1) // 2
     got_f = got_b = None
+    made = None
     for k in range(1, n_f + 1):
         part = terms[(n_y - n_f - 1 + k) % n_y].astype(jnp.float32)
         if got_f is not None:
             part = part + got_f.astype(jnp.float32)
         got_f = lax.ppermute(part.astype(jnp.bfloat16), "dp", dp_shift(n_y, n_z, 1, 0))
-    for k in range(1, n_b + 1):
-        part = terms[n_b + 1 - k].astype(jnp.float32)
-        if got_b is not None:
-            part = part + got_b.astype(jnp.float32)
-        got_b = lax.ppermute(part.astype(jnp.bfloat16), "dp", dp_shift(n_y, n_z, -1, 0))
+        if k <= n_b:
+            part = terms[n_b + 1 - k].astype(jnp.float32)
+            if got_b is not None:
+                part = part + got_b.astype(jnp.float32)
+            got_b = lax.ppermute(part.astype(jnp.bfloat16), "dp", dp_shift(n_y, n_z, -1, 0))
+        if k == 1 and late is not None:
+            got_f, got_b, made = late(got_f, got_b)
     acc = terms[0].astype(jnp.float32)
     if got_f is not None:
         acc = acc + got_f.astype(jnp.float32)
@@ -76,7 +79,7 @@
     for b in range(1, n_z):
         sent = lax.ppermute(acc[b].astype(jnp.bfloat16), "dp", dp_shift(n_y, n_z, 0, -b))
         total = total + sent.astype(jnp.float32)
-    return total.astype(jnp.bfloat16)
+    return total.astype(jnp.bfloat16), made
 
 
 def per_device(activations, out_grad, up_blocks, up_rows, down_blocks, down_rows):
@@ -117,9 +120,6 @@
     picked_in = full_input.reshape(tokens, row_blocks, block_size)[:, up_index]
     preact = jnp.einsum("tgki,gkio->tgo", picked_in, up_tiles, preferred_element_type=jnp.float32)
     hidden = (preact * normal_cdf(preact)).astype(jnp.bfloat16)
-    product = jnp.einsum("tgh,gkho->tgko", hidden, down_tiles, preferred_element_type=jnp.float32)
-    out_start = jnp.zeros((tokens, row_blocks, block_size), jnp.float32)
-    out_part = out_start.at[:, down_rows].add(product.reshape(tokens, groups * K, block_size))
     picked_grad = full_grad.reshape(tokens, row_blocks, block_size)[:, down_index]
     down_term = (
         jnp.einsum("tgh,tgko->gkho", hidden, picked_grad, preferred_element_type=jnp.float32)
@@ -129,23 +129,35 @@
         "tgko,gkho->tgh", picked_grad, down_tiles, preferred_element_type=jnp.float32
     )
     preact_grad = (hidden_grad * gelu_slope(preact)).astype(jnp.bfloat16)
-    back = jnp.einsum("tgo,gkio->tgki", preact_grad, up_tiles, preferred_element_type=jnp.float32)
-    in_start = jnp.zeros((tokens, row_blocks, block_size), jnp.float32)
-    in_part = in_start.at[:, up_rows].add(back.reshape(tokens, groups * K, block_size))
     up_term = (
         jnp.einsum("tgki,tgo->gkio", picked_in, preact_grad, preferred_element_type=jnp.float32)
         * scale
     )
-
-    parts = jnp.stack([out_part, in_part]).astype(jnp.bfloat16)
-    parts = parts.reshape(2, tokens, n_tensor, shard_width)
-    mine = scatter_sum(jnp.moveaxis(parts, 2, 0), "tensor")
-    both = gather_all(mine, "tensor")
-    both = jnp.moveaxis(both, 0, 2).reshape(2, tokens, width)
-
     terms = jnp.stack([up_term, down_term]).astype(jnp.bfloat16)
     terms = terms.reshape(2, n_y, n_z, per_dev, block_size, block_size)
-    grads = dp_scatter_rel(jnp.moveaxis(terms, 0, 2), n_y, n_z)
+
+    def late(got_f, got_b):
+        got_f, got_b, h, pg = lax.optimization_barrier((got_f, got_b, hidden, preact_grad))
+        product = jnp.einsum("gkho,tgh->gkot", down_tiles, h, preferred_element_type=jnp.float32)
+        span = jnp.arange(row_blocks, dtype=jnp.int32)
+        highest = lax.Precision.HIGHEST
+        down_hot = (down_index[..., None] == span).astype(jnp.float32)
+        out_t = jnp.einsum(
+            "gkr,gkot->rot", down_hot, product, precision=highest, preferred_element_type=jnp.float32
+        )
+        back = jnp.einsum("gkio,tgo->gkit", up_tiles, pg, preferred_element_type=jnp.float32)
+        up_hot = (up_index[..., None] == span).astype(jnp.float32)
+        in_t = jnp.einsum(
+            "gkr,gkit->rit", up_hot, back, precision=highest, preferred_element_type=jnp.float32
+        )
+        parts = jnp.stack([out_t, in_t]).astype(jnp.bfloat16)
+        parts = parts.reshape(2, n_tensor, shard_width // block_size, block_size, tokens)
+        parts = jnp.transpose(parts, (1, 0, 4, 2, 3)).reshape(n_tensor, 2, tokens, shard_width)
+        mine = scatter_sum(parts, "tensor")
+        both = gather_all(mine, "tensor")
+        return got_f, got_b, jnp.moveaxis(both, 0, 2).reshape(2, tokens, width)
+
+    grads, both = dp_scatter_rel(jnp.moveaxis(terms, 0, 2), n_y, n_z, late)
     return (both[0], both[1], grads[0], grads[1])
 
 

time: 294 us -> 282 us (0.959)
  other arithmetic: 34.5 us -> 12.6 us
  waiting for transfers between devices: 85.4 us -> 101 us
  local copies, waits for them, and re-layouts: 58.7 us -> 54.4 us
    all_to_all x1, waiting for transfers between devices: 0.01 us -> 25.7 us  [scatter_sum(): got = lax.all_to_all(x, axis_name, 0, 0, tiled=True)]
    scatter-add x2 -> x0, other arithmetic: 17.6 us -> none  [the longest x1 8.8 us: per_device(): in_start.at[:, up_rows].add(back.reshape(tokens, groups * K, block_size))]
    reshape x2 -> x0, local copies, waits for them, and re-layouts: 11.4 us -> none  [the longest x1 5.71 us: per_device(): product.reshape(tokens, groups * K, block_size)]
    ppermute x3, waiting for transfers between devices: 27.4 us -> 19.4 us  [dp_scatter_rel(): lax.ppermute(part.astype(jnp.bfloat16), 'dp', dp_shift(n_y, n_z, -1, 0))]
    ppermute x4, waiting for transfers between devices: 21.4 us -> 14.6 us  [dp_scatter_rel(): lax.ppermute(part.astype(jnp.bfloat16), 'dp', dp_shift(n_y, n_z, 1, 0))]
    ppermute x4, waiting for transfers between devices: 25.3 us -> 30.6 us  [dp_gather_rel(): cur_f = lax.ppermute(cur_f, 'dp', dp_shift(n_y, n_z, 1, 0))]
    another operation x4, local copies, waits for them, and re-layouts: 4.56 us -> 8.4 us  [the longest x1 4.3 us: per_device(): down_tiles = down_all.reshape(groups, K, block_size, block_size)]
    dot_general x2 -> x4, matrix products: 7.91 us -> 6.32 us  [the longest x1 2.28 us: late(): jnp.einsum('gkho,tgh->gkot', down_tiles, h, preferred_element_type=jnp.fl...]
  transfers between devices with their start and end apart: 23 -> 23, of which waited for: 16 -> 13; matrix products, arithmetic and copies ran while one was open for 15% -> 12% of each run, Pallas kernels for 0% -> 0%
where the time goes in v13:
time: 282 us; the launch traced here: 278 us
  waiting for transfers between devices  101 us (36%)
  starting transfers between devices  94.1 us (33%)
  local copies, waits for them, and re-layouts  54.4 us (19%)
  matrix products  14.3 us (5%)
  other arithmetic  12.6 us (4%)
    ppermute x4, waiting for transfers between devices, dp_gather_rel(): cur_f = lax.ppermute(cur_f, 'dp', dp_shift(n_y, n_z, 1, 0))  30.6 us
    all_to_all x1, waiting for transfers between devices, scatter_sum(): got = lax.all_to_all(x, axis_name, 0, 0, tiled=True)  25.7 us
    ppermute x3, waiting for transfers between devices, dp_scatter_rel(): lax.ppermute(part.astype(jnp.bfloat16), 'dp', dp_shift(n_y, n_z, -1, 0))  19.4 us
    ppermute x3, starting transfers between devices, dp_gather_rel(): lax.ppermute(x, 'dp', dp_shift(n_y, n_z, 0, b))  18.9 us
    ppermute x3, starting transfers between devices, dp_gather_rel(): cur_b = lax.ppermute(cur_b, 'dp', dp_shift(n_y, n_z, -1, 0))  15.7 us
    ppermute x4, waiting for transfers between devices, dp_scatter_rel(): lax.ppermute(part.astype(jnp.bfloat16), 'dp', dp_shift(n_y, n_z, 1, 0))  14.6 us
    ppermute x3, starting transfers between devices, dp_scatter_rel(): lax.ppermute(part.astype(jnp.bfloat16), 'dp', dp_shift(n_y, n_z, -1, 0))  11.5 us
    ppermute x3, starting transfers between devices, dp_scatter_rel(): lax.ppermute(acc[b].astype(jnp.bfloat16), 'dp', dp_shift(n_y, n_z, 0, -b))  11.1 us
  transfers between devices with their start and end apart: 23, of which 13 were waited for; matrix products, arithmetic and copies ran while one was open for 12% of the time, Pallas kernels for 0%

profile of v13, /device:TPU:6, one launch (start us, length us, event | category | flops | bytes accessed | tf_op | source)
XLA Modules:
  0.0 278.0 jit_solution(15422804725881758459)
XLA Ops:
  1.5 6.1 %collective-permute-start = (bf16[2,2,128,128]{3,2,1,0:T(8,128)(2,1)S(1)}, bf16[2,2,128,128]{3,2,1,0:T(8,128)(2,1)S(1)}, u32[]{:S(2)}, u32[]{:S(2)}) collective-permute-start(bf16[2,2,128,128]{3,2,1,0:T(8,128)(2,1)S(1)} %get-tuple-element.34), channel_id=1, source_target_pairs={{0,1},{1,2},{2,3},{3,0},{4,5},{5,6},{6,7},{7,4},{8,9},{9,10},{10,1... | collective-permute-start | bytes 393224 | tf_op jit(solution)/shard_map/ppermute | solution.py:42
  7.6 9.1 %collective-permute-start.1 = (bf16[2,2,128,128]{3,2,1,0:T(8,128)(2,1)S(1)}, bf16[2,2,128,128]{3,2,1,0:T(8,128)(2,1)S(1)}, u32[]{:S(2)}, u32[]{:S(2)}) collective-permute-start(bf16[2,2,128,128]{3,2,1,0:T(8,128)(2,1)S(1)} %get-tuple-element.34), channel_id=1, source_target_pairs={{0,2},{1,3},{2,0},{3,1},{4,6},{5,7},{6,4},{7,5},{8,10},{9,11},{10,... | collective-permute-start | bytes 393224 | tf_op jit(solution)/shard_map/ppermute | solution.py:42
  16.8 3.7 %collective-permute-start.2 = (bf16[2,2,128,128]{3,2,1,0:T(8,128)(2,1)S(1)}, bf16[2,2,128,128]{3,2,1,0:T(8,128)(2,1)S(1)}, u32[]{:S(2)}, u32[]{:S(2)}) collective-permute-start(bf16[2,2,128,128]{3,2,1,0:T(8,128)(2,1)S(1)} %get-tuple-element.34), channel_id=1, source_target_pairs={{0,3},{1,0},{2,1},{3,2},{4,7},{5,4},{6,5},{7,6},{8,11},{9,8},{10,9... | collective-permute-start | bytes 393224 | tf_op jit(solution)/shard_map/ppermute | solution.py:42
  23.3 5.8 %all-to-all-start = ((bf16[16,2,128,256]{2,3,1,0:T(8,128)(2,1)}), bf16[16,2,128,256]{2,3,1,0:T(8,128)(2,1)S(1)}, u32[]{:S(2)}, u32[]{:S(2)}) async-start(bf16[16,2,128,256]{2,3,1,0:T(8,128)(2,1)} %broadcast_in_dim.4), calls=%async_computation | async-start | bytes 4194304 | tf_op jit(solution)/shard_map/all_to_all | solution.py:22
  30.1 3.5 %collective-permute-start.3 = (bf16[4,2,2,128,128]{4,3,2,1,0:T(8,128)(2,1)S(1)}, bf16[4,2,2,128,128]{4,3,2,1,0:T(8,128)(2,1)S(1)}, u32[]{:S(2)}, u32[]{:S(2)}) collective-permute-start(bf16[4,2,2,128,128]{4,3,2,1,0:T(8,128)(2,1)S(1)} %pad_maximum_fusion.1), channel_id=1, source_target_pairs={{0,4},{1,5},{2,6},{3,7},{4,8},{5,9},{6,10},{7,11},{8,12},{9,13},{1... | collective-permute-start | bytes 1572872 | tf_op jit(solution)/shard_map/ppermute | solution.py:48
  33.7 13.9 %collective-permute-done.3 = bf16[4,2,2,128,128]{4,3,2,1,0:T(8,128)(2,1)S(1)} collective-permute-done((bf16[4,2,2,128,128]{4,3,2,1,0:T(8,128)(2,1)S(1)}, bf16[4,2,2,128,128]{4,3,2,1,0:T(8,128)(2,1)S(1)}, u32[]{:S(2)}, u32[]{:S(2)}) %collective-permute-start.3) | collective-permute-done | bytes 524320 | tf_op jit(solution)/shard_map/ppermute | solution.py:48
  47.6 1.9 collective-permute-start.4
  51.0 5.1 %collective-permute-start.7 = (bf16[4,2,2,128,128]{4,3,2,1,0:T(8,128)(2,1)S(1)}, bf16[4,2,2,128,128]{4,3,2,1,0:T(8,128)(2,1)}, u32[]{:S(2)}, u32[]{:S(2)}) collective-permute-start(bf16[4,2,2,128,128]{4,3,2,1,0:T(8,128)(2,1)S(1)} %pad_maximum_fusion.1), channel_id=1, source_target_pairs={{0,28},{1,29},{2,30},{3,31},{4,0},{5,1},{6,2},{7,3},{8,4},{9,5},{1... | collective-permute-start | bytes 1572872 | tf_op jit(solution)/shard_map/ppermute | solution.py:51
  58.2 5.9 %collective-permute-done.4 = bf16[4,2,2,128,128]{4,3,2,1,0:T(8,128)(2,1)} collective-permute-done((bf16[4,2,2,128,128]{4,3,2,1,0:T(8,128)(2,1)S(1)}, bf16[4,2,2,128,128]{4,3,2,1,0:T(8,128)(2,1)}, u32[]{:S(2)}, u32[]{:S(2)}) %collective-permute-start.4) | collective-permute-done | bytes 524320 | tf_op jit(solution)/shard_map/ppermute | solution.py:48
  64.1 1.9 collective-permute-start.5
  67.3 5.1 %collective-permute-start.8 = (bf16[4,2,2,128,128]{4,3,2,1,0:T(8,128)(2,1)}, bf16[4,2,2,128,128]{4,3,2,1,0:T(8,128)(2,1)S(1)}, u32[]{:S(2)}, u32[]{:S(2)}) collective-permute-start(bf16[4,2,2,128,128]{4,3,2,1,0:T(8,128)(2,1)} %collective-permute-done.7), channel_id=1, source_target_pairs={{0,28},{1,29},{2,30},{3,31},{4,0},{5,1},{6,2},{7,3},{8,4},{9,5},{1... | collective-permute-start | bytes 1572872 | tf_op jit(solution)/shard_map/ppermute | solution.py:51
  73.6 6.3 %collective-permute-done.5 = bf16[4,2,2,128,128]{4,3,2,1,0:T(8,128)(2,1)} collective-permute-done((bf16[4,2,2,128,128]{4,3,2,1,0:T(8,128)(2,1)}, bf16[4,2,2,128,128]{4,3,2,1,0:T(8,128)(2,1)}, u32[]{:S(2)}, u32[]{:S(2)}) %collective-permute-start.5) | collective-permute-done | bytes 524320 | tf_op jit(solution)/shard_map/ppermute | solution.py:48
  79.9 1.9 collective-permute-start.6
  82.4 5.5 %collective-permute-start.9 = (bf16[4,2,2,128,128]{4,3,2,1,0:T(8,128)(2,1)S(1)}, bf16[4,2,2,128,128]{4,3,2,1,0:T(8,128)(2,1)S(1)}, u32[]{:S(2)}, u32[]{:S(2)}) collective-permute-start(bf16[4,2,2,128,128]{4,3,2,1,0:T(8,128)(2,1)S(1)} %collective-permute-done.8), channel_id=1, source_target_pairs={{0,28},{1,29},{2,30},{3,31},{4,0},{5,1},{6,2},{7,3},{8,4},{9,5},{1... | collective-permute-start | bytes 1572872 | tf_op jit(solution)/shard_map/ppermute | solution.py:51
  90.1 4.5 %collective-permute-done.6 = bf16[4,2,2,128,128]{4,3,2,1,0:T(8,128)(2,1)S(1)} collective-permute-done((bf16[4,2,2,128,128]{4,3,2,1,0:T(8,128)(2,1)}, bf16[4,2,2,128,128]{4,3,2,1,0:T(8,128)(2,1)S(1)}, u32[]{:S(2)}, u32[]{:S(2)}) %collective-permute-start.6) | collective-permute-done | bytes 524320 | tf_op jit(solution)/shard_map/ppermute | solution.py:48
  97.8 2.6 fusion.37
  102.7 2.2 gather_fusion.2
  104.8 2.6 copy.54
  107.5 2.2 gather_fusion.3
  109.6 3.9 %copy.56 = bf16[8,8,128,128]{2,3,1,0:T(8,128)(2,1)} copy(bf16[8,8,128,128]{3,2,1,0:T(8,128)(2,1)} %bitcast.176) | data formatting | bytes 4194304 | tf_op jit(solution)/shard_map/gather | solution.py:123
  113.6 2.6 multiply_convert_fusion.2
  116.2 2.1 multiply_convert_fusion
  118.3 4.1 %copy.63 = bf16[1,8,4,2,128,128]{5,4,3,0,2,1:T(8,128)(2,1)} copy(bf16[1,8,4,2,128,128]{4,5,3,2,1,0:T(8,128)(2,1)} %bitcast.181) | data formatting | bytes 4194304 | tf_op jit(solution)/shard_map/stack | solution.py:136
  122.3 2.5 fusion.3
  126.9 2.0 copy-done.4
  129.9 2.8 %collective-permute-start.10 = (bf16[4,2,2,128,128]{4,3,2,1,0:T(8,128)(2,1)}, bf16[4,2,2,128,128]{4,3,2,1,0:T(8,128)(2,1)S(1)}, u32[]{:S(2)}, u32[]{:S(2)}) collective-permute-start(bf16[4,2,2,128,128]{4,3,2,1,0:T(8,128)(2,1)} %get-tuple-element.21), channel_id=1, source_target_pairs={{0,4},{1,5},{2,6},{3,7},{4,8},{5,9},{6,10},{7,11},{8,12},{9,13},{1... | collective-permute-start | bytes 1572872 | tf_op jit(solution)/shard_map/ppermute | solution.py:65
  132.7 4.9 %collective-permute-start.11 = (bf16[4,2,2,128,128]{4,3,2,1,0:T(8,128)(2,1)}, bf16[4,2,2,128,128]{4,3,2,1,0:T(8,128)(2,1)}, u32[]{:S(2)}, u32[]{:S(2)}) collective-permute-start(bf16[4,2,2,128,128]{4,3,2,1,0:T(8,128)(2,1)} %get-tuple-element.20), channel_id=1, source_target_pairs={{0,28},{1,29},{2,30},{3,31},{4,0},{5,1},{6,2},{7,3},{8,4},{9,5},{1... | collective-permute-start | bytes 1572872 | tf_op jit(solution)/shard_map/ppermute | solution.py:70
  137.8 4.3 %copy.64 = bf16[8,8,128,128]{2,1,0,3:T(8,128)(2,1)} copy(bf16[8,8,128,128]{3,2,1,0:T(8,128)(2,1)} %bitcast.184) | data formatting | bytes 4194304 | tf_op jit(solution)/shard_map/reshape;squeeze | solution.py:117
  142.1 2.6 copy.58
  144.7 3.3 %copy.66 = bf16[8,8,128,128]{3,1,0,2:T(8,128)(2,1)S(1)} copy(bf16[8,8,128,128]{2,3,1,0:T(8,128)(2,1)} %bitcast.182) | data formatting | bytes 4194304 | tf_op jit(solution)/shard_map/reshape;squeeze | solution.py:116
  148.0 2.3 fusion.22
  156.7 6.1 %all-to-all-start.1 = ((bf16[16,2,128,256]{2,3,1,0:T(8,128)(2,1)}), bf16[16,2,128,256]{2,3,1,0:T(8,128)(2,1)S(1)}, u32[]{:S(2)}, u32[]{:S(2)}) async-start(bf16[16,2,128,256]{2,3,1,0:T(8,128)(2,1)} %bitcast.178), calls=%async_computation.1 | async-start | bytes 4194304 | tf_op jit(solution)/shard_map/all_to_all | solution.py:26
  164.1 2.4 collective-permute-start.12
  166.6 25.7 %all-to-all-done.1 = bf16[16,2,128,256]{2,3,1,0:T(8,128)(2,1)S(1)} async-done(((bf16[16,2,128,256]{2,3,1,0:T(8,128)(2,1)}), bf16[16,2,128,256]{2,3,1,0:T(8,128)(2,1)S(1)}, u32[]{:S(2)}, u32[]{:S(2)}) %all-to-all-start.1) | async-done | bytes 2097184 | tf_op jit(solution)/shard_map/all_to_all | solution.py:26
  194.3 4.9 %all-to-all-start.2 = ((bf16[16,2,128,256]{3,2,1,0:T(8,128)(2,1)}), bf16[16,2,128,256]{3,2,1,0:T(8,128)(2,1)S(1)}, u32[]{:S(2)}, u32[]{:S(2)}) async-start(bf16[16,2,128,256]{3,2,1,0:T(8,128)(2,1)} %broadcast_in_dim.5), calls=%async_computation.2 | async-start | bytes 4194304 | tf_op jit(solution)/shard_map/all_to_all | solution.py:22
  200.4 2.4 collective-permute-start.13
  202.9 14.6 %collective-permute-done.13 = bf16[4,2,2,128,128]{4,3,2,1,0:T(8,128)(2,1)S(1)} collective-permute-done((bf16[4,2,2,128,128]{4,3,2,1,0:T(8,128)(2,1)S(1)}, bf16[4,2,2,128,128]{4,3,2,1,0:T(8,128)(2,1)S(1)}, u32[]{:S(2)}, u32[]{:S(2)}) %collective-permute-start.13) | collective-permute-done | bytes 524320 | tf_op jit(solution)/shard_map/ppermute | solution.py:65
  219.2 2.7 collective-permute-start.15
  221.9 3.1 %collective-permute-start.14 = (bf16[4,2,2,128,128]{4,3,2,1,0:T(8,128)(2,1)S(1)}, bf16[4,2,2,128,128]{4,3,2,1,0:T(8,128)(2,1)S(1)}, u32[]{:S(2)}, u32[]{:S(2)}) collective-permute-start(bf16[4,2,2,128,128]{4,3,2,1,0:T(8,128)(2,1)S(1)} %get-tuple-element.18), channel_id=1, source_target_pairs={{0,4},{1,5},{2,6},{3,7},{4,8},{5,9},{6,10},{7,11},{8,12},{9,13},{1... | collective-permute-start | bytes 1572872 | tf_op jit(solution)/shard_map/ppermute | solution.py:65
  225.1 9.2 %collective-permute-done.15 = bf16[4,2,2,128,128]{4,3,2,1,0:T(8,128)(2,1)S(1)} collective-permute-done((bf16[4,2,2,128,128]{4,3,2,1,0:T(8,128)(2,1)S(1)}, bf16[4,2,2,128,128]{4,3,2,1,0:T(8,128)(2,1)S(1)}, u32[]{:S(2)}, u32[]{:S(2)}) %collective-permute-start.15) | collective-permute-done | bytes 524320 | tf_op jit(solution)/shard_map/ppermute | solution.py:70
  235.5 3.9 %collective-permute-start.16 = (bf16[4,2,2,128,128]{4,3,2,1,0:T(8,128)(2,1)S(1)}, bf16[4,2,2,128,128]{4,3,2,1,0:T(8,128)(2,1)S(1)}, u32[]{:S(2)}, u32[]{:S(2)}) collective-permute-start(bf16[4,2,2,128,128]{4,3,2,1,0:T(8,128)(2,1)S(1)} %fusion.5), channel_id=1, source_target_pairs={{0,28},{1,29},{2,30},{3,31},{4,0},{5,1},{6,2},{7,3},{8,4},{9,5},{1... | collective-permute-start | bytes 1572872 | tf_op jit(solution)/shard_map/ppermute | solution.py:70
  239.4 10.2 %collective-permute-done.16 = bf16[4,2,2,128,128]{4,3,2,1,0:T(8,128)(2,1)S(1)} collective-permute-done((bf16[4,2,2,128,128]{4,3,2,1,0:T(8,128)(2,1)S(1)}, bf16[4,2,2,128,128]{4,3,2,1,0:T(8,128)(2,1)S(1)}, u32[]{:S(2)}, u32[]{:S(2)}) %collective-permute-start.16) | collective-permute-done | bytes 524320 | tf_op jit(solution)/shard_map/ppermute | solution.py:70
  251.0 4.4 %collective-permute-start.17 = (bf16[2,2,128,128]{3,2,1,0:T(8,128)(2,1)S(1)}, bf16[2,2,128,128]{3,2,1,0:T(8,128)(2,1)S(1)}, u32[]{:S(2)}, u32[]{:S(2)}) collective-permute-start(bf16[2,2,128,128]{3,2,1,0:T(8,128)(2,1)S(1)} %get-tuple-element.28), channel_id=1, source_target_pairs={{0,3},{1,0},{2,1},{3,2},{4,7},{5,4},{6,5},{7,6},{8,11},{9,8},{10,9... | collective-permute-start | bytes 393224 | tf_op jit(solution)/shard_map/ppermute | solution.py:80
  255.4 4.2 %collective-permute-start.18 = (bf16[2,2,128,128]{3,2,1,0:T(8,128)(2,1)S(1)}, bf16[2,2,128,128]{3,2,1,0:T(8,128)(2,1)S(1)}, u32[]{:S(2)}, u32[]{:S(2)}) collective-permute-start(bf16[2,2,128,128]{3,2,1,0:T(8,128)(2,1)S(1)} %get-tuple-element.30), channel_id=1, source_target_pairs={{0,2},{1,3},{2,0},{3,1},{4,6},{5,7},{6,4},{7,5},{8,10},{9,11},{10,... | collective-permute-start | bytes 393224 | tf_op jit(solution)/shard_map/ppermute | solution.py:80
  259.6 2.5 collective-permute-start.19
  262.1 6.1 %collective-permute-done.18 = bf16[2,2,128,128]{3,2,1,0:T(8,128)(2,1)S(1)} collective-permute-done((bf16[2,2,128,128]{3,2,1,0:T(8,128)(2,1)S(1)}, bf16[2,2,128,128]{3,2,1,0:T(8,128)(2,1)S(1)}, u32[]{:S(2)}, u32[]{:S(2)}) %collective-permute-start.18) | collective-permute-done | bytes 131104 | tf_op jit(solution)/shard_map/ppermute | solution.py:80
  268.2 2.4 collective-permute-done.19
  271.3 2.4 copy.71
  (96 shorter events, 42.3 us)
Async XLA Ops:
  0.6 55.5 %copy-start = (s32[64]{0:T(128)S(1)}, s32[64]{0:T(128)}, u32[]{:S(2)}) copy-start(s32[64]{0:T(128)} %param.9) | copy-start | bytes 772
  1.5 27.6 %collective-permute-start = (bf16[2,2,128,128]{3,2,1,0:T(8,128)(2,1)S(1)}, bf16[2,2,128,128]{3,2,1,0:T(8,128)(2,1)S(1)}, u32[]{:S(2)}, u32[]{:S(2)}) collective-permute-start(bf16[2,2,128,128]{3,2,1,0:T(8,128)(2,1)S(1)} %get-tuple-element.34), channel_id=1, source_target_pairs={{0,1},{1,2},{2,3},{3,0},{4,5},{5,6},{6,7},{7,4},{8,9},{9,10},{10,1... | collective-permute-start | bytes 393224 | tf_op jit(solution)/shard_map/ppermute | solution.py:42
  7.6 21.5 %collective-permute-start.1 = (bf16[2,2,128,128]{3,2,1,0:T(8,128)(2,1)S(1)}, bf16[2,2,128,128]{3,2,1,0:T(8,128)(2,1)S(1)}, u32[]{:S(2)}, u32[]{:S(2)}) collective-permute-start(bf16[2,2,128,128]{3,2,1,0:T(8,128)(2,1)S(1)} %get-tuple-element.34), channel_id=1, source_target_pairs={{0,2},{1,3},{2,0},{3,1},{4,6},{5,7},{6,4},{7,5},{8,10},{9,11},{10,... | collective-permute-start | bytes 393224 | tf_op jit(solution)/shard_map/ppermute | solution.py:42
  16.8 12.6 %collective-permute-start.2 = (bf16[2,2,128,128]{3,2,1,0:T(8,128)(2,1)S(1)}, bf16[2,2,128,128]{3,2,1,0:T(8,128)(2,1)S(1)}, u32[]{:S(2)}, u32[]{:S(2)}) collective-permute-start(bf16[2,2,128,128]{3,2,1,0:T(8,128)(2,1)S(1)} %get-tuple-element.34), channel_id=1, source_target_pairs={{0,3},{1,0},{2,1},{3,2},{4,7},{5,4},{6,5},{7,6},{8,11},{9,8},{10,9... | collective-permute-start | bytes 393224 | tf_op jit(solution)/shard_map/ppermute | solution.py:42
  23.3 42.7 %copy-start.2 = (s32[64]{0:T(128)S(1)}, s32[64]{0:T(128)}, u32[]{:S(2)}) copy-start(s32[64]{0:T(128)} %param.11) | copy-start | bytes 772
  23.3 77.1 %all-to-all-start = ((bf16[16,2,128,256]{2,3,1,0:T(8,128)(2,1)}), bf16[16,2,128,256]{2,3,1,0:T(8,128)(2,1)S(1)}, u32[]{:S(2)}, u32[]{:S(2)}) async-start(bf16[16,2,128,256]{2,3,1,0:T(8,128)(2,1)} %broadcast_in_dim.4), calls=%async_computation | async-start | bytes 4194304 | tf_op jit(solution)/shard_map/all_to_all | solution.py:22
  29.4 0.7 copy-start.9
  30.1 17.5 %collective-permute-start.3 = (bf16[4,2,2,128,128]{4,3,2,1,0:T(8,128)(2,1)S(1)}, bf16[4,2,2,128,128]{4,3,2,1,0:T(8,128)(2,1)S(1)}, u32[]{:S(2)}, u32[]{:S(2)}) collective-permute-start(bf16[4,2,2,128,128]{4,3,2,1,0:T(8,128)(2,1)S(1)} %pad_maximum_fusion.1), channel_id=1, source_target_pairs={{0,4},{1,5},{2,6},{3,7},{4,8},{5,9},{6,10},{7,11},{8,12},{9,13},{1... | collective-permute-start | bytes 1572872 | tf_op jit(solution)/shard_map/ppermute | solution.py:48
  47.6 16.5 %collective-permute-start.4 = (bf16[4,2,2,128,128]{4,3,2,1,0:T(8,128)(2,1)S(1)}, bf16[4,2,2,128,128]{4,3,2,1,0:T(8,128)(2,1)}, u32[]{:S(2)}, u32[]{:S(2)}) collective-permute-start(bf16[4,2,2,128,128]{4,3,2,1,0:T(8,128)(2,1)S(1)} %collective-permute-done.3), channel_id=1, source_target_pairs={{0,4},{1,5},{2,6},{3,7},{4,8},{5,9},{6,10},{7,11},{8,12},{9,13},{1... | collective-permute-start | bytes 1572872 | tf_op jit(solution)/shard_map/ppermute | solution.py:48
  51.0 15.9 %collective-permute-start.7 = (bf16[4,2,2,128,128]{4,3,2,1,0:T(8,128)(2,1)S(1)}, bf16[4,2,2,128,128]{4,3,2,1,0:T(8,128)(2,1)}, u32[]{:S(2)}, u32[]{:S(2)}) collective-permute-start(bf16[4,2,2,128,128]{4,3,2,1,0:T(8,128)(2,1)S(1)} %pad_maximum_fusion.1), channel_id=1, source_target_pairs={{0,28},{1,29},{2,30},{3,31},{4,0},{5,1},{6,2},{7,3},{8,4},{9,5},{1... | collective-permute-start | bytes 1572872 | tf_op jit(solution)/shard_map/ppermute | solution.py:51
  64.1 15.8 %collective-permute-start.5 = (bf16[4,2,2,128,128]{4,3,2,1,0:T(8,128)(2,1)}, bf16[4,2,2,128,128]{4,3,2,1,0:T(8,128)(2,1)}, u32[]{:S(2)}, u32[]{:S(2)}) collective-permute-start(bf16[4,2,2,128,128]{4,3,2,1,0:T(8,128)(2,1)} %collective-permute-done.4), channel_id=1, source_target_pairs={{0,4},{1,5},{2,6},{3,7},{4,8},{5,9},{6,10},{7,11},{8,12},{9,13},{1... | collective-permute-start | bytes 1572872 | tf_op jit(solution)/shard_map/ppermute | solution.py:48
  66.8 0.5 copy-start.11
  67.3 15.1 %collective-permute-start.8 = (bf16[4,2,2,128,128]{4,3,2,1,0:T(8,128)(2,1)}, bf16[4,2,2,128,128]{4,3,2,1,0:T(8,128)(2,1)S(1)}, u32[]{:S(2)}, u32[]{:S(2)}) collective-permute-start(bf16[4,2,2,128,128]{4,3,2,1,0:T(8,128)(2,1)} %collective-permute-done.7), channel_id=1, source_target_pairs={{0,28},{1,29},{2,30},{3,31},{4,0},{5,1},{6,2},{7,3},{8,4},{9,5},{1... | collective-permute-start | bytes 1572872 | tf_op jit(solution)/shard_map/ppermute | solution.py:51
  79.9 14.8 %collective-permute-start.6 = (bf16[4,2,2,128,128]{4,3,2,1,0:T(8,128)(2,1)}, bf16[4,2,2,128,128]{4,3,2,1,0:T(8,128)(2,1)S(1)}, u32[]{:S(2)}, u32[]{:S(2)}) collective-permute-start(bf16[4,2,2,128,128]{4,3,2,1,0:T(8,128)(2,1)} %collective-permute-done.5), channel_id=1, source_target_pairs={{0,4},{1,5},{2,6},{3,7},{4,8},{5,9},{6,10},{7,11},{8,12},{9,13},{1... | collective-permute-start | bytes 1572872 | tf_op jit(solution)/shard_map/ppermute | solution.py:48
  82.4 14.2 %collective-permute-start.9 = (bf16[4,2,2,128,128]{4,3,2,1,0:T(8,128)(2,1)S(1)}, bf16[4,2,2,128,128]{4,3,2,1,0:T(8,128)(2,1)S(1)}, u32[]{:S(2)}, u32[]{:S(2)}) collective-permute-start(bf16[4,2,2,128,128]{4,3,2,1,0:T(8,128)(2,1)S(1)} %collective-permute-done.8), channel_id=1, source_target_pairs={{0,28},{1,29},{2,30},{3,31},{4,0},{5,1},{6,2},{7,3},{8,4},{9,5},{1... | collective-permute-start | bytes 1572872 | tf_op jit(solution)/shard_map/ppermute | solution.py:51
  113.6 2.6 copy-start.7
  118.3 4.1 %copy-start.5 = (bf16[64,128,128]{2,1,0:T(8,128)(2,1)S(1)}, bf16[64,128,128]{2,1,0:T(8,128)(2,1)}, u32[]{:S(2)}) copy-start(bf16[64,128,128]{2,1,0:T(8,128)(2,1)} %gather_fusion.3) | copy-start | bytes 6291460
  122.3 2.5 copy-start.6
  124.9 1.6 copy-start.8
  126.9 2.0 copy-start.4
  128.8 8.8 %copy-start.12 = (s32[64]{0:T(128)S(1)}, s32[64]{0:T(128)}, u32[]{:S(2)}) copy-start(s32[64]{0:T(128)} %copy-done.11) | copy-start | bytes 772
  128.8 8.8 %copy-start.10 = (s32[64]{0:T(128)S(1)}, s32[64]{0:T(128)}, u32[]{:S(2)}) copy-start(s32[64]{0:T(128)} %gather_fusion.1) | copy-start | bytes 772
  129.9 18.1 %collective-permute-start.10 = (bf16[4,2,2,128,128]{4,3,2,1,0:T(8,128)(2,1)}, bf16[4,2,2,128,128]{4,3,2,1,0:T(8,128)(2,1)S(1)}, u32[]{:S(2)}, u32[]{:S(2)}) collective-permute-start(bf16[4,2,2,128,128]{4,3,2,1,0:T(8,128)(2,1)} %get-tuple-element.21), channel_id=1, source_target_pairs={{0,4},{1,5},{2,6},{3,7},{4,8},{5,9},{6,10},{7,11},{8,12},{9,13},{1... | collective-permute-start | bytes 1572872 | tf_op jit(solution)/shard_map/ppermute | solution.py:65
  132.7 15.3 %collective-permute-start.11 = (bf16[4,2,2,128,128]{4,3,2,1,0:T(8,128)(2,1)}, bf16[4,2,2,128,128]{4,3,2,1,0:T(8,128)(2,1)}, u32[]{:S(2)}, u32[]{:S(2)}) collective-permute-start(bf16[4,2,2,128,128]{4,3,2,1,0:T(8,128)(2,1)} %get-tuple-element.20), channel_id=1, source_target_pairs={{0,28},{1,29},{2,30},{3,31},{4,0},{5,1},{6,2},{7,3},{8,4},{9,5},{1... | collective-permute-start | bytes 1572872 | tf_op jit(solution)/shard_map/ppermute | solution.py:70
  137.8 4.3 %copy-start.3 = (bf16[1,8,4,2,128,128]{5,4,3,0,2,1:T(8,128)(2,1)S(1)}, bf16[1,8,4,2,128,128]{5,4,3,0,2,1:T(8,128)(2,1)}, u32[]{:S(2)}) copy-start(bf16[1,8,4,2,128,128]{5,4,3,0,2,1:T(8,128)(2,1)} %get-tuple-element.23) | copy-start | bytes 6291460
  156.7 35.5 %all-to-all-start.1 = ((bf16[16,2,128,256]{2,3,1,0:T(8,128)(2,1)}), bf16[16,2,128,256]{2,3,1,0:T(8,128)(2,1)S(1)}, u32[]{:S(2)}, u32[]{:S(2)}) async-start(bf16[16,2,128,256]{2,3,1,0:T(8,128)(2,1)} %bitcast.178), calls=%async_computation.1 | async-start | bytes 4194304 | tf_op jit(solution)/shard_map/all_to_all | solution.py:26
  164.1 35.1 %collective-permute-start.12 = (bf16[4,2,2,128,128]{4,3,2,1,0:T(8,128)(2,1)S(1)}, bf16[4,2,2,128,128]{4,3,2,1,0:T(8,128)(2,1)S(1)}, u32[]{:S(2)}, u32[]{:S(2)}) collective-permute-start(bf16[4,2,2,128,128]{4,3,2,1,0:T(8,128)(2,1)S(1)} %fusion.6), channel_id=1, source_target_pairs={{0,4},{1,5},{2,6},{3,7},{4,8},{5,9},{6,10},{7,11},{8,12},{9,13},{1... | collective-permute-start | bytes 1572872 | tf_op jit(solution)/shard_map/ppermute | solution.py:65
  194.3 77.0 %all-to-all-start.2 = ((bf16[16,2,128,256]{3,2,1,0:T(8,128)(2,1)}), bf16[16,2,128,256]{3,2,1,0:T(8,128)(2,1)S(1)}, u32[]{:S(2)}, u32[]{:S(2)}) async-start(bf16[16,2,128,256]{3,2,1,0:T(8,128)(2,1)} %broadcast_in_dim.5), calls=%async_computation.2 | async-start | bytes 4194304 | tf_op jit(solution)/shard_map/all_to_all | solution.py:22
  200.4 17.1 %collective-permute-start.13 = (bf16[4,2,2,128,128]{4,3,2,1,0:T(8,128)(2,1)S(1)}, bf16[4,2,2,128,128]{4,3,2,1,0:T(8,128)(2,1)S(1)}, u32[]{:S(2)}, u32[]{:S(2)}) collective-permute-start(bf16[4,2,2,128,128]{4,3,2,1,0:T(8,128)(2,1)S(1)} %fusion.7), channel_id=1, source_target_pairs={{0,4},{1,5},{2,6},{3,7},{4,8},{5,9},{6,10},{7,11},{8,12},{9,13},{1... | collective-permute-start | bytes 1572872 | tf_op jit(solution)/shard_map/ppermute | solution.py:65
  219.2 15.0 %collective-permute-start.15 = (bf16[4,2,2,128,128]{4,3,2,1,0:T(8,128)(2,1)S(1)}, bf16[4,2,2,128,128]{4,3,2,1,0:T(8,128)(2,1)S(1)}, u32[]{:S(2)}, u32[]{:S(2)}) collective-permute-start(bf16[4,2,2,128,128]{4,3,2,1,0:T(8,128)(2,1)S(1)} %get-tuple-element.19), channel_id=1, source_target_pairs={{0,28},{1,29},{2,30},{3,31},{4,0},{5,1},{6,2},{7,3},{8,4},{9,5},{1... | collective-permute-start | bytes 1572872 | tf_op jit(solution)/shard_map/ppermute | solution.py:70
  221.9 17.5 %collective-permute-start.14 = (bf16[4,2,2,128,128]{4,3,2,1,0:T(8,128)(2,1)S(1)}, bf16[4,2,2,128,128]{4,3,2,1,0:T(8,128)(2,1)S(1)}, u32[]{:S(2)}, u32[]{:S(2)}) collective-permute-start(bf16[4,2,2,128,128]{4,3,2,1,0:T(8,128)(2,1)S(1)} %get-tuple-element.18), channel_id=1, source_target_pairs={{0,4},{1,5},{2,6},{3,7},{4,8},{5,9},{6,10},{7,11},{8,12},{9,13},{1... | collective-permute-start | bytes 1572872 | tf_op jit(solution)/shard_map/ppermute | solution.py:65
  235.5 14.1 %collective-permute-start.16 = (bf16[4,2,2,128,128]{4,3,2,1,0:T(8,128)(2,1)S(1)}, bf16[4,2,2,128,128]{4,3,2,1,0:T(8,128)(2,1)S(1)}, u32[]{:S(2)}, u32[]{:S(2)}) collective-permute-start(bf16[4,2,2,128,128]{4,3,2,1,0:T(8,128)(2,1)S(1)} %fusion.5), channel_id=1, source_target_pairs={{0,28},{1,29},{2,30},{3,31},{4,0},{5,1},{6,2},{7,3},{8,4},{9,5},{1... | collective-permute-start | bytes 1572872 | tf_op jit(solution)/shard_map/ppermute | solution.py:70
  251.0 11.1 %collective-permute-start.17 = (bf16[2,2,128,128]{3,2,1,0:T(8,128)(2,1)S(1)}, bf16[2,2,128,128]{3,2,1,0:T(8,128)(2,1)S(1)}, u32[]{:S(2)}, u32[]{:S(2)}) collective-permute-start(bf16[2,2,128,128]{3,2,1,0:T(8,128)(2,1)S(1)} %get-tuple-element.28), channel_id=1, source_target_pairs={{0,3},{1,0},{2,1},{3,2},{4,7},{5,4},{6,5},{7,6},{8,11},{9,8},{10,9... | collective-permute-start | bytes 393224 | tf_op jit(solution)/shard_map/ppermute | solution.py:80
  255.4 12.8 %collective-permute-start.18 = (bf16[2,2,128,128]{3,2,1,0:T(8,128)(2,1)S(1)}, bf16[2,2,128,128]{3,2,1,0:T(8,128)(2,1)S(1)}, u32[]{:S(2)}, u32[]{:S(2)}) collective-permute-start(bf16[2,2,128,128]{3,2,1,0:T(8,128)(2,1)S(1)} %get-tuple-element.30), channel_id=1, source_target_pairs={{0,2},{1,3},{2,0},{3,1},{4,6},{5,7},{6,4},{7,5},{8,10},{9,11},{10,... | collective-permute-start | bytes 393224 | tf_op jit(solution)/shard_map/ppermute | solution.py:80
  259.6 11.0 %collective-permute-start.19 = (bf16[2,2,128,128]{3,2,1,0:T(8,128)(2,1)S(1)}, bf16[2,2,128,128]{3,2,1,0:T(8,128)(2,1)S(1)}, u32[]{:S(2)}, u32[]{:S(2)}) collective-permute-start(bf16[2,2,128,128]{3,2,1,0:T(8,128)(2,1)S(1)} %get-tuple-element.29), channel_id=1, source_target_pairs={{0,1},{1,2},{2,3},{3,0},{4,5},{5,6},{6,7},{7,4},{8,9},{9,10},{10,1... | collective-permute-start | bytes 393224 | tf_op jit(solution)/shard_map/ppermute | solution.py:80
  275.3 2.6 copy-start.1

commit v14 on v11

--- a/solution.py
+++ b/solution.py
@@ -54,7 +54,7 @@
     return jnp.stack(rel)
 
 
-def dp_scatter_rel(terms, n_y, n_z, tie=None):
+def dp_scatter_rel(terms, n_y, n_z, tie=None, after=None):
     n_f, n_b = n_y // 2, (n_y - 1) // 2
     got_f = got_b = None
     for k in range(1, n_f + 1):
@@ -69,11 +69,15 @@
         got_b = lax.ppermute(part.astype(jnp.bfloat16), "dp", dp_shift(n_y, n_z, -1, 0))
         if k == 1 and tie is not None:
             got_b, tie = lax.optimization_barrier((got_b, tie))
+            if after is not None:
+                tie = after(tie)
     acc = terms[0].astype(jnp.float32)
     if got_f is not None:
         acc = acc + got_f.astype(jnp.float32)
     if got_b is not None:
         acc = acc + got_b.astype(jnp.float32)
+    if after is not None:
+        acc, tie = lax.optimization_barrier((acc, tie))
     total = acc[0]
     for b in range(1, n_z):
         sent = lax.ppermute(acc[b].astype(jnp.bfloat16), "dp", dp_shift(n_y, n_z, 0, -b))
@@ -151,10 +155,13 @@
     mine = scatter_sum(parts, "tensor")
     terms = jnp.stack([up_term, down_term]).astype(jnp.bfloat16)
     terms = terms.reshape(2, n_y, n_z, per_dev, block_size, block_size)
-    grads, mine = dp_scatter_rel(jnp.moveaxis(terms, 0, 2), n_y, n_z, mine)
-    both = gather_all(mine, "tensor")
-    both = jnp.moveaxis(both, 0, 2).reshape(2, tokens, width)
-    return (both[0], both[1], grads[0], grads[1])
+    def outputs(mine):
+        both = gather_all(mine, "tensor")
+        both = jnp.moveaxis(both, 0, 2).reshape(2, tokens, width)
+        return (both[0], both[1])
+
+    grads, outs = dp_scatter_rel(jnp.moveaxis(terms, 0, 2), n_y, n_z, mine, outputs)
+    return (outs[0], outs[1], grads[0], grads[1])
 
 
 def solution(mesh):

time: 265 us -> 277 us (1.045)
  waiting for transfers between devices: 91.8 us -> 99.8 us
  local copies, waits for them, and re-layouts: 47.7 us -> 52 us
    all_to_all x1, waiting for transfers between devices: 0.01 us -> 5.25 us  [scatter_sum(): got = lax.all_to_all(x, axis_name, 0, 0, tiled=True)]
    ppermute x3, waiting for transfers between devices: 16.9 us -> 21.1 us  [dp_scatter_rel(): lax.ppermute(part.astype(jnp.bfloat16), 'dp', dp_shift(n_y, n_z, -1, 0))]
    unnamed x28 -> x32, local copies, waits for them, and re-layouts: 5.12 us -> 6.78 us
  transfers between devices with their start and end apart: 23 -> 23, of which waited for: 15 -> 16; matrix products, arithmetic and copies ran while one was open for 16% -> 17% of each run, Pallas kernels for 0% -> 0%
where the time goes in v14:
time: 277 us; the launch traced here: 274 us
  waiting for transfers between devices  99.8 us (36%)
  starting transfers between devices  94.2 us (34%)
  local copies, waits for them, and re-layouts  52 us (19%)
  other arithmetic  13.5 us (5%)
  matrix products  13.2 us (5%)
    ppermute x4, waiting for transfers between devices, dp_gather_rel(): cur_f = lax.ppermute(cur_f, 'dp', dp_shift(n_y, n_z, 1, 0))  36.2 us
    ppermute x4, waiting for transfers between devices, dp_scatter_rel(): lax.ppermute(part.astype(jnp.bfloat16), 'dp', dp_shift(n_y, n_z, 1, 0))  30 us
    ppermute x3, waiting for transfers between devices, dp_scatter_rel(): lax.ppermute(part.astype(jnp.bfloat16), 'dp', dp_shift(n_y, n_z, -1, 0))  21.1 us
    ppermute x3, starting transfers between devices, dp_gather_rel(): lax.ppermute(x, 'dp', dp_shift(n_y, n_z, 0, b))  18.9 us
    ppermute x3, starting transfers between devices, dp_gather_rel(): cur_b = lax.ppermute(cur_b, 'dp', dp_shift(n_y, n_z, -1, 0))  16 us
    all_to_all x2, starting transfers between devices, gather_all(): return lax.all_to_all(spread, axis_name, 0, 0, tiled=True)  11.6 us
    ppermute x3, starting transfers between devices, dp_scatter_rel(): lax.ppermute(acc[b].astype(jnp.bfloat16), 'dp', dp_shift(n_y, n_z, 0, -b))  11.5 us
    ppermute x3, starting transfers between devices, dp_scatter_rel(): lax.ppermute(part.astype(jnp.bfloat16), 'dp', dp_shift(n_y, n_z, -1, 0))  11.1 us
  transfers between devices with their start and end apart: 23, of which 16 were waited for; matrix products, arithmetic and copies ran while one was open for 17% of the time, Pallas kernels for 0%

profile of v14, /device:TPU:6, one launch (start us, length us, event | category | flops | bytes accessed | tf_op | source)
XLA Modules:
  0.0 274.0 jit_solution(10989722475054964138)
XLA Ops:
  1.5 6.1 %collective-permute-start = (bf16[2,2,128,128]{3,2,1,0:T(8,128)(2,1)S(1)}, bf16[2,2,128,128]{3,2,1,0:T(8,128)(2,1)S(1)}, u32[]{:S(2)}, u32[]{:S(2)}) collective-permute-start(bf16[2,2,128,128]{3,2,1,0:T(8,128)(2,1)S(1)} %get-tuple-element.34), channel_id=1, source_target_pairs={{0,1},{1,2},{2,3},{3,0},{4,5},{5,6},{6,7},{7,4},{8,9},{9,10},{10,1... | collective-permute-start | bytes 393224 | tf_op jit(solution)/shard_map/ppermute | solution.py:42
  7.6 9.1 %collective-permute-start.1 = (bf16[2,2,128,128]{3,2,1,0:T(8,128)(2,1)S(1)}, bf16[2,2,128,128]{3,2,1,0:T(8,128)(2,1)S(1)}, u32[]{:S(2)}, u32[]{:S(2)}) collective-permute-start(bf16[2,2,128,128]{3,2,1,0:T(8,128)(2,1)S(1)} %get-tuple-element.34), channel_id=1, source_target_pairs={{0,2},{1,3},{2,0},{3,1},{4,6},{5,7},{6,4},{7,5},{8,10},{9,11},{10,... | collective-permute-start | bytes 393224 | tf_op jit(solution)/shard_map/ppermute | solution.py:42
  16.8 3.7 %collective-permute-start.2 = (bf16[2,2,128,128]{3,2,1,0:T(8,128)(2,1)S(1)}, bf16[2,2,128,128]{3,2,1,0:T(8,128)(2,1)S(1)}, u32[]{:S(2)}, u32[]{:S(2)}) collective-permute-start(bf16[2,2,128,128]{3,2,1,0:T(8,128)(2,1)S(1)} %get-tuple-element.34), channel_id=1, source_target_pairs={{0,3},{1,0},{2,1},{3,2},{4,7},{5,4},{6,5},{7,6},{8,11},{9,8},{10,9... | collective-permute-start | bytes 393224 | tf_op jit(solution)/shard_map/ppermute | solution.py:42
  23.3 5.8 %all-to-all-start = ((bf16[16,2,128,256]{2,3,1,0:T(8,128)(2,1)}), bf16[16,2,128,256]{2,3,1,0:T(8,128)(2,1)}, u32[]{:S(2)}, u32[]{:S(2)}) async-start(bf16[16,2,128,256]{2,3,1,0:T(8,128)(2,1)} %broadcast_in_dim.4), calls=%async_computation | async-start | bytes 4194304 | tf_op jit(solution)/shard_map/all_to_all | solution.py:22
  29.4 3.5 %collective-permute-start.3 = (bf16[4,2,2,128,128]{4,3,2,1,0:T(8,128)(2,1)S(1)}, bf16[4,2,2,128,128]{4,3,2,1,0:T(8,128)(2,1)S(1)}, u32[]{:S(2)}, u32[]{:S(2)}) collective-permute-start(bf16[4,2,2,128,128]{4,3,2,1,0:T(8,128)(2,1)S(1)} %pad_maximum_fusion.1), channel_id=1, source_target_pairs={{0,4},{1,5},{2,6},{3,7},{4,8},{5,9},{6,10},{7,11},{8,12},{9,13},{1... | collective-permute-start | bytes 1572872 | tf_op jit(solution)/shard_map/ppermute | solution.py:48
  33.0 13.9 %collective-permute-done.3 = bf16[4,2,2,128,128]{4,3,2,1,0:T(8,128)(2,1)S(1)} collective-permute-done((bf16[4,2,2,128,128]{4,3,2,1,0:T(8,128)(2,1)S(1)}, bf16[4,2,2,128,128]{4,3,2,1,0:T(8,128)(2,1)S(1)}, u32[]{:S(2)}, u32[]{:S(2)}) %collective-permute-start.3) | collective-permute-done | bytes 524320 | tf_op jit(solution)/shard_map/ppermute | solution.py:48
  46.9 1.9 collective-permute-start.4
  49.0 5.1 %collective-permute-start.7 = (bf16[4,2,2,128,128]{4,3,2,1,0:T(8,128)(2,1)S(1)}, bf16[4,2,2,128,128]{4,3,2,1,0:T(8,128)(2,1)S(1)}, u32[]{:S(2)}, u32[]{:S(2)}) collective-permute-start(bf16[4,2,2,128,128]{4,3,2,1,0:T(8,128)(2,1)S(1)} %pad_maximum_fusion.1), channel_id=1, source_target_pairs={{0,28},{1,29},{2,30},{3,31},{4,0},{5,1},{6,2},{7,3},{8,4},{9,5},{1... | collective-permute-start | bytes 1572872 | tf_op jit(solution)/shard_map/ppermute | solution.py:51
  55.0 8.4 %collective-permute-done.4 = bf16[4,2,2,128,128]{4,3,2,1,0:T(8,128)(2,1)S(1)} collective-permute-done((bf16[4,2,2,128,128]{4,3,2,1,0:T(8,128)(2,1)S(1)}, bf16[4,2,2,128,128]{4,3,2,1,0:T(8,128)(2,1)S(1)}, u32[]{:S(2)}, u32[]{:S(2)}) %collective-permute-start.4) | collective-permute-done | bytes 524320 | tf_op jit(solution)/shard_map/ppermute | solution.py:48
  63.4 1.9 collective-permute-start.5
  66.2 5.1 %collective-permute-start.8 = (bf16[4,2,2,128,128]{4,3,2,1,0:T(8,128)(2,1)S(1)}, bf16[4,2,2,128,128]{4,3,2,1,0:T(8,128)(2,1)S(1)}, u32[]{:S(2)}, u32[]{:S(2)}) collective-permute-start(bf16[4,2,2,128,128]{4,3,2,1,0:T(8,128)(2,1)S(1)} %collective-permute-done.7), channel_id=1, source_target_pairs={{0,28},{1,29},{2,30},{3,31},{4,0},{5,1},{6,2},{7,3},{8,4},{9,5},{1... | collective-permute-start | bytes 1572872 | tf_op jit(solution)/shard_map/ppermute | solution.py:51
  71.7 7.3 %collective-permute-done.5 = bf16[4,2,2,128,128]{4,3,2,1,0:T(8,128)(2,1)S(1)} collective-permute-done((bf16[4,2,2,128,128]{4,3,2,1,0:T(8,128)(2,1)S(1)}, bf16[4,2,2,128,128]{4,3,2,1,0:T(8,128)(2,1)S(1)}, u32[]{:S(2)}, u32[]{:S(2)}) %collective-permute-start.5) | collective-permute-done | bytes 524320 | tf_op jit(solution)/shard_map/ppermute | solution.py:48
  79.0 1.9 collective-permute-start.6
  81.1 5.8 %collective-permute-start.9 = (bf16[4,2,2,128,128]{4,3,2,1,0:T(8,128)(2,1)S(1)}, bf16[4,2,2,128,128]{4,3,2,1,0:T(8,128)(2,1)S(1)}, u32[]{:S(2)}, u32[]{:S(2)}) collective-permute-start(bf16[4,2,2,128,128]{4,3,2,1,0:T(8,128)(2,1)S(1)} %collective-permute-done.8), channel_id=1, source_target_pairs={{0,28},{1,29},{2,30},{3,31},{4,0},{5,1},{6,2},{7,3},{8,4},{9,5},{1... | collective-permute-start | bytes 1572872 | tf_op jit(solution)/shard_map/ppermute | solution.py:51
  87.0 6.7 %collective-permute-done.6 = bf16[4,2,2,128,128]{4,3,2,1,0:T(8,128)(2,1)S(1)} collective-permute-done((bf16[4,2,2,128,128]{4,3,2,1,0:T(8,128)(2,1)S(1)}, bf16[4,2,2,128,128]{4,3,2,1,0:T(8,128)(2,1)S(1)}, u32[]{:S(2)}, u32[]{:S(2)}) %collective-permute-start.6) | collective-permute-done | bytes 524320 | tf_op jit(solution)/shard_map/ppermute | solution.py:48
  97.5 4.7 %copy.64 = bf16[8,8,128,128]{2,1,0,3:T(8,128)(2,1)} copy(bf16[8,8,128,128]{3,2,1,0:T(8,128)(2,1)} %bitcast.180) | data formatting | bytes 4194304 | tf_op jit(solution)/shard_map/reshape;squeeze | solution.py:120
  102.2 2.6 copy.58
  104.8 4.1 %copy.66 = bf16[8,8,128,128]{3,1,0,2:T(8,128)(2,1)} copy(bf16[8,8,128,128]{2,3,1,0:T(8,128)(2,1)} %bitcast.179) | data formatting | bytes 4194304 | tf_op jit(solution)/shard_map/reshape;squeeze | solution.py:119
  113.4 2.5 convolution_bitcast_fusion
  121.4 2.2 gather_fusion.3
  123.6 3.2 %fusion.3 = bf16[128,8,128]{0,2,1:T(8,128)(2,1)S(1)} fusion(bf16[8,8,128,128]{3,2,1,0:T(8,128)(2,1)} %bitcast.181, bf16[128,8,8,128]{3,0,2,1:T(8,128)(2,1)} %bitcast.173, f32[128,8,128]{0,2,1:T(8,128)} %copy-done.9), kind=kOutput, calls=%fused_computation.16 | convolution fusion | flops 269746176 | bytes 4980736 | tf_op jit(solution)/shard_map/tgko,gkho->tgh/dot_general | solution.py:138
  132.0 5.9 %all-to-all-start.1 = ((bf16[16,2,128,256]{2,3,1,0:T(8,128)(2,1)}), bf16[16,2,128,256]{2,3,1,0:T(8,128)(2,1)}, u32[]{:S(2)}, u32[]{:S(2)}) async-start(bf16[16,2,128,256]{2,3,1,0:T(8,128)(2,1)} %bitcast.175), calls=%async_computation.1 | async-start | bytes 4194304 | tf_op jit(solution)/shard_map/all_to_all | solution.py:26
  137.9 2.6 copy.54
  140.5 3.1 %copy.56 = bf16[8,8,128,128]{2,3,1,0:T(8,128)(2,1)S(1)} copy(bf16[8,8,128,128]{3,2,1,0:T(8,128)(2,1)} %bitcast.174) | data formatting | bytes 4194304 | tf_op jit(solution)/shard_map/gather | solution.py:133
  143.6 2.1 multiply_convert_fusion
  145.7 4.1 %copy.63 = bf16[1,8,4,2,128,128]{5,4,3,0,2,1:T(8,128)(2,1)} copy(bf16[1,8,4,2,128,128]{4,5,3,2,1,0:T(8,128)(2,1)} %bitcast.178) | data formatting | bytes 4194304 | tf_op jit(solution)/shard_map/stack | solution.py:156
  151.7 2.0 copy-done.4
  154.6 5.6 %collective-permute-start.14 = (bf16[4,2,2,128,128]{4,3,2,1,0:T(8,128)(2,1)S(1)}, bf16[4,2,2,128,128]{4,3,2,1,0:T(8,128)(2,1)S(1)}, u32[]{:S(2)}, u32[]{:S(2)}) collective-permute-start(bf16[4,2,2,128,128]{4,3,2,1,0:T(8,128)(2,1)S(1)} %get-tuple-element.21), channel_id=1, source_target_pairs={{0,28},{1,29},{2,30},{3,31},{4,0},{5,1},{6,2},{7,3},{8,4},{9,5},{1... | collective-permute-start | bytes 1572872 | tf_op jit(solution)/shard_map/ppermute | solution.py:69
  160.2 1.9 collective-permute-start.10
  162.1 5.2 %all-to-all-done.1 = bf16[16,2,128,256]{2,3,1,0:T(8,128)(2,1)} async-done(((bf16[16,2,128,256]{2,3,1,0:T(8,128)(2,1)}), bf16[16,2,128,256]{2,3,1,0:T(8,128)(2,1)}, u32[]{:S(2)}, u32[]{:S(2)}) %all-to-all-start.1) | async-done | bytes 2097184 | tf_op jit(solution)/shard_map/all_to_all | solution.py:26
  167.4 1.9 reduce_sum.12
  169.3 2.4 collective-permute-done.14
  173.4 5.7 %all-to-all-start.2 = ((bf16[16,2,128,256]{3,2,1,0:T(8,128)(2,1)}), bf16[16,2,128,256]{3,2,1,0:T(8,128)(2,1)S(1)}, u32[]{:S(2)}, u32[]{:S(2)}) async-start(bf16[16,2,128,256]{3,2,1,0:T(8,128)(2,1)} %broadcast_in_dim.5), calls=%async_computation.2 | async-start | bytes 4194304 | tf_op jit(solution)/shard_map/all_to_all | solution.py:22
  180.4 2.4 collective-permute-start.11
  182.8 15.4 %collective-permute-done.11 = bf16[4,2,2,128,128]{4,3,2,1,0:T(8,128)(2,1)S(1)} collective-permute-done((bf16[4,2,2,128,128]{4,3,2,1,0:T(8,128)(2,1)S(1)}, bf16[4,2,2,128,128]{4,3,2,1,0:T(8,128)(2,1)S(1)}, u32[]{:S(2)}, u32[]{:S(2)}) %collective-permute-start.11) | collective-permute-done | bytes 524320 | tf_op jit(solution)/shard_map/ppermute | solution.py:64
  199.4 1.9 collective-permute-start.12
  201.4 14.6 %collective-permute-done.12 = bf16[4,2,2,128,128]{4,3,2,1,0:T(8,128)(2,1)S(1)} collective-permute-done((bf16[4,2,2,128,128]{4,3,2,1,0:T(8,128)(2,1)S(1)}, bf16[4,2,2,128,128]{4,3,2,1,0:T(8,128)(2,1)S(1)}, u32[]{:S(2)}, u32[]{:S(2)}) %collective-permute-start.12) | collective-permute-done | bytes 524320 | tf_op jit(solution)/shard_map/ppermute | solution.py:64
  217.5 2.1 collective-permute-start.15
  219.6 3.7 %collective-permute-start.13 = (bf16[4,2,2,128,128]{4,3,2,1,0:T(8,128)(2,1)S(1)}, bf16[4,2,2,128,128]{4,3,2,1,0:T(8,128)(2,1)S(1)}, u32[]{:S(2)}, u32[]{:S(2)}) collective-permute-start(bf16[4,2,2,128,128]{4,3,2,1,0:T(8,128)(2,1)S(1)} %get-tuple-element.18), channel_id=1, source_target_pairs={{0,4},{1,5},{2,6},{3,7},{4,8},{5,9},{6,10},{7,11},{8,12},{9,13},{1... | collective-permute-start | bytes 1572872 | tf_op jit(solution)/shard_map/ppermute | solution.py:64
  223.4 8.6 %collective-permute-done.15 = bf16[4,2,2,128,128]{4,3,2,1,0:T(8,128)(2,1)S(1)} collective-permute-done((bf16[4,2,2,128,128]{4,3,2,1,0:T(8,128)(2,1)S(1)}, bf16[4,2,2,128,128]{4,3,2,1,0:T(8,128)(2,1)S(1)}, u32[]{:S(2)}, u32[]{:S(2)}) %collective-permute-start.15) | collective-permute-done | bytes 524320 | tf_op jit(solution)/shard_map/ppermute | solution.py:69
  233.2 3.4 %collective-permute-start.16 = (bf16[4,2,2,128,128]{4,3,2,1,0:T(8,128)(2,1)S(1)}, bf16[4,2,2,128,128]{4,3,2,1,0:T(8,128)(2,1)S(1)}, u32[]{:S(2)}, u32[]{:S(2)}) collective-permute-start(bf16[4,2,2,128,128]{4,3,2,1,0:T(8,128)(2,1)S(1)} %fusion.5), channel_id=1, source_target_pairs={{0,28},{1,29},{2,30},{3,31},{4,0},{5,1},{6,2},{7,3},{8,4},{9,5},{1... | collective-permute-start | bytes 1572872 | tf_op jit(solution)/shard_map/ppermute | solution.py:69
  236.7 10.1 %collective-permute-done.16 = bf16[4,2,2,128,128]{4,3,2,1,0:T(8,128)(2,1)S(1)} collective-permute-done((bf16[4,2,2,128,128]{4,3,2,1,0:T(8,128)(2,1)S(1)}, bf16[4,2,2,128,128]{4,3,2,1,0:T(8,128)(2,1)S(1)}, u32[]{:S(2)}, u32[]{:S(2)}) %collective-permute-start.16) | collective-permute-done | bytes 524320 | tf_op jit(solution)/shard_map/ppermute | solution.py:69
  248.1 2.4 copy.71
  252.9 4.6 %collective-permute-start.17 = (bf16[2,2,128,128]{3,2,1,0:T(8,128)(2,1)}, bf16[2,2,128,128]{3,2,1,0:T(8,128)(2,1)S(1)}, u32[]{:S(2)}, u32[]{:S(2)}) collective-permute-start(bf16[2,2,128,128]{3,2,1,0:T(8,128)(2,1)} %get-tuple-element.28), channel_id=1, source_target_pairs={{0,3},{1,0},{2,1},{3,2},{4,7},{5,4},{6,5},{7,6},{8,11},{9,8},{10,9... | collective-permute-start | bytes 393224 | tf_op jit(solution)/shard_map/ppermute | solution.py:83
  257.5 3.9 %collective-permute-start.18 = (bf16[2,2,128,128]{3,2,1,0:T(8,128)(2,1)}, bf16[2,2,128,128]{3,2,1,0:T(8,128)(2,1)S(1)}, u32[]{:S(2)}, u32[]{:S(2)}) collective-permute-start(bf16[2,2,128,128]{3,2,1,0:T(8,128)(2,1)} %get-tuple-element.30), channel_id=1, source_target_pairs={{0,2},{1,3},{2,0},{3,1},{4,6},{5,7},{6,4},{7,5},{8,10},{9,11},{10,... | collective-permute-start | bytes 393224 | tf_op jit(solution)/shard_map/ppermute | solution.py:83
  261.5 3.0 %collective-permute-start.19 = (bf16[2,2,128,128]{3,2,1,0:T(8,128)(2,1)S(1)}, bf16[2,2,128,128]{3,2,1,0:T(8,128)(2,1)}, u32[]{:S(2)}, u32[]{:S(2)}) collective-permute-start(bf16[2,2,128,128]{3,2,1,0:T(8,128)(2,1)S(1)} %get-tuple-element.29), channel_id=1, source_target_pairs={{0,1},{1,2},{2,3},{3,0},{4,5},{5,6},{6,7},{7,4},{8,9},{9,10},{10,1... | collective-permute-start | bytes 393224 | tf_op jit(solution)/shard_map/ppermute | solution.py:83
  267.4 2.1 collective-permute-done.18
  269.5 2.9 %collective-permute-done.19 = bf16[2,2,128,128]{3,2,1,0:T(8,128)(2,1)} collective-permute-done((bf16[2,2,128,128]{3,2,1,0:T(8,128)(2,1)S(1)}, bf16[2,2,128,128]{3,2,1,0:T(8,128)(2,1)}, u32[]{:S(2)}, u32[]{:S(2)}) %collective-permute-start.19) | collective-permute-done | bytes 131104 | tf_op jit(solution)/shard_map/ppermute | solution.py:83
  (95 shorter events, 43.6 us)
Async XLA Ops:
  0.6 53.5 %copy-start = (s32[64]{0:T(128)S(1)}, s32[64]{0:T(128)}, u32[]{:S(2)}) copy-start(s32[64]{0:T(128)} %param.9) | copy-start | bytes 772
  1.5 27.6 %collective-permute-start = (bf16[2,2,128,128]{3,2,1,0:T(8,128)(2,1)S(1)}, bf16[2,2,128,128]{3,2,1,0:T(8,128)(2,1)S(1)}, u32[]{:S(2)}, u32[]{:S(2)}) collective-permute-start(bf16[2,2,128,128]{3,2,1,0:T(8,128)(2,1)S(1)} %get-tuple-element.34), channel_id=1, source_target_pairs={{0,1},{1,2},{2,3},{3,0},{4,5},{5,6},{6,7},{7,4},{8,9},{9,10},{10,1... | collective-permute-start | bytes 393224 | tf_op jit(solution)/shard_map/ppermute | solution.py:42
  7.6 21.5 %collective-permute-start.1 = (bf16[2,2,128,128]{3,2,1,0:T(8,128)(2,1)S(1)}, bf16[2,2,128,128]{3,2,1,0:T(8,128)(2,1)S(1)}, u32[]{:S(2)}, u32[]{:S(2)}) collective-permute-start(bf16[2,2,128,128]{3,2,1,0:T(8,128)(2,1)S(1)} %get-tuple-element.34), channel_id=1, source_target_pairs={{0,2},{1,3},{2,0},{3,1},{4,6},{5,7},{6,4},{7,5},{8,10},{9,11},{10,... | collective-permute-start | bytes 393224 | tf_op jit(solution)/shard_map/ppermute | solution.py:42
  16.8 12.6 %collective-permute-start.2 = (bf16[2,2,128,128]{3,2,1,0:T(8,128)(2,1)S(1)}, bf16[2,2,128,128]{3,2,1,0:T(8,128)(2,1)S(1)}, u32[]{:S(2)}, u32[]{:S(2)}) collective-permute-start(bf16[2,2,128,128]{3,2,1,0:T(8,128)(2,1)S(1)} %get-tuple-element.34), channel_id=1, source_target_pairs={{0,3},{1,0},{2,1},{3,2},{4,7},{5,4},{6,5},{7,6},{8,11},{9,8},{10,9... | collective-permute-start | bytes 393224 | tf_op jit(solution)/shard_map/ppermute | solution.py:42
  23.3 42.0 %copy-start.2 = (s32[64]{0:T(128)S(1)}, s32[64]{0:T(128)}, u32[]{:S(2)}) copy-start(s32[64]{0:T(128)} %param.11) | copy-start | bytes 772
  23.3 85.6 %all-to-all-start = ((bf16[16,2,128,256]{2,3,1,0:T(8,128)(2,1)}), bf16[16,2,128,256]{2,3,1,0:T(8,128)(2,1)}, u32[]{:S(2)}, u32[]{:S(2)}) async-start(bf16[16,2,128,256]{2,3,1,0:T(8,128)(2,1)} %broadcast_in_dim.4), calls=%async_computation | async-start | bytes 4194304 | tf_op jit(solution)/shard_map/all_to_all | solution.py:22
  29.4 17.5 %collective-permute-start.3 = (bf16[4,2,2,128,128]{4,3,2,1,0:T(8,128)(2,1)S(1)}, bf16[4,2,2,128,128]{4,3,2,1,0:T(8,128)(2,1)S(1)}, u32[]{:S(2)}, u32[]{:S(2)}) collective-permute-start(bf16[4,2,2,128,128]{4,3,2,1,0:T(8,128)(2,1)S(1)} %pad_maximum_fusion.1), channel_id=1, source_target_pairs={{0,4},{1,5},{2,6},{3,7},{4,8},{5,9},{6,10},{7,11},{8,12},{9,13},{1... | collective-permute-start | bytes 1572872 | tf_op jit(solution)/shard_map/ppermute | solution.py:48
  46.9 16.5 %collective-permute-start.4 = (bf16[4,2,2,128,128]{4,3,2,1,0:T(8,128)(2,1)S(1)}, bf16[4,2,2,128,128]{4,3,2,1,0:T(8,128)(2,1)S(1)}, u32[]{:S(2)}, u32[]{:S(2)}) collective-permute-start(bf16[4,2,2,128,128]{4,3,2,1,0:T(8,128)(2,1)S(1)} %collective-permute-done.3), channel_id=1, source_target_pairs={{0,4},{1,5},{2,6},{3,7},{4,8},{5,9},{6,10},{7,11},{8,12},{9,13},{1... | collective-permute-start | bytes 1572872 | tf_op jit(solution)/shard_map/ppermute | solution.py:48
  49.0 17.2 %collective-permute-start.7 = (bf16[4,2,2,128,128]{4,3,2,1,0:T(8,128)(2,1)S(1)}, bf16[4,2,2,128,128]{4,3,2,1,0:T(8,128)(2,1)S(1)}, u32[]{:S(2)}, u32[]{:S(2)}) collective-permute-start(bf16[4,2,2,128,128]{4,3,2,1,0:T(8,128)(2,1)S(1)} %pad_maximum_fusion.1), channel_id=1, source_target_pairs={{0,28},{1,29},{2,30},{3,31},{4,0},{5,1},{6,2},{7,3},{8,4},{9,5},{1... | collective-permute-start | bytes 1572872 | tf_op jit(solution)/shard_map/ppermute | solution.py:51
  63.4 15.6 %collective-permute-start.5 = (bf16[4,2,2,128,128]{4,3,2,1,0:T(8,128)(2,1)S(1)}, bf16[4,2,2,128,128]{4,3,2,1,0:T(8,128)(2,1)S(1)}, u32[]{:S(2)}, u32[]{:S(2)}) collective-permute-start(bf16[4,2,2,128,128]{4,3,2,1,0:T(8,128)(2,1)S(1)} %collective-permute-done.4), channel_id=1, source_target_pairs={{0,4},{1,5},{2,6},{3,7},{4,8},{5,9},{6,10},{7,11},{8,12},{9,13},{1... | collective-permute-start | bytes 1572872 | tf_op jit(solution)/shard_map/ppermute | solution.py:48
  66.2 14.9 %collective-permute-start.8 = (bf16[4,2,2,128,128]{4,3,2,1,0:T(8,128)(2,1)S(1)}, bf16[4,2,2,128,128]{4,3,2,1,0:T(8,128)(2,1)S(1)}, u32[]{:S(2)}, u32[]{:S(2)}) collective-permute-start(bf16[4,2,2,128,128]{4,3,2,1,0:T(8,128)(2,1)S(1)} %collective-permute-done.7), channel_id=1, source_target_pairs={{0,28},{1,29},{2,30},{3,31},{4,0},{5,1},{6,2},{7,3},{8,4},{9,5},{1... | collective-permute-start | bytes 1572872 | tf_op jit(solution)/shard_map/ppermute | solution.py:51
  79.0 14.7 %collective-permute-start.6 = (bf16[4,2,2,128,128]{4,3,2,1,0:T(8,128)(2,1)S(1)}, bf16[4,2,2,128,128]{4,3,2,1,0:T(8,128)(2,1)S(1)}, u32[]{:S(2)}, u32[]{:S(2)}) collective-permute-start(bf16[4,2,2,128,128]{4,3,2,1,0:T(8,128)(2,1)S(1)} %collective-permute-done.5), channel_id=1, source_target_pairs={{0,4},{1,5},{2,6},{3,7},{4,8},{5,9},{6,10},{7,11},{8,12},{9,13},{1... | collective-permute-start | bytes 1572872 | tf_op jit(solution)/shard_map/ppermute | solution.py:48
  81.1 14.4 %collective-permute-start.9 = (bf16[4,2,2,128,128]{4,3,2,1,0:T(8,128)(2,1)S(1)}, bf16[4,2,2,128,128]{4,3,2,1,0:T(8,128)(2,1)S(1)}, u32[]{:S(2)}, u32[]{:S(2)}) collective-permute-start(bf16[4,2,2,128,128]{4,3,2,1,0:T(8,128)(2,1)S(1)} %collective-permute-done.8), channel_id=1, source_target_pairs={{0,28},{1,29},{2,30},{3,31},{4,0},{5,1},{6,2},{7,3},{8,4},{9,5},{1... | collective-permute-start | bytes 1572872 | tf_op jit(solution)/shard_map/ppermute | solution.py:51
  97.5 4.7 %copy-start.3 = (bf16[1,8,4,2,128,128]{5,4,3,0,2,1:T(8,128)(2,1)}, bf16[1,8,4,2,128,128]{5,4,3,0,2,1:T(8,128)(2,1)S(1)}, u32[]{:S(2)}) copy-start(bf16[1,8,4,2,128,128]{5,4,3,0,2,1:T(8,128)(2,1)S(1)} %get-tuple-element.23) | copy-start | bytes 6291460
  113.4 2.5 copy-start.6
  115.9 0.8 copy-start.9
  123.6 3.2 %copy-start.5 = (bf16[8,8,128,128]{3,1,0,2:T(8,128)(2,1)S(1)}, bf16[8,8,128,128]{3,1,0,2:T(8,128)(2,1)}, u32[]{:S(2)}) copy-start(bf16[8,8,128,128]{3,1,0,2:T(8,128)(2,1)} %copy.66) | copy-start | bytes 6291460
  129.2 1.2 copy-start.11
  132.0 35.4 %all-to-all-start.1 = ((bf16[16,2,128,256]{2,3,1,0:T(8,128)(2,1)}), bf16[16,2,128,256]{2,3,1,0:T(8,128)(2,1)}, u32[]{:S(2)}, u32[]{:S(2)}) async-start(bf16[16,2,128,256]{2,3,1,0:T(8,128)(2,1)} %bitcast.175), calls=%async_computation.1 | async-start | bytes 4194304 | tf_op jit(solution)/shard_map/all_to_all | solution.py:26
  140.5 3.1 %copy-start.10 = (f32[128,8,128]{0,2,1:T(8,128)S(1)}, f32[128,8,128]{0,2,1:T(8,128)}, u32[]{:S(2)}) copy-start(f32[128,8,128]{0,2,1:T(8,128)} %copy-done.9) | copy-start | bytes 1572868
  145.7 4.1 %copy-start.7 = (bf16[8,8,128,128]{2,3,1,0:T(8,128)(2,1)S(1)}, bf16[8,8,128,128]{2,3,1,0:T(8,128)(2,1)}, u32[]{:S(2)}) copy-start(bf16[8,8,128,128]{2,3,1,0:T(8,128)(2,1)} %copy.54) | copy-start | bytes 6291460
  149.8 1.6 copy-start.8
  151.7 2.0 copy-start.4
  154.6 17.1 %collective-permute-start.14 = (bf16[4,2,2,128,128]{4,3,2,1,0:T(8,128)(2,1)S(1)}, bf16[4,2,2,128,128]{4,3,2,1,0:T(8,128)(2,1)S(1)}, u32[]{:S(2)}, u32[]{:S(2)}) collective-permute-start(bf16[4,2,2,128,128]{4,3,2,1,0:T(8,128)(2,1)S(1)} %get-tuple-element.21), channel_id=1, source_target_pairs={{0,28},{1,29},{2,30},{3,31},{4,0},{5,1},{6,2},{7,3},{8,4},{9,5},{1... | collective-permute-start | bytes 1572872 | tf_op jit(solution)/shard_map/ppermute | solution.py:69
  160.2 18.9 %collective-permute-start.10 = (bf16[4,2,2,128,128]{4,3,2,1,0:T(8,128)(2,1)}, bf16[4,2,2,128,128]{4,3,2,1,0:T(8,128)(2,1)S(1)}, u32[]{:S(2)}, u32[]{:S(2)}) collective-permute-start(bf16[4,2,2,128,128]{4,3,2,1,0:T(8,128)(2,1)} %get-tuple-element.20), channel_id=1, source_target_pairs={{0,4},{1,5},{2,6},{3,7},{4,8},{5,9},{6,10},{7,11},{8,12},{9,13},{1... | collective-permute-start | bytes 1572872 | tf_op jit(solution)/shard_map/ppermute | solution.py:64
  173.4 74.7 %all-to-all-start.2 = ((bf16[16,2,128,256]{3,2,1,0:T(8,128)(2,1)}), bf16[16,2,128,256]{3,2,1,0:T(8,128)(2,1)S(1)}, u32[]{:S(2)}, u32[]{:S(2)}) async-start(bf16[16,2,128,256]{3,2,1,0:T(8,128)(2,1)} %broadcast_in_dim.5), calls=%async_computation.2 | async-start | bytes 4194304 | tf_op jit(solution)/shard_map/all_to_all | solution.py:22
  180.4 17.8 %collective-permute-start.11 = (bf16[4,2,2,128,128]{4,3,2,1,0:T(8,128)(2,1)S(1)}, bf16[4,2,2,128,128]{4,3,2,1,0:T(8,128)(2,1)S(1)}, u32[]{:S(2)}, u32[]{:S(2)}) collective-permute-start(bf16[4,2,2,128,128]{4,3,2,1,0:T(8,128)(2,1)S(1)} %fusion.6), channel_id=1, source_target_pairs={{0,4},{1,5},{2,6},{3,7},{4,8},{5,9},{6,10},{7,11},{8,12},{9,13},{1... | collective-permute-start | bytes 1572872 | tf_op jit(solution)/shard_map/ppermute | solution.py:64
  199.4 16.6 %collective-permute-start.12 = (bf16[4,2,2,128,128]{4,3,2,1,0:T(8,128)(2,1)S(1)}, bf16[4,2,2,128,128]{4,3,2,1,0:T(8,128)(2,1)S(1)}, u32[]{:S(2)}, u32[]{:S(2)}) collective-permute-start(bf16[4,2,2,128,128]{4,3,2,1,0:T(8,128)(2,1)S(1)} %fusion.7), channel_id=1, source_target_pairs={{0,4},{1,5},{2,6},{3,7},{4,8},{5,9},{6,10},{7,11},{8,12},{9,13},{1... | collective-permute-start | bytes 1572872 | tf_op jit(solution)/shard_map/ppermute | solution.py:64
  217.5 14.5 %collective-permute-start.15 = (bf16[4,2,2,128,128]{4,3,2,1,0:T(8,128)(2,1)S(1)}, bf16[4,2,2,128,128]{4,3,2,1,0:T(8,128)(2,1)S(1)}, u32[]{:S(2)}, u32[]{:S(2)}) collective-permute-start(bf16[4,2,2,128,128]{4,3,2,1,0:T(8,128)(2,1)S(1)} %get-tuple-element.19), channel_id=1, source_target_pairs={{0,28},{1,29},{2,30},{3,31},{4,0},{5,1},{6,2},{7,3},{8,4},{9,5},{1... | collective-permute-start | bytes 1572872 | tf_op jit(solution)/shard_map/ppermute | solution.py:69
  219.6 17.0 %collective-permute-start.13 = (bf16[4,2,2,128,128]{4,3,2,1,0:T(8,128)(2,1)S(1)}, bf16[4,2,2,128,128]{4,3,2,1,0:T(8,128)(2,1)S(1)}, u32[]{:S(2)}, u32[]{:S(2)}) collective-permute-start(bf16[4,2,2,128,128]{4,3,2,1,0:T(8,128)(2,1)S(1)} %get-tuple-element.18), channel_id=1, source_target_pairs={{0,4},{1,5},{2,6},{3,7},{4,8},{5,9},{6,10},{7,11},{8,12},{9,13},{1... | collective-permute-start | bytes 1572872 | tf_op jit(solution)/shard_map/ppermute | solution.py:64
  233.2 13.5 %collective-permute-start.16 = (bf16[4,2,2,128,128]{4,3,2,1,0:T(8,128)(2,1)S(1)}, bf16[4,2,2,128,128]{4,3,2,1,0:T(8,128)(2,1)S(1)}, u32[]{:S(2)}, u32[]{:S(2)}) collective-permute-start(bf16[4,2,2,128,128]{4,3,2,1,0:T(8,128)(2,1)S(1)} %fusion.5), channel_id=1, source_target_pairs={{0,28},{1,29},{2,30},{3,31},{4,0},{5,1},{6,2},{7,3},{8,4},{9,5},{1... | collective-permute-start | bytes 1572872 | tf_op jit(solution)/shard_map/ppermute | solution.py:69
  252.9 14.4 %collective-permute-start.17 = (bf16[2,2,128,128]{3,2,1,0:T(8,128)(2,1)}, bf16[2,2,128,128]{3,2,1,0:T(8,128)(2,1)S(1)}, u32[]{:S(2)}, u32[]{:S(2)}) collective-permute-start(bf16[2,2,128,128]{3,2,1,0:T(8,128)(2,1)} %get-tuple-element.28), channel_id=1, source_target_pairs={{0,3},{1,0},{2,1},{3,2},{4,7},{5,4},{6,5},{7,6},{8,11},{9,8},{10,9... | collective-permute-start | bytes 393224 | tf_op jit(solution)/shard_map/ppermute | solution.py:83
  257.5 11.9 %collective-permute-start.18 = (bf16[2,2,128,128]{3,2,1,0:T(8,128)(2,1)}, bf16[2,2,128,128]{3,2,1,0:T(8,128)(2,1)S(1)}, u32[]{:S(2)}, u32[]{:S(2)}) collective-permute-start(bf16[2,2,128,128]{3,2,1,0:T(8,128)(2,1)} %get-tuple-element.30), channel_id=1, source_target_pairs={{0,2},{1,3},{2,0},{3,1},{4,6},{5,7},{6,4},{7,5},{8,10},{9,11},{10,... | collective-permute-start | bytes 393224 | tf_op jit(solution)/shard_map/ppermute | solution.py:83
  261.5 10.9 %collective-permute-start.19 = (bf16[2,2,128,128]{3,2,1,0:T(8,128)(2,1)S(1)}, bf16[2,2,128,128]{3,2,1,0:T(8,128)(2,1)}, u32[]{:S(2)}, u32[]{:S(2)}) collective-permute-start(bf16[2,2,128,128]{3,2,1,0:T(8,128)(2,1)S(1)} %get-tuple-element.29), channel_id=1, source_target_pairs={{0,1},{1,2},{2,3},{3,0},{4,5},{5,6},{6,7},{7,4},{8,9},{9,10},{10,1... | collective-permute-start | bytes 393224 | tf_op jit(solution)/shard_map/ppermute | solution.py:83
  264.5 9.6 %copy-start.1 = (s32[64]{0:T(128)S(1)}, s32[64]{0:T(128)}, u32[]{:S(2)}) copy-start(s32[64]{0:T(128)} %param.9) | copy-start | bytes 772

commit v15 on v11

--- a/solution.py
+++ b/solution.py
@@ -67,7 +67,7 @@
         if got_b is not None:
             part = part + got_b.astype(jnp.float32)
         got_b = lax.ppermute(part.astype(jnp.bfloat16), "dp", dp_shift(n_y, n_z, -1, 0))
-        if k == 1 and tie is not None:
+        if k == min(2, n_b) and tie is not None:
             got_b, tie = lax.optimization_barrier((got_b, tie))
     acc = terms[0].astype(jnp.float32)
     if got_f is not None:

time: 265 us -> 277 us (1.045)
  waiting for transfers between devices: 91.8 us -> 106 us
    ppermute x4, waiting for transfers between devices: 29.3 us -> 49.3 us  [dp_scatter_rel(): lax.ppermute(part.astype(jnp.bfloat16), 'dp', dp_shift(n_y, n_z, 1, 0))]
    ppermute x3, waiting for transfers between devices: 16.9 us -> 11.5 us  [dp_scatter_rel(): lax.ppermute(part.astype(jnp.bfloat16), 'dp', dp_shift(n_y, n_z, -1, 0))]
  transfers between devices with their start and end apart: 23 -> 23, of which waited for: 15 -> 15; matrix products, arithmetic and copies ran while one was open for 16% -> 14% of each run, Pallas kernels for 0% -> 0%
where the time goes in v15:
time: 277 us; the launch traced here: 272 us
  waiting for transfers between devices  106 us (38%)
  starting transfers between devices  93.7 us (34%)
  local copies, waits for them, and re-layouts  48.5 us (18%)
  matrix products  13.2 us (5%)
  other arithmetic  9.42 us (3%)
    ppermute x4, waiting for transfers between devices, dp_scatter_rel(): lax.ppermute(part.astype(jnp.bfloat16), 'dp', dp_shift(n_y, n_z, 1, 0))  49.3 us
    ppermute x4, waiting for transfers between devices, dp_gather_rel(): cur_f = lax.ppermute(cur_f, 'dp', dp_shift(n_y, n_z, 1, 0))  36.2 us
    ppermute x3, starting transfers between devices, dp_gather_rel(): lax.ppermute(x, 'dp', dp_shift(n_y, n_z, 0, b))  18.9 us
    ppermute x3, starting transfers between devices, dp_gather_rel(): cur_b = lax.ppermute(cur_b, 'dp', dp_shift(n_y, n_z, -1, 0))  16 us
    ppermute x3, starting transfers between devices, dp_scatter_rel(): lax.ppermute(part.astype(jnp.bfloat16), 'dp', dp_shift(n_y, n_z, -1, 0))  12.2 us
    all_to_all x2, starting transfers between devices, gather_all(): return lax.all_to_all(spread, axis_name, 0, 0, tiled=True)  11.6 us
    ppermute x3, starting transfers between devices, dp_scatter_rel(): lax.ppermute(acc[b].astype(jnp.bfloat16), 'dp', dp_shift(n_y, n_z, 0, -b))  11.5 us
    ppermute x3, waiting for transfers between devices, dp_scatter_rel(): lax.ppermute(part.astype(jnp.bfloat16), 'dp', dp_shift(n_y, n_z, -1, 0))  11.5 us
  transfers between devices with their start and end apart: 23, of which 15 were waited for; matrix products, arithmetic and copies ran while one was open for 14% of the time, Pallas kernels for 0%

profile of v15, /device:TPU:6, one launch (start us, length us, event | category | flops | bytes accessed | tf_op | source)
XLA Modules:
  0.0 272.4 jit_solution(15823443501335288764)
XLA Ops:
  1.5 6.1 %collective-permute-start = (bf16[2,2,128,128]{3,2,1,0:T(8,128)(2,1)S(1)}, bf16[2,2,128,128]{3,2,1,0:T(8,128)(2,1)S(1)}, u32[]{:S(2)}, u32[]{:S(2)}) collective-permute-start(bf16[2,2,128,128]{3,2,1,0:T(8,128)(2,1)S(1)} %get-tuple-element.32), channel_id=1, source_target_pairs={{0,1},{1,2},{2,3},{3,0},{4,5},{5,6},{6,7},{7,4},{8,9},{9,10},{10,1... | collective-permute-start | bytes 393224 | tf_op jit(solution)/shard_map/ppermute | solution.py:42
  7.6 9.1 %collective-permute-start.1 = (bf16[2,2,128,128]{3,2,1,0:T(8,128)(2,1)S(1)}, bf16[2,2,128,128]{3,2,1,0:T(8,128)(2,1)S(1)}, u32[]{:S(2)}, u32[]{:S(2)}) collective-permute-start(bf16[2,2,128,128]{3,2,1,0:T(8,128)(2,1)S(1)} %get-tuple-element.32), channel_id=1, source_target_pairs={{0,2},{1,3},{2,0},{3,1},{4,6},{5,7},{6,4},{7,5},{8,10},{9,11},{10,... | collective-permute-start | bytes 393224 | tf_op jit(solution)/shard_map/ppermute | solution.py:42
  16.8 3.7 %collective-permute-start.2 = (bf16[2,2,128,128]{3,2,1,0:T(8,128)(2,1)S(1)}, bf16[2,2,128,128]{3,2,1,0:T(8,128)(2,1)S(1)}, u32[]{:S(2)}, u32[]{:S(2)}) collective-permute-start(bf16[2,2,128,128]{3,2,1,0:T(8,128)(2,1)S(1)} %get-tuple-element.32), channel_id=1, source_target_pairs={{0,3},{1,0},{2,1},{3,2},{4,7},{5,4},{6,5},{7,6},{8,11},{9,8},{10,9... | collective-permute-start | bytes 393224 | tf_op jit(solution)/shard_map/ppermute | solution.py:42
  21.5 1.9 broadcast_in_dim.4
  23.3 5.8 %all-to-all-start = ((bf16[16,2,128,256]{2,3,1,0:T(8,128)(2,1)}), bf16[16,2,128,256]{2,3,1,0:T(8,128)(2,1)}, u32[]{:S(2)}, u32[]{:S(2)}) async-start(bf16[16,2,128,256]{2,3,1,0:T(8,128)(2,1)} %broadcast_in_dim.4), calls=%async_computation | async-start | bytes 4194304 | tf_op jit(solution)/shard_map/all_to_all | solution.py:22
  29.4 3.5 %collective-permute-start.3 = (bf16[4,2,2,128,128]{4,3,2,1,0:T(8,128)(2,1)S(1)}, bf16[4,2,2,128,128]{4,3,2,1,0:T(8,128)(2,1)S(1)}, u32[]{:S(2)}, u32[]{:S(2)}) collective-permute-start(bf16[4,2,2,128,128]{4,3,2,1,0:T(8,128)(2,1)S(1)} %pad_maximum_fusion.1), channel_id=1, source_target_pairs={{0,4},{1,5},{2,6},{3,7},{4,8},{5,9},{6,10},{7,11},{8,12},{9,13},{1... | collective-permute-start | bytes 1572872 | tf_op jit(solution)/shard_map/ppermute | solution.py:48
  33.0 13.9 %collective-permute-done.3 = bf16[4,2,2,128,128]{4,3,2,1,0:T(8,128)(2,1)S(1)} collective-permute-done((bf16[4,2,2,128,128]{4,3,2,1,0:T(8,128)(2,1)S(1)}, bf16[4,2,2,128,128]{4,3,2,1,0:T(8,128)(2,1)S(1)}, u32[]{:S(2)}, u32[]{:S(2)}) %collective-permute-start.3) | collective-permute-done | bytes 524320 | tf_op jit(solution)/shard_map/ppermute | solution.py:48
  46.9 1.9 collective-permute-start.4
  49.0 5.1 %collective-permute-start.7 = (bf16[4,2,2,128,128]{4,3,2,1,0:T(8,128)(2,1)S(1)}, bf16[4,2,2,128,128]{4,3,2,1,0:T(8,128)(2,1)S(1)}, u32[]{:S(2)}, u32[]{:S(2)}) collective-permute-start(bf16[4,2,2,128,128]{4,3,2,1,0:T(8,128)(2,1)S(1)} %pad_maximum_fusion.1), channel_id=1, source_target_pairs={{0,28},{1,29},{2,30},{3,31},{4,0},{5,1},{6,2},{7,3},{8,4},{9,5},{1... | collective-permute-start | bytes 1572872 | tf_op jit(solution)/shard_map/ppermute | solution.py:51
  55.0 8.4 %collective-permute-done.4 = bf16[4,2,2,128,128]{4,3,2,1,0:T(8,128)(2,1)S(1)} collective-permute-done((bf16[4,2,2,128,128]{4,3,2,1,0:T(8,128)(2,1)S(1)}, bf16[4,2,2,128,128]{4,3,2,1,0:T(8,128)(2,1)S(1)}, u32[]{:S(2)}, u32[]{:S(2)}) %collective-permute-start.4) | collective-permute-done | bytes 524320 | tf_op jit(solution)/shard_map/ppermute | solution.py:48
  63.4 1.9 collective-permute-start.5
  66.2 5.1 %collective-permute-start.8 = (bf16[4,2,2,128,128]{4,3,2,1,0:T(8,128)(2,1)S(1)}, bf16[4,2,2,128,128]{4,3,2,1,0:T(8,128)(2,1)S(1)}, u32[]{:S(2)}, u32[]{:S(2)}) collective-permute-start(bf16[4,2,2,128,128]{4,3,2,1,0:T(8,128)(2,1)S(1)} %collective-permute-done.7), channel_id=1, source_target_pairs={{0,28},{1,29},{2,30},{3,31},{4,0},{5,1},{6,2},{7,3},{8,4},{9,5},{1... | collective-permute-start | bytes 1572872 | tf_op jit(solution)/shard_map/ppermute | solution.py:51
  71.7 7.3 %collective-permute-done.5 = bf16[4,2,2,128,128]{4,3,2,1,0:T(8,128)(2,1)S(1)} collective-permute-done((bf16[4,2,2,128,128]{4,3,2,1,0:T(8,128)(2,1)S(1)}, bf16[4,2,2,128,128]{4,3,2,1,0:T(8,128)(2,1)S(1)}, u32[]{:S(2)}, u32[]{:S(2)}) %collective-permute-start.5) | collective-permute-done | bytes 524320 | tf_op jit(solution)/shard_map/ppermute | solution.py:48
  79.0 1.9 collective-permute-start.6
  81.1 5.8 %collective-permute-start.9 = (bf16[4,2,2,128,128]{4,3,2,1,0:T(8,128)(2,1)S(1)}, bf16[4,2,2,128,128]{4,3,2,1,0:T(8,128)(2,1)S(1)}, u32[]{:S(2)}, u32[]{:S(2)}) collective-permute-start(bf16[4,2,2,128,128]{4,3,2,1,0:T(8,128)(2,1)S(1)} %collective-permute-done.8), channel_id=1, source_target_pairs={{0,28},{1,29},{2,30},{3,31},{4,0},{5,1},{6,2},{7,3},{8,4},{9,5},{1... | collective-permute-start | bytes 1572872 | tf_op jit(solution)/shard_map/ppermute | solution.py:51
  87.0 6.7 %collective-permute-done.6 = bf16[4,2,2,128,128]{4,3,2,1,0:T(8,128)(2,1)S(1)} collective-permute-done((bf16[4,2,2,128,128]{4,3,2,1,0:T(8,128)(2,1)S(1)}, bf16[4,2,2,128,128]{4,3,2,1,0:T(8,128)(2,1)S(1)}, u32[]{:S(2)}, u32[]{:S(2)}) %collective-permute-start.6) | collective-permute-done | bytes 524320 | tf_op jit(solution)/shard_map/ppermute | solution.py:48
  95.7 1.8 fusion.37
  97.5 4.7 %copy.64 = bf16[8,8,128,128]{2,1,0,3:T(8,128)(2,1)} copy(bf16[8,8,128,128]{3,2,1,0:T(8,128)(2,1)} %bitcast.183) | data formatting | bytes 4194304 | tf_op jit(solution)/shard_map/reshape;squeeze | solution.py:116
  102.2 2.6 copy.58
  104.8 4.1 %copy.66 = bf16[8,8,128,128]{3,1,0,2:T(8,128)(2,1)} copy(bf16[8,8,128,128]{2,3,1,0:T(8,128)(2,1)} %bitcast.182) | data formatting | bytes 4194304 | tf_op jit(solution)/shard_map/reshape;squeeze | solution.py:115
  108.9 1.7 copy.95
  113.4 2.5 convolution_bitcast_fusion
  121.4 2.1 gather_fusion.3
  123.6 3.2 %fusion.3 = bf16[128,8,128]{0,2,1:T(8,128)(2,1)S(1)} fusion(bf16[8,8,128,128]{3,2,1,0:T(8,128)(2,1)} %bitcast.184, bf16[128,8,8,128]{3,0,2,1:T(8,128)(2,1)} %bitcast.176, f32[128,8,128]{0,2,1:T(8,128)} %copy-done.9), kind=kOutput, calls=%fused_computation.16 | convolution fusion | flops 269746176 | bytes 4980736 | tf_op jit(solution)/shard_map/tgko,gkho->tgh/dot_general | solution.py:134
  132.0 5.9 %all-to-all-start.1 = ((bf16[16,2,128,256]{2,3,1,0:T(8,128)(2,1)}), bf16[16,2,128,256]{2,3,1,0:T(8,128)(2,1)}, u32[]{:S(2)}, u32[]{:S(2)}) async-start(bf16[16,2,128,256]{2,3,1,0:T(8,128)(2,1)} %bitcast.178), calls=%async_computation.1 | async-start | bytes 4194304 | tf_op jit(solution)/shard_map/all_to_all | solution.py:26
  137.9 2.6 copy.54
  140.5 3.1 %copy.56 = bf16[8,8,128,128]{2,3,1,0:T(8,128)(2,1)S(1)} copy(bf16[8,8,128,128]{3,2,1,0:T(8,128)(2,1)} %bitcast.177) | data formatting | bytes 4194304 | tf_op jit(solution)/shard_map/gather | solution.py:129
  143.6 2.1 multiply_convert_fusion
  145.6 4.1 %copy.63 = bf16[1,8,4,2,128,128]{5,4,3,0,2,1:T(8,128)(2,1)} copy(bf16[1,8,4,2,128,128]{4,5,3,2,1,0:T(8,128)(2,1)} %bitcast.181) | data formatting | bytes 4194304 | tf_op jit(solution)/shard_map/stack | solution.py:152
  151.8 2.7 collective-permute-start.12
  154.5 4.8 %collective-permute-start.10 = (bf16[4,2,2,128,128]{4,3,2,1,0:T(8,128)(2,1)S(1)}, bf16[4,2,2,128,128]{4,3,2,1,0:T(8,128)(2,1)S(1)}, u32[]{:S(2)}, u32[]{:S(2)}) collective-permute-start(bf16[4,2,2,128,128]{4,3,2,1,0:T(8,128)(2,1)S(1)} %get-tuple-element.19), channel_id=1, source_target_pairs={{0,28},{1,29},{2,30},{3,31},{4,0},{5,1},{6,2},{7,3},{8,4},{9,5},{1... | collective-permute-start | bytes 1572872 | tf_op jit(solution)/shard_map/ppermute | solution.py:69
  159.3 10.3 %collective-permute-done.12 = bf16[4,2,2,128,128]{4,3,2,1,0:T(8,128)(2,1)S(1)} collective-permute-done((bf16[4,2,2,128,128]{4,3,2,1,0:T(8,128)(2,1)S(1)}, bf16[4,2,2,128,128]{4,3,2,1,0:T(8,128)(2,1)S(1)}, u32[]{:S(2)}, u32[]{:S(2)}) %collective-permute-start.12) | collective-permute-done | bytes 524320 | tf_op jit(solution)/shard_map/ppermute | solution.py:64
  169.8 1.9 collective-permute-start.13
  171.7 14.6 %collective-permute-done.13 = bf16[4,2,2,128,128]{4,3,2,1,0:T(8,128)(2,1)S(1)} collective-permute-done((bf16[4,2,2,128,128]{4,3,2,1,0:T(8,128)(2,1)S(1)}, bf16[4,2,2,128,128]{4,3,2,1,0:T(8,128)(2,1)S(1)}, u32[]{:S(2)}, u32[]{:S(2)}) %collective-permute-start.13) | collective-permute-done | bytes 524320 | tf_op jit(solution)/shard_map/ppermute | solution.py:64
  186.7 2.2 collective-permute-start.11
  188.9 1.9 reduce_sum.12
  190.8 10.3 %collective-permute-done.11 = bf16[4,2,2,128,128]{4,3,2,1,0:T(8,128)(2,1)S(1)} collective-permute-done((bf16[4,2,2,128,128]{4,3,2,1,0:T(8,128)(2,1)S(1)}, bf16[4,2,2,128,128]{4,3,2,1,0:T(8,128)(2,1)S(1)}, u32[]{:S(2)}, u32[]{:S(2)}) %collective-permute-start.11) | collective-permute-done | bytes 524320 | tf_op jit(solution)/shard_map/ppermute | solution.py:69
  202.9 5.7 %all-to-all-start.2 = ((bf16[16,2,128,256]{3,2,1,0:T(8,128)(2,1)}), bf16[16,2,128,256]{3,2,1,0:T(8,128)(2,1)S(1)}, u32[]{:S(2)}, u32[]{:S(2)}) async-start(bf16[16,2,128,256]{3,2,1,0:T(8,128)(2,1)} %broadcast_in_dim.5), calls=%async_computation.2 | async-start | bytes 4194304 | tf_op jit(solution)/shard_map/all_to_all | solution.py:22
  208.6 1.9 collective-permute-start.14
  210.5 15.2 %collective-permute-done.14 = bf16[4,2,2,128,128]{4,3,2,1,0:T(8,128)(2,1)S(1)} collective-permute-done((bf16[4,2,2,128,128]{4,3,2,1,0:T(8,128)(2,1)S(1)}, bf16[4,2,2,128,128]{4,3,2,1,0:T(8,128)(2,1)S(1)}, u32[]{:S(2)}, u32[]{:S(2)}) %collective-permute-start.14) | collective-permute-done | bytes 524320 | tf_op jit(solution)/shard_map/ppermute | solution.py:64
  227.3 1.9 collective-permute-start.15
  229.2 5.1 %collective-permute-start.16 = (bf16[4,2,2,128,128]{4,3,2,1,0:T(8,128)(2,1)S(1)}, bf16[4,2,2,128,128]{4,3,2,1,0:T(8,128)(2,1)S(1)}, u32[]{:S(2)}, u32[]{:S(2)}) collective-permute-start(bf16[4,2,2,128,128]{4,3,2,1,0:T(8,128)(2,1)S(1)} %get-tuple-element.15), channel_id=1, source_target_pairs={{0,28},{1,29},{2,30},{3,31},{4,0},{5,1},{6,2},{7,3},{8,4},{9,5},{1... | collective-permute-start | bytes 1572872 | tf_op jit(solution)/shard_map/ppermute | solution.py:69
  234.4 9.2 %collective-permute-done.15 = bf16[4,2,2,128,128]{4,3,2,1,0:T(8,128)(2,1)S(1)} collective-permute-done((bf16[4,2,2,128,128]{4,3,2,1,0:T(8,128)(2,1)S(1)}, bf16[4,2,2,128,128]{4,3,2,1,0:T(8,128)(2,1)S(1)}, u32[]{:S(2)}, u32[]{:S(2)}) %collective-permute-start.15) | collective-permute-done | bytes 524320 | tf_op jit(solution)/shard_map/ppermute | solution.py:64
  246.1 4.6 %collective-permute-start.17 = (bf16[2,2,128,128]{3,2,1,0:T(8,128)(2,1)S(1)}, bf16[2,2,128,128]{3,2,1,0:T(8,128)(2,1)S(1)}, u32[]{:S(2)}, u32[]{:S(2)}) collective-permute-start(bf16[2,2,128,128]{3,2,1,0:T(8,128)(2,1)S(1)} %get-tuple-element.26), channel_id=1, source_target_pairs={{0,3},{1,0},{2,1},{3,2},{4,7},{5,4},{6,5},{7,6},{8,11},{9,8},{10,9... | collective-permute-start | bytes 393224 | tf_op jit(solution)/shard_map/ppermute | solution.py:79
  250.7 3.9 %collective-permute-start.18 = (bf16[2,2,128,128]{3,2,1,0:T(8,128)(2,1)S(1)}, bf16[2,2,128,128]{3,2,1,0:T(8,128)(2,1)S(1)}, u32[]{:S(2)}, u32[]{:S(2)}) collective-permute-start(bf16[2,2,128,128]{3,2,1,0:T(8,128)(2,1)S(1)} %get-tuple-element.28), channel_id=1, source_target_pairs={{0,2},{1,3},{2,0},{3,1},{4,6},{5,7},{6,4},{7,5},{8,10},{9,11},{10,... | collective-permute-start | bytes 393224 | tf_op jit(solution)/shard_map/ppermute | solution.py:79
  254.7 3.0 %collective-permute-start.19 = (bf16[2,2,128,128]{3,2,1,0:T(8,128)(2,1)S(1)}, bf16[2,2,128,128]{3,2,1,0:T(8,128)(2,1)S(1)}, u32[]{:S(2)}, u32[]{:S(2)}) collective-permute-start(bf16[2,2,128,128]{3,2,1,0:T(8,128)(2,1)S(1)} %get-tuple-element.27), channel_id=1, source_target_pairs={{0,1},{1,2},{2,3},{3,0},{4,5},{5,6},{6,7},{7,4},{8,9},{9,10},{10,1... | collective-permute-start | bytes 393224 | tf_op jit(solution)/shard_map/ppermute | solution.py:79
  257.7 6.6 %collective-permute-done.18 = bf16[2,2,128,128]{3,2,1,0:T(8,128)(2,1)S(1)} collective-permute-done((bf16[2,2,128,128]{3,2,1,0:T(8,128)(2,1)S(1)}, bf16[2,2,128,128]{3,2,1,0:T(8,128)(2,1)S(1)}, u32[]{:S(2)}, u32[]{:S(2)}) %collective-permute-start.18) | collective-permute-done | bytes 131104 | tf_op jit(solution)/shard_map/ppermute | solution.py:79
  265.7 2.4 copy.71
  (93 shorter events, 34.3 us)
Async XLA Ops:
  0.6 53.5 %copy-start = (s32[64]{0:T(128)S(1)}, s32[64]{0:T(128)}, u32[]{:S(2)}) copy-start(s32[64]{0:T(128)} %param.9) | copy-start | bytes 772
  1.5 27.6 %collective-permute-start = (bf16[2,2,128,128]{3,2,1,0:T(8,128)(2,1)S(1)}, bf16[2,2,128,128]{3,2,1,0:T(8,128)(2,1)S(1)}, u32[]{:S(2)}, u32[]{:S(2)}) collective-permute-start(bf16[2,2,128,128]{3,2,1,0:T(8,128)(2,1)S(1)} %get-tuple-element.32), channel_id=1, source_target_pairs={{0,1},{1,2},{2,3},{3,0},{4,5},{5,6},{6,7},{7,4},{8,9},{9,10},{10,1... | collective-permute-start | bytes 393224 | tf_op jit(solution)/shard_map/ppermute | solution.py:42
  7.6 21.5 %collective-permute-start.1 = (bf16[2,2,128,128]{3,2,1,0:T(8,128)(2,1)S(1)}, bf16[2,2,128,128]{3,2,1,0:T(8,128)(2,1)S(1)}, u32[]{:S(2)}, u32[]{:S(2)}) collective-permute-start(bf16[2,2,128,128]{3,2,1,0:T(8,128)(2,1)S(1)} %get-tuple-element.32), channel_id=1, source_target_pairs={{0,2},{1,3},{2,0},{3,1},{4,6},{5,7},{6,4},{7,5},{8,10},{9,11},{10,... | collective-permute-start | bytes 393224 | tf_op jit(solution)/shard_map/ppermute | solution.py:42
  16.8 12.6 %collective-permute-start.2 = (bf16[2,2,128,128]{3,2,1,0:T(8,128)(2,1)S(1)}, bf16[2,2,128,128]{3,2,1,0:T(8,128)(2,1)S(1)}, u32[]{:S(2)}, u32[]{:S(2)}) collective-permute-start(bf16[2,2,128,128]{3,2,1,0:T(8,128)(2,1)S(1)} %get-tuple-element.32), channel_id=1, source_target_pairs={{0,3},{1,0},{2,1},{3,2},{4,7},{5,4},{6,5},{7,6},{8,11},{9,8},{10,9... | collective-permute-start | bytes 393224 | tf_op jit(solution)/shard_map/ppermute | solution.py:42
  23.3 42.0 %copy-start.2 = (s32[64]{0:T(128)S(1)}, s32[64]{0:T(128)}, u32[]{:S(2)}) copy-start(s32[64]{0:T(128)} %param.11) | copy-start | bytes 772
  23.3 85.6 %all-to-all-start = ((bf16[16,2,128,256]{2,3,1,0:T(8,128)(2,1)}), bf16[16,2,128,256]{2,3,1,0:T(8,128)(2,1)}, u32[]{:S(2)}, u32[]{:S(2)}) async-start(bf16[16,2,128,256]{2,3,1,0:T(8,128)(2,1)} %broadcast_in_dim.4), calls=%async_computation | async-start | bytes 4194304 | tf_op jit(solution)/shard_map/all_to_all | solution.py:22
  29.4 17.5 %collective-permute-start.3 = (bf16[4,2,2,128,128]{4,3,2,1,0:T(8,128)(2,1)S(1)}, bf16[4,2,2,128,128]{4,3,2,1,0:T(8,128)(2,1)S(1)}, u32[]{:S(2)}, u32[]{:S(2)}) collective-permute-start(bf16[4,2,2,128,128]{4,3,2,1,0:T(8,128)(2,1)S(1)} %pad_maximum_fusion.1), channel_id=1, source_target_pairs={{0,4},{1,5},{2,6},{3,7},{4,8},{5,9},{6,10},{7,11},{8,12},{9,13},{1... | collective-permute-start | bytes 1572872 | tf_op jit(solution)/shard_map/ppermute | solution.py:48
  46.9 16.5 %collective-permute-start.4 = (bf16[4,2,2,128,128]{4,3,2,1,0:T(8,128)(2,1)S(1)}, bf16[4,2,2,128,128]{4,3,2,1,0:T(8,128)(2,1)S(1)}, u32[]{:S(2)}, u32[]{:S(2)}) collective-permute-start(bf16[4,2,2,128,128]{4,3,2,1,0:T(8,128)(2,1)S(1)} %collective-permute-done.3), channel_id=1, source_target_pairs={{0,4},{1,5},{2,6},{3,7},{4,8},{5,9},{6,10},{7,11},{8,12},{9,13},{1... | collective-permute-start | bytes 1572872 | tf_op jit(solution)/shard_map/ppermute | solution.py:48
  49.0 17.2 %collective-permute-start.7 = (bf16[4,2,2,128,128]{4,3,2,1,0:T(8,128)(2,1)S(1)}, bf16[4,2,2,128,128]{4,3,2,1,0:T(8,128)(2,1)S(1)}, u32[]{:S(2)}, u32[]{:S(2)}) collective-permute-start(bf16[4,2,2,128,128]{4,3,2,1,0:T(8,128)(2,1)S(1)} %pad_maximum_fusion.1), channel_id=1, source_target_pairs={{0,28},{1,29},{2,30},{3,31},{4,0},{5,1},{6,2},{7,3},{8,4},{9,5},{1... | collective-permute-start | bytes 1572872 | tf_op jit(solution)/shard_map/ppermute | solution.py:51
  63.4 15.6 %collective-permute-start.5 = (bf16[4,2,2,128,128]{4,3,2,1,0:T(8,128)(2,1)S(1)}, bf16[4,2,2,128,128]{4,3,2,1,0:T(8,128)(2,1)S(1)}, u32[]{:S(2)}, u32[]{:S(2)}) collective-permute-start(bf16[4,2,2,128,128]{4,3,2,1,0:T(8,128)(2,1)S(1)} %collective-permute-done.4), channel_id=1, source_target_pairs={{0,4},{1,5},{2,6},{3,7},{4,8},{5,9},{6,10},{7,11},{8,12},{9,13},{1... | collective-permute-start | bytes 1572872 | tf_op jit(solution)/shard_map/ppermute | solution.py:48
  66.2 14.9 %collective-permute-start.8 = (bf16[4,2,2,128,128]{4,3,2,1,0:T(8,128)(2,1)S(1)}, bf16[4,2,2,128,128]{4,3,2,1,0:T(8,128)(2,1)S(1)}, u32[]{:S(2)}, u32[]{:S(2)}) collective-permute-start(bf16[4,2,2,128,128]{4,3,2,1,0:T(8,128)(2,1)S(1)} %collective-permute-done.7), channel_id=1, source_target_pairs={{0,28},{1,29},{2,30},{3,31},{4,0},{5,1},{6,2},{7,3},{8,4},{9,5},{1... | collective-permute-start | bytes 1572872 | tf_op jit(solution)/shard_map/ppermute | solution.py:51
  79.0 14.7 %collective-permute-start.6 = (bf16[4,2,2,128,128]{4,3,2,1,0:T(8,128)(2,1)S(1)}, bf16[4,2,2,128,128]{4,3,2,1,0:T(8,128)(2,1)S(1)}, u32[]{:S(2)}, u32[]{:S(2)}) collective-permute-start(bf16[4,2,2,128,128]{4,3,2,1,0:T(8,128)(2,1)S(1)} %collective-permute-done.5), channel_id=1, source_target_pairs={{0,4},{1,5},{2,6},{3,7},{4,8},{5,9},{6,10},{7,11},{8,12},{9,13},{1... | collective-permute-start | bytes 1572872 | tf_op jit(solution)/shard_map/ppermute | solution.py:48
  81.1 14.4 %collective-permute-start.9 = (bf16[4,2,2,128,128]{4,3,2,1,0:T(8,128)(2,1)S(1)}, bf16[4,2,2,128,128]{4,3,2,1,0:T(8,128)(2,1)S(1)}, u32[]{:S(2)}, u32[]{:S(2)}) collective-permute-start(bf16[4,2,2,128,128]{4,3,2,1,0:T(8,128)(2,1)S(1)} %collective-permute-done.8), channel_id=1, source_target_pairs={{0,28},{1,29},{2,30},{3,31},{4,0},{5,1},{6,2},{7,3},{8,4},{9,5},{1... | collective-permute-start | bytes 1572872 | tf_op jit(solution)/shard_map/ppermute | solution.py:51
  97.5 4.7 %copy-start.3 = (bf16[1,8,4,2,128,128]{5,4,3,0,2,1:T(8,128)(2,1)}, bf16[1,8,4,2,128,128]{5,4,3,0,2,1:T(8,128)(2,1)S(1)}, u32[]{:S(2)}) copy-start(bf16[1,8,4,2,128,128]{5,4,3,0,2,1:T(8,128)(2,1)S(1)} %get-tuple-element.21) | copy-start | bytes 6291460
  113.4 2.5 copy-start.6
  116.0 0.8 copy-start.9
  123.6 3.2 %copy-start.5 = (bf16[8,8,128,128]{3,1,0,2:T(8,128)(2,1)S(1)}, bf16[8,8,128,128]{3,1,0,2:T(8,128)(2,1)}, u32[]{:S(2)}) copy-start(bf16[8,8,128,128]{3,1,0,2:T(8,128)(2,1)} %copy.66) | copy-start | bytes 6291460
  129.2 1.2 copy-start.11
  132.0 57.0 %all-to-all-start.1 = ((bf16[16,2,128,256]{2,3,1,0:T(8,128)(2,1)}), bf16[16,2,128,256]{2,3,1,0:T(8,128)(2,1)}, u32[]{:S(2)}, u32[]{:S(2)}) async-start(bf16[16,2,128,256]{2,3,1,0:T(8,128)(2,1)} %bitcast.178), calls=%async_computation.1 | async-start | bytes 4194304 | tf_op jit(solution)/shard_map/all_to_all | solution.py:26
  140.5 3.1 %copy-start.10 = (f32[128,8,128]{0,2,1:T(8,128)S(1)}, f32[128,8,128]{0,2,1:T(8,128)}, u32[]{:S(2)}) copy-start(f32[128,8,128]{0,2,1:T(8,128)} %copy-done.9) | copy-start | bytes 1572868
  145.6 4.1 %copy-start.7 = (bf16[8,8,128,128]{2,3,1,0:T(8,128)(2,1)S(1)}, bf16[8,8,128,128]{2,3,1,0:T(8,128)(2,1)}, u32[]{:S(2)}) copy-start(bf16[8,8,128,128]{2,3,1,0:T(8,128)(2,1)} %copy.54) | copy-start | bytes 6291460
  149.7 1.6 copy-start.8
  151.7 35.0 %copy-start.4 = (bf16[8,4,2,2,128,128]{5,4,3,2,1,0:T(8,128)(2,1)}, bf16[8,4,2,2,128,128]{5,4,3,2,1,0:T(8,128)(2,1)S(1)}, u32[]{:S(2)}) copy-start(bf16[8,4,2,2,128,128]{5,4,3,2,1,0:T(8,128)(2,1)S(1)} %maximum_bitcast_fusion) | copy-start | bytes 12582916
  151.8 17.8 %collective-permute-start.12 = (bf16[4,2,2,128,128]{4,3,2,1,0:T(8,128)(2,1)S(1)}, bf16[4,2,2,128,128]{4,3,2,1,0:T(8,128)(2,1)S(1)}, u32[]{:S(2)}, u32[]{:S(2)}) collective-permute-start(bf16[4,2,2,128,128]{4,3,2,1,0:T(8,128)(2,1)S(1)} %get-tuple-element.18), channel_id=1, source_target_pairs={{0,4},{1,5},{2,6},{3,7},{4,8},{5,9},{6,10},{7,11},{8,12},{9,13},{1... | collective-permute-start | bytes 1572872 | tf_op jit(solution)/shard_map/ppermute | solution.py:64
  154.5 17.2 %collective-permute-start.10 = (bf16[4,2,2,128,128]{4,3,2,1,0:T(8,128)(2,1)S(1)}, bf16[4,2,2,128,128]{4,3,2,1,0:T(8,128)(2,1)S(1)}, u32[]{:S(2)}, u32[]{:S(2)}) collective-permute-start(bf16[4,2,2,128,128]{4,3,2,1,0:T(8,128)(2,1)S(1)} %get-tuple-element.19), channel_id=1, source_target_pairs={{0,28},{1,29},{2,30},{3,31},{4,0},{5,1},{6,2},{7,3},{8,4},{9,5},{1... | collective-permute-start | bytes 1572872 | tf_op jit(solution)/shard_map/ppermute | solution.py:69
  169.8 16.6 %collective-permute-start.13 = (bf16[4,2,2,128,128]{4,3,2,1,0:T(8,128)(2,1)S(1)}, bf16[4,2,2,128,128]{4,3,2,1,0:T(8,128)(2,1)S(1)}, u32[]{:S(2)}, u32[]{:S(2)}) collective-permute-start(bf16[4,2,2,128,128]{4,3,2,1,0:T(8,128)(2,1)S(1)} %fusion.5), channel_id=1, source_target_pairs={{0,4},{1,5},{2,6},{3,7},{4,8},{5,9},{6,10},{7,11},{8,12},{9,13},{1... | collective-permute-start | bytes 1572872 | tf_op jit(solution)/shard_map/ppermute | solution.py:64
  186.7 14.5 %collective-permute-start.11 = (bf16[4,2,2,128,128]{4,3,2,1,0:T(8,128)(2,1)S(1)}, bf16[4,2,2,128,128]{4,3,2,1,0:T(8,128)(2,1)S(1)}, u32[]{:S(2)}, u32[]{:S(2)}) collective-permute-start(bf16[4,2,2,128,128]{4,3,2,1,0:T(8,128)(2,1)S(1)} %get-tuple-element.17), channel_id=1, source_target_pairs={{0,28},{1,29},{2,30},{3,31},{4,0},{5,1},{6,2},{7,3},{8,4},{9,5},{1... | collective-permute-start | bytes 1572872 | tf_op jit(solution)/shard_map/ppermute | solution.py:69
  202.9 62.8 %all-to-all-start.2 = ((bf16[16,2,128,256]{3,2,1,0:T(8,128)(2,1)}), bf16[16,2,128,256]{3,2,1,0:T(8,128)(2,1)S(1)}, u32[]{:S(2)}, u32[]{:S(2)}) async-start(bf16[16,2,128,256]{3,2,1,0:T(8,128)(2,1)} %broadcast_in_dim.5), calls=%async_computation.2 | async-start | bytes 4194304 | tf_op jit(solution)/shard_map/all_to_all | solution.py:22
  208.6 17.1 %collective-permute-start.14 = (bf16[4,2,2,128,128]{4,3,2,1,0:T(8,128)(2,1)S(1)}, bf16[4,2,2,128,128]{4,3,2,1,0:T(8,128)(2,1)S(1)}, u32[]{:S(2)}, u32[]{:S(2)}) collective-permute-start(bf16[4,2,2,128,128]{4,3,2,1,0:T(8,128)(2,1)S(1)} %get-tuple-element.16), channel_id=1, source_target_pairs={{0,4},{1,5},{2,6},{3,7},{4,8},{5,9},{6,10},{7,11},{8,12},{9,13},{1... | collective-permute-start | bytes 1572872 | tf_op jit(solution)/shard_map/ppermute | solution.py:64
  227.3 16.3 %collective-permute-start.15 = (bf16[4,2,2,128,128]{4,3,2,1,0:T(8,128)(2,1)S(1)}, bf16[4,2,2,128,128]{4,3,2,1,0:T(8,128)(2,1)S(1)}, u32[]{:S(2)}, u32[]{:S(2)}) collective-permute-start(bf16[4,2,2,128,128]{4,3,2,1,0:T(8,128)(2,1)S(1)} %get-tuple-element.14), channel_id=1, source_target_pairs={{0,4},{1,5},{2,6},{3,7},{4,8},{5,9},{6,10},{7,11},{8,12},{9,13},{1... | collective-permute-start | bytes 1572872 | tf_op jit(solution)/shard_map/ppermute | solution.py:64
  229.2 15.5 %collective-permute-start.16 = (bf16[4,2,2,128,128]{4,3,2,1,0:T(8,128)(2,1)S(1)}, bf16[4,2,2,128,128]{4,3,2,1,0:T(8,128)(2,1)S(1)}, u32[]{:S(2)}, u32[]{:S(2)}) collective-permute-start(bf16[4,2,2,128,128]{4,3,2,1,0:T(8,128)(2,1)S(1)} %get-tuple-element.15), channel_id=1, source_target_pairs={{0,28},{1,29},{2,30},{3,31},{4,0},{5,1},{6,2},{7,3},{8,4},{9,5},{1... | collective-permute-start | bytes 1572872 | tf_op jit(solution)/shard_map/ppermute | solution.py:69
  246.1 11.6 %collective-permute-start.17 = (bf16[2,2,128,128]{3,2,1,0:T(8,128)(2,1)S(1)}, bf16[2,2,128,128]{3,2,1,0:T(8,128)(2,1)S(1)}, u32[]{:S(2)}, u32[]{:S(2)}) collective-permute-start(bf16[2,2,128,128]{3,2,1,0:T(8,128)(2,1)S(1)} %get-tuple-element.26), channel_id=1, source_target_pairs={{0,3},{1,0},{2,1},{3,2},{4,7},{5,4},{6,5},{7,6},{8,11},{9,8},{10,9... | collective-permute-start | bytes 393224 | tf_op jit(solution)/shard_map/ppermute | solution.py:79
  250.7 13.5 %collective-permute-start.18 = (bf16[2,2,128,128]{3,2,1,0:T(8,128)(2,1)S(1)}, bf16[2,2,128,128]{3,2,1,0:T(8,128)(2,1)S(1)}, u32[]{:S(2)}, u32[]{:S(2)}) collective-permute-start(bf16[2,2,128,128]{3,2,1,0:T(8,128)(2,1)S(1)} %get-tuple-element.28), channel_id=1, source_target_pairs={{0,2},{1,3},{2,0},{3,1},{4,6},{5,7},{6,4},{7,5},{8,10},{9,11},{10,... | collective-permute-start | bytes 393224 | tf_op jit(solution)/shard_map/ppermute | solution.py:79
  254.7 10.3 %collective-permute-start.19 = (bf16[2,2,128,128]{3,2,1,0:T(8,128)(2,1)S(1)}, bf16[2,2,128,128]{3,2,1,0:T(8,128)(2,1)S(1)}, u32[]{:S(2)}, u32[]{:S(2)}) collective-permute-start(bf16[2,2,128,128]{3,2,1,0:T(8,128)(2,1)S(1)} %get-tuple-element.27), channel_id=1, source_target_pairs={{0,1},{1,2},{2,3},{3,0},{4,5},{5,6},{6,7},{7,4},{8,9},{9,10},{10,1... | collective-permute-start | bytes 393224 | tf_op jit(solution)/shard_map/ppermute | solution.py:79
  269.8 2.6 copy-start.1

commit v16 on v11

--- a/solution.py
+++ b/solution.py
@@ -49,6 +49,9 @@
         fwd.append(cur_f)
         if k <= n_b:
             cur_b = lax.ppermute(cur_b, "dp", dp_shift(n_y, n_z, -1, 0))
+            if k == 1:
+                cur_f, cur_b = lax.optimization_barrier((cur_f, cur_b))
+                fwd[-1] = cur_f
             bwd.append(cur_b)
     rel = fwd + [bwd[n_y - a - 1] for a in range(len(fwd), n_y)]
     return jnp.stack(rel)

time: 265 us -> 266 us (level)
  transfers between devices with their start and end apart: 23 -> 23, of which waited for: 15 -> 16; matrix products, arithmetic and copies ran while one was open for 16% -> 16% of each run, Pallas kernels for 0% -> 0%
where the time goes in v16:
time: 266 us; the launch traced here: 261 us
  starting transfers between devices  94.2 us (35%)
  waiting for transfers between devices  92.5 us (35%)
  local copies, waits for them, and re-layouts  47.7 us (18%)
  matrix products  13.9 us (5%)
  other arithmetic  11.7 us (4%)
    ppermute x4, waiting for transfers between devices, dp_gather_rel(): cur_f = lax.ppermute(cur_f, 'dp', dp_shift(n_y, n_z, 1, 0))  36 us
    ppermute x4, waiting for transfers between devices, dp_scatter_rel(): lax.ppermute(part.astype(jnp.bfloat16), 'dp', dp_shift(n_y, n_z, 1, 0))  29.3 us
    ppermute x3, starting transfers between devices, dp_gather_rel(): lax.ppermute(x, 'dp', dp_shift(n_y, n_z, 0, b))  18.9 us
    ppermute x3, waiting for transfers between devices, dp_scatter_rel(): lax.ppermute(part.astype(jnp.bfloat16), 'dp', dp_shift(n_y, n_z, -1, 0))  16.9 us
    ppermute x3, starting transfers between devices, dp_gather_rel(): cur_b = lax.ppermute(cur_b, 'dp', dp_shift(n_y, n_z, -1, 0))  14.7 us
    ppermute x3, starting transfers between devices, dp_scatter_rel(): lax.ppermute(acc[b].astype(jnp.bfloat16), 'dp', dp_shift(n_y, n_z, 0, -b))  11.8 us
    all_to_all x2, starting transfers between devices, gather_all(): return lax.all_to_all(spread, axis_name, 0, 0, tiled=True)  11.6 us
    ppermute x4, starting transfers between devices, dp_gather_rel(): cur_f = lax.ppermute(cur_f, 'dp', dp_shift(n_y, n_z, 1, 0))  10.8 us
  transfers between devices with their start and end apart: 23, of which 16 were waited for; matrix products, arithmetic and copies ran while one was open for 16% of the time, Pallas kernels for 0%

profile of v16, /device:TPU:6, one launch (start us, length us, event | category | flops | bytes accessed | tf_op | source)
XLA Modules:
  0.0 261.2 jit_solution(17654710494538776137)
XLA Ops:
  1.5 6.1 %collective-permute-start = (bf16[2,2,128,128]{3,2,1,0:T(8,128)(2,1)S(1)}, bf16[2,2,128,128]{3,2,1,0:T(8,128)(2,1)S(1)}, u32[]{:S(2)}, u32[]{:S(2)}) collective-permute-start(bf16[2,2,128,128]{3,2,1,0:T(8,128)(2,1)S(1)} %get-tuple-element.34), channel_id=1, source_target_pairs={{0,1},{1,2},{2,3},{3,0},{4,5},{5,6},{6,7},{7,4},{8,9},{9,10},{10,1... | collective-permute-start | bytes 393224 | tf_op jit(solution)/shard_map/ppermute | solution.py:42
  7.6 9.1 %collective-permute-start.1 = (bf16[2,2,128,128]{3,2,1,0:T(8,128)(2,1)S(1)}, bf16[2,2,128,128]{3,2,1,0:T(8,128)(2,1)S(1)}, u32[]{:S(2)}, u32[]{:S(2)}) collective-permute-start(bf16[2,2,128,128]{3,2,1,0:T(8,128)(2,1)S(1)} %get-tuple-element.34), channel_id=1, source_target_pairs={{0,2},{1,3},{2,0},{3,1},{4,6},{5,7},{6,4},{7,5},{8,10},{9,11},{10,... | collective-permute-start | bytes 393224 | tf_op jit(solution)/shard_map/ppermute | solution.py:42
  16.8 3.7 %collective-permute-start.2 = (bf16[2,2,128,128]{3,2,1,0:T(8,128)(2,1)S(1)}, bf16[2,2,128,128]{3,2,1,0:T(8,128)(2,1)S(1)}, u32[]{:S(2)}, u32[]{:S(2)}) collective-permute-start(bf16[2,2,128,128]{3,2,1,0:T(8,128)(2,1)S(1)} %get-tuple-element.34), channel_id=1, source_target_pairs={{0,3},{1,0},{2,1},{3,2},{4,7},{5,4},{6,5},{7,6},{8,11},{9,8},{10,9... | collective-permute-start | bytes 393224 | tf_op jit(solution)/shard_map/ppermute | solution.py:42
  23.3 5.8 %all-to-all-start = ((bf16[16,2,128,256]{2,3,1,0:T(8,128)(2,1)}), bf16[16,2,128,256]{2,3,1,0:T(8,128)(2,1)}, u32[]{:S(2)}, u32[]{:S(2)}) async-start(bf16[16,2,128,256]{2,3,1,0:T(8,128)(2,1)} %broadcast_in_dim.4), calls=%async_computation | async-start | bytes 4194304 | tf_op jit(solution)/shard_map/all_to_all | solution.py:22
  29.4 3.5 %collective-permute-start.3 = (bf16[4,2,2,128,128]{4,3,2,1,0:T(8,128)(2,1)S(1)}, bf16[4,2,2,128,128]{4,3,2,1,0:T(8,128)(2,1)S(1)}, u32[]{:S(2)}, u32[]{:S(2)}) collective-permute-start(bf16[4,2,2,128,128]{4,3,2,1,0:T(8,128)(2,1)S(1)} %pad_maximum_fusion.1), channel_id=1, source_target_pairs={{0,4},{1,5},{2,6},{3,7},{4,8},{5,9},{6,10},{7,11},{8,12},{9,13},{1... | collective-permute-start | bytes 1572872 | tf_op jit(solution)/shard_map/ppermute | solution.py:48
  32.9 3.8 %collective-permute-start.4 = (bf16[4,2,2,128,128]{4,3,2,1,0:T(8,128)(2,1)S(1)}, bf16[4,2,2,128,128]{4,3,2,1,0:T(8,128)(2,1)S(1)}, u32[]{:S(2)}, u32[]{:S(2)}) collective-permute-start(bf16[4,2,2,128,128]{4,3,2,1,0:T(8,128)(2,1)S(1)} %pad_maximum_fusion.1), channel_id=1, source_target_pairs={{0,28},{1,29},{2,30},{3,31},{4,0},{5,1},{6,2},{7,3},{8,4},{9,5},{1... | collective-permute-start | bytes 1572872 | tf_op jit(solution)/shard_map/ppermute | solution.py:51
  36.9 10.0 %collective-permute-done.3 = bf16[4,2,2,128,128]{4,3,2,1,0:T(8,128)(2,1)S(1)} collective-permute-done((bf16[4,2,2,128,128]{4,3,2,1,0:T(8,128)(2,1)S(1)}, bf16[4,2,2,128,128]{4,3,2,1,0:T(8,128)(2,1)S(1)}, u32[]{:S(2)}, u32[]{:S(2)}) %collective-permute-start.3) | collective-permute-done | bytes 524320 | tf_op jit(solution)/shard_map/ppermute | solution.py:48
  48.4 3.5 %collective-permute-start.5 = (bf16[4,2,2,128,128]{4,3,2,1,0:T(8,128)(2,1)S(1)}, bf16[4,2,2,128,128]{4,3,2,1,0:T(8,128)(2,1)S(1)}, u32[]{:S(2)}, u32[]{:S(2)}) collective-permute-start(bf16[4,2,2,128,128]{4,3,2,1,0:T(8,128)(2,1)S(1)} %collective-permute-done.3), channel_id=1, source_target_pairs={{0,4},{1,5},{2,6},{3,7},{4,8},{5,9},{6,10},{7,11},{8,12},{9,13},{1... | collective-permute-start | bytes 1572872 | tf_op jit(solution)/shard_map/ppermute | solution.py:48
  52.9 12.1 %collective-permute-done.5 = bf16[4,2,2,128,128]{4,3,2,1,0:T(8,128)(2,1)S(1)} collective-permute-done((bf16[4,2,2,128,128]{4,3,2,1,0:T(8,128)(2,1)S(1)}, bf16[4,2,2,128,128]{4,3,2,1,0:T(8,128)(2,1)S(1)}, u32[]{:S(2)}, u32[]{:S(2)}) %collective-permute-start.5) | collective-permute-done | bytes 524320 | tf_op jit(solution)/shard_map/ppermute | solution.py:48
  65.0 2.0 collective-permute-start.6
  67.9 5.1 %collective-permute-start.8 = (bf16[4,2,2,128,128]{4,3,2,1,0:T(8,128)(2,1)S(1)}, bf16[4,2,2,128,128]{4,3,2,1,0:T(8,128)(2,1)S(1)}, u32[]{:S(2)}, u32[]{:S(2)}) collective-permute-start(bf16[4,2,2,128,128]{4,3,2,1,0:T(8,128)(2,1)S(1)} %collective-permute-done.4), channel_id=1, source_target_pairs={{0,28},{1,29},{2,30},{3,31},{4,0},{5,1},{6,2},{7,3},{8,4},{9,5},{1... | collective-permute-start | bytes 1572872 | tf_op jit(solution)/shard_map/ppermute | solution.py:51
  73.3 7.2 %collective-permute-done.6 = bf16[4,2,2,128,128]{4,3,2,1,0:T(8,128)(2,1)S(1)} collective-permute-done((bf16[4,2,2,128,128]{4,3,2,1,0:T(8,128)(2,1)S(1)}, bf16[4,2,2,128,128]{4,3,2,1,0:T(8,128)(2,1)S(1)}, u32[]{:S(2)}, u32[]{:S(2)}) %collective-permute-start.6) | collective-permute-done | bytes 524320 | tf_op jit(solution)/shard_map/ppermute | solution.py:48
  80.6 1.9 collective-permute-start.7
  82.7 5.8 %collective-permute-start.9 = (bf16[4,2,2,128,128]{4,3,2,1,0:T(8,128)(2,1)S(1)}, bf16[4,2,2,128,128]{4,3,2,1,0:T(8,128)(2,1)S(1)}, u32[]{:S(2)}, u32[]{:S(2)}) collective-permute-start(bf16[4,2,2,128,128]{4,3,2,1,0:T(8,128)(2,1)S(1)} %collective-permute-done.8), channel_id=1, source_target_pairs={{0,28},{1,29},{2,30},{3,31},{4,0},{5,1},{6,2},{7,3},{8,4},{9,5},{1... | collective-permute-start | bytes 1572872 | tf_op jit(solution)/shard_map/ppermute | solution.py:51
  88.6 6.7 %collective-permute-done.7 = bf16[4,2,2,128,128]{4,3,2,1,0:T(8,128)(2,1)S(1)} collective-permute-done((bf16[4,2,2,128,128]{4,3,2,1,0:T(8,128)(2,1)S(1)}, bf16[4,2,2,128,128]{4,3,2,1,0:T(8,128)(2,1)S(1)}, u32[]{:S(2)}, u32[]{:S(2)}) %collective-permute-start.7) | collective-permute-done | bytes 524320 | tf_op jit(solution)/shard_map/ppermute | solution.py:48
  99.0 4.6 %copy.64 = bf16[8,8,128,128]{2,1,0,3:T(8,128)(2,1)} copy(bf16[8,8,128,128]{3,2,1,0:T(8,128)(2,1)} %bitcast.183) | data formatting | bytes 4194304 | tf_op jit(solution)/shard_map/reshape;squeeze | solution.py:119
  103.7 2.6 copy.58
  106.3 4.2 %copy.66 = bf16[8,8,128,128]{3,1,0,2:T(8,128)(2,1)} copy(bf16[8,8,128,128]{2,3,1,0:T(8,128)(2,1)} %bitcast.182) | data formatting | bytes 4194304 | tf_op jit(solution)/shard_map/reshape;squeeze | solution.py:118
  114.3 2.2 gather_fusion.1
  116.5 3.2 %convolution_bitcast_fusion = f32[128,8,128]{0,2,1:T(8,128)} fusion(bf16[8,8,128,128]{3,2,1,0:T(8,128)(2,1)} %bitcast.175, bf16[128,8,8,128]{3,0,2,1:T(8,128)(2,1)S(1)} %bitcast.173), kind=kOutput, calls=%fused_computation.13 | convolution fusion | flops 268435456 | bytes 4718592 | tf_op jit(solution)/shard_map/tgki,gkio->tgo/dot_general | solution.py:123
  119.7 2.2 gather_fusion.3
  121.9 3.2 %fusion.3 = bf16[128,8,128]{0,2,1:T(8,128)(2,1)S(1)} fusion(bf16[8,8,128,128]{3,2,1,0:T(8,128)(2,1)} %bitcast.184, bf16[128,8,8,128]{3,0,2,1:T(8,128)(2,1)} %bitcast.176, f32[128,8,128]{0,2,1:T(8,128)} %convolution_bitcast_fusion), kind=kOutput, calls=%fused_computation.16 | convolution fusion | flops 269746176 | bytes 4980736 | tf_op jit(solution)/shard_map/tgko,gkho->tgh/dot_general | solution.py:137
  133.5 5.9 %all-to-all-start.1 = ((bf16[16,2,128,256]{2,3,1,0:T(8,128)(2,1)}), bf16[16,2,128,256]{2,3,1,0:T(8,128)(2,1)}, u32[]{:S(2)}, u32[]{:S(2)}) async-start(bf16[16,2,128,256]{2,3,1,0:T(8,128)(2,1)} %bitcast.178), calls=%async_computation.1 | async-start | bytes 4194304 | tf_op jit(solution)/shard_map/all_to_all | solution.py:26
  139.3 2.6 %copy.54 = bf16[8,8,128,128]{2,3,1,0:T(8,128)(2,1)} copy(bf16[8,8,128,128]{3,2,1,0:T(8,128)(2,1)S(1)} %bitcast.174) | data formatting | bytes 4194304 | tf_op jit(solution)/shard_map/gather | solution.py:122
  141.9 3.0 %copy.56 = bf16[8,8,128,128]{2,3,1,0:T(8,128)(2,1)S(1)} copy(bf16[8,8,128,128]{3,2,1,0:T(8,128)(2,1)} %bitcast.177) | data formatting | bytes 4194304 | tf_op jit(solution)/shard_map/gather | solution.py:132
  145.0 2.1 multiply_convert_fusion
  147.1 4.1 %copy.63 = bf16[1,8,4,2,128,128]{5,4,3,0,2,1:T(8,128)(2,1)} copy(bf16[1,8,4,2,128,128]{4,5,3,2,1,0:T(8,128)(2,1)} %bitcast.181) | data formatting | bytes 4194304 | tf_op jit(solution)/shard_map/stack | solution.py:155
  153.2 2.7 %collective-permute-start.11 = (bf16[4,2,2,128,128]{4,3,2,1,0:T(8,128)(2,1)S(1)}, bf16[4,2,2,128,128]{4,3,2,1,0:T(8,128)(2,1)S(1)}, u32[]{:S(2)}, u32[]{:S(2)}) collective-permute-start(bf16[4,2,2,128,128]{4,3,2,1,0:T(8,128)(2,1)S(1)} %get-tuple-element.20), channel_id=1, source_target_pairs={{0,4},{1,5},{2,6},{3,7},{4,8},{5,9},{6,10},{7,11},{8,12},{9,13},{1... | collective-permute-start | bytes 1572872 | tf_op jit(solution)/shard_map/ppermute | solution.py:67
  155.9 4.8 %collective-permute-start.10 = (bf16[4,2,2,128,128]{4,3,2,1,0:T(8,128)(2,1)S(1)}, bf16[4,2,2,128,128]{4,3,2,1,0:T(8,128)(2,1)}, u32[]{:S(2)}, u32[]{:S(2)}) collective-permute-start(bf16[4,2,2,128,128]{4,3,2,1,0:T(8,128)(2,1)S(1)} %get-tuple-element.21), channel_id=1, source_target_pairs={{0,28},{1,29},{2,30},{3,31},{4,0},{5,1},{6,2},{7,3},{8,4},{9,5},{1... | collective-permute-start | bytes 1572872 | tf_op jit(solution)/shard_map/ppermute | solution.py:72
  160.7 10.3 %collective-permute-done.11 = bf16[4,2,2,128,128]{4,3,2,1,0:T(8,128)(2,1)S(1)} collective-permute-done((bf16[4,2,2,128,128]{4,3,2,1,0:T(8,128)(2,1)S(1)}, bf16[4,2,2,128,128]{4,3,2,1,0:T(8,128)(2,1)S(1)}, u32[]{:S(2)}, u32[]{:S(2)}) %collective-permute-start.11) | collective-permute-done | bytes 524320 | tf_op jit(solution)/shard_map/ppermute | solution.py:67
  171.2 1.9 collective-permute-start.12
  173.1 1.9 reduce_sum.12
  176.8 5.7 %all-to-all-start.2 = ((bf16[16,2,128,256]{3,2,1,0:T(8,128)(2,1)}), bf16[16,2,128,256]{3,2,1,0:T(8,128)(2,1)S(1)}, u32[]{:S(2)}, u32[]{:S(2)}) async-start(bf16[16,2,128,256]{3,2,1,0:T(8,128)(2,1)} %broadcast_in_dim.5), calls=%async_computation.2 | async-start | bytes 4194304 | tf_op jit(solution)/shard_map/all_to_all | solution.py:22
  182.5 5.3 %collective-permute-done.12 = bf16[4,2,2,128,128]{4,3,2,1,0:T(8,128)(2,1)S(1)} collective-permute-done((bf16[4,2,2,128,128]{4,3,2,1,0:T(8,128)(2,1)S(1)}, bf16[4,2,2,128,128]{4,3,2,1,0:T(8,128)(2,1)S(1)}, u32[]{:S(2)}, u32[]{:S(2)}) %collective-permute-start.12) | collective-permute-done | bytes 524320 | tf_op jit(solution)/shard_map/ppermute | solution.py:67
  189.0 1.9 collective-permute-start.13
  190.9 13.7 %collective-permute-done.13 = bf16[4,2,2,128,128]{4,3,2,1,0:T(8,128)(2,1)S(1)} collective-permute-done((bf16[4,2,2,128,128]{4,3,2,1,0:T(8,128)(2,1)S(1)}, bf16[4,2,2,128,128]{4,3,2,1,0:T(8,128)(2,1)S(1)}, u32[]{:S(2)}, u32[]{:S(2)}) %collective-permute-start.13) | collective-permute-done | bytes 524320 | tf_op jit(solution)/shard_map/ppermute | solution.py:67
  206.4 1.9 collective-permute-start.15
  208.3 3.9 %collective-permute-start.14 = (bf16[4,2,2,128,128]{4,3,2,1,0:T(8,128)(2,1)S(1)}, bf16[4,2,2,128,128]{4,3,2,1,0:T(8,128)(2,1)S(1)}, u32[]{:S(2)}, u32[]{:S(2)}) collective-permute-start(bf16[4,2,2,128,128]{4,3,2,1,0:T(8,128)(2,1)S(1)} %get-tuple-element.18), channel_id=1, source_target_pairs={{0,4},{1,5},{2,6},{3,7},{4,8},{5,9},{6,10},{7,11},{8,12},{9,13},{1... | collective-permute-start | bytes 1572872 | tf_op jit(solution)/shard_map/ppermute | solution.py:67
  212.2 7.7 %collective-permute-done.15 = bf16[4,2,2,128,128]{4,3,2,1,0:T(8,128)(2,1)S(1)} collective-permute-done((bf16[4,2,2,128,128]{4,3,2,1,0:T(8,128)(2,1)S(1)}, bf16[4,2,2,128,128]{4,3,2,1,0:T(8,128)(2,1)S(1)}, u32[]{:S(2)}, u32[]{:S(2)}) %collective-permute-start.15) | collective-permute-done | bytes 524320 | tf_op jit(solution)/shard_map/ppermute | solution.py:72
  221.2 3.4 %collective-permute-start.16 = (bf16[4,2,2,128,128]{4,3,2,1,0:T(8,128)(2,1)S(1)}, bf16[4,2,2,128,128]{4,3,2,1,0:T(8,128)(2,1)S(1)}, u32[]{:S(2)}, u32[]{:S(2)}) collective-permute-start(bf16[4,2,2,128,128]{4,3,2,1,0:T(8,128)(2,1)S(1)} %fusion.5), channel_id=1, source_target_pairs={{0,28},{1,29},{2,30},{3,31},{4,0},{5,1},{6,2},{7,3},{8,4},{9,5},{1... | collective-permute-start | bytes 1572872 | tf_op jit(solution)/shard_map/ppermute | solution.py:72
  224.6 9.2 %collective-permute-done.16 = bf16[4,2,2,128,128]{4,3,2,1,0:T(8,128)(2,1)S(1)} collective-permute-done((bf16[4,2,2,128,128]{4,3,2,1,0:T(8,128)(2,1)S(1)}, bf16[4,2,2,128,128]{4,3,2,1,0:T(8,128)(2,1)S(1)}, u32[]{:S(2)}, u32[]{:S(2)}) %collective-permute-start.16) | collective-permute-done | bytes 524320 | tf_op jit(solution)/shard_map/ppermute | solution.py:72
  235.1 4.7 %collective-permute-start.17 = (bf16[2,2,128,128]{3,2,1,0:T(8,128)(2,1)S(1)}, bf16[2,2,128,128]{3,2,1,0:T(8,128)(2,1)S(1)}, u32[]{:S(2)}, u32[]{:S(2)}) collective-permute-start(bf16[2,2,128,128]{3,2,1,0:T(8,128)(2,1)S(1)} %get-tuple-element.28), channel_id=1, source_target_pairs={{0,3},{1,0},{2,1},{3,2},{4,7},{5,4},{6,5},{7,6},{8,11},{9,8},{10,9... | collective-permute-start | bytes 393224 | tf_op jit(solution)/shard_map/ppermute | solution.py:82
  239.8 3.9 %collective-permute-start.18 = (bf16[2,2,128,128]{3,2,1,0:T(8,128)(2,1)S(1)}, bf16[2,2,128,128]{3,2,1,0:T(8,128)(2,1)S(1)}, u32[]{:S(2)}, u32[]{:S(2)}) collective-permute-start(bf16[2,2,128,128]{3,2,1,0:T(8,128)(2,1)S(1)} %get-tuple-element.30), channel_id=1, source_target_pairs={{0,2},{1,3},{2,0},{3,1},{4,6},{5,7},{6,4},{7,5},{8,10},{9,11},{10,... | collective-permute-start | bytes 393224 | tf_op jit(solution)/shard_map/ppermute | solution.py:82
  243.7 3.3 %collective-permute-start.19 = (bf16[2,2,128,128]{3,2,1,0:T(8,128)(2,1)S(1)}, bf16[2,2,128,128]{3,2,1,0:T(8,128)(2,1)S(1)}, u32[]{:S(2)}, u32[]{:S(2)}) collective-permute-start(bf16[2,2,128,128]{3,2,1,0:T(8,128)(2,1)S(1)} %get-tuple-element.29), channel_id=1, source_target_pairs={{0,1},{1,2},{2,3},{3,0},{4,5},{5,6},{6,7},{7,4},{8,9},{9,10},{10,1... | collective-permute-start | bytes 393224 | tf_op jit(solution)/shard_map/ppermute | solution.py:82
  247.0 2.2 collective-permute-done.17
  249.1 2.6 collective-permute-done.18
  251.7 2.1 collective-permute-done.19
  254.6 2.3 copy.71
  (90 shorter events, 38.6 us)
Async XLA Ops:
  0.6 51.4 %copy-start = (s32[64]{0:T(128)S(1)}, s32[64]{0:T(128)}, u32[]{:S(2)}) copy-start(s32[64]{0:T(128)} %param.9) | copy-start | bytes 772
  1.5 27.6 %collective-permute-start = (bf16[2,2,128,128]{3,2,1,0:T(8,128)(2,1)S(1)}, bf16[2,2,128,128]{3,2,1,0:T(8,128)(2,1)S(1)}, u32[]{:S(2)}, u32[]{:S(2)}) collective-permute-start(bf16[2,2,128,128]{3,2,1,0:T(8,128)(2,1)S(1)} %get-tuple-element.34), channel_id=1, source_target_pairs={{0,1},{1,2},{2,3},{3,0},{4,5},{5,6},{6,7},{7,4},{8,9},{9,10},{10,1... | collective-permute-start | bytes 393224 | tf_op jit(solution)/shard_map/ppermute | solution.py:42
  7.6 21.5 %collective-permute-start.1 = (bf16[2,2,128,128]{3,2,1,0:T(8,128)(2,1)S(1)}, bf16[2,2,128,128]{3,2,1,0:T(8,128)(2,1)S(1)}, u32[]{:S(2)}, u32[]{:S(2)}) collective-permute-start(bf16[2,2,128,128]{3,2,1,0:T(8,128)(2,1)S(1)} %get-tuple-element.34), channel_id=1, source_target_pairs={{0,2},{1,3},{2,0},{3,1},{4,6},{5,7},{6,4},{7,5},{8,10},{9,11},{10,... | collective-permute-start | bytes 393224 | tf_op jit(solution)/shard_map/ppermute | solution.py:42
  16.8 12.6 %collective-permute-start.2 = (bf16[2,2,128,128]{3,2,1,0:T(8,128)(2,1)S(1)}, bf16[2,2,128,128]{3,2,1,0:T(8,128)(2,1)S(1)}, u32[]{:S(2)}, u32[]{:S(2)}) collective-permute-start(bf16[2,2,128,128]{3,2,1,0:T(8,128)(2,1)S(1)} %get-tuple-element.34), channel_id=1, source_target_pairs={{0,3},{1,0},{2,1},{3,2},{4,7},{5,4},{6,5},{7,6},{8,11},{9,8},{10,9... | collective-permute-start | bytes 393224 | tf_op jit(solution)/shard_map/ppermute | solution.py:42
  23.3 43.7 %copy-start.2 = (s32[64]{0:T(128)S(1)}, s32[64]{0:T(128)}, u32[]{:S(2)}) copy-start(s32[64]{0:T(128)} %param.11) | copy-start | bytes 772
  23.3 87.2 %all-to-all-start = ((bf16[16,2,128,256]{2,3,1,0:T(8,128)(2,1)}), bf16[16,2,128,256]{2,3,1,0:T(8,128)(2,1)}, u32[]{:S(2)}, u32[]{:S(2)}) async-start(bf16[16,2,128,256]{2,3,1,0:T(8,128)(2,1)} %broadcast_in_dim.4), calls=%async_computation | async-start | bytes 4194304 | tf_op jit(solution)/shard_map/all_to_all | solution.py:22
  29.4 17.5 %collective-permute-start.3 = (bf16[4,2,2,128,128]{4,3,2,1,0:T(8,128)(2,1)S(1)}, bf16[4,2,2,128,128]{4,3,2,1,0:T(8,128)(2,1)S(1)}, u32[]{:S(2)}, u32[]{:S(2)}) collective-permute-start(bf16[4,2,2,128,128]{4,3,2,1,0:T(8,128)(2,1)S(1)} %pad_maximum_fusion.1), channel_id=1, source_target_pairs={{0,4},{1,5},{2,6},{3,7},{4,8},{5,9},{6,10},{7,11},{8,12},{9,13},{1... | collective-permute-start | bytes 1572872 | tf_op jit(solution)/shard_map/ppermute | solution.py:48
  32.9 15.5 %collective-permute-start.4 = (bf16[4,2,2,128,128]{4,3,2,1,0:T(8,128)(2,1)S(1)}, bf16[4,2,2,128,128]{4,3,2,1,0:T(8,128)(2,1)S(1)}, u32[]{:S(2)}, u32[]{:S(2)}) collective-permute-start(bf16[4,2,2,128,128]{4,3,2,1,0:T(8,128)(2,1)S(1)} %pad_maximum_fusion.1), channel_id=1, source_target_pairs={{0,28},{1,29},{2,30},{3,31},{4,0},{5,1},{6,2},{7,3},{8,4},{9,5},{1... | collective-permute-start | bytes 1572872 | tf_op jit(solution)/shard_map/ppermute | solution.py:51
  48.4 16.6 %collective-permute-start.5 = (bf16[4,2,2,128,128]{4,3,2,1,0:T(8,128)(2,1)S(1)}, bf16[4,2,2,128,128]{4,3,2,1,0:T(8,128)(2,1)S(1)}, u32[]{:S(2)}, u32[]{:S(2)}) collective-permute-start(bf16[4,2,2,128,128]{4,3,2,1,0:T(8,128)(2,1)S(1)} %collective-permute-done.3), channel_id=1, source_target_pairs={{0,4},{1,5},{2,6},{3,7},{4,8},{5,9},{6,10},{7,11},{8,12},{9,13},{1... | collective-permute-start | bytes 1572872 | tf_op jit(solution)/shard_map/ppermute | solution.py:48
  65.0 15.6 %collective-permute-start.6 = (bf16[4,2,2,128,128]{4,3,2,1,0:T(8,128)(2,1)S(1)}, bf16[4,2,2,128,128]{4,3,2,1,0:T(8,128)(2,1)S(1)}, u32[]{:S(2)}, u32[]{:S(2)}) collective-permute-start(bf16[4,2,2,128,128]{4,3,2,1,0:T(8,128)(2,1)S(1)} %collective-permute-done.5), channel_id=1, source_target_pairs={{0,4},{1,5},{2,6},{3,7},{4,8},{5,9},{6,10},{7,11},{8,12},{9,13},{1... | collective-permute-start | bytes 1572872 | tf_op jit(solution)/shard_map/ppermute | solution.py:48
  67.9 14.8 %collective-permute-start.8 = (bf16[4,2,2,128,128]{4,3,2,1,0:T(8,128)(2,1)S(1)}, bf16[4,2,2,128,128]{4,3,2,1,0:T(8,128)(2,1)S(1)}, u32[]{:S(2)}, u32[]{:S(2)}) collective-permute-start(bf16[4,2,2,128,128]{4,3,2,1,0:T(8,128)(2,1)S(1)} %collective-permute-done.4), channel_id=1, source_target_pairs={{0,28},{1,29},{2,30},{3,31},{4,0},{5,1},{6,2},{7,3},{8,4},{9,5},{1... | collective-permute-start | bytes 1572872 | tf_op jit(solution)/shard_map/ppermute | solution.py:51
  80.6 14.6 %collective-permute-start.7 = (bf16[4,2,2,128,128]{4,3,2,1,0:T(8,128)(2,1)S(1)}, bf16[4,2,2,128,128]{4,3,2,1,0:T(8,128)(2,1)S(1)}, u32[]{:S(2)}, u32[]{:S(2)}) collective-permute-start(bf16[4,2,2,128,128]{4,3,2,1,0:T(8,128)(2,1)S(1)} %collective-permute-done.6), channel_id=1, source_target_pairs={{0,4},{1,5},{2,6},{3,7},{4,8},{5,9},{6,10},{7,11},{8,12},{9,13},{1... | collective-permute-start | bytes 1572872 | tf_op jit(solution)/shard_map/ppermute | solution.py:48
  82.7 14.4 %collective-permute-start.9 = (bf16[4,2,2,128,128]{4,3,2,1,0:T(8,128)(2,1)S(1)}, bf16[4,2,2,128,128]{4,3,2,1,0:T(8,128)(2,1)S(1)}, u32[]{:S(2)}, u32[]{:S(2)}) collective-permute-start(bf16[4,2,2,128,128]{4,3,2,1,0:T(8,128)(2,1)S(1)} %collective-permute-done.8), channel_id=1, source_target_pairs={{0,28},{1,29},{2,30},{3,31},{4,0},{5,1},{6,2},{7,3},{8,4},{9,5},{1... | collective-permute-start | bytes 1572872 | tf_op jit(solution)/shard_map/ppermute | solution.py:51
  99.0 4.6 %copy-start.3 = (bf16[1,8,4,2,128,128]{5,4,3,0,2,1:T(8,128)(2,1)}, bf16[1,8,4,2,128,128]{5,4,3,0,2,1:T(8,128)(2,1)S(1)}, u32[]{:S(2)}) copy-start(bf16[1,8,4,2,128,128]{5,4,3,0,2,1:T(8,128)(2,1)S(1)} %get-tuple-element.23) | copy-start | bytes 6291460
  121.9 3.2 %copy-start.6 = (bf16[8,8,128,128]{2,1,0,3:T(8,128)(2,1)S(1)}, bf16[8,8,128,128]{2,1,0,3:T(8,128)(2,1)}, u32[]{:S(2)}) copy-start(bf16[8,8,128,128]{2,1,0,3:T(8,128)(2,1)} %copy.64) | copy-start | bytes 6291460
  121.9 3.2 %copy-start.9 = (f32[128,8,128]{0,2,1:T(8,128)S(1)}, f32[128,8,128]{0,2,1:T(8,128)}, u32[]{:S(2)}) copy-start(f32[128,8,128]{0,2,1:T(8,128)} %convolution_bitcast_fusion) | copy-start | bytes 1572868
  127.5 1.6 copy-start.5
  133.5 39.6 %all-to-all-start.1 = ((bf16[16,2,128,256]{2,3,1,0:T(8,128)(2,1)}), bf16[16,2,128,256]{2,3,1,0:T(8,128)(2,1)}, u32[]{:S(2)}, u32[]{:S(2)}) async-start(bf16[16,2,128,256]{2,3,1,0:T(8,128)(2,1)} %bitcast.178), calls=%async_computation.1 | async-start | bytes 4194304 | tf_op jit(solution)/shard_map/all_to_all | solution.py:26
  147.1 4.1 %copy-start.7 = (bf16[8,8,128,128]{2,3,1,0:T(8,128)(2,1)S(1)}, bf16[8,8,128,128]{2,3,1,0:T(8,128)(2,1)}, u32[]{:S(2)}) copy-start(bf16[8,8,128,128]{2,3,1,0:T(8,128)(2,1)} %copy.54) | copy-start | bytes 6291460
  151.1 1.6 copy-start.8
  153.1 17.9 %copy-start.4 = (bf16[8,4,2,2,128,128]{5,4,3,2,1,0:T(8,128)(2,1)}, bf16[8,4,2,2,128,128]{5,4,3,2,1,0:T(8,128)(2,1)S(1)}, u32[]{:S(2)}) copy-start(bf16[8,4,2,2,128,128]{5,4,3,2,1,0:T(8,128)(2,1)S(1)} %maximum_bitcast_fusion) | copy-start | bytes 12582916
  153.2 17.8 %collective-permute-start.11 = (bf16[4,2,2,128,128]{4,3,2,1,0:T(8,128)(2,1)S(1)}, bf16[4,2,2,128,128]{4,3,2,1,0:T(8,128)(2,1)S(1)}, u32[]{:S(2)}, u32[]{:S(2)}) collective-permute-start(bf16[4,2,2,128,128]{4,3,2,1,0:T(8,128)(2,1)S(1)} %get-tuple-element.20), channel_id=1, source_target_pairs={{0,4},{1,5},{2,6},{3,7},{4,8},{5,9},{6,10},{7,11},{8,12},{9,13},{1... | collective-permute-start | bytes 1572872 | tf_op jit(solution)/shard_map/ppermute | solution.py:67
  155.9 19.1 %collective-permute-start.10 = (bf16[4,2,2,128,128]{4,3,2,1,0:T(8,128)(2,1)S(1)}, bf16[4,2,2,128,128]{4,3,2,1,0:T(8,128)(2,1)}, u32[]{:S(2)}, u32[]{:S(2)}) collective-permute-start(bf16[4,2,2,128,128]{4,3,2,1,0:T(8,128)(2,1)S(1)} %get-tuple-element.21), channel_id=1, source_target_pairs={{0,28},{1,29},{2,30},{3,31},{4,0},{5,1},{6,2},{7,3},{8,4},{9,5},{1... | collective-permute-start | bytes 1572872 | tf_op jit(solution)/shard_map/ppermute | solution.py:72
  171.2 16.6 %collective-permute-start.12 = (bf16[4,2,2,128,128]{4,3,2,1,0:T(8,128)(2,1)S(1)}, bf16[4,2,2,128,128]{4,3,2,1,0:T(8,128)(2,1)S(1)}, u32[]{:S(2)}, u32[]{:S(2)}) collective-permute-start(bf16[4,2,2,128,128]{4,3,2,1,0:T(8,128)(2,1)S(1)} %fusion.6), channel_id=1, source_target_pairs={{0,4},{1,5},{2,6},{3,7},{4,8},{5,9},{6,10},{7,11},{8,12},{9,13},{1... | collective-permute-start | bytes 1572872 | tf_op jit(solution)/shard_map/ppermute | solution.py:67
  176.8 77.8 %all-to-all-start.2 = ((bf16[16,2,128,256]{3,2,1,0:T(8,128)(2,1)}), bf16[16,2,128,256]{3,2,1,0:T(8,128)(2,1)S(1)}, u32[]{:S(2)}, u32[]{:S(2)}) async-start(bf16[16,2,128,256]{3,2,1,0:T(8,128)(2,1)} %broadcast_in_dim.5), calls=%async_computation.2 | async-start | bytes 4194304 | tf_op jit(solution)/shard_map/all_to_all | solution.py:22
  189.0 15.7 %collective-permute-start.13 = (bf16[4,2,2,128,128]{4,3,2,1,0:T(8,128)(2,1)S(1)}, bf16[4,2,2,128,128]{4,3,2,1,0:T(8,128)(2,1)S(1)}, u32[]{:S(2)}, u32[]{:S(2)}) collective-permute-start(bf16[4,2,2,128,128]{4,3,2,1,0:T(8,128)(2,1)S(1)} %fusion.7), channel_id=1, source_target_pairs={{0,4},{1,5},{2,6},{3,7},{4,8},{5,9},{6,10},{7,11},{8,12},{9,13},{1... | collective-permute-start | bytes 1572872 | tf_op jit(solution)/shard_map/ppermute | solution.py:67
  206.4 13.5 %collective-permute-start.15 = (bf16[4,2,2,128,128]{4,3,2,1,0:T(8,128)(2,1)S(1)}, bf16[4,2,2,128,128]{4,3,2,1,0:T(8,128)(2,1)S(1)}, u32[]{:S(2)}, u32[]{:S(2)}) collective-permute-start(bf16[4,2,2,128,128]{4,3,2,1,0:T(8,128)(2,1)S(1)} %get-tuple-element.19), channel_id=1, source_target_pairs={{0,28},{1,29},{2,30},{3,31},{4,0},{5,1},{6,2},{7,3},{8,4},{9,5},{1... | collective-permute-start | bytes 1572872 | tf_op jit(solution)/shard_map/ppermute | solution.py:72
  208.3 16.3 %collective-permute-start.14 = (bf16[4,2,2,128,128]{4,3,2,1,0:T(8,128)(2,1)S(1)}, bf16[4,2,2,128,128]{4,3,2,1,0:T(8,128)(2,1)S(1)}, u32[]{:S(2)}, u32[]{:S(2)}) collective-permute-start(bf16[4,2,2,128,128]{4,3,2,1,0:T(8,128)(2,1)S(1)} %get-tuple-element.18), channel_id=1, source_target_pairs={{0,4},{1,5},{2,6},{3,7},{4,8},{5,9},{6,10},{7,11},{8,12},{9,13},{1... | collective-permute-start | bytes 1572872 | tf_op jit(solution)/shard_map/ppermute | solution.py:67
  221.2 12.6 %collective-permute-start.16 = (bf16[4,2,2,128,128]{4,3,2,1,0:T(8,128)(2,1)S(1)}, bf16[4,2,2,128,128]{4,3,2,1,0:T(8,128)(2,1)S(1)}, u32[]{:S(2)}, u32[]{:S(2)}) collective-permute-start(bf16[4,2,2,128,128]{4,3,2,1,0:T(8,128)(2,1)S(1)} %fusion.5), channel_id=1, source_target_pairs={{0,28},{1,29},{2,30},{3,31},{4,0},{5,1},{6,2},{7,3},{8,4},{9,5},{1... | collective-permute-start | bytes 1572872 | tf_op jit(solution)/shard_map/ppermute | solution.py:72
  235.1 14.0 %collective-permute-start.17 = (bf16[2,2,128,128]{3,2,1,0:T(8,128)(2,1)S(1)}, bf16[2,2,128,128]{3,2,1,0:T(8,128)(2,1)S(1)}, u32[]{:S(2)}, u32[]{:S(2)}) collective-permute-start(bf16[2,2,128,128]{3,2,1,0:T(8,128)(2,1)S(1)} %get-tuple-element.28), channel_id=1, source_target_pairs={{0,3},{1,0},{2,1},{3,2},{4,7},{5,4},{6,5},{7,6},{8,11},{9,8},{10,9... | collective-permute-start | bytes 393224 | tf_op jit(solution)/shard_map/ppermute | solution.py:82
  239.8 11.9 %collective-permute-start.18 = (bf16[2,2,128,128]{3,2,1,0:T(8,128)(2,1)S(1)}, bf16[2,2,128,128]{3,2,1,0:T(8,128)(2,1)S(1)}, u32[]{:S(2)}, u32[]{:S(2)}) collective-permute-start(bf16[2,2,128,128]{3,2,1,0:T(8,128)(2,1)S(1)} %get-tuple-element.30), channel_id=1, source_target_pairs={{0,2},{1,3},{2,0},{3,1},{4,6},{5,7},{6,4},{7,5},{8,10},{9,11},{10,... | collective-permute-start | bytes 393224 | tf_op jit(solution)/shard_map/ppermute | solution.py:82
  243.7 10.1 %collective-permute-start.19 = (bf16[2,2,128,128]{3,2,1,0:T(8,128)(2,1)S(1)}, bf16[2,2,128,128]{3,2,1,0:T(8,128)(2,1)S(1)}, u32[]{:S(2)}, u32[]{:S(2)}) collective-permute-start(bf16[2,2,128,128]{3,2,1,0:T(8,128)(2,1)S(1)} %get-tuple-element.29), channel_id=1, source_target_pairs={{0,1},{1,2},{2,3},{3,0},{4,5},{5,6},{6,7},{7,4},{8,9},{9,10},{10,1... | collective-permute-start | bytes 393224 | tf_op jit(solution)/shard_map/ppermute | solution.py:82
  258.6 2.6 %copy-start.1 = (s32[64]{0:T(128)S(1)}, s32[64]{0:T(128)}, u32[]{:S(2)}) copy-start(s32[64]{0:T(128)} %param.9) | copy-start | bytes 772
